TPU v7x, 32 devices: a whole 2x2x4 slice. The times are simulated.
32 devices in a mesh: ctx: 4 (over y, x), tp: 8 (over z, core).
Axes of the slice: x: 2, y: 2, z: 4, core: 2. Of those that a mesh axis runs over, the one named last changes fastest.
Arguments:
- resid: bfloat16 [1024, 4096], P('ctx', 'tp'), may hold values from -6 to 6
- attn_gain: bfloat16 [4096], replicated, may hold values from 0.5 to 1.5
- mlp_gain: bfloat16 [4096], replicated, may hold values from 0.5 to 1.5
- w_query: bfloat16 [4096, 4096], P(None, 'tp'), may hold values from -0.09375 to 0.09375
- w_kv: bfloat16 [4096, 1024], P(None, 'tp'), may hold values from -0.09375 to 0.09375
- w_out: bfloat16 [4096, 4096], P('tp'), may hold values from -0.09375 to 0.09375
- w_gate: bfloat16 [4096, 11008], P(None, 'tp'), may hold values from -0.09375 to 0.09375
- w_up: bfloat16 [4096, 11008], P(None, 'tp'), may hold values from -0.09375 to 0.09375
- w_down: bfloat16 [11008, 4096], P('tp'), may hold values from -0.0546875 to 0.0546875
- kv_cache: bfloat16 [32, 128, 1024], P('ctx'), may hold values from -70 to 70
- cache_len: int32 [4], replicated, may hold values from 1 to 2048
- span_len: int32 [4], replicated, may hold values from 1 to 256
- slot_req: int32 [32], P('ctx'), may hold values from 0 to 4, as said below
- slot_blk: int32 [32], P('ctx'), may hold values from 0 to 15, as said below
Outputs:
- layer_out: bfloat16 [1024, 4096], P('ctx', 'tp')
- new_kv: bfloat16 [1024, 1024], P('ctx', 'tp')
Inputs may be any that keep to these rules, and one draw needn't show every extreme that they name: `slot_req`: each request r holds ceil(cache_len[r] / 128) blocks, and each of its blocks stands in exactly one slot; every other slot is empty. `slot_blk`: block numbers of live slots are below their request's block count; empty slots carry 0.
All inputs are finite; a program needn't handle non-finite values.
Results may differ from a plain program's by a relative error of at most 0.035.
Values may be sent and summed in bfloat16 or wider, within the bound.
No kernel may reach another device: no remote copies, remote signals or barrier semaphores. Data moves between devices by JAX's collectives and lax.ppermute only.
A program may use at most 128 MiB of HBM per device.

v0:
```python
import jax
import jax.numpy as jnp
from jax import lax
from jax.sharding import PartitionSpec as P

HQ = 32
KVH = 4
HD = 128
BLK = 128


THETA = 5000000.0
EPS = 1e-05
NEG = -1e30


def rms_norm(values, gain):
    wide = values.astype(jnp.float32)
    factor = lax.rsqrt(jnp.mean(wide * wide, axis=-1, keepdims=True) + EPS)
    return (wide * factor * gain.astype(jnp.float32)).astype(jnp.bfloat16)


def rotate(vectors, positions):
    width = vectors.shape[-1]
    half = width // 2
    freqs = THETA ** (-(jnp.arange(half, dtype=jnp.float32) * 2.0 / width))
    angles = positions.astype(jnp.float32)[:, None] * freqs[None, :]
    cosine = jnp.cos(angles)[:, None, :]
    sine = jnp.sin(angles)[:, None, :]
    first = vectors[..., :half]
    second = vectors[..., half:]
    return jnp.concatenate(
        [first * cosine - second * sine, second * cosine + first * sine], axis=-1
    )


def combine(left, right):
    peak = jnp.maximum(left[0], right[0])
    left_f = jnp.exp(left[0] - peak)
    right_f = jnp.exp(right[0] - peak)
    return (
        peak,
        left[1] * left_f + right[1] * right_f,
        left[2] * left_f[..., None] + right[2] * right_f[..., None],
    )


def slot_partial(q_rows, keys, vals, valid):
    scores = jnp.einsum("chd,bd->hcb", q_rows, keys, preferred_element_type=jnp.float32) * HD ** (
        -0.5
    )
    peak = jnp.max(jnp.where(valid[None, None, :], scores, NEG), axis=2)
    weights = jnp.where(valid[None, None, :], jnp.exp(scores - peak[..., None]), 0.0)
    total = jnp.sum(weights, axis=2)
    summed = jnp.einsum(
        "hcb,bd->hcd", weights.astype(jnp.bfloat16), vals, preferred_element_type=jnp.float32
    )
    return (peak, total, summed)


def column_term(rows, weight):
    return lax.dot_general(
        weight, rows, (((0,), (1,)), ((), ())), preferred_element_type=jnp.float32
    )


def per_device(
    resid,
    attn_gain,
    mlp_gain,
    w_query,
    w_kv,
    w_out,
    w_gate,
    w_up,
    w_down,
    kv_cache,
    cache_len,
    span_len,
    slot_req,
    slot_blk,
):
    span_size = resid.shape[0]
    req_count = lax.axis_size("ctx")
    q_cols = w_query.shape[1]
    heads_dev = q_cols // HD
    ctx_rank = lax.axis_index("ctx")
    tp_rank = lax.axis_index("tp")
    group = tp_rank * heads_dev // (HQ // KVH)
    my_len = cache_len[ctx_rank]
    my_span = span_len[ctx_rank]
    offsets = jnp.arange(span_size, dtype=jnp.int32)
    positions = my_len + offsets
    live_rows = offsets < my_span
    full_resid = lax.all_gather(resid, "tp", axis=1, tiled=True)
    x_norm = rms_norm(full_resid, attn_gain)
    query = rotate(
        jnp.dot(x_norm, w_query, preferred_element_type=jnp.float32).reshape(
            span_size, heads_dev, HD
        ),
        positions,
    ).astype(jnp.bfloat16)
    kv_piece = jnp.dot(x_norm, w_kv, preferred_element_type=jnp.float32).astype(jnp.bfloat16)
    kv_width = kv_piece.shape[1]
    kv_all = lax.all_gather(kv_piece, "tp", axis=1, tiled=True)
    all_keys = rotate(
        kv_all[:, : KVH * HD].astype(jnp.float32).reshape(span_size, KVH, HD), positions
    ).astype(jnp.bfloat16)
    joined = jnp.concatenate([all_keys.reshape(span_size, KVH * HD), kv_all[:, KVH * HD :]], axis=1)
    mine = lax.dynamic_slice_in_dim(joined, tp_rank * kv_width, kv_width, 1)
    new_kv = jnp.where(live_rows[:, None], mine, jnp.zeros_like(mine))
    new_keys = lax.dynamic_index_in_dim(all_keys, group, 1, keepdims=False)
    new_vals = lax.dynamic_slice_in_dim(kv_all, KVH * HD + group * HD, HD, 1)
    q_all = lax.all_gather(query.reshape(span_size, q_cols), "ctx", axis=0, tiled=True).reshape(
        req_count, span_size, heads_dev, HD
    )
    cache_keys = lax.dynamic_slice_in_dim(kv_cache, group * HD, HD, 2)
    cache_vals = lax.dynamic_slice_in_dim(kv_cache, KVH * HD + group * HD, HD, 2)
    live = slot_req < req_count
    safe_req = jnp.where(live, slot_req, 0)
    key_pos = slot_blk[:, None] * BLK + jnp.arange(BLK, dtype=jnp.int32)[None, :]
    slot_valid = live[:, None] & (key_pos < cache_len[safe_req][:, None])
    q_slots = jnp.take(q_all, safe_req, axis=0)
    tops, totals, sums = jax.vmap(slot_partial)(q_slots, cache_keys, cache_vals, slot_valid)
    member = slot_req[:, None] == jnp.arange(req_count, dtype=jnp.int32)[None, :]
    req_top = jnp.max(jnp.where(member[:, :, None, None], tops[:, None], NEG), axis=0)
    factor = jnp.where(
        live[:, None, None], jnp.exp(tops - jnp.take(req_top, safe_req, axis=0)), 0.0
    )
    member_f = member.astype(jnp.float32)
    req_total = jnp.einsum(
        "sr,shc->rhc", member_f, factor * totals, precision=lax.Precision.HIGHEST
    )
    req_sum = jnp.einsum(
        "sr,shcd->rhcd", member_f, factor[..., None] * sums, precision=lax.Precision.HIGHEST
    )
    new_ok = (offsets[None, :] <= offsets[:, None]) & (offsets[None, :] < my_span)
    new_scores = jnp.einsum(
        "chd,jd->hcj", query, new_keys, preferred_element_type=jnp.float32
    ) * HD ** (-0.5)
    new_top = jnp.max(jnp.where(new_ok[None], new_scores, NEG), axis=2)
    new_weights = jnp.where(new_ok[None], jnp.exp(new_scores - new_top[..., None]), 0.0)
    new_total = jnp.sum(new_weights, axis=2)
    new_sum = jnp.einsum(
        "hcj,jd->hcd",
        new_weights.astype(jnp.bfloat16),
        new_vals,
        preferred_element_type=jnp.float32,
    )
    own_req = (jnp.arange(req_count, dtype=jnp.int32) == ctx_rank)[:, None, None]
    local_state = combine(
        (req_top, req_total, req_sum),
        (
            jnp.where(own_req, new_top[None], NEG),
            jnp.where(own_req, new_total[None], 0.0),
            jnp.where(own_req[..., None], new_sum[None], 0.0),
        ),
    )
    swapped = (
        lax.all_to_all(
            local_state[0][:, None].astype(jnp.bfloat16),
            "ctx",
            split_axis=0,
            concat_axis=1,
            tiled=True,
        ).astype(jnp.float32),
        lax.all_to_all(
            local_state[1][:, None].astype(jnp.bfloat16),
            "ctx",
            split_axis=0,
            concat_axis=1,
            tiled=True,
        ).astype(jnp.float32),
        lax.all_to_all(
            local_state[2][:, None].astype(jnp.bfloat16),
            "ctx",
            split_axis=0,
            concat_axis=1,
            tiled=True,
        ).astype(jnp.float32),
    )
    peaks = swapped[0][0]
    best = jnp.max(peaks, axis=0)
    scaled = jnp.exp(peaks - best[None])
    final_total = jnp.sum(swapped[1][0] * scaled, axis=0)
    final_sum = jnp.sum(swapped[2][0] * scaled[..., None], axis=0)
    attn_rows = (
        (final_sum / final_total[..., None])
        .transpose(1, 0, 2)
        .reshape(span_size, q_cols)
        .astype(jnp.bfloat16)
    )
    head_sum = lax.psum_scatter(
        column_term(attn_rows, w_out).astype(jnp.bfloat16), "tp", scatter_dimension=0, tiled=True
    ).astype(jnp.float32)
    mid = (resid.astype(jnp.float32) + head_sum.T).astype(jnp.bfloat16)
    full_mid = lax.all_gather(mid, "tp", axis=1, tiled=True)
    x_two = rms_norm(full_mid, mlp_gain)
    gate = jnp.dot(x_two, w_gate, preferred_element_type=jnp.float32)
    up_part = jnp.dot(x_two, w_up, preferred_element_type=jnp.float32)
    hidden = (jax.nn.silu(gate) * up_part).astype(jnp.bfloat16)
    down_sum = lax.psum_scatter(
        column_term(hidden, w_down).astype(jnp.bfloat16), "tp", scatter_dimension=0, tiled=True
    ).astype(jnp.float32)
    layer_out = (mid.astype(jnp.float32) + down_sum.T).astype(jnp.bfloat16)
    layer_out = jnp.where(live_rows[:, None], layer_out, jnp.zeros_like(layer_out))
    return (layer_out, new_kv)


def solution(mesh):
    return jax.shard_map(
        per_device,
        mesh=mesh,
        in_specs=(
            P("ctx", "tp"),
            P(),
            P(),
            P(None, "tp"),
            P(None, "tp"),
            P("tp", None),
            P(None, "tp"),
            P(None, "tp"),
            P("tp", None),
            P("ctx", None, None),
            P(),
            P(),
            P("ctx"),
            P("ctx"),
        ),
        out_specs=(P("ctx", "tp"), P("ctx", "tp")),
        check_vma=False,
    )
```

profile of v0, /device:TPU:0, one launch (start us, length us, event | category | flops | bytes accessed | tf_op | source)
XLA Modules:
  0.0 302.9 jit_solution(10670920059659276076)
XLA Ops:
  7.2 0.7 all-gather.4.cloned.1.call-update
  8.0 1.2 dynamic_slice.24
  9.2 1.2 dynamic_slice.22
  10.5 0.7 compare_and_fusion
  11.1 1.3 gather_fusion
  12.4 0.7 convert_element_type.142
  13.2 0.7 iota_compare_fusion.2
  13.8 0.7 add_convert_fusion.1
  14.5 0.5 multiply_cosine_fusion
  15.0 26.4 %all-gather.4.cloned.1.call-done = bf16[256,4096]{1,0:T(8,128)(2,1)} async-done(((bf16[256,512]{1,0:T(8,128)(2,1)}), bf16[256,4096]{1,0:T(8,128)(2,1)}) %all-gather.4.cloned.1.call-update) | async-done | bytes 2097168 | tf_op jit(solution)/shard_map/all_gather | solution.py:95
  41.5 2.1 fusion.2
  43.5 4.1 %fusion.42 = f32[256,512]{1,0:T(8,128)S(1)} fusion(bf16[4096,512]{1,0:T(8,128)(2,1)} %param.17, bf16[256,4096]{1,0:T(8,128)(2,1)} %all-gather.4.cloned.1.call-done, f32[4096]{0:T(1024)S(1)} %convert_element_type.142, f32[256]{0:T(256)S(1)} %add_rsqrt_fusion.1), kind=kOutput, calls=%fused_computation.53 | convolution fusion | flops 1077936128 | bytes 6833152 | tf_op jit(solution)/shard_map/dot_general | solution.py:98
  47.9 2.7 convolution_convert_fusion.2
  50.5 13.9 %all_gather.14 = bf16[256,1024]{1,0:T(8,128)(2,1)S(1)} all-gather(bf16[256,128]{1,0:T(8,128)(2,1)S(1)} %convolution_convert_fusion.2), channel_id=1, replica_groups=mesh['ctx'=4,'tp'=8] {'tp'}, dimensions={1}, use_global_device_ids=true | all-gather | bytes 589824 | tf_op jit(solution)/shard_map/all_gather | solution.py:105
  64.4 1.3 fusion.86
  65.6 0.9 fusion.84
  66.6 1.2 reshape.294
  67.8 0.3 fusion.85
  68.1 1.5 multiply_subtract_fusion
  69.9 0.9 copy.84
  71.6 1.3 fusion.44
  72.9 23.1 %all-gather.6.cloned.1.call-done = bf16[1024,512]{0,1:T(8,128)(2,1)} async-done(((bf16[256,512]{0,1:T(8,128)(2,1)}), bf16[1024,512]{0,1:T(8,128)(2,1)}) %all-gather.6.cloned.1.call-update) | async-done | bytes 1048592 | tf_op jit(solution)/shard_map/all_gather | solution.py:114
  95.9 2.6 reshape.331
  98.6 1.7 copy.86
  100.3 2.1 gather_fusion.1
  102.4 4.7 %fusion.8 = (f32[8,4,256]{2,1,0:T(4,128)S(1)}, f32[8,128,256,4]{2,1,3,0:T(8,128)}) fusion(pred[8,128]{1,0:T(8,128)(4,1)S(1)} %fusion.71, bf16[8,256,4,128]{3,1,2,0:T(8,128)(2,1)} %gather_fusion.1, pred[8]{0:T(512)(128)(4,1)S(1)} %get-tuple-element.4, bf16[8,128,1024]{2,1,0:T(8,128)(2,1)S(1)} %copy-done, s32[]{:T(128)S(6)} %select_n.112), kind=kOutput, calls=%fused_computation.19 | convolution fusion | flops 272621568 | bytes 6587908 | tf_op jit(solution)/shard_map/vmap(chd,bd->hcb)/dot_general | solution.py:49
  107.2 0.6 gather_fusion.2
  107.8 0.7 fusion.70
  108.6 3.3 %fusion.13 = f32[8,4,256]{2,1,0:T(4,128)S(1)} fusion(f32[8,128,256,4]{2,1,3,0:T(8,128)} %get-tuple-element.26, f32[8,4,256]{2,1,0:T(4,128)S(1)} %get-tuple-element.25, pred[8,128]{1,0:T(8,128)(4,1)S(1)} %fusion.71), kind=kLoop, calls=%fused_computation.24 | loop fusion | flops 4186112 | bytes 4260864 | tf_op jit(solution)/shard_map/vmap()/reduce_sum | solution.py:54
  111.9 3.2 %all-to-all-start.1 = ((bf16[4,1,4,256]{3,2,1,0:T(4,128)(2,1)}), bf16[4,1,4,256]{3,2,1,0:T(4,128)(2,1)S(1)}, u32[]{:S(2)}, u32[]{:S(2)}) async-start(bf16[4,1,4,256]{3,2,1,0:T(4,128)(2,1)} %fusion.70), calls=%async_computation.1 | async-start | bytes 16384 | tf_op jit(solution)/shard_map/all_to_all | solution.py:160
  115.2 5.2 %convolution_multiply_fusion.1 = f32[8,4,256,128]{3,2,1,0:T(8,128)} fusion(f32[8,128,256,4]{2,1,3,0:T(8,128)} %get-tuple-element.26, f32[8,4,256]{2,1,0:T(4,128)S(1)} %get-tuple-element.25, f32[8,4,256]{2,1,0:T(4,128)S(1)} %get-tuple-element.3, pred[8,128]{1,0:T(8,128)(4,1)S(1)} %fusion.71, bf16[8,128,1024]{2,1,0:T(8,128)(2,1)S(1)} %copy-done, ...), kind=kOutput, calls=%fused_computation.28 | convolution fusion | flops 273678336 | bytes 8717316 | tf_op jit(solution)/shard_map/vmap(hcb,bd->hcd)/dot_general | solution.py:55
  121.0 0.6 copy.101
  121.6 4.2 %all-to-all-start.2 = ((bf16[4,1,4,256]{3,2,1,0:T(4,128)(2,1)}), bf16[4,1,4,256]{3,2,1,0:T(4,128)(2,1)S(1)}, u32[]{:S(2)}, u32[]{:S(2)}) async-start(bf16[4,1,4,256]{3,2,1,0:T(4,128)(2,1)} %copy.101), calls=%async_computation.2 | async-start | bytes 16384 | tf_op jit(solution)/shard_map/all_to_all | solution.py:167
  125.8 10.1 %fusion.27 = bf16[4,1,4,256,128]{4,0,3,2,1:T(4,128)(2,1)S(1)} fusion(f32[8,4,256,128]{3,2,1,0:T(8,128)} %convolution_multiply_fusion.1, f32[4,4,256]{0,2,1:T(8,128)S(1)} %copy.96, f32[4,256,128]{2,1,0:T(8,128)S(1)} %copy-done.5, f32[4,4,256]{0,2,1:T(8,128)S(1)} %copy.94, pred[4]{0:T(512)(128)(4,1)S(1)} %iota_compare_fusion.3, s32[8]{0:T(128)S(1)} %copy-done.7), kind=kOutput, calls=%fused_computation.39 | convolution fusion | flops 52953120 | bytes 5799972 | tf_op jit(solution)/shard_map/sr,shcd->rhcd/dot_general | solution.py:134
  135.9 1.2 copy.97
  137.0 4.2 %all-to-all-start = ((bf16[4,1,4,256,128]{4,3,2,1,0:T(8,128)(2,1)}), bf16[4,1,4,256,128]{4,3,2,1,0:T(8,128)(2,1)S(1)}, u32[]{:S(2)}, u32[]{:S(2)}) async-start(bf16[4,1,4,256,128]{4,3,2,1,0:T(8,128)(2,1)} %copy.97), calls=%async_computation | async-start | bytes 2097152 | tf_op jit(solution)/shard_map/all_to_all | solution.py:174
  141.3 12.7 %all-to-all-done = bf16[4,1,4,256,128]{4,3,2,1,0:T(8,128)(2,1)S(1)} async-done(((bf16[4,1,4,256,128]{4,3,2,1,0:T(8,128)(2,1)}), bf16[4,1,4,256,128]{4,3,2,1,0:T(8,128)(2,1)S(1)}, u32[]{:S(2)}, u32[]{:S(2)}) %all-to-all-start) | async-done | bytes 1048608 | tf_op jit(solution)/shard_map/all_to_all | solution.py:174
  154.0 0.7 fusion.17
  155.2 4.9 %fusion.1 = bf16[4096,256]{0,1:T(8,128)(2,1)} fusion(bf16[256,512]{0,1:T(8,128)(2,1)S(1)} %bitcast.108, bf16[512,4096]{1,0:T(8,128)(2,1)} %param.19), kind=kOutput, calls=%fused_computation.10 | convolution fusion | flops 1074790400 | bytes 6553600 | tf_op jit(solution)/shard_map/dot_general | solution.py:62
  160.1 36.0 %reduce-scatter.3.cloned.1.call-done = bf16[512,256]{0,1:T(8,128)(2,1)} async-done(((bf16[4096,256]{0,1:T(8,128)(2,1)}), bf16[512,256]{0,1:T(8,128)(2,1)}) %reduce-scatter.3.cloned.1.call-update) | async-done | bytes 262160 | tf_op jit(solution)/shard_map/reduce_scatter | solution.py:193
  196.1 1.7 fusion.47
  197.9 27.8 %all-gather.8.cloned.1.call-done = bf16[256,4096]{1,0:T(8,128)(2,1)} async-done(((bf16[256,512]{1,0:T(8,128)(2,1)}), bf16[256,4096]{1,0:T(8,128)(2,1)}) %all-gather.8.cloned.1.call-update) | async-done | bytes 2097168 | tf_op jit(solution)/shard_map/all_gather | solution.py:197
  225.7 2.1 fusion.5
  227.8 9.2 %fusion.39 = f32[256,1376]{0,1:T(8,128)} fusion(bf16[4096,1376]{0,1:T(8,128)(2,1)} %param.20, bf16[256,4096]{1,0:T(8,128)(2,1)} %all-gather.8.cloned.1.call-done, f32[4096]{0:T(1024)S(1)} %convert_element_type.169, f32[256]{0:T(256)S(1)} %add_rsqrt_fusion), kind=kOutput, calls=%fused_computation.52 | convolution fusion | flops 2889875456 | bytes 14795776 | tf_op jit(solution)/shard_map/dot_general | solution.py:199
  237.0 22.2 %fusion = bf16[4096,256]{0,1:T(8,128)(2,1)} fusion(bf16[1376,4096]{1,0:T(8,128)(2,1)} %param.22, bf16[4096,1376]{0,1:T(8,128)(2,1)} %param.21, f32[256,1376]{0,1:T(8,128)} %fusion.39, bf16[256,4096]{1,0:T(8,128)(2,1)} %all-gather.8.cloned.1.call-done, f32[4096]{0:T(1024)S(1)} %convert_element_type.169, f32[256]{0:T(256)S(1)} %add_rsqrt_fusion), kind=kOutput, calls=%fused_computation.9 | convolution fusion | flops 5778718720 | bytes 28165120 | tf_op jit(solution)/shard_map/dot_general | solution.py:62
  259.2 0.7 fusion.63
  260.0 34.7 %reduce-scatter.5.cloned.1.call-done = bf16[512,256]{0,1:T(8,128)(2,1)} async-done(((bf16[4096,256]{0,1:T(8,128)(2,1)}), bf16[512,256]{0,1:T(8,128)(2,1)}) %reduce-scatter.5.cloned.1.call-update) | async-done | bytes 262160 | tf_op jit(solution)/shard_map/reduce_scatter | solution.py:202
  294.7 1.8 fusion.52
  (56 shorter events, 2.9 us)
Async XLA Ops:
  7.2 95.3 %copy-start = (bf16[8,128,1024]{2,1,0:T(8,128)(2,1)S(1)}, bf16[8,128,1024]{2,1,0:T(8,128)(2,1)}, u32[]{:S(2)}) copy-start(bf16[8,128,1024]{2,1,0:T(8,128)(2,1)} %param.23) | copy-start | bytes 6291460
  7.2 34.3 %all-gather.4.cloned.1.call-start = ((), (), s32[]{:S(2)}) async-start(), calls=%async_computation.5 | async-start | bytes 2359296 | tf_op jit(solution)/shard_map/all_gather | solution.py:95
  7.9 88.0 %all-gather.6.cloned.1.call-start = ((), (), s32[]{:S(2)}) async-start(), calls=%async_computation.6 | async-start | bytes 1310720 | tf_op jit(solution)/shard_map/all_gather | solution.py:114
  67.8 3.0 copy-start.7
  67.8 3.0 %copy-start.8 = (s32[8]{0:T(128)S(1)}, s32[8]{0:T(128)}, u32[]{:S(2)}) copy-start(s32[8]{0:T(128)} %param.27) | copy-start | bytes 100
  111.9 9.7 %all-to-all-start.1 = ((bf16[4,1,4,256]{3,2,1,0:T(4,128)(2,1)}), bf16[4,1,4,256]{3,2,1,0:T(4,128)(2,1)S(1)}, u32[]{:S(2)}, u32[]{:S(2)}) async-start(bf16[4,1,4,256]{3,2,1,0:T(4,128)(2,1)} %fusion.70), calls=%async_computation.1 | async-start | bytes 16384 | tf_op jit(solution)/shard_map/all_to_all | solution.py:160
  115.2 10.6 %copy-start.5 = (f32[4,256,128]{2,1,0:T(8,128)S(1)}, f32[4,256,128]{2,1,0:T(8,128)}, u32[]{:S(2)}) copy-start(f32[4,256,128]{2,1,0:T(8,128)} %fusion.44) | copy-start | bytes 1572868
  121.6 15.4 %all-to-all-start.2 = ((bf16[4,1,4,256]{3,2,1,0:T(4,128)(2,1)}), bf16[4,1,4,256]{3,2,1,0:T(4,128)(2,1)S(1)}, u32[]{:S(2)}, u32[]{:S(2)}) async-start(bf16[4,1,4,256]{3,2,1,0:T(4,128)(2,1)} %copy.101), calls=%async_computation.2 | async-start | bytes 16384 | tf_op jit(solution)/shard_map/all_to_all | solution.py:167
  137.0 17.0 %all-to-all-start = ((bf16[4,1,4,256,128]{4,3,2,1,0:T(8,128)(2,1)}), bf16[4,1,4,256,128]{4,3,2,1,0:T(8,128)(2,1)S(1)}, u32[]{:S(2)}, u32[]{:S(2)}) async-start(bf16[4,1,4,256,128]{4,3,2,1,0:T(8,128)(2,1)} %copy.97), calls=%async_computation | async-start | bytes 2097152 | tf_op jit(solution)/shard_map/all_to_all | solution.py:174
  141.2 54.8 %reduce-scatter.3.cloned.1.call-start = ((), (), s32[]{:S(2)}) async-start(), calls=%async_computation.7 | async-start | bytes 2359296 | tf_op jit(solution)/shard_map/reduce_scatter | solution.py:193
  155.1 40.9 %copy-start.3 = (bf16[256,512]{1,0:T(8,128)(2,1)S(1)}, bf16[256,512]{1,0:T(8,128)(2,1)}, u32[]{:S(2)}) copy-start(bf16[256,512]{1,0:T(8,128)(2,1)} %param.14) | copy-start | bytes 786436
  155.1 42.7 %copy-start.6 = (bf16[4096]{0:T(1024)(128)(2,1)S(1)}, bf16[4096]{0:T(1024)(128)(2,1)}, u32[]{:S(2)}) copy-start(bf16[4096]{0:T(1024)(128)(2,1)} %param.16) | copy-start | bytes 24580
  160.0 65.7 %all-gather.8.cloned.1.call-start = ((), (), s32[]{:S(2)}) async-start(), calls=%async_computation.8 | async-start | bytes 2359296 | tf_op jit(solution)/shard_map/all_gather | solution.py:197
  197.8 96.8 %reduce-scatter.5.cloned.1.call-start = ((), (), s32[]{:S(2)}) async-start(), calls=%async_computation.9 | async-start | bytes 2359296 | tf_op jit(solution)/shard_map/reduce_scatter | solution.py:202
  237.0 22.3 %copy-start.4 = (bf16[256,512]{1,0:T(8,128)(2,1)S(1)}, bf16[256,512]{1,0:T(8,128)(2,1)}, u32[]{:S(2)}) copy-start(bf16[256,512]{1,0:T(8,128)(2,1)} %get-tuple-element.10) | copy-start | bytes 786436
  237.0 57.7 %copy-start.2 = (bf16[256,512]{1,0:T(8,128)(2,1)S(1)}, bf16[256,512]{1,0:T(8,128)(2,1)}, u32[]{:S(2)}) copy-start(bf16[256,512]{1,0:T(8,128)(2,1)} %fusion.47) | copy-start | bytes 786436
  237.0 59.4 %copy-start.1 = (bf16[8,128,1024]{2,1,0:T(8,128)(2,1)S(1)}, bf16[8,128,1024]{2,1,0:T(8,128)(2,1)}, u32[]{:S(2)}) copy-start(bf16[8,128,1024]{2,1,0:T(8,128)(2,1)} %param.23) | copy-start | bytes 6291460
Sparse Core Ops, SparseCore 0:
  9.6 31.7 all-gather.3
  70.9 24.9 all-gather.5
  160.2 35.8 reduce-scatter.2
  197.9 27.7 all-gather.7
  259.3 35.2 reduce-scatter.4
where the time goes:
time: 304 us; the launch traced here: 303 us
  waiting for transfers between devices  161 us (53%)
  matrix products  64.7 us (21%)
  other arithmetic  20 us (7%)
  local copies, waits for them, and re-layouts  17.2 us (6%)
  between operations  14.1 us (5%)
  blocking collectives  13.9 us (5%)
  starting transfers between devices  11.7 us (4%)
    reduce_scatter x1, waiting for transfers between devices, per_device(): lax.psum_scatter(column_term(attn_rows, w_out).astype(jnp.bfloat16), 'tp'...  36 us
    reduce_scatter x1, waiting for transfers between devices, per_device(): lax.psum_scatter(column_term(hidden, w_down).astype(jnp.bfloat16), 'tp',...  34.7 us
    all_gather x1, waiting for transfers between devices, per_device(): full_mid = lax.all_gather(mid, 'tp', axis=1, tiled=True)  27.8 us
    dot_general x2, matrix products, column_term(): lax.dot_general(weight, rows, (((0,), (1,)), ((), ())), preferred_element...  27 us
    all_gather x1, waiting for transfers between devices, per_device(): full_resid = lax.all_gather(resid, 'tp', axis=1, tiled=True)  26.4 us
    all_gather x1, waiting for transfers between devices, per_device(): lax.all_gather(query.reshape(span_size, q_cols), 'ctx', axis=0, tiled=True)  23.1 us
    all_gather x1, blocking collectives, per_device(): kv_all = lax.all_gather(kv_piece, 'tp', axis=1, tiled=True)  13.9 us
    all_to_all x1, waiting for transfers between devices, per_device(): lax.all_to_all(local_state[2][:, None].astype(jnp.bfloat16), 'ctx', split...  12.7 us
  transfers between devices with their start and end apart: 8, of which 6 were waited for; matrix products, arithmetic and copies ran while one was open for 9% of the time, Pallas kernels for 0%

commit v1 on v0

v1 whole, which is shorter than its diff:
```python
import jax
import jax.numpy as jnp
from jax import lax
from jax.sharding import PartitionSpec as P

HQ = 32
KVH = 4
HD = 128
BLK = 128


THETA = 5000000.0
EPS = 1e-05
NEG = -1e30


def rms_norm(values, gain):
    wide = values.astype(jnp.float32)
    factor = lax.rsqrt(jnp.mean(wide * wide, axis=-1, keepdims=True) + EPS)
    return (wide * factor * gain.astype(jnp.float32)).astype(jnp.bfloat16)


def rotate(vectors, positions):
    width = vectors.shape[-1]
    half = width // 2
    freqs = THETA ** (-(jnp.arange(half, dtype=jnp.float32) * 2.0 / width))
    angles = positions.astype(jnp.float32)[:, None] * freqs[None, :]
    cosine = jnp.cos(angles)[:, None, :]
    sine = jnp.sin(angles)[:, None, :]
    first = vectors[..., :half]
    second = vectors[..., half:]
    return jnp.concatenate(
        [first * cosine - second * sine, second * cosine + first * sine], axis=-1
    )


def column_term(rows, weight):
    return lax.dot_general(
        weight, rows, (((0,), (1,)), ((), ())), preferred_element_type=jnp.float32
    )


def gather_ctx(value, count):
    parts = [value]
    for shift in range(1, count):
        pairs = [(i, (i + shift) % count) for i in range(count)]
        parts.append(lax.ppermute(value, "ctx", pairs))
    return parts


def per_device(
    resid,
    attn_gain,
    mlp_gain,
    w_query,
    w_kv,
    w_out,
    w_gate,
    w_up,
    w_down,
    kv_cache,
    cache_len,
    span_len,
    slot_req,
    slot_blk,
):
    span_size = resid.shape[0]
    ctx_count = lax.axis_size("ctx")
    q_cols = w_query.shape[1]
    heads_dev = q_cols // HD
    ctx_rank = lax.axis_index("ctx")
    tp_rank = lax.axis_index("tp")
    group = tp_rank * heads_dev // (HQ // KVH)
    my_len = cache_len[ctx_rank]
    my_span = span_len[ctx_rank]
    offsets = jnp.arange(span_size, dtype=jnp.int32)
    positions = my_len + offsets
    live_rows = offsets < my_span

    own_cache = jnp.concatenate(
        [
            lax.dynamic_slice_in_dim(kv_cache, group * HD, HD, 2),
            lax.dynamic_slice_in_dim(kv_cache, KVH * HD + group * HD, HD, 2),
        ],
        axis=2,
    )
    own_meta = jnp.stack([slot_req, slot_blk])
    cache_all = jnp.concatenate(gather_ctx(own_cache, ctx_count), axis=0)
    meta_all = jnp.concatenate(gather_ctx(own_meta, ctx_count), axis=1)

    full_resid = lax.all_gather(resid, "tp", axis=1, tiled=True)
    x_norm = rms_norm(full_resid, attn_gain)
    query = rotate(
        jnp.dot(x_norm, w_query, preferred_element_type=jnp.float32).reshape(
            span_size, heads_dev, HD
        ),
        positions,
    ).astype(jnp.bfloat16)
    kv_piece = jnp.dot(x_norm, w_kv, preferred_element_type=jnp.float32).astype(jnp.bfloat16)
    kv_width = kv_piece.shape[1]
    kv_all = lax.all_gather(kv_piece, "tp", axis=1, tiled=True)
    all_keys = rotate(
        kv_all[:, : KVH * HD].astype(jnp.float32).reshape(span_size, KVH, HD), positions
    ).astype(jnp.bfloat16)
    joined = jnp.concatenate([all_keys.reshape(span_size, KVH * HD), kv_all[:, KVH * HD :]], axis=1)
    mine = lax.dynamic_slice_in_dim(joined, tp_rank * kv_width, kv_width, 1)
    new_kv = jnp.where(live_rows[:, None], mine, jnp.zeros_like(mine))
    new_keys = lax.dynamic_index_in_dim(all_keys, group, 1, keepdims=False)
    new_vals = lax.dynamic_slice_in_dim(kv_all, KVH * HD + group * HD, HD, 1)

    cache_rows = cache_all.shape[0] * BLK
    keys = jnp.concatenate([cache_all[..., :HD].reshape(cache_rows, HD), new_keys], axis=0)
    vals = jnp.concatenate([cache_all[..., HD:].reshape(cache_rows, HD), new_vals], axis=0)
    key_pos = meta_all[1][:, None] * BLK + jnp.arange(BLK, dtype=jnp.int32)[None, :]
    cache_ok = ((meta_all[0][:, None] == ctx_rank) & (key_pos < my_len)).reshape(cache_rows)
    new_ok = (offsets[None, :] <= offsets[:, None]) & (offsets[None, :] < my_span)
    valid = jnp.concatenate(
        [jnp.broadcast_to(cache_ok[None, :], (span_size, cache_rows)), new_ok], axis=1
    )
    scores = jnp.einsum(
        "chd,kd->hck", query, keys, preferred_element_type=jnp.float32
    ) * HD ** (-0.5)
    peak = jnp.max(jnp.where(valid[None], scores, NEG), axis=2)
    weights = jnp.where(valid[None], jnp.exp(scores - peak[..., None]), 0.0)
    total = jnp.sum(weights, axis=2)
    summed = jnp.einsum(
        "hck,kd->hcd", weights.astype(jnp.bfloat16), vals, preferred_element_type=jnp.float32
    )
    attn_rows = (
        (summed / total[..., None])
        .transpose(1, 0, 2)
        .reshape(span_size, q_cols)
        .astype(jnp.bfloat16)
    )
    head_sum = lax.psum_scatter(
        column_term(attn_rows, w_out).astype(jnp.bfloat16), "tp", scatter_dimension=0, tiled=True
    ).astype(jnp.float32)
    mid = (resid.astype(jnp.float32) + head_sum.T).astype(jnp.bfloat16)
    full_mid = lax.all_gather(mid, "tp", axis=1, tiled=True)
    x_two = rms_norm(full_mid, mlp_gain)
    gate = jnp.dot(x_two, w_gate, preferred_element_type=jnp.float32)
    up_part = jnp.dot(x_two, w_up, preferred_element_type=jnp.float32)
    hidden = (jax.nn.silu(gate) * up_part).astype(jnp.bfloat16)
    down_sum = lax.psum_scatter(
        column_term(hidden, w_down).astype(jnp.bfloat16), "tp", scatter_dimension=0, tiled=True
    ).astype(jnp.float32)
    layer_out = (mid.astype(jnp.float32) + down_sum.T).astype(jnp.bfloat16)
    layer_out = jnp.where(live_rows[:, None], layer_out, jnp.zeros_like(layer_out))
    return (layer_out, new_kv)


def solution(mesh):
    return jax.shard_map(
        per_device,
        mesh=mesh,
        in_specs=(
            P("ctx", "tp"),
            P(),
            P(),
            P(None, "tp"),
            P(None, "tp"),
            P("tp", None),
            P(None, "tp"),
            P(None, "tp"),
            P("tp", None),
            P("ctx", None, None),
            P(),
            P(),
            P("ctx"),
            P("ctx"),
        ),
        out_specs=(P("ctx", "tp"), P("ctx", "tp")),
        check_vma=False,
    )
```

time: 304 us -> 242 us (0.80)
  waiting for transfers between devices: 161 us -> 108 us
  other arithmetic: 20 us -> 38 us
  matrix products: 64.7 us -> 51.5 us
  local copies, waits for them, and re-layouts: 17.2 us -> 6.72 us
    all_gather x1, waiting for transfers between devices: 26.4 us -> 0.01 us  [per_device(): full_resid = lax.all_gather(resid, 'tp', axis=1, tiled=True)]
    all_gather x1 -> x0, waiting for transfers between devices: 23.1 us -> none  [per_device(): lax.all_gather(query.reshape(span_size, q_cols), 'ctx', axis=0, tiled=True)]
    sub x0 -> x1, other arithmetic: none -> 18.6 us  [per_device(): weights = jnp.where(valid[None], jnp.exp(scores - peak[..., None]), 0.0)]
    all_to_all x3 -> x0, waiting for transfers between devices: 12.7 us -> none  [the longest x1 12.7 us: per_device(): lax.all_to_all(local_state[2][:, None].astype(jnp.bfloat16), 'ctx', split...]
    all_to_all x3 -> x0, starting transfers between devices: 11.6 us -> none  [the longest x1 4.19 us: per_device(): lax.all_to_all(local_state[2][:, None].astype(jnp.bfloat16), 'ctx', split...]
    ppermute x0 -> x6, waiting for transfers between devices: none -> 10.4 us  [gather_ctx(): parts.append(lax.ppermute(value, 'ctx', pairs))]
    ppermute x0 -> x6, starting transfers between devices: none -> 8.95 us  [gather_ctx(): parts.append(lax.ppermute(value, 'ctx', pairs))]
    dot_general x6 -> x2, matrix products: 21.7 us -> 13.7 us  [the longest x1 8.66 us: per_device(): jnp.einsum('chd,kd->hck', query, keys, preferred_element_type=jnp.float32)]
  transfers between devices with their start and end apart: 8 -> 10, of which waited for: 6 -> 4; matrix products, arithmetic and copies ran while one was open for 9% -> 7% of each run, Pallas kernels for 0% -> 0%
where the time goes in v1:
time: 242 us
  waiting for transfers between devices  108 us (45%)
  matrix products  51.5 us (21%)
  other arithmetic  38 us (16%)
  blocking collectives  14.3 us (6%)
  between operations  14 us (6%)
  starting transfers between devices  9.33 us (4%)
  local copies, waits for them, and re-layouts  6.72 us (3%)
    reduce_scatter x1, waiting for transfers between devices, per_device(): lax.psum_scatter(column_term(attn_rows, w_out).astype(jnp.bfloat16), 'tp'...  34.6 us
    reduce_scatter x1, waiting for transfers between devices, per_device(): lax.psum_scatter(column_term(hidden, w_down).astype(jnp.bfloat16), 'tp',...  34.6 us
    all_gather x1, waiting for transfers between devices, per_device(): full_mid = lax.all_gather(mid, 'tp', axis=1, tiled=True)  27.9 us
    dot_general x2, matrix products, column_term(): lax.dot_general(weight, rows, (((0,), (1,)), ((), ())), preferred_element...  24.8 us
    sub x1, other arithmetic, per_device(): weights = jnp.where(valid[None], jnp.exp(scores - peak[..., None]), 0.0)  18.6 us
    all_gather x1, blocking collectives, per_device(): kv_all = lax.all_gather(kv_piece, 'tp', axis=1, tiled=True)  14.3 us
    ppermute x6, waiting for transfers between devices, gather_ctx(): parts.append(lax.ppermute(value, 'ctx', pairs))  10.4 us
    dot_general x1, matrix products, per_device(): gate = jnp.dot(x_two, w_gate, preferred_element_type=jnp.float32)  9.17 us
  transfers between devices with their start and end apart: 10, of which 4 were waited for; matrix products, arithmetic and copies ran while one was open for 7% of the time, Pallas kernels for 0%

profile of v1, /device:TPU:0, one launch (start us, length us, event | category | flops | bytes accessed | tf_op | source)
XLA Modules:
  0.0 242.1 jit_solution(6783432989193067769)
XLA Ops:
  7.2 0.7 all-gather.3.cloned.1.call-update
  8.0 0.7 pad_add_fusion.1
  8.6 3.9 %collective-permute-start.2 = (s32[2,8]{1,0:T(2,128)S(1)}, s32[2,8]{1,0:T(2,128)S(1)}, u32[]{:S(2)}, u32[]{:S(2)}) collective-permute-start(s32[2,8]{1,0:T(2,128)S(1)} %pad_add_fusion.1), channel_id=1, source_target_pairs={{0,24},{8,0},{16,8},{24,16},{1,25},{9,1},{17,9},{25,17},{2,26},{10... | collective-permute-start | bytes 200 | tf_op jit(solution)/shard_map/ppermute | solution.py:47
  12.5 0.5 collective-permute-start.1
  13.0 0.6 collective-permute-start
  13.6 1.1 constant_dynamic-slice_fusion.2
  14.8 2.4 collective-permute-start.5
  17.2 1.5 collective-permute-start.4
  18.7 1.2 dynamic_slice.22
  19.9 1.3 dynamic_slice.23
  21.2 0.7 convert_element_type.78
  21.9 0.7 iota_compare_fusion.1
  22.6 0.7 add_convert_fusion.1
  23.3 0.5 multiply_cosine_fusion
  24.0 0.8 pad_add_fusion.2
  24.7 0.7 fusion.50
  25.5 5.1 %pad_add_fusion = pred[256,4352]{0,1:T(8,128)(4,1)} fusion(pred[256,256]{0,1:T(8,128)(4,1)S(1)} %fusion.46, pred[4352]{0:T(1024)(128)(4,1)S(1)} %pad.8.clone), kind=kLoop, calls=%fused_computation.20 | loop fusion | flops 1114112 | bytes 1184000 | tf_op jit(solution)/shard_map/concatenate | solution.py:117
  30.6 10.4 %collective-permute-done.4 = bf16[8,128,256]{2,1,0:T(8,128)(2,1)S(1)} collective-permute-done((bf16[8,128,256]{2,1,0:T(8,128)(2,1)S(1)}, bf16[8,128,256]{2,1,0:T(8,128)(2,1)S(1)}, u32[]{:S(2)}, u32[]{:S(2)}) %collective-permute-start.4) | collective-permute-done | bytes 524320 | tf_op jit(solution)/shard_map/ppermute | solution.py:47
  41.0 0.2 pad_maximum_fusion
  41.2 0.6 fusion.56
  41.8 1.3 copy.25
  43.1 2.2 fusion.12
  45.4 2.6 %convolution_convert_fusion.2 = bf16[256,128]{1,0:T(8,128)(2,1)S(1)} fusion(bf16[4096,128]{1,0:T(8,128)(2,1)S(1)} %copy-done, bf16[256,4096]{1,0:T(8,128)(2,1)} %all-gather.3.cloned.1.call-done, f32[4096]{0:T(1024)S(1)} %convert_element_type.78, f32[256]{0:T(256)S(1)} %add_rsqrt_fusion.1), kind=kOutput, calls=%fused_computation.33 | convolution fusion | flops 272662528 | bytes 3228672 | tf_op jit(solution)/shard_map/dot_general | solution.py:99
  48.0 14.3 %all_gather.10 = bf16[256,1024]{1,0:T(8,128)(2,1)S(1)} all-gather(bf16[256,128]{1,0:T(8,128)(2,1)S(1)} %convolution_convert_fusion.2), channel_id=1, replica_groups=mesh['ctx'=4,'tp'=8] {'tp'}, dimensions={1}, use_global_device_ids=true | all-gather | bytes 589824 | tf_op jit(solution)/shard_map/all_gather | solution.py:101
  62.4 1.3 fusion.37
  63.7 0.2 reshape.158
  63.9 0.1 copy.21
  64.0 0.2 reshape.161
  64.2 0.3 fusion.59
  64.5 0.3 fusion.58
  64.9 0.1 multiply_subtract_fusion
  65.0 0.1 maximum_convert_fusion
  65.2 0.1 subtract_convert_fusion
  65.3 8.7 %fusion.30 = f32[4352,256,4]{1,0,2:T(8,128)} fusion(bf16[256,128]{1,0:T(8,128)(2,1)S(1)} %dynamic-slice_bitcast_fusion, bf16[4096,128]{1,0:T(8,128)(2,1)S(1)} %bitcast.69, bf16[256,4,64]{2,0,1:T(8,128)(2,1)S(1)} %get-tuple-element.7, bf16[256,4,64]{2,0,1:T(8,128)(2,1)S(1)} %get-tuple-element.6), kind=kOutput, calls=%fused_computation.38 | convolution fusion | flops 1143603200 | bytes 19202048 | tf_op jit(solution)/shard_map/chd,kd->hck/dot_general | solution.py:120
  74.0 18.6 %fusion.60 = (f32[4,256]{1,0:T(4,128)S(1)}, bf16[4,256,4352]{1,2,0:T(8,128)(2,1)}) fusion(f32[4352,256,4]{1,0,2:T(8,128)} %fusion.30, pred[256,4352]{0,1:T(8,128)(4,1)} %pad_add_fusion), kind=kOutput, calls=%fused_computation.92 | output fusion | flops 31199488 | bytes 27856896 | tf_op jit(solution)/shard_map/sub | solution.py:124
  92.6 5.0 %fusion.25 = bf16[256,4,128]{0,2,1:T(8,128)(2,1)S(1)} fusion(bf16[4,256,4352]{1,2,0:T(8,128)(2,1)} %get-tuple-element.19, bf16[256,128]{0,1:T(8,128)(2,1)S(1)} %copy.21, bf16[4096,128]{0,1:T(8,128)(2,1)S(1)} %copy-done.6, f32[256,4]{0,1:T(4,128)S(1)} %bitcast.76), kind=kOutput, calls=%fused_computation.32 | convolution fusion | flops 1143341056 | bytes 10293248 | tf_op jit(solution)/shard_map/hck,kd->hcd/dot_general | solution.py:126
  97.7 2.7 %fusion.11 = bf16[4096,256]{0,1:T(8,128)(2,1)} fusion(bf16[256,512]{0,1:T(8,128)(2,1)S(1)} %bitcast.71, bf16[512,4096]{1,0:T(8,128)(2,1)S(1)} %copy-done.2), kind=kOutput, calls=%fused_computation.19 | convolution fusion | flops 1074790400 | bytes 6553600 | tf_op jit(solution)/shard_map/dot_general | solution.py:38
  100.4 34.6 %reduce-scatter.3.cloned.1.call-done = bf16[512,256]{0,1:T(8,128)(2,1)} async-done(((bf16[4096,256]{0,1:T(8,128)(2,1)}), bf16[512,256]{0,1:T(8,128)(2,1)}) %reduce-scatter.3.cloned.1.call-update) | async-done | bytes 262160 | tf_op jit(solution)/shard_map/reduce_scatter | solution.py:135
  135.0 1.7 fusion.41
  136.8 0.3 reduce-scatter.5.cloned.1.call-start
  137.1 27.9 %all-gather.5.cloned.1.call-done = bf16[256,4096]{1,0:T(8,128)(2,1)} async-done(((bf16[256,512]{1,0:T(8,128)(2,1)}), bf16[256,4096]{1,0:T(8,128)(2,1)}) %all-gather.5.cloned.1.call-update) | async-done | bytes 2097168 | tf_op jit(solution)/shard_map/all_gather | solution.py:139
  164.9 2.1 fusion.15
  167.0 9.2 %fusion.35 = f32[256,1376]{0,1:T(8,128)} fusion(bf16[4096,1376]{0,1:T(8,128)(2,1)} %param.20, bf16[256,4096]{1,0:T(8,128)(2,1)} %all-gather.5.cloned.1.call-done, f32[4096]{0:T(1024)S(1)} %convert_element_type.91, f32[256]{0:T(256)S(1)} %add_rsqrt_fusion), kind=kOutput, calls=%fused_computation.41 | convolution fusion | flops 2889875456 | bytes 14795776 | tf_op jit(solution)/shard_map/dot_general | solution.py:141
  176.2 22.1 %fusion.10 = bf16[4096,256]{0,1:T(8,128)(2,1)} fusion(bf16[1376,4096]{1,0:T(8,128)(2,1)} %param.22, bf16[4096,1376]{0,1:T(8,128)(2,1)} %param.21, f32[256,1376]{0,1:T(8,128)} %fusion.35, bf16[256,4096]{1,0:T(8,128)(2,1)} %all-gather.5.cloned.1.call-done, f32[4096]{0:T(1024)S(1)} %convert_element_type.91, f32[256]{0:T(256)S(1)} %add_rsqrt_fusion), kind=kOutput, calls=%fused_computation.18 | convolution fusion | flops 5778718720 | bytes 28165120 | tf_op jit(solution)/shard_map/dot_general | solution.py:38
  198.4 0.1 copy_bitcast_fusion
  198.5 0.7 fusion.48
  199.3 34.6 %reduce-scatter.5.cloned.1.call-done = bf16[512,256]{0,1:T(8,128)(2,1)} async-done(((bf16[4096,256]{0,1:T(8,128)(2,1)}), bf16[512,256]{0,1:T(8,128)(2,1)}) %reduce-scatter.5.cloned.1.call-update) | async-done | bytes 262160 | tf_op jit(solution)/shard_map/reduce_scatter | solution.py:144
  233.8 1.8 fusion.42
  (43 shorter events, 0.6 us)
Async XLA Ops:
  7.2 38.2 %copy-start = (bf16[4096,128]{1,0:T(8,128)(2,1)S(1)}, bf16[4096,128]{1,0:T(8,128)(2,1)}, u32[]{:S(2)}) copy-start(bf16[4096,128]{1,0:T(8,128)(2,1)} %param.18) | copy-start | bytes 3145732
  7.2 36.0 %all-gather.3.cloned.1.call-start = ((), (), s32[]{:S(2)}) async-start(), calls=%async_computation.2 | async-start | bytes 2359296 | tf_op jit(solution)/shard_map/all_gather | solution.py:91
  7.9 127.1 %reduce-scatter.3.cloned.1.call-start = ((), (), s32[]{:S(2)}) async-start(), calls=%async_computation.3 | async-start | bytes 2359296 | tf_op jit(solution)/shard_map/reduce_scatter | solution.py:135
  8.6 15.2 %collective-permute-start.2 = (s32[2,8]{1,0:T(2,128)S(1)}, s32[2,8]{1,0:T(2,128)S(1)}, u32[]{:S(2)}, u32[]{:S(2)}) collective-permute-start(s32[2,8]{1,0:T(2,128)S(1)} %pad_add_fusion.1), channel_id=1, source_target_pairs={{0,24},{8,0},{16,8},{24,16},{1,25},{9,1},{17,9},{25,17},{2,26},{10... | collective-permute-start | bytes 200 | tf_op jit(solution)/shard_map/ppermute | solution.py:47
  12.5 11.4 %collective-permute-start.1 = (s32[2,8]{1,0:T(2,128)S(1)}, s32[2,8]{1,0:T(2,128)S(1)}, u32[]{:S(2)}, u32[]{:S(2)}) collective-permute-start(s32[2,8]{1,0:T(2,128)S(1)} %pad_add_fusion.1), channel_id=1, source_target_pairs={{0,16},{8,24},{16,0},{24,8},{1,17},{9,25},{17,1},{25,9},{2,18},{10... | collective-permute-start | bytes 200 | tf_op jit(solution)/shard_map/ppermute | solution.py:47
  13.0 10.9 %collective-permute-start = (s32[2,8]{1,0:T(2,128)S(1)}, s32[2,8]{1,0:T(2,128)S(1)}, u32[]{:S(2)}, u32[]{:S(2)}) collective-permute-start(s32[2,8]{1,0:T(2,128)S(1)} %pad_add_fusion.1), channel_id=1, source_target_pairs={{0,8},{8,16},{16,24},{24,0},{1,9},{9,17},{17,25},{25,1},{2,10},{10... | collective-permute-start | bytes 200 | tf_op jit(solution)/shard_map/ppermute | solution.py:47
  14.8 15.8 %collective-permute-start.5 = (bf16[8,128,256]{2,1,0:T(8,128)(2,1)S(1)}, bf16[8,128,256]{2,1,0:T(8,128)(2,1)S(1)}, u32[]{:S(2)}, u32[]{:S(2)}) collective-permute-start(bf16[8,128,256]{2,1,0:T(8,128)(2,1)S(1)} %pad_maximum_fusion.1), channel_id=1, source_target_pairs={{0,24},{8,0},{16,8},{24,16},{1,25},{9,1},{17,9},{25,17},{2,26},{10... | collective-permute-start | bytes 1572872 | tf_op jit(solution)/shard_map/ppermute | solution.py:47
  17.2 23.8 %collective-permute-start.4 = (bf16[8,128,256]{2,1,0:T(8,128)(2,1)S(1)}, bf16[8,128,256]{2,1,0:T(8,128)(2,1)S(1)}, u32[]{:S(2)}, u32[]{:S(2)}) collective-permute-start(bf16[8,128,256]{2,1,0:T(8,128)(2,1)S(1)} %pad_maximum_fusion.1), channel_id=1, source_target_pairs={{0,16},{8,24},{16,0},{24,8},{1,17},{9,25},{17,1},{25,9},{2,18},{10... | collective-permute-start | bytes 1572872 | tf_op jit(solution)/shard_map/ppermute | solution.py:47
  23.9 17.1 %collective-permute-start.3 = (bf16[8,128,256]{2,1,0:T(8,128)(2,1)S(1)}, bf16[8,128,256]{2,1,0:T(8,128)(2,1)S(1)}, u32[]{:S(2)}, u32[]{:S(2)}) collective-permute-start(bf16[8,128,256]{2,1,0:T(8,128)(2,1)S(1)} %pad_maximum_fusion.1), channel_id=1, source_target_pairs={{0,8},{8,16},{16,24},{24,0},{1,9},{9,17},{17,25},{25,1},{2,10},{10... | collective-permute-start | bytes 1572872 | tf_op jit(solution)/shard_map/ppermute | solution.py:47
  43.1 19.2 %copy-start.4 = (bf16[256,4096]{1,0:T(8,128)(2,1)S(1)}, bf16[256,4096]{1,0:T(8,128)(2,1)}, u32[]{:S(2)}) copy-start(bf16[256,4096]{1,0:T(8,128)(2,1)} %all-gather.3.cloned.1.call-done) | copy-start | bytes 6291460
  43.1 19.2 %copy-start.8 = (bf16[4096,512]{1,0:T(8,128)(2,1)S(1)}, bf16[4096,512]{1,0:T(8,128)(2,1)}, u32[]{:S(2)}) copy-start(bf16[4096,512]{1,0:T(8,128)(2,1)} %param.17) | copy-start | bytes 12582916
  74.0 18.6 %copy-start.6 = (bf16[4096,128]{0,1:T(8,128)(2,1)S(1)}, bf16[4096,128]{0,1:T(8,128)(2,1)}, u32[]{:S(2)}) copy-start(bf16[4096,128]{0,1:T(8,128)(2,1)} %copy.25) | copy-start | bytes 3145732
  92.6 5.0 %copy-start.2 = (bf16[512,4096]{1,0:T(8,128)(2,1)S(1)}, bf16[512,4096]{1,0:T(8,128)(2,1)}, u32[]{:S(2)}) copy-start(bf16[512,4096]{1,0:T(8,128)(2,1)} %param.19) | copy-start | bytes 12582916
  97.6 37.4 %copy-start.5 = (bf16[256,512]{1,0:T(8,128)(2,1)S(1)}, bf16[256,512]{1,0:T(8,128)(2,1)}, u32[]{:S(2)}) copy-start(bf16[256,512]{1,0:T(8,128)(2,1)} %param.14) | copy-start | bytes 786436
  97.6 39.4 %copy-start.7 = (bf16[4096]{0:T(1024)(128)(2,1)S(1)}, bf16[4096]{0:T(1024)(128)(2,1)}, u32[]{:S(2)}) copy-start(bf16[4096]{0:T(1024)(128)(2,1)} %param.16) | copy-start | bytes 24580
  100.3 64.6 %all-gather.5.cloned.1.call-start = ((), (), s32[]{:S(2)}) async-start(), calls=%async_computation.4 | async-start | bytes 2359296 | tf_op jit(solution)/shard_map/all_gather | solution.py:139
  136.8 97.0 %reduce-scatter.5.cloned.1.call-start = ((), (), s32[]{:S(2)}) async-start(), calls=%async_computation.5 | async-start | bytes 2359296 | tf_op jit(solution)/shard_map/reduce_scatter | solution.py:144
  176.2 57.6 %copy-start.3 = (bf16[256,512]{1,0:T(8,128)(2,1)S(1)}, bf16[256,512]{1,0:T(8,128)(2,1)}, u32[]{:S(2)}) copy-start(bf16[256,512]{1,0:T(8,128)(2,1)} %fusion.41) | copy-start | bytes 786436
  176.2 59.4 %copy-start.1 = (bf16[4096,128]{1,0:T(8,128)(2,1)S(1)}, bf16[4096,128]{1,0:T(8,128)(2,1)}, u32[]{:S(2)}) copy-start(bf16[4096,128]{1,0:T(8,128)(2,1)} %param.18) | copy-start | bytes 3145732
Sparse Core Ops, SparseCore 0:
  9.6 31.7 all-gather.2
  100.4 34.5 reduce-scatter.2
  137.2 27.6 all-gather.4
  198.5 35.2 reduce-scatter.4

commit v2 on v1

--- a/solution.py
+++ b/solution.py
@@ -132,11 +132,11 @@
         .reshape(span_size, q_cols)
         .astype(jnp.bfloat16)
     )
-    head_sum = lax.psum_scatter(
-        column_term(attn_rows, w_out).astype(jnp.bfloat16), "tp", scatter_dimension=0, tiled=True
-    ).astype(jnp.float32)
-    mid = (resid.astype(jnp.float32) + head_sum.T).astype(jnp.bfloat16)
-    full_mid = lax.all_gather(mid, "tp", axis=1, tiled=True)
+    head_sum = lax.psum(
+        jnp.dot(attn_rows, w_out, preferred_element_type=jnp.float32).astype(jnp.bfloat16), "tp"
+    )
+    full_mid = (full_resid.astype(jnp.float32) + head_sum.astype(jnp.float32)).astype(jnp.bfloat16)
+    mid = lax.dynamic_slice_in_dim(full_mid, tp_rank * resid.shape[1], resid.shape[1], 1)
     x_two = rms_norm(full_mid, mlp_gain)
     gate = jnp.dot(x_two, w_gate, preferred_element_type=jnp.float32)
     up_part = jnp.dot(x_two, w_up, preferred_element_type=jnp.float32)

time: 242 us -> 249 us (1.029)
  other arithmetic: 38 us -> 41.7 us
  local copies, waits for them, and re-layouts: 6.72 us -> 9.32 us
    psum x0 -> x1, waiting for transfers between devices: none -> 63.7 us  [per_device(): lax.psum(jnp.dot(attn_rows, w_out, preferred_element_type=jnp.float32).as...]
    reduce_scatter x1 -> x0, waiting for transfers between devices: 34.6 us -> none  [per_device(): lax.psum_scatter(column_term(attn_rows, w_out).astype(jnp.bfloat16), 'tp'...]
    all_gather x1 -> x0, waiting for transfers between devices: 27.9 us -> none  [per_device(): full_mid = lax.all_gather(mid, 'tp', axis=1, tiled=True)]
    dot_general x2 -> x1, matrix products: 24.8 us -> 21.7 us  [column_term(): lax.dot_general(weight, rows, (((0,), (1,)), ((), ())), preferred_element...]
    dot_general x0 -> x1, matrix products: none -> 2.66 us  [per_device(): jnp.dot(attn_rows, w_out, preferred_element_type=jnp.float32)]
  transfers between devices with their start and end apart: 10 -> 9, of which waited for: 4 -> 3; matrix products, arithmetic and copies ran while one was open for 7% -> 7% of each run, Pallas kernels for 0% -> 0%
where the time goes in v2:
time: 249 us; the launch traced here: 248 us
  waiting for transfers between devices  109 us (44%)
  matrix products  51.2 us (21%)
  other arithmetic  41.7 us (17%)
  blocking collectives  14.3 us (6%)
  between operations  14 us (6%)
  local copies, waits for them, and re-layouts  9.32 us (4%)
  starting transfers between devices  9.02 us (4%)
    psum x1, waiting for transfers between devices, per_device(): lax.psum(jnp.dot(attn_rows, w_out, preferred_element_type=jnp.float32).as...  63.7 us
    reduce_scatter x1, waiting for transfers between devices, per_device(): lax.psum_scatter(column_term(hidden, w_down).astype(jnp.bfloat16), 'tp',...  34.7 us
    dot_general x1, matrix products, column_term(): lax.dot_general(weight, rows, (((0,), (1,)), ((), ())), preferred_element...  21.7 us
    sub x1, other arithmetic, per_device(): weights = jnp.where(valid[None], jnp.exp(scores - peak[..., None]), 0.0)  18.7 us
    all_gather x1, blocking collectives, per_device(): kv_all = lax.all_gather(kv_piece, 'tp', axis=1, tiled=True)  14.3 us
    ppermute x6, waiting for transfers between devices, gather_ctx(): parts.append(lax.ppermute(value, 'ctx', pairs))  9.82 us
    ppermute x6, starting transfers between devices, gather_ctx(): parts.append(lax.ppermute(value, 'ctx', pairs))  8.9 us
    dot_general x1, matrix products, per_device(): jnp.einsum('chd,kd->hck', query, keys, preferred_element_type=jnp.float32)  8.67 us
  transfers between devices with their start and end apart: 9, of which 3 were waited for; matrix products, arithmetic and copies ran while one was open for 7% of the time, Pallas kernels for 0%

profile of v2, /device:TPU:0, one launch (start us, length us, event | category | flops | bytes accessed | tf_op | source)
XLA Modules:
  0.0 248.4 jit_solution(2127436485068741131)
XLA Ops:
  7.2 0.7 all-gather.2.cloned.1.call-update
  8.0 0.7 pad_add_fusion.1
  8.6 3.9 %collective-permute-start.2 = (s32[2,8]{1,0:T(2,128)S(1)}, s32[2,8]{1,0:T(2,128)S(1)}, u32[]{:S(2)}, u32[]{:S(2)}) collective-permute-start(s32[2,8]{1,0:T(2,128)S(1)} %pad_add_fusion.1), channel_id=1, source_target_pairs={{0,24},{8,0},{16,8},{24,16},{1,25},{9,1},{17,9},{25,17},{2,26},{10... | collective-permute-start | bytes 200 | tf_op jit(solution)/shard_map/ppermute | solution.py:47
  12.5 0.5 collective-permute-start.1
  13.0 0.6 collective-permute-start
  13.6 1.1 constant_dynamic-slice_fusion.2
  14.7 0.1 pad_maximum_fusion.1
  14.8 2.4 collective-permute-start.5
  17.2 1.5 collective-permute-start.4
  18.7 1.2 dynamic_slice.25
  19.9 1.3 dynamic_slice.26
  21.2 0.7 convert_element_type.74
  21.9 0.7 iota_compare_fusion.1
  22.6 0.7 add_convert_fusion.1
  23.2 0.1 fusion.45
  23.3 1.2 multiply_cosine_fusion
  24.5 0.8 pad_add_fusion.2
  25.3 0.7 fusion.49
  26.0 5.1 %pad_add_fusion = pred[256,4352]{0,1:T(8,128)(4,1)} fusion(pred[256,256]{0,1:T(8,128)(4,1)S(1)} %fusion.45, pred[4352]{0:T(1024)(128)(4,1)S(1)} %pad.8.clone), kind=kLoop, calls=%fused_computation.20 | loop fusion | flops 1114112 | bytes 1184000 | tf_op jit(solution)/shard_map/concatenate | solution.py:117
  31.1 9.8 %collective-permute-done.4 = bf16[8,128,256]{2,1,0:T(8,128)(2,1)S(1)} collective-permute-done((bf16[8,128,256]{2,1,0:T(8,128)(2,1)S(1)}, bf16[8,128,256]{2,1,0:T(8,128)(2,1)S(1)}, u32[]{:S(2)}, u32[]{:S(2)}) %collective-permute-start.4) | collective-permute-done | bytes 524320 | tf_op jit(solution)/shard_map/ppermute | solution.py:47
  41.0 0.2 pad_maximum_fusion
  41.2 1.6 fusion.56
  42.8 1.3 copy.25
  44.1 2.2 fusion.14
  46.3 2.4 convolution_convert_fusion.2
  48.7 14.3 %all_gather.7 = bf16[256,1024]{1,0:T(8,128)(2,1)S(1)} all-gather(bf16[256,128]{1,0:T(8,128)(2,1)S(1)} %convolution_convert_fusion.2), channel_id=1, replica_groups=mesh['ctx'=4,'tp'=8] {'tp'}, dimensions={1}, use_global_device_ids=true | all-gather | bytes 589824 | tf_op jit(solution)/shard_map/all_gather | solution.py:101
  63.0 0.9 fusion.57
  63.9 0.7 copy.21
  64.7 3.5 %fusion.37 = f32[256,512]{1,0:T(8,128)S(1)} fusion(bf16[4096,512]{1,0:T(8,128)(2,1)} %param.17, bf16[256,4096]{1,0:T(8,128)(2,1)S(1)} %copy-done.2, f32[4096]{0:T(1024)S(1)} %convert_element_type.74, f32[256]{0:T(256)S(1)} %add_rsqrt_fusion.1), kind=kOutput, calls=%fused_computation.43 | convolution fusion | flops 1077936128 | bytes 6833152 | tf_op jit(solution)/shard_map/dot_general | solution.py:94
  68.2 0.2 reshape.158
  68.4 1.2 reshape.161
  69.6 0.3 fusion.59
  69.9 0.3 fusion.58
  70.3 1.0 multiply_subtract_fusion
  71.3 0.1 maximum_convert_fusion
  71.5 1.0 subtract_convert_fusion
  72.6 8.7 %fusion.30 = f32[4352,256,4]{1,0,2:T(8,128)} fusion(bf16[256,128]{1,0:T(8,128)(2,1)S(1)} %dynamic-slice_bitcast_fusion, bf16[4096,128]{1,0:T(8,128)(2,1)S(1)} %bitcast.63, bf16[256,4,64]{2,0,1:T(8,128)(2,1)S(1)} %get-tuple-element.9, bf16[256,4,64]{2,0,1:T(8,128)(2,1)S(1)} %get-tuple-element.8), kind=kOutput, calls=%fused_computation.39 | convolution fusion | flops 1143603200 | bytes 19202048 | tf_op jit(solution)/shard_map/chd,kd->hck/dot_general | solution.py:120
  81.2 18.7 %fusion.60 = (f32[4,256]{1,0:T(4,128)S(1)}, bf16[4,256,4352]{1,2,0:T(8,128)(2,1)}) fusion(f32[4352,256,4]{1,0,2:T(8,128)} %fusion.30, pred[256,4352]{0,1:T(8,128)(4,1)} %pad_add_fusion), kind=kOutput, calls=%fused_computation.91 | output fusion | flops 31199488 | bytes 27856896 | tf_op jit(solution)/shard_map/sub | solution.py:124
  100.0 5.3 %fusion.25 = bf16[256,4,128]{0,2,1:T(8,128)(2,1)S(1)} fusion(bf16[4,256,4352]{1,2,0:T(8,128)(2,1)} %get-tuple-element.21, bf16[256,128]{0,1:T(8,128)(2,1)S(1)} %copy-done.8, bf16[4096,128]{0,1:T(8,128)(2,1)} %copy.25, f32[256,4]{0,1:T(4,128)S(1)} %bitcast.70), kind=kOutput, calls=%fused_computation.33 | convolution fusion | flops 1143341056 | bytes 10293248 | tf_op jit(solution)/shard_map/hck,kd->hcd/dot_general | solution.py:126
  105.3 2.7 %convolution_convert_fusion = bf16[256,4096]{1,0:T(8,128)(2,1)} fusion(bf16[256,512]{0,1:T(8,128)(2,1)S(1)} %bitcast.65, bf16[512,4096]{1,0:T(8,128)(2,1)S(1)} %copy-done.3), kind=kOutput, calls=%fused_computation.17 | convolution fusion | flops 1074790400 | bytes 6553600 | tf_op jit(solution)/shard_map/dot_general | solution.py:136
  108.1 63.7 %all-reduce.2.cloned.1.call-done = bf16[256,4096]{1,0:T(8,128)(2,1)} async-done(((bf16[256,4096]{1,0:T(8,128)(2,1)}), bf16[256,4096]{1,0:T(8,128)(2,1)}) %all-reduce.2.cloned.1.call-update) | async-done | bytes 2097168 | tf_op jit(solution)/shard_map/psum | solution.py:135
  171.8 3.9 %fusion.11 = (f32[256]{0:T(256)S(1)}, bf16[256,4096]{1,0:T(8,128)(2,1)}) fusion(bf16[256,4096]{1,0:T(8,128)(2,1)} %all-reduce.2.cloned.1.call-done, bf16[256,4096]{1,0:T(8,128)(2,1)S(1)} %copy-done.2), kind=kLoop, calls=%fused_computation.21 | loop fusion | flops 7339776 | bytes 6292480 | tf_op jit(solution)/shard_map/reduce_sum | solution.py:19
  175.7 7.0 %fusion.35 = f32[256,1376]{0,1:T(8,128)S(1)} fusion(bf16[4096,1376]{0,1:T(8,128)(2,1)} %param.20, bf16[256,4096]{1,0:T(8,128)(2,1)} %get-tuple-element.3, f32[4096]{0:T(1024)S(1)} %convert_element_type.87, f32[256]{0:T(256)S(1)} %add_rsqrt_fusion), kind=kOutput, calls=%fused_computation.42 | convolution fusion | flops 2889875456 | bytes 14795776 | tf_op jit(solution)/shard_map/dot_general | solution.py:141
  182.7 21.7 %fusion.10 = bf16[4096,256]{0,1:T(8,128)(2,1)} fusion(bf16[1376,4096]{1,0:T(8,128)(2,1)} %param.22, bf16[4096,1376]{0,1:T(8,128)(2,1)} %param.21, f32[256,1376]{0,1:T(8,128)S(1)} %fusion.35, bf16[256,4096]{1,0:T(8,128)(2,1)} %get-tuple-element.3, f32[4096]{0:T(1024)S(1)} %convert_element_type.87, f32[256]{0:T(256)S(1)} %add_rsqrt_fusion), kind=kOutput, calls=%fused_computation.19 | convolution fusion | flops 5778718720 | bytes 28165120 | tf_op jit(solution)/shard_map/dot_general | solution.py:38
  204.5 0.1 copy_bitcast_fusion
  204.6 0.7 fusion.47
  205.4 34.7 %reduce-scatter.2.cloned.1.call-done = bf16[512,256]{0,1:T(8,128)(2,1)} async-done(((bf16[4096,256]{0,1:T(8,128)(2,1)}), bf16[512,256]{0,1:T(8,128)(2,1)}) %reduce-scatter.2.cloned.1.call-update) | async-done | bytes 262160 | tf_op jit(solution)/shard_map/reduce_scatter | solution.py:144
  240.1 1.8 fusion.41
  (41 shorter events, 0.3 us)
Async XLA Ops:
  7.2 39.1 %copy-start = (bf16[4096,128]{1,0:T(8,128)(2,1)S(1)}, bf16[4096,128]{1,0:T(8,128)(2,1)}, u32[]{:S(2)}) copy-start(bf16[4096,128]{1,0:T(8,128)(2,1)} %param.18) | copy-start | bytes 3145732
  7.2 36.9 %all-gather.2.cloned.1.call-start = ((), (), s32[]{:S(2)}) async-start(), calls=%async_computation.1 | async-start | bytes 2359296 | tf_op jit(solution)/shard_map/all_gather | solution.py:91
  7.9 163.9 %all-reduce.2.cloned.1.call-start = ((), (), s32[]{:S(2)}) async-start(), calls=%async_computation.2 | async-start | bytes 4194304 | tf_op jit(solution)/shard_map/psum | solution.py:135
  8.6 15.9 %collective-permute-start.2 = (s32[2,8]{1,0:T(2,128)S(1)}, s32[2,8]{1,0:T(2,128)S(1)}, u32[]{:S(2)}, u32[]{:S(2)}) collective-permute-start(s32[2,8]{1,0:T(2,128)S(1)} %pad_add_fusion.1), channel_id=1, source_target_pairs={{0,24},{8,0},{16,8},{24,16},{1,25},{9,1},{17,9},{25,17},{2,26},{10... | collective-permute-start | bytes 200 | tf_op jit(solution)/shard_map/ppermute | solution.py:47
  12.5 12.0 %collective-permute-start.1 = (s32[2,8]{1,0:T(2,128)S(1)}, s32[2,8]{1,0:T(2,128)S(1)}, u32[]{:S(2)}, u32[]{:S(2)}) collective-permute-start(s32[2,8]{1,0:T(2,128)S(1)} %pad_add_fusion.1), channel_id=1, source_target_pairs={{0,16},{8,24},{16,0},{24,8},{1,17},{9,25},{17,1},{25,9},{2,18},{10... | collective-permute-start | bytes 200 | tf_op jit(solution)/shard_map/ppermute | solution.py:47
  13.0 11.5 %collective-permute-start = (s32[2,8]{1,0:T(2,128)S(1)}, s32[2,8]{1,0:T(2,128)S(1)}, u32[]{:S(2)}, u32[]{:S(2)}) collective-permute-start(s32[2,8]{1,0:T(2,128)S(1)} %pad_add_fusion.1), channel_id=1, source_target_pairs={{0,8},{8,16},{16,24},{24,0},{1,9},{9,17},{17,25},{25,1},{2,10},{10... | collective-permute-start | bytes 200 | tf_op jit(solution)/shard_map/ppermute | solution.py:47
  14.8 16.4 %collective-permute-start.5 = (bf16[8,128,256]{2,1,0:T(8,128)(2,1)S(1)}, bf16[8,128,256]{2,1,0:T(8,128)(2,1)S(1)}, u32[]{:S(2)}, u32[]{:S(2)}) collective-permute-start(bf16[8,128,256]{2,1,0:T(8,128)(2,1)S(1)} %pad_maximum_fusion.1), channel_id=1, source_target_pairs={{0,24},{8,0},{16,8},{24,16},{1,25},{9,1},{17,9},{25,17},{2,26},{10... | collective-permute-start | bytes 1572872 | tf_op jit(solution)/shard_map/ppermute | solution.py:47
  17.2 23.8 %collective-permute-start.4 = (bf16[8,128,256]{2,1,0:T(8,128)(2,1)S(1)}, bf16[8,128,256]{2,1,0:T(8,128)(2,1)S(1)}, u32[]{:S(2)}, u32[]{:S(2)}) collective-permute-start(bf16[8,128,256]{2,1,0:T(8,128)(2,1)S(1)} %pad_maximum_fusion.1), channel_id=1, source_target_pairs={{0,16},{8,24},{16,0},{24,8},{1,17},{9,25},{17,1},{25,9},{2,18},{10... | collective-permute-start | bytes 1572872 | tf_op jit(solution)/shard_map/ppermute | solution.py:47
  24.5 16.4 %collective-permute-start.3 = (bf16[8,128,256]{2,1,0:T(8,128)(2,1)S(1)}, bf16[8,128,256]{2,1,0:T(8,128)(2,1)S(1)}, u32[]{:S(2)}, u32[]{:S(2)}) collective-permute-start(bf16[8,128,256]{2,1,0:T(8,128)(2,1)S(1)} %pad_maximum_fusion.1), channel_id=1, source_target_pairs={{0,8},{8,16},{16,24},{24,0},{1,9},{9,17},{17,25},{25,1},{2,10},{10... | collective-permute-start | bytes 1572872 | tf_op jit(solution)/shard_map/ppermute | solution.py:47
  44.1 20.6 %copy-start.2 = (bf16[256,4096]{1,0:T(8,128)(2,1)S(1)}, bf16[256,4096]{1,0:T(8,128)(2,1)}, u32[]{:S(2)}) copy-start(bf16[256,4096]{1,0:T(8,128)(2,1)} %all-gather.2.cloned.1.call-done) | copy-start | bytes 6291460
  69.6 3.0 %copy-start.4 = (bf16[32,128,128]{2,1,0:T(8,128)(2,1)S(1)}, bf16[32,128,128]{2,1,0:T(8,128)(2,1)}, u32[]{:S(2)}) copy-start(bf16[32,128,128]{2,1,0:T(8,128)(2,1)} %get-tuple-element.5) | copy-start | bytes 3145732
  71.3 9.9 %copy-start.5 = (bf16[256,4,64]{2,0,1:T(8,128)(2,1)}, bf16[256,4,64]{2,0,1:T(8,128)(2,1)S(1)}, u32[]{:S(2)}) copy-start(bf16[256,4,64]{2,0,1:T(8,128)(2,1)S(1)} %get-tuple-element.11) | copy-start | bytes 393220
  81.2 18.7 %copy-start.8 = (bf16[256,128]{0,1:T(8,128)(2,1)S(1)}, bf16[256,128]{0,1:T(8,128)(2,1)}, u32[]{:S(2)}) copy-start(bf16[256,128]{0,1:T(8,128)(2,1)} %copy.21) | copy-start | bytes 196612
  100.0 5.3 %copy-start.3 = (bf16[512,4096]{1,0:T(8,128)(2,1)S(1)}, bf16[512,4096]{1,0:T(8,128)(2,1)}, u32[]{:S(2)}) copy-start(bf16[512,4096]{1,0:T(8,128)(2,1)} %param.19) | copy-start | bytes 12582916
  105.3 2.7 %copy-start.9 = (bf16[4096]{0:T(1024)(128)(2,1)S(1)}, bf16[4096]{0:T(1024)(128)(2,1)}, u32[]{:S(2)}) copy-start(bf16[4096]{0:T(1024)(128)(2,1)} %param.16) | copy-start | bytes 24580
  108.0 132.1 %reduce-scatter.2.cloned.1.call-start = ((), (), s32[]{:S(2)}) async-start(), calls=%async_computation.3 | async-start | bytes 2359296 | tf_op jit(solution)/shard_map/reduce_scatter | solution.py:144
  182.7 21.8 %copy-start.6 = (bf16[256,4,64]{2,0,1:T(8,128)(2,1)S(1)}, bf16[256,4,64]{2,0,1:T(8,128)(2,1)}, u32[]{:S(2)}) copy-start(bf16[256,4,64]{2,0,1:T(8,128)(2,1)} %copy-done.5) | copy-start | bytes 393220
  182.7 21.9 %copy-start.7 = (bf16[256,512]{1,0:T(8,128)(2,1)S(1)}, bf16[256,512]{1,0:T(8,128)(2,1)}, u32[]{:S(2)}) copy-start(bf16[256,512]{1,0:T(8,128)(2,1)} %get-tuple-element.12) | copy-start | bytes 786436
  182.7 59.2 %copy-start.1 = (bf16[4096,128]{1,0:T(8,128)(2,1)S(1)}, bf16[4096,128]{1,0:T(8,128)(2,1)}, u32[]{:S(2)}) copy-start(bf16[4096,128]{1,0:T(8,128)(2,1)} %param.18) | copy-start | bytes 3145732
Sparse Core Ops, SparseCore 0:
  9.6 31.7 all-gather.1
  108.1 63.6 all-reduce.1
  204.6 35.4 reduce-scatter.1

commit v3 on v1

--- a/solution.py
+++ b/solution.py
@@ -2,6 +2,8 @@
 import jax.numpy as jnp
 from jax import lax
 from jax.sharding import PartitionSpec as P
+from jax.experimental import pallas as pl
+from jax.experimental.pallas import tpu as pltpu
 
 HQ = 32
 KVH = 4
@@ -38,6 +40,99 @@
     return lax.dot_general(
         weight, rows, (((0,), (1,)), ((), ())), preferred_element_type=jnp.float32
     )
+
+
+def attn_kernel(limit_ref, span_ref, q_ref, cache_ref, nk_ref, nv_ref, o_ref, m_scr, t_scr, acc_scr):
+    slots = cache_ref.shape[0]
+    span_size = nk_ref.shape[0]
+    heads = q_ref.shape[0] // span_size
+    scale = HD ** (-0.5)
+    q_all = q_ref[...]
+    col = lax.broadcasted_iota(jnp.int32, (1, BLK), 1)
+    row_i = lax.broadcasted_iota(jnp.int32, (span_size, span_size), 0)
+    col_j = lax.broadcasted_iota(jnp.int32, (span_size, span_size), 1)
+    new_ok = (col_j <= row_i) & (col_j < span_ref[0])
+    dims = (((1,), (1,)), ((), ()))
+
+    def cache_scores(s):
+        keys = cache_ref[s, :, :HD]
+        return lax.dot_general(q_all, keys, dims, preferred_element_type=jnp.float32) * scale
+
+    def new_scores(h):
+        rows = q_ref[h * span_size : (h + 1) * span_size, :]
+        return lax.dot_general(rows, nk_ref[...], dims, preferred_element_type=jnp.float32) * scale
+
+    m_scr[...] = jnp.full(m_scr.shape, NEG, jnp.float32)
+
+    def max_step(s, carry):
+        lim = limit_ref[s]
+
+        @pl.when(lim > 0)
+        def _():
+            sc = jnp.where(col < lim, cache_scores(s), NEG)
+            m_scr[...] = jnp.maximum(m_scr[...], jnp.max(sc, axis=1, keepdims=True))
+
+        return carry
+
+    lax.fori_loop(0, slots, max_step, 0)
+    for h in range(heads):
+        part = slice(h * span_size, (h + 1) * span_size)
+        sc = jnp.where(new_ok, new_scores(h), NEG)
+        m_scr[part, :] = jnp.maximum(m_scr[part, :], jnp.max(sc, axis=1, keepdims=True))
+
+    t_scr[...] = jnp.zeros(t_scr.shape, jnp.float32)
+    acc_scr[...] = jnp.zeros(acc_scr.shape, jnp.float32)
+
+    def sum_step(s, carry):
+        lim = limit_ref[s]
+
+        @pl.when(lim > 0)
+        def _():
+            w = jnp.where(col < lim, jnp.exp(cache_scores(s) - m_scr[...]), 0.0)
+            t_scr[...] += jnp.sum(w, axis=1, keepdims=True)
+            acc_scr[...] += jnp.dot(
+                w.astype(jnp.bfloat16), cache_ref[s, :, HD:], preferred_element_type=jnp.float32
+            )
+
+        return carry
+
+    lax.fori_loop(0, slots, sum_step, 0)
+    for h in range(heads):
+        part = slice(h * span_size, (h + 1) * span_size)
+        w = jnp.where(new_ok, jnp.exp(new_scores(h) - m_scr[part, :]), 0.0)
+        t_scr[part, :] += jnp.sum(w, axis=1, keepdims=True)
+        acc_scr[part, :] += jnp.dot(
+            w.astype(jnp.bfloat16), nv_ref[...], preferred_element_type=jnp.float32
+        )
+    o_ref[...] = (acc_scr[...] / t_scr[...]).astype(o_ref.dtype)
+
+
+def local_attention(limit, span, q_rows, cache_all, new_keys, new_vals):
+    rows = q_rows.shape[0]
+
+    def whole(shape):
+        return pl.BlockSpec(shape, lambda i, *_: (0,) * len(shape))
+
+    return pl.pallas_call(
+        attn_kernel,
+        out_shape=jax.ShapeDtypeStruct((rows, HD), jnp.bfloat16),
+        grid_spec=pltpu.PrefetchScalarGridSpec(
+            num_scalar_prefetch=2,
+            grid=(1,),
+            in_specs=[
+                whole(q_rows.shape),
+                whole(cache_all.shape),
+                whole(new_keys.shape),
+                whole(new_vals.shape),
+            ],
+            out_specs=whole((rows, HD)),
+            scratch_shapes=[
+                pltpu.VMEM((rows, 1), jnp.float32),
+                pltpu.VMEM((rows, 1), jnp.float32),
+                pltpu.VMEM((rows, HD), jnp.float32),
+            ],
+        ),
+    )(limit, span, q_rows, cache_all, new_keys, new_vals)
 
 
 def gather_ctx(value, count):
@@ -108,29 +203,15 @@
     new_keys = lax.dynamic_index_in_dim(all_keys, group, 1, keepdims=False)
     new_vals = lax.dynamic_slice_in_dim(kv_all, KVH * HD + group * HD, HD, 1)
 
-    cache_rows = cache_all.shape[0] * BLK
-    keys = jnp.concatenate([cache_all[..., :HD].reshape(cache_rows, HD), new_keys], axis=0)
-    vals = jnp.concatenate([cache_all[..., HD:].reshape(cache_rows, HD), new_vals], axis=0)
-    key_pos = meta_all[1][:, None] * BLK + jnp.arange(BLK, dtype=jnp.int32)[None, :]
-    cache_ok = ((meta_all[0][:, None] == ctx_rank) & (key_pos < my_len)).reshape(cache_rows)
-    new_ok = (offsets[None, :] <= offsets[:, None]) & (offsets[None, :] < my_span)
-    valid = jnp.concatenate(
-        [jnp.broadcast_to(cache_ok[None, :], (span_size, cache_rows)), new_ok], axis=1
-    )
-    scores = jnp.einsum(
-        "chd,kd->hck", query, keys, preferred_element_type=jnp.float32
-    ) * HD ** (-0.5)
-    peak = jnp.max(jnp.where(valid[None], scores, NEG), axis=2)
-    weights = jnp.where(valid[None], jnp.exp(scores - peak[..., None]), 0.0)
-    total = jnp.sum(weights, axis=2)
-    summed = jnp.einsum(
-        "hck,kd->hcd", weights.astype(jnp.bfloat16), vals, preferred_element_type=jnp.float32
+    limit = jnp.where(
+        meta_all[0] == ctx_rank, jnp.clip(my_len - meta_all[1] * BLK, 0, BLK), 0
+    ).astype(jnp.int32)
+    q_rows = query.transpose(1, 0, 2).reshape(heads_dev * span_size, HD)
+    attn_heads = local_attention(
+        limit, my_span.reshape(1).astype(jnp.int32), q_rows, cache_all, new_keys, new_vals
     )
     attn_rows = (
-        (summed / total[..., None])
-        .transpose(1, 0, 2)
-        .reshape(span_size, q_cols)
-        .astype(jnp.bfloat16)
+        attn_heads.reshape(heads_dev, span_size, HD).transpose(1, 0, 2).reshape(span_size, q_cols)
     )
     head_sum = lax.psum_scatter(
         column_term(attn_rows, w_out).astype(jnp.bfloat16), "tp", scatter_dimension=0, tiled=True

time: 242 us -> 231 us (0.955)
  other arithmetic: 38 us -> 17.6 us
  waiting for transfers between devices: 108 us -> 124 us
  matrix products: 51.5 us -> 37.5 us
  Pallas kernels: 0 us -> 7.98 us
    sub x1 -> x0, other arithmetic: 18.6 us -> none  [per_device(): weights = jnp.where(valid[None], jnp.exp(scores - peak[..., None]), 0.0)]
    dot_general x2 -> x0, matrix products: 13.7 us -> none  [the longest x1 8.66 us: per_device(): jnp.einsum('chd,kd->hck', query, keys, preferred_element_type=jnp.float32)]
    reduce_scatter x1, waiting for transfers between devices: 34.6 us -> 43.7 us  [per_device(): lax.psum_scatter(column_term(attn_rows, w_out).astype(jnp.bfloat16), 'tp'...]
    pallas_call x0 -> x1, Pallas kernels: none -> 7.98 us  [local_attention(): pl.pallas_call(attn_kernel, out_shape=jax.ShapeDtypeStruct((rows, HD), jn...]
    ppermute x6, waiting for transfers between devices: 10.4 us -> 17.4 us  [gather_ctx(): parts.append(lax.ppermute(value, 'ctx', pairs))]
    concatenate x1, other arithmetic: 5.12 us -> 0.85 us  [rotate(): jnp.concatenate([first * cosine - second * sine, second * cosine + first...]
  transfers between devices with their start and end apart: 10 -> 10, of which waited for: 4 -> 4; matrix products, arithmetic and copies ran while one was open for 7% -> 5% of each run, Pallas kernels for 0% -> 0%
where the time goes in v3:
time: 231 us; the launch traced here: 230 us
  waiting for transfers between devices  124 us (54%)
  matrix products  37.5 us (16%)
  other arithmetic  17.6 us (8%)
  blocking collectives  14.2 us (6%)
  between operations  14 us (6%)
  starting transfers between devices  8.23 us (4%)
  Pallas kernels  7.98 us (3%)
  local copies, waits for them, and re-layouts  6.97 us (3%)
    reduce_scatter x1, waiting for transfers between devices, per_device(): lax.psum_scatter(column_term(attn_rows, w_out).astype(jnp.bfloat16), 'tp'...  43.7 us
    reduce_scatter x1, waiting for transfers between devices, per_device(): lax.psum_scatter(column_term(hidden, w_down).astype(jnp.bfloat16), 'tp',...  33.9 us
    all_gather x1, waiting for transfers between devices, per_device(): full_mid = lax.all_gather(mid, 'tp', axis=1, tiled=True)  28 us
    dot_general x2, matrix products, column_term(): lax.dot_general(weight, rows, (((0,), (1,)), ((), ())), preferred_element...  26.6 us
    ppermute x6, waiting for transfers between devices, gather_ctx(): parts.append(lax.ppermute(value, 'ctx', pairs))  17.4 us
    all_gather x1, blocking collectives, per_device(): kv_all = lax.all_gather(kv_piece, 'tp', axis=1, tiled=True)  14.2 us
    ppermute x6, starting transfers between devices, gather_ctx(): parts.append(lax.ppermute(value, 'ctx', pairs))  8.07 us
    pallas_call x1, Pallas kernels, local_attention(): pl.pallas_call(attn_kernel, out_shape=jax.ShapeDtypeStruct((rows, HD), jn...  7.98 us
  transfers between devices with their start and end apart: 10, of which 4 were waited for; matrix products, arithmetic and copies ran while one was open for 5% of the time, Pallas kernels for 0%

profile of v3, /device:TPU:0, one launch (start us, length us, event | category | flops | bytes accessed | tf_op | source)
XLA Modules:
  0.0 230.4 jit_solution(14514217188703691895)
XLA Ops:
  7.2 0.7 all-gather.3.cloned.1.call-update
  8.0 0.7 pad_add_fusion
  8.6 3.9 %collective-permute-start.2 = (s32[2,8]{1,0:T(2,128)S(1)}, s32[2,8]{1,0:T(2,128)S(1)}, u32[]{:S(2)}, u32[]{:S(2)}) collective-permute-start(s32[2,8]{1,0:T(2,128)S(1)} %pad_add_fusion), channel_id=1, source_target_pairs={{0,24},{8,0},{16,8},{24,16},{1,25},{9,1},{17,9},{25,17},{2,26},{10... | collective-permute-start | bytes 200 | tf_op jit(solution)/shard_map/ppermute | solution.py:142
  12.5 0.5 collective-permute-start.1
  13.0 1.1 constant_dynamic-slice_fusion.2
  14.1 0.1 pad_maximum_fusion.1
  14.2 0.1 collective-permute-start.5
  14.3 2.0 collective-permute-start.4
  16.3 1.5 collective-permute-start.3
  17.8 1.2 dynamic_slice.22.span_ref
  19.0 1.2 dynamic_slice.23
  20.2 0.7 convert_element_type.69
  21.0 0.7 add_convert_fusion.1
  21.6 0.5 multiply_cosine_fusion
  22.2 0.1 collective-permute-start
  22.2 17.4 %collective-permute-done = s32[2,8]{1,0:T(2,128)S(1)} collective-permute-done((s32[2,8]{1,0:T(2,128)S(1)}, s32[2,8]{1,0:T(2,128)S(1)}, u32[]{:S(2)}, u32[]{:S(2)}) %collective-permute-start) | collective-permute-done | bytes 96 | tf_op jit(solution)/shard_map/ppermute | solution.py:142
  39.7 0.8 pad_add_fusion.1
  40.4 1.2 fusion.21.limit_ref
  41.6 2.4 %pad_maximum_fusion.cache_ref = bf16[32,128,256]{2,1,0:T(8,128)(2,1)} fusion(bf16[8,128,256]{2,1,0:T(8,128)(2,1)S(1)} %collective-permute-done.5, bf16[8,128,256]{2,1,0:T(8,128)(2,1)S(1)} %collective-permute-done.4, bf16[8,128,256]{2,1,0:T(8,128)(2,1)} %collective-permute-done.3, bf16[8,128,128]{2,1,0:T(8,128)(2,1)S(1)} %get-tuple-element.3, ...), kind=kLoop, calls=%fused_computation.16 | loop fusion | flops 10485760 | bytes 4194304 | tf_op jit(solution)/shard_map/concatenate | solution.py:183
  44.1 2.2 fusion.2
  46.3 2.6 %convolution_convert_fusion.2 = bf16[256,128]{1,0:T(8,128)(2,1)S(1)} fusion(bf16[4096,128]{1,0:T(8,128)(2,1)S(1)} %copy-done, bf16[256,4096]{1,0:T(8,128)(2,1)} %all-gather.3.cloned.1.call-done, f32[4096]{0:T(1024)S(1)} %convert_element_type.69, f32[256]{0:T(256)S(1)} %add_rsqrt_fusion.1), kind=kOutput, calls=%fused_computation.17 | convolution fusion | flops 272662528 | bytes 3228672 | tf_op jit(solution)/shard_map/dot_general | solution.py:194
  48.9 14.2 %all_gather.10 = bf16[256,1024]{1,0:T(8,128)(2,1)S(1)} all-gather(bf16[256,128]{1,0:T(8,128)(2,1)S(1)} %convolution_convert_fusion.2), channel_id=1, replica_groups=mesh['ctx'=4,'tp'=8] {'tp'}, dimensions={1}, use_global_device_ids=true | all-gather | bytes 589824 | tf_op jit(solution)/shard_map/all_gather | solution.py:196
  63.2 0.6 constant_dynamic-slice_fusion.nv_ref
  63.8 0.1 fusion.23
  63.9 1.3 fusion.14
  65.2 0.2 reshape.116
  65.4 0.2 reshape.123
  65.6 0.3 fusion.24
  65.9 0.3 fusion.25
  66.3 0.1 multiply_subtract_fusion
  66.4 0.1 maximum_convert_fusion
  66.6 0.6 dynamic-slice_bitcast_fusion.nk_ref
  67.2 0.1 subtract_convert_fusion
  67.3 0.9 pad_maximum_fusion.2
  68.2 8.0 %shard_map.149 = bf16[1024,128]{1,0:T(8,128)(2,1)} custom-call(s32[32]{0:T(128)} %fusion.21.limit_ref, s32[1]{0:T(128)} %dynamic_slice.22.span_ref, bf16[1024,128]{1,0:T(8,128)(2,1)} %bitcast.41, bf16[32,128,256]{2,1,0:T(8,128)(2,1)} %pad_maximum_fusion.cache_ref, bf16[256,128]{1,0:T(8,128)(2,1)} %dynamic-slice_bitcast_fusion.nk_ref, ...), custom_call_target="tpu_custom_call" | custom-call | tf_op jit(solution)/shard_map/pallas_call | solution.py:116
  76.2 1.1 copy.21
  77.3 4.8 %fusion.1 = bf16[4096,256]{0,1:T(8,128)(2,1)} fusion(bf16[256,512]{0,1:T(8,128)(2,1)S(1)} %bitcast.43, bf16[512,4096]{1,0:T(8,128)(2,1)} %param.19), kind=kOutput, calls=%fused_computation.7 | convolution fusion | flops 1074790400 | bytes 6553600 | tf_op jit(solution)/shard_map/dot_general | solution.py:40
  82.2 43.7 %reduce-scatter.3.cloned.1.call-done = bf16[512,256]{0,1:T(8,128)(2,1)} async-done(((bf16[4096,256]{0,1:T(8,128)(2,1)}), bf16[512,256]{0,1:T(8,128)(2,1)}) %reduce-scatter.3.cloned.1.call-update) | async-done | bytes 262160 | tf_op jit(solution)/shard_map/reduce_scatter | solution.py:216
  125.9 1.7 fusion.17
  127.7 28.0 %all-gather.5.cloned.1.call-done = bf16[256,4096]{1,0:T(8,128)(2,1)} async-done(((bf16[256,512]{1,0:T(8,128)(2,1)}), bf16[256,4096]{1,0:T(8,128)(2,1)}) %all-gather.5.cloned.1.call-update) | async-done | bytes 2097168 | tf_op jit(solution)/shard_map/all_gather | solution.py:220
  155.8 2.1 fusion.5
  157.9 7.0 %fusion.11 = f32[256,1376]{0,1:T(8,128)S(1)} fusion(bf16[4096,1376]{0,1:T(8,128)(2,1)} %param.20, bf16[256,4096]{1,0:T(8,128)(2,1)} %all-gather.5.cloned.1.call-done, f32[4096]{0:T(1024)S(1)} %convert_element_type.79, f32[256]{0:T(256)S(1)} %add_rsqrt_fusion), kind=kOutput, calls=%fused_computation.18 | convolution fusion | flops 2889875456 | bytes 14795776 | tf_op jit(solution)/shard_map/dot_general | solution.py:222
  164.9 21.8 %fusion = bf16[4096,256]{0,1:T(8,128)(2,1)} fusion(bf16[1376,4096]{1,0:T(8,128)(2,1)} %param.22, bf16[4096,1376]{0,1:T(8,128)(2,1)} %param.21, f32[256,1376]{0,1:T(8,128)S(1)} %fusion.11, bf16[256,4096]{1,0:T(8,128)(2,1)} %all-gather.5.cloned.1.call-done, f32[4096]{0:T(1024)S(1)} %convert_element_type.79, f32[256]{0:T(256)S(1)} %add_rsqrt_fusion), kind=kOutput, calls=%fused_computation.6 | convolution fusion | flops 5778718720 | bytes 28165120 | tf_op jit(solution)/shard_map/dot_general | solution.py:40
  186.7 0.6 iota_compare_fusion
  187.2 0.1 copy_bitcast_fusion
  187.4 0.7 fusion.20
  188.1 33.9 %reduce-scatter.5.cloned.1.call-done = bf16[512,256]{0,1:T(8,128)(2,1)} async-done(((bf16[4096,256]{0,1:T(8,128)(2,1)}), bf16[512,256]{0,1:T(8,128)(2,1)}) %reduce-scatter.5.cloned.1.call-update) | async-done | bytes 262160 | tf_op jit(solution)/shard_map/reduce_scatter | solution.py:225
  222.1 1.8 fusion.18
  (31 shorter events, 0.3 us)
Async XLA Ops:
  7.2 39.2 %copy-start = (bf16[4096,128]{1,0:T(8,128)(2,1)S(1)}, bf16[4096,128]{1,0:T(8,128)(2,1)}, u32[]{:S(2)}) copy-start(bf16[4096,128]{1,0:T(8,128)(2,1)} %param.18) | copy-start | bytes 3145732
  7.2 36.9 %all-gather.3.cloned.1.call-start = ((), (), s32[]{:S(2)}) async-start(), calls=%async_computation.2 | async-start | bytes 2359296 | tf_op jit(solution)/shard_map/all_gather | solution.py:186
  7.9 118.0 %reduce-scatter.3.cloned.1.call-start = ((), (), s32[]{:S(2)}) async-start(), calls=%async_computation.3 | async-start | bytes 2359296 | tf_op jit(solution)/shard_map/reduce_scatter | solution.py:216
  8.6 13.5 %collective-permute-start.2 = (s32[2,8]{1,0:T(2,128)S(1)}, s32[2,8]{1,0:T(2,128)S(1)}, u32[]{:S(2)}, u32[]{:S(2)}) collective-permute-start(s32[2,8]{1,0:T(2,128)S(1)} %pad_add_fusion), channel_id=1, source_target_pairs={{0,24},{8,0},{16,8},{24,16},{1,25},{9,1},{17,9},{25,17},{2,26},{10... | collective-permute-start | bytes 200 | tf_op jit(solution)/shard_map/ppermute | solution.py:142
  12.5 9.7 %collective-permute-start.1 = (s32[2,8]{1,0:T(2,128)S(1)}, s32[2,8]{1,0:T(2,128)S(1)}, u32[]{:S(2)}, u32[]{:S(2)}) collective-permute-start(s32[2,8]{1,0:T(2,128)S(1)} %pad_add_fusion), channel_id=1, source_target_pairs={{0,16},{8,24},{16,0},{24,8},{1,17},{9,25},{17,1},{25,9},{2,18},{10... | collective-permute-start | bytes 200 | tf_op jit(solution)/shard_map/ppermute | solution.py:142
  14.2 27.4 %collective-permute-start.5 = (bf16[8,128,256]{2,1,0:T(8,128)(2,1)S(1)}, bf16[8,128,256]{2,1,0:T(8,128)(2,1)S(1)}, u32[]{:S(2)}, u32[]{:S(2)}) collective-permute-start(bf16[8,128,256]{2,1,0:T(8,128)(2,1)S(1)} %pad_maximum_fusion.1), channel_id=1, source_target_pairs={{0,24},{8,0},{16,8},{24,16},{1,25},{9,1},{17,9},{25,17},{2,26},{10... | collective-permute-start | bytes 1572872 | tf_op jit(solution)/shard_map/ppermute | solution.py:142
  14.3 27.3 %collective-permute-start.4 = (bf16[8,128,256]{2,1,0:T(8,128)(2,1)S(1)}, bf16[8,128,256]{2,1,0:T(8,128)(2,1)S(1)}, u32[]{:S(2)}, u32[]{:S(2)}) collective-permute-start(bf16[8,128,256]{2,1,0:T(8,128)(2,1)S(1)} %pad_maximum_fusion.1), channel_id=1, source_target_pairs={{0,16},{8,24},{16,0},{24,8},{1,17},{9,25},{17,1},{25,9},{2,18},{10... | collective-permute-start | bytes 1572872 | tf_op jit(solution)/shard_map/ppermute | solution.py:142
  16.3 25.3 %collective-permute-start.3 = (bf16[8,128,256]{2,1,0:T(8,128)(2,1)S(1)}, bf16[8,128,256]{2,1,0:T(8,128)(2,1)}, u32[]{:S(2)}, u32[]{:S(2)}) collective-permute-start(bf16[8,128,256]{2,1,0:T(8,128)(2,1)S(1)} %pad_maximum_fusion.1), channel_id=1, source_target_pairs={{0,8},{8,16},{16,24},{24,0},{1,9},{9,17},{17,25},{25,1},{2,10},{10... | collective-permute-start | bytes 1572872 | tf_op jit(solution)/shard_map/ppermute | solution.py:142
  22.2 17.5 %collective-permute-start = (s32[2,8]{1,0:T(2,128)S(1)}, s32[2,8]{1,0:T(2,128)S(1)}, u32[]{:S(2)}, u32[]{:S(2)}) collective-permute-start(s32[2,8]{1,0:T(2,128)S(1)} %pad_add_fusion), channel_id=1, source_target_pairs={{0,8},{8,16},{16,24},{24,0},{1,9},{9,17},{17,25},{25,1},{2,10},{10... | collective-permute-start | bytes 200 | tf_op jit(solution)/shard_map/ppermute | solution.py:142
  44.1 19.8 %copy-start.3 = (bf16[256,4096]{1,0:T(8,128)(2,1)S(1)}, bf16[256,4096]{1,0:T(8,128)(2,1)}, u32[]{:S(2)}) copy-start(bf16[256,4096]{1,0:T(8,128)(2,1)} %all-gather.3.cloned.1.call-done) | copy-start | bytes 6291460
  44.1 19.8 %copy-start.6 = (bf16[4096,512]{1,0:T(8,128)(2,1)S(1)}, bf16[4096,512]{1,0:T(8,128)(2,1)}, u32[]{:S(2)}) copy-start(bf16[4096,512]{1,0:T(8,128)(2,1)} %param.17) | copy-start | bytes 12582916
  77.3 48.7 %copy-start.4 = (bf16[256,512]{1,0:T(8,128)(2,1)S(1)}, bf16[256,512]{1,0:T(8,128)(2,1)}, u32[]{:S(2)}) copy-start(bf16[256,512]{1,0:T(8,128)(2,1)} %param.14) | copy-start | bytes 786436
  77.3 50.4 %copy-start.5 = (bf16[4096]{0:T(1024)(128)(2,1)S(1)}, bf16[4096]{0:T(1024)(128)(2,1)}, u32[]{:S(2)}) copy-start(bf16[4096]{0:T(1024)(128)(2,1)} %param.16) | copy-start | bytes 24580
  82.2 73.6 %all-gather.5.cloned.1.call-start = ((), (), s32[]{:S(2)}) async-start(), calls=%async_computation.4 | async-start | bytes 2359296 | tf_op jit(solution)/shard_map/all_gather | solution.py:220
  127.7 94.4 %reduce-scatter.5.cloned.1.call-start = ((), (), s32[]{:S(2)}) async-start(), calls=%async_computation.5 | async-start | bytes 2359296 | tf_op jit(solution)/shard_map/reduce_scatter | solution.py:225
  164.8 57.2 %copy-start.2 = (bf16[256,512]{1,0:T(8,128)(2,1)S(1)}, bf16[256,512]{1,0:T(8,128)(2,1)}, u32[]{:S(2)}) copy-start(bf16[256,512]{1,0:T(8,128)(2,1)} %fusion.17) | copy-start | bytes 786436
  164.8 59.0 %copy-start.1 = (bf16[4096,128]{1,0:T(8,128)(2,1)S(1)}, bf16[4096,128]{1,0:T(8,128)(2,1)}, u32[]{:S(2)}) copy-start(bf16[4096,128]{1,0:T(8,128)(2,1)} %param.18) | copy-start | bytes 3145732
Sparse Core Ops, SparseCore 0:
  9.6 31.7 all-gather.2
  82.3 43.6 reduce-scatter.2
  128.1 27.6 all-gather.4
  186.8 35.2 reduce-scatter.4

commit v4 on v1

--- a/solution.py
+++ b/solution.py
@@ -2,6 +2,8 @@
 import jax.numpy as jnp
 from jax import lax
 from jax.sharding import PartitionSpec as P
+from jax.experimental import pallas as pl
+from jax.experimental.pallas import tpu as pltpu
 
 HQ = 32
 KVH = 4
@@ -38,6 +40,96 @@
     return lax.dot_general(
         weight, rows, (((0,), (1,)), ((), ())), preferred_element_type=jnp.float32
     )
+
+
+def attn_kernel(
+    idx_ref, cnt_ref, span_ref, q_ref, cache_ref, bias_ref, nk_ref, nv_ref, o_ref
+):
+    span_size = nk_ref.shape[0]
+    chunk = BLK
+    scale = HD ** (-0.5)
+    dims = (((1,), (1,)), ((), ()))
+    count = cnt_ref[0]
+    span = span_ref[0]
+    row = lax.broadcasted_iota(jnp.int32, (chunk, BLK), 0)
+    col = lax.broadcasted_iota(jnp.int32, (chunk, BLK), 1)
+
+    def raw(q, keys):
+        return lax.dot_general(q, keys, dims, preferred_element_type=jnp.float32)
+
+    def one_chunk(c, carry):
+        start = pl.multiple_of(c * chunk, chunk)
+        q = q_ref[pl.ds(start, chunk), :]
+        first = lax.rem(start, span_size)
+
+        def new_ok(jb):
+            j = jb * BLK + col
+            return (j <= first + row) & (j < span)
+
+        def max_step(i, top):
+            slot = idx_ref[i]
+            return jnp.maximum(top, raw(q, cache_ref[slot, :, :HD]) + bias_ref[pl.ds(slot, 1), :])
+
+        top = lax.fori_loop(0, count, max_step, jnp.full((chunk, BLK), NEG, jnp.float32))
+        for jb in range(span_size // BLK):
+            sc = raw(q, nk_ref[jb * BLK : (jb + 1) * BLK, :])
+            top = jnp.maximum(top, jnp.where(new_ok(jb), sc, NEG))
+        peak = jnp.max(top, axis=1, keepdims=True) * scale
+
+        def sum_step(i, acc):
+            slot = idx_ref[i]
+            sc = raw(q, cache_ref[slot, :, :HD]) * scale + bias_ref[pl.ds(slot, 1), :]
+            w = jnp.exp(sc - peak)
+            pv = jnp.dot(w.astype(jnp.bfloat16), cache_ref[slot, :, HD:], preferred_element_type=jnp.float32)
+            return (acc[0] + w, acc[1] + pv)
+
+        zeros = jnp.zeros((chunk, BLK), jnp.float32)
+        total, summed = lax.fori_loop(0, count, sum_step, (zeros, jnp.zeros((chunk, HD), jnp.float32)))
+        for jb in range(span_size // BLK):
+            sc = raw(q, nk_ref[jb * BLK : (jb + 1) * BLK, :]) * scale
+            w = jnp.where(new_ok(jb), jnp.exp(sc - peak), 0.0)
+            total = total + w
+            summed = summed + jnp.dot(
+                w.astype(jnp.bfloat16), nv_ref[jb * BLK : (jb + 1) * BLK, :], preferred_element_type=jnp.float32
+            )
+        o_ref[pl.ds(start, chunk), :] = (summed / jnp.sum(total, axis=1, keepdims=True)).astype(o_ref.dtype)
+        return carry
+
+    lax.fori_loop(0, q_ref.shape[0] // chunk, one_chunk, 0)
+
+
+def local_attention(limit, span, q_rows, cache_all, new_keys, new_vals):
+    rows = q_rows.shape[0]
+    slots = limit.shape[0]
+    live = limit > 0
+    place = jnp.where(live, jnp.cumsum(live.astype(jnp.int32)) - 1, slots)
+    order = jnp.zeros((slots,), jnp.int32).at[place].set(
+        jnp.arange(slots, dtype=jnp.int32), mode="drop"
+    )
+    count = jnp.sum(live.astype(jnp.int32)).reshape(1)
+    bias = jnp.where(
+        jnp.arange(BLK, dtype=jnp.int32)[None, :] < limit[:, None], 0.0, NEG
+    ).astype(jnp.float32)
+
+    def whole(shape):
+        return pl.BlockSpec(shape, lambda i, *_: (0,) * len(shape))
+
+    return pl.pallas_call(
+        attn_kernel,
+        out_shape=jax.ShapeDtypeStruct((rows, HD), jnp.bfloat16),
+        grid_spec=pltpu.PrefetchScalarGridSpec(
+            num_scalar_prefetch=3,
+            grid=(1,),
+            in_specs=[
+                whole(q_rows.shape),
+                whole(cache_all.shape),
+                whole(bias.shape),
+                whole(new_keys.shape),
+                whole(new_vals.shape),
+            ],
+            out_specs=whole((rows, HD)),
+        ),
+    )(order, count, span, q_rows, cache_all, bias, new_keys, new_vals)
 
 
 def gather_ctx(value, count):
@@ -108,29 +200,15 @@
     new_keys = lax.dynamic_index_in_dim(all_keys, group, 1, keepdims=False)
     new_vals = lax.dynamic_slice_in_dim(kv_all, KVH * HD + group * HD, HD, 1)
 
-    cache_rows = cache_all.shape[0] * BLK
-    keys = jnp.concatenate([cache_all[..., :HD].reshape(cache_rows, HD), new_keys], axis=0)
-    vals = jnp.concatenate([cache_all[..., HD:].reshape(cache_rows, HD), new_vals], axis=0)
-    key_pos = meta_all[1][:, None] * BLK + jnp.arange(BLK, dtype=jnp.int32)[None, :]
-    cache_ok = ((meta_all[0][:, None] == ctx_rank) & (key_pos < my_len)).reshape(cache_rows)
-    new_ok = (offsets[None, :] <= offsets[:, None]) & (offsets[None, :] < my_span)
-    valid = jnp.concatenate(
-        [jnp.broadcast_to(cache_ok[None, :], (span_size, cache_rows)), new_ok], axis=1
-    )
-    scores = jnp.einsum(
-        "chd,kd->hck", query, keys, preferred_element_type=jnp.float32
-    ) * HD ** (-0.5)
-    peak = jnp.max(jnp.where(valid[None], scores, NEG), axis=2)
-    weights = jnp.where(valid[None], jnp.exp(scores - peak[..., None]), 0.0)
-    total = jnp.sum(weights, axis=2)
-    summed = jnp.einsum(
-        "hck,kd->hcd", weights.astype(jnp.bfloat16), vals, preferred_element_type=jnp.float32
+    limit = jnp.where(
+        meta_all[0] == ctx_rank, jnp.clip(my_len - meta_all[1] * BLK, 0, BLK), 0
+    ).astype(jnp.int32)
+    q_rows = query.transpose(1, 0, 2).reshape(heads_dev * span_size, HD)
+    attn_heads = local_attention(
+        limit, my_span.reshape(1).astype(jnp.int32), q_rows, cache_all, new_keys, new_vals
     )
     attn_rows = (
-        (summed / total[..., None])
-        .transpose(1, 0, 2)
-        .reshape(span_size, q_cols)
-        .astype(jnp.bfloat16)
+        attn_heads.reshape(heads_dev, span_size, HD).transpose(1, 0, 2).reshape(span_size, q_cols)
     )
     head_sum = lax.psum_scatter(
         column_term(attn_rows, w_out).astype(jnp.bfloat16), "tp", scatter_dimension=0, tiled=True

time: 242 us -> 278 us (1.15)
  waiting for transfers between devices: 108 us -> 150 us
  Pallas kernels: 0 us -> 25.9 us
  other arithmetic: 38 us -> 18.6 us
  matrix products: 51.5 us -> 37.5 us
    reduce_scatter x1, waiting for transfers between devices: 34.6 us -> 73.5 us  [per_device(): lax.psum_scatter(column_term(attn_rows, w_out).astype(jnp.bfloat16), 'tp'...]
    pallas_call x0 -> x1, Pallas kernels: none -> 25.9 us  [local_attention(): pl.pallas_call(attn_kernel, out_shape=jax.ShapeDtypeStruct((rows, HD), jn...]
    sub x1 -> x0, other arithmetic: 18.6 us -> none  [per_device(): weights = jnp.where(valid[None], jnp.exp(scores - peak[..., None]), 0.0)]
    dot_general x2 -> x0, matrix products: 13.7 us -> none  [the longest x1 8.66 us: per_device(): jnp.einsum('chd,kd->hck', query, keys, preferred_element_type=jnp.float32)]
    concatenate x1, other arithmetic: 5.12 us -> 0.85 us  [rotate(): jnp.concatenate([first * cosine - second * sine, second * cosine + first...]
    ppermute x6, waiting for transfers between devices: 10.4 us -> 13.4 us  [gather_ctx(): parts.append(lax.ppermute(value, 'ctx', pairs))]
  transfers between devices with their start and end apart: 10 -> 10, of which waited for: 4 -> 5; matrix products, arithmetic and copies ran while one was open for 7% -> 5% of each run, Pallas kernels for 0% -> 0%
where the time goes in v4:
time: 278 us; the launch traced here: 277 us
  waiting for transfers between devices  150 us (54%)
  matrix products  37.5 us (13%)
  Pallas kernels  25.9 us (9%)
  other arithmetic  18.6 us (7%)
  blocking collectives  14.3 us (5%)
  between operations  14 us (5%)
  starting transfers between devices  9.11 us (3%)
  local copies, waits for them, and re-layouts  8.51 us (3%)
    reduce_scatter x1, waiting for transfers between devices, per_device(): lax.psum_scatter(column_term(attn_rows, w_out).astype(jnp.bfloat16), 'tp'...  73.5 us
    reduce_scatter x1, waiting for transfers between devices, per_device(): lax.psum_scatter(column_term(hidden, w_down).astype(jnp.bfloat16), 'tp',...  33.8 us
    all_gather x1, waiting for transfers between devices, per_device(): full_mid = lax.all_gather(mid, 'tp', axis=1, tiled=True)  28.2 us
    dot_general x2, matrix products, column_term(): lax.dot_general(weight, rows, (((0,), (1,)), ((), ())), preferred_element...  26.6 us
    pallas_call x1, Pallas kernels, local_attention(): pl.pallas_call(attn_kernel, out_shape=jax.ShapeDtypeStruct((rows, HD), jn...  25.9 us
    all_gather x1, blocking collectives, per_device(): kv_all = lax.all_gather(kv_piece, 'tp', axis=1, tiled=True)  14.3 us
    ppermute x6, waiting for transfers between devices, gather_ctx(): parts.append(lax.ppermute(value, 'ctx', pairs))  13.4 us
    ppermute x6, starting transfers between devices, gather_ctx(): parts.append(lax.ppermute(value, 'ctx', pairs))  8.96 us
  transfers between devices with their start and end apart: 10, of which 5 were waited for; matrix products, arithmetic and copies ran while one was open for 5% of the time, Pallas kernels for 0%

profile of v4, /device:TPU:0, one launch (start us, length us, event | category | flops | bytes accessed | tf_op | source)
XLA Modules:
  0.0 277.5 jit_solution(13546205312836048158)
XLA Ops:
  7.2 0.7 all-gather.3.cloned.1.call-update
  8.0 0.7 pad_add_fusion
  8.6 3.9 %collective-permute-start.2 = (s32[2,8]{1,0:T(2,128)S(1)}, s32[2,8]{1,0:T(2,128)S(1)}, u32[]{:S(2)}, u32[]{:S(2)}) collective-permute-start(s32[2,8]{1,0:T(2,128)S(1)} %pad_add_fusion), channel_id=1, source_target_pairs={{0,24},{8,0},{16,8},{24,16},{1,25},{9,1},{17,9},{25,17},{2,26},{10... | collective-permute-start | bytes 200 | tf_op jit(solution)/shard_map/ppermute | solution.py:139
  12.5 0.5 collective-permute-start.1
  13.0 0.6 collective-permute-start
  13.6 1.1 constant_dynamic-slice_fusion.2
  14.8 2.4 collective-permute-start.5
  17.2 1.5 collective-permute-start.4
  18.7 1.3 dynamic_slice.22.span_ref
  20.0 1.2 dynamic_slice.23
  21.3 0.7 convert_element_type.84
  22.0 0.7 add_convert_fusion.1
  22.6 0.5 multiply_cosine_fusion
  23.3 0.8 pad_add_fusion.1
  24.0 1.3 fusion.23
  25.7 1.2 scatter_custom_fusion.idx_ref
  26.9 0.7 fusion.22.bias_ref
  27.6 2.5 collective-permute-done.5
  30.1 10.9 %collective-permute-done.4 = bf16[8,128,256]{2,1,0:T(8,128)(2,1)S(1)} collective-permute-done((bf16[8,128,256]{2,1,0:T(8,128)(2,1)S(1)}, bf16[8,128,256]{2,1,0:T(8,128)(2,1)S(1)}, u32[]{:S(2)}, u32[]{:S(2)}) %collective-permute-start.4) | collective-permute-done | bytes 524320 | tf_op jit(solution)/shard_map/ppermute | solution.py:139
  41.0 2.4 pad_maximum_fusion.cache_ref
  43.3 2.2 fusion.2
  45.6 2.6 convolution_convert_fusion.2
  48.2 14.3 %all_gather.10 = bf16[256,1024]{1,0:T(8,128)(2,1)S(1)} all-gather(bf16[256,128]{1,0:T(8,128)(2,1)S(1)} %convolution_convert_fusion.2), channel_id=1, replica_groups=mesh['ctx'=4,'tp'=8] {'tp'}, dimensions={1}, use_global_device_ids=true | all-gather | bytes 589824 | tf_op jit(solution)/shard_map/all_gather | solution.py:193
  62.5 0.6 constant_dynamic-slice_fusion.nv_ref
  63.2 1.3 fusion.14
  64.5 0.2 reshape.200
  64.7 0.2 reshape.209
  64.8 0.3 fusion.29
  65.2 0.3 fusion.30
  65.5 0.1 multiply_subtract_fusion
  65.7 0.1 maximum_convert_fusion
  65.8 0.6 dynamic-slice_bitcast_fusion.nk_ref
  66.5 0.1 subtract_convert_fusion
  66.6 0.9 pad_maximum_fusion.2
  67.5 25.9 %shard_map.149 = bf16[1024,128]{1,0:T(8,128)(2,1)} custom-call(s32[32]{0:T(128)} %scatter_custom_fusion.idx_ref, s32[1]{0:T(128)} %bitcast.6.cnt_ref, s32[1]{0:T(128)} %dynamic_slice.22.span_ref, bf16[1024,128]{1,0:T(8,128)(2,1)} %bitcast.48, bf16[32,128,256]{2,1,0:T(8,128)(2,1)} %pad_maximum_fusion.cache_ref, f32[32,128]{1,0:T(8,128)} %fusion.22.bias_ref, ...), custom_call_target="tpu_custom_call" | custom-call | tf_op jit(solution)/shard_map/pallas_call | solution.py:117
  93.4 1.1 copy.25
  94.5 4.8 %fusion.1 = bf16[4096,256]{0,1:T(8,128)(2,1)} fusion(bf16[256,512]{0,1:T(8,128)(2,1)S(1)} %bitcast.47, bf16[512,4096]{1,0:T(8,128)(2,1)} %param.19), kind=kOutput, calls=%fused_computation.8 | convolution fusion | flops 1074790400 | bytes 6553600 | tf_op jit(solution)/shard_map/dot_general | solution.py:40
  99.4 73.5 %reduce-scatter.3.cloned.1.call-done = bf16[512,256]{0,1:T(8,128)(2,1)} async-done(((bf16[4096,256]{0,1:T(8,128)(2,1)}), bf16[512,256]{0,1:T(8,128)(2,1)}) %reduce-scatter.3.cloned.1.call-update) | async-done | bytes 262160 | tf_op jit(solution)/shard_map/reduce_scatter | solution.py:213
  172.9 1.7 fusion.17
  174.7 28.2 %all-gather.5.cloned.1.call-done = bf16[256,4096]{1,0:T(8,128)(2,1)} async-done(((bf16[256,512]{1,0:T(8,128)(2,1)}), bf16[256,4096]{1,0:T(8,128)(2,1)}) %all-gather.5.cloned.1.call-update) | async-done | bytes 2097168 | tf_op jit(solution)/shard_map/all_gather | solution.py:217
  202.9 2.1 fusion.5
  205.0 7.0 %fusion.11 = f32[256,1376]{0,1:T(8,128)S(1)} fusion(bf16[4096,1376]{0,1:T(8,128)(2,1)} %param.20, bf16[256,4096]{1,0:T(8,128)(2,1)} %all-gather.5.cloned.1.call-done, f32[4096]{0:T(1024)S(1)} %convert_element_type.94, f32[256]{0:T(256)S(1)} %add_rsqrt_fusion), kind=kOutput, calls=%fused_computation.19 | convolution fusion | flops 2889875456 | bytes 14795776 | tf_op jit(solution)/shard_map/dot_general | solution.py:219
  212.0 21.8 %fusion = bf16[4096,256]{0,1:T(8,128)(2,1)} fusion(bf16[1376,4096]{1,0:T(8,128)(2,1)} %param.22, bf16[4096,1376]{0,1:T(8,128)(2,1)} %param.21, f32[256,1376]{0,1:T(8,128)S(1)} %fusion.11, bf16[256,4096]{1,0:T(8,128)(2,1)} %all-gather.5.cloned.1.call-done, f32[4096]{0:T(1024)S(1)} %convert_element_type.94, f32[256]{0:T(256)S(1)} %add_rsqrt_fusion), kind=kOutput, calls=%fused_computation.7 | convolution fusion | flops 5778718720 | bytes 28165120 | tf_op jit(solution)/shard_map/dot_general | solution.py:40
  233.8 0.7 iota_compare_fusion.1
  234.5 0.1 copy_bitcast_fusion
  234.6 0.7 fusion.20
  235.4 33.8 %reduce-scatter.5.cloned.1.call-done = bf16[512,256]{0,1:T(8,128)(2,1)} async-done(((bf16[4096,256]{0,1:T(8,128)(2,1)}), bf16[512,256]{0,1:T(8,128)(2,1)}) %reduce-scatter.5.cloned.1.call-update) | async-done | bytes 262160 | tf_op jit(solution)/shard_map/reduce_scatter | solution.py:222
  269.2 1.8 fusion.18
  (39 shorter events, 0.8 us)
Async XLA Ops:
  7.2 38.4 %copy-start = (bf16[4096,128]{1,0:T(8,128)(2,1)S(1)}, bf16[4096,128]{1,0:T(8,128)(2,1)}, u32[]{:S(2)}) copy-start(bf16[4096,128]{1,0:T(8,128)(2,1)} %param.18) | copy-start | bytes 3145732
  7.2 36.1 %all-gather.3.cloned.1.call-start = ((), (), s32[]{:S(2)}) async-start(), calls=%async_computation.2 | async-start | bytes 2359296 | tf_op jit(solution)/shard_map/all_gather | solution.py:183
  7.9 165.0 %reduce-scatter.3.cloned.1.call-start = ((), (), s32[]{:S(2)}) async-start(), calls=%async_computation.3 | async-start | bytes 2359296 | tf_op jit(solution)/shard_map/reduce_scatter | solution.py:213
  8.6 14.5 %collective-permute-start.2 = (s32[2,8]{1,0:T(2,128)S(1)}, s32[2,8]{1,0:T(2,128)S(1)}, u32[]{:S(2)}, u32[]{:S(2)}) collective-permute-start(s32[2,8]{1,0:T(2,128)S(1)} %pad_add_fusion), channel_id=1, source_target_pairs={{0,24},{8,0},{16,8},{24,16},{1,25},{9,1},{17,9},{25,17},{2,26},{10... | collective-permute-start | bytes 200 | tf_op jit(solution)/shard_map/ppermute | solution.py:139
  12.5 10.7 %collective-permute-start.1 = (s32[2,8]{1,0:T(2,128)S(1)}, s32[2,8]{1,0:T(2,128)S(1)}, u32[]{:S(2)}, u32[]{:S(2)}) collective-permute-start(s32[2,8]{1,0:T(2,128)S(1)} %pad_add_fusion), channel_id=1, source_target_pairs={{0,16},{8,24},{16,0},{24,8},{1,17},{9,25},{17,1},{25,9},{2,18},{10... | collective-permute-start | bytes 200 | tf_op jit(solution)/shard_map/ppermute | solution.py:139
  13.0 10.2 %collective-permute-start = (s32[2,8]{1,0:T(2,128)S(1)}, s32[2,8]{1,0:T(2,128)S(1)}, u32[]{:S(2)}, u32[]{:S(2)}) collective-permute-start(s32[2,8]{1,0:T(2,128)S(1)} %pad_add_fusion), channel_id=1, source_target_pairs={{0,8},{8,16},{16,24},{24,0},{1,9},{9,17},{17,25},{25,1},{2,10},{10... | collective-permute-start | bytes 200 | tf_op jit(solution)/shard_map/ppermute | solution.py:139
  14.8 15.3 %collective-permute-start.5 = (bf16[8,128,256]{2,1,0:T(8,128)(2,1)S(1)}, bf16[8,128,256]{2,1,0:T(8,128)(2,1)S(1)}, u32[]{:S(2)}, u32[]{:S(2)}) collective-permute-start(bf16[8,128,256]{2,1,0:T(8,128)(2,1)S(1)} %pad_maximum_fusion.1), channel_id=1, source_target_pairs={{0,24},{8,0},{16,8},{24,16},{1,25},{9,1},{17,9},{25,17},{2,26},{10... | collective-permute-start | bytes 1572872 | tf_op jit(solution)/shard_map/ppermute | solution.py:139
  17.2 23.8 %collective-permute-start.4 = (bf16[8,128,256]{2,1,0:T(8,128)(2,1)S(1)}, bf16[8,128,256]{2,1,0:T(8,128)(2,1)S(1)}, u32[]{:S(2)}, u32[]{:S(2)}) collective-permute-start(bf16[8,128,256]{2,1,0:T(8,128)(2,1)S(1)} %pad_maximum_fusion.1), channel_id=1, source_target_pairs={{0,16},{8,24},{16,0},{24,8},{1,17},{9,25},{17,1},{25,9},{2,18},{10... | collective-permute-start | bytes 1572872 | tf_op jit(solution)/shard_map/ppermute | solution.py:139
  23.2 17.8 %collective-permute-start.3 = (bf16[8,128,256]{2,1,0:T(8,128)(2,1)S(1)}, bf16[8,128,256]{2,1,0:T(8,128)(2,1)}, u32[]{:S(2)}, u32[]{:S(2)}) collective-permute-start(bf16[8,128,256]{2,1,0:T(8,128)(2,1)S(1)} %pad_maximum_fusion.1), channel_id=1, source_target_pairs={{0,8},{8,16},{16,24},{24,0},{1,9},{9,17},{17,25},{25,1},{2,10},{10... | collective-permute-start | bytes 1572872 | tf_op jit(solution)/shard_map/ppermute | solution.py:139
  43.3 19.8 %copy-start.3 = (bf16[256,4096]{1,0:T(8,128)(2,1)S(1)}, bf16[256,4096]{1,0:T(8,128)(2,1)}, u32[]{:S(2)}) copy-start(bf16[256,4096]{1,0:T(8,128)(2,1)} %all-gather.3.cloned.1.call-done) | copy-start | bytes 6291460
  43.3 19.9 %copy-start.6 = (bf16[4096,512]{1,0:T(8,128)(2,1)S(1)}, bf16[4096,512]{1,0:T(8,128)(2,1)}, u32[]{:S(2)}) copy-start(bf16[4096,512]{1,0:T(8,128)(2,1)} %param.17) | copy-start | bytes 12582916
  94.5 78.4 %copy-start.4 = (bf16[256,512]{1,0:T(8,128)(2,1)S(1)}, bf16[256,512]{1,0:T(8,128)(2,1)}, u32[]{:S(2)}) copy-start(bf16[256,512]{1,0:T(8,128)(2,1)} %param.14) | copy-start | bytes 786436
  94.5 80.2 %copy-start.5 = (bf16[4096]{0:T(1024)(128)(2,1)S(1)}, bf16[4096]{0:T(1024)(128)(2,1)}, u32[]{:S(2)}) copy-start(bf16[4096]{0:T(1024)(128)(2,1)} %param.16) | copy-start | bytes 24580
  99.4 103.5 %all-gather.5.cloned.1.call-start = ((), (), s32[]{:S(2)}) async-start(), calls=%async_computation.4 | async-start | bytes 2359296 | tf_op jit(solution)/shard_map/all_gather | solution.py:217
  174.6 94.6 %reduce-scatter.5.cloned.1.call-start = ((), (), s32[]{:S(2)}) async-start(), calls=%async_computation.5 | async-start | bytes 2359296 | tf_op jit(solution)/shard_map/reduce_scatter | solution.py:222
  211.9 57.3 %copy-start.2 = (bf16[256,512]{1,0:T(8,128)(2,1)S(1)}, bf16[256,512]{1,0:T(8,128)(2,1)}, u32[]{:S(2)}) copy-start(bf16[256,512]{1,0:T(8,128)(2,1)} %fusion.17) | copy-start | bytes 786436
  212.0 59.0 %copy-start.1 = (bf16[4096,128]{1,0:T(8,128)(2,1)S(1)}, bf16[4096,128]{1,0:T(8,128)(2,1)}, u32[]{:S(2)}) copy-start(bf16[4096,128]{1,0:T(8,128)(2,1)} %param.18) | copy-start | bytes 3145732
Sparse Core Ops, SparseCore 0:
  9.6 31.7 all-gather.2
  99.5 73.3 reduce-scatter.2
  175.1 27.7 all-gather.4
  233.9 35.2 reduce-scatter.4

commit v5 on v3

--- a/solution.py
+++ b/solution.py
@@ -133,6 +133,35 @@
             ],
         ),
     )(limit, span, q_rows, cache_all, new_keys, new_vals)
+
+
+def kv_routes(tp_count, kv_width):
+    per_head = HD // kv_width
+    heads_dev = HQ // tp_count
+    needs = []
+    for dev in range(tp_count):
+        group = dev * heads_dev // (HQ // KVH)
+        keys = [group * per_head + u for u in range(per_head)]
+        vals = [KVH * per_head + group * per_head + u for u in range(per_head)]
+        own_head = dev * kv_width // HD
+        own = [own_head * per_head + u for u in range(per_head)] if own_head < KVH else [dev] * per_head
+        needs.append(keys + vals + own)
+    rounds = []
+    for entry in range(len(needs[0])):
+        sets = []
+        for dev in range(tp_count):
+            src = needs[dev][entry]
+            if src == dev:
+                continue
+            for pairs in sets:
+                if all(a != src for a, _ in pairs):
+                    pairs.append((src, dev))
+                    break
+            else:
+                sets.append([(src, dev)])
+        rounds.append(sets)
+    selfs = [[needs[dev][entry] == dev for dev in range(tp_count)] for entry in range(len(needs[0]))]
+    return per_head, rounds, selfs
 
 
 def gather_ctx(value, count):
@@ -185,23 +214,41 @@
 
     full_resid = lax.all_gather(resid, "tp", axis=1, tiled=True)
     x_norm = rms_norm(full_resid, attn_gain)
+    kv_piece = jnp.dot(x_norm, w_kv, preferred_element_type=jnp.float32).astype(jnp.bfloat16)
+    kv_width = kv_piece.shape[1]
+    tp_count = lax.axis_size("tp")
+    per_head, rounds, selfs = kv_routes(tp_count, kv_width)
+    blocks = []
+    for entry, sets in enumerate(rounds):
+        is_self = jnp.asarray(selfs[entry])[tp_rank]
+        got = jnp.where(is_self, kv_piece, jnp.zeros_like(kv_piece))
+        for pairs in sets:
+            got = got + lax.ppermute(kv_piece, "tp", pairs)
+        blocks.append(got)
+
+    def head_of(parts):
+        return jnp.concatenate(parts, axis=1) if len(parts) > 1 else parts[0]
+
+    def rotated(raw):
+        return (
+            rotate(raw.astype(jnp.float32).reshape(span_size, 1, HD), positions)
+            .astype(jnp.bfloat16)
+            .reshape(span_size, HD)
+        )
+
+    new_keys = rotated(head_of(blocks[:per_head]))
+    new_vals = head_of(blocks[per_head : 2 * per_head])
+    own_rot = lax.dynamic_slice_in_dim(
+        rotated(head_of(blocks[2 * per_head :])), (tp_rank * kv_width) % HD, kv_width, 1
+    )
+    mine = jnp.where(tp_rank * kv_width < KVH * HD, own_rot, kv_piece)
+    new_kv = jnp.where(live_rows[:, None], mine, jnp.zeros_like(mine))
     query = rotate(
         jnp.dot(x_norm, w_query, preferred_element_type=jnp.float32).reshape(
             span_size, heads_dev, HD
         ),
         positions,
     ).astype(jnp.bfloat16)
-    kv_piece = jnp.dot(x_norm, w_kv, preferred_element_type=jnp.float32).astype(jnp.bfloat16)
-    kv_width = kv_piece.shape[1]
-    kv_all = lax.all_gather(kv_piece, "tp", axis=1, tiled=True)
-    all_keys = rotate(
-        kv_all[:, : KVH * HD].astype(jnp.float32).reshape(span_size, KVH, HD), positions
-    ).astype(jnp.bfloat16)
-    joined = jnp.concatenate([all_keys.reshape(span_size, KVH * HD), kv_all[:, KVH * HD :]], axis=1)
-    mine = lax.dynamic_slice_in_dim(joined, tp_rank * kv_width, kv_width, 1)
-    new_kv = jnp.where(live_rows[:, None], mine, jnp.zeros_like(mine))
-    new_keys = lax.dynamic_index_in_dim(all_keys, group, 1, keepdims=False)
-    new_vals = lax.dynamic_slice_in_dim(kv_all, KVH * HD + group * HD, HD, 1)
 
     limit = jnp.where(
         meta_all[0] == ctx_rank, jnp.clip(my_len - meta_all[1] * BLK, 0, BLK), 0

time: 231 us -> 233 us (level)
  blocking collectives: 14.2 us -> 0 us
  Pallas kernels: 7.98 us -> 19 us
  waiting for transfers between devices: 124 us -> 119 us
  starting transfers between devices: 8.23 us -> 13.1 us
  other arithmetic: 17.6 us -> 20.3 us
    all_gather x1 -> x0, blocking collectives: 14.2 us -> none  [per_device(): kv_all = lax.all_gather(kv_piece, 'tp', axis=1, tiled=True)]
    pallas_call x1, Pallas kernels: 7.98 us -> 19 us  [local_attention(): pl.pallas_call(attn_kernel, out_shape=jax.ShapeDtypeStruct((rows, HD), jn...]
    ppermute x0 -> x4, starting transfers between devices: none -> 4.79 us  [per_device(): got = got + lax.ppermute(kv_piece, 'tp', pairs)]
    ppermute x6, waiting for transfers between devices: 17.4 us -> 14.1 us  [gather_ctx(): parts.append(lax.ppermute(value, 'ctx', pairs))]
    reduce_scatter x1, waiting for transfers between devices: 43.7 us -> 40.4 us  [per_device(): lax.psum_scatter(column_term(attn_rows, w_out).astype(jnp.bfloat16), 'tp'...]
    dot_general x1, matrix products: 6.96 us -> 9.31 us  [per_device(): gate = jnp.dot(x_two, w_gate, preferred_element_type=jnp.float32)]
  transfers between devices with their start and end apart: 10 -> 14, of which waited for: 4 -> 4; matrix products, arithmetic and copies ran while one was open for 5% -> 7% of each run, Pallas kernels for 0% -> 0%
where the time goes in v5:
time: 233 us
  waiting for transfers between devices  119 us (51%)
  matrix products  39.5 us (17%)
  other arithmetic  20.3 us (9%)
  Pallas kernels  19 us (8%)
  between operations  14 us (6%)
  starting transfers between devices  13.1 us (6%)
  local copies, waits for them, and re-layouts  7.83 us (3%)
    reduce_scatter x1, waiting for transfers between devices, per_device(): lax.psum_scatter(column_term(attn_rows, w_out).astype(jnp.bfloat16), 'tp'...  40.4 us
    reduce_scatter x1, waiting for transfers between devices, per_device(): lax.psum_scatter(column_term(hidden, w_down).astype(jnp.bfloat16), 'tp',...  35.5 us
    all_gather x1, waiting for transfers between devices, per_device(): full_mid = lax.all_gather(mid, 'tp', axis=1, tiled=True)  28.1 us
    dot_general x2, matrix products, column_term(): lax.dot_general(weight, rows, (((0,), (1,)), ((), ())), preferred_element...  26.3 us
    pallas_call x1, Pallas kernels, local_attention(): pl.pallas_call(attn_kernel, out_shape=jax.ShapeDtypeStruct((rows, HD), jn...  19 us
    ppermute x6, waiting for transfers between devices, gather_ctx(): parts.append(lax.ppermute(value, 'ctx', pairs))  14.1 us
    dot_general x1, matrix products, per_device(): gate = jnp.dot(x_two, w_gate, preferred_element_type=jnp.float32)  9.31 us
    ppermute x6, starting transfers between devices, gather_ctx(): parts.append(lax.ppermute(value, 'ctx', pairs))  8.02 us
  transfers between devices with their start and end apart: 14, of which 4 were waited for; matrix products, arithmetic and copies ran while one was open for 7% of the time, Pallas kernels for 0%

profile of v5, /device:TPU:0, one launch (start us, length us, event | category | flops | bytes accessed | tf_op | source)
XLA Modules:
  0.0 232.6 jit_solution(17755937607437564288)
XLA Ops:
  7.2 0.7 all-gather.3.cloned.1.call-update
  8.0 0.7 pad_add_fusion
  8.6 3.9 %collective-permute-start.2 = (s32[2,8]{1,0:T(2,128)S(1)}, s32[2,8]{1,0:T(2,128)S(1)}, u32[]{:S(2)}, u32[]{:S(2)}) collective-permute-start(s32[2,8]{1,0:T(2,128)S(1)} %pad_add_fusion), channel_id=1, source_target_pairs={{0,24},{8,0},{16,8},{24,16},{1,25},{9,1},{17,9},{25,17},{2,26},{10... | collective-permute-start | bytes 200 | tf_op jit(solution)/shard_map/ppermute | solution.py:171
  12.5 0.5 collective-permute-start.1
  13.0 1.1 constant_dynamic-slice_fusion.1
  14.1 0.1 pad_maximum_fusion.1
  14.2 0.1 collective-permute-start.5
  14.3 2.0 collective-permute-start.4
  16.3 1.5 collective-permute-start.3
  17.8 1.3 dynamic_slice.22.span_ref
  19.1 1.2 dynamic_slice.23
  20.3 1.3 dynamic_slice.27
  21.6 1.3 dynamic_slice.26
  22.9 0.7 iota_compare_fusion
  23.6 0.7 add_convert_fusion.1
  24.3 0.5 multiply_cosine_fusion.1
  24.8 0.7 convert_element_type.72
  25.5 14.1 %collective-permute-done = s32[2,8]{1,0:T(2,128)S(1)} collective-permute-done((s32[2,8]{1,0:T(2,128)S(1)}, s32[2,8]{1,0:T(2,128)S(1)}, u32[]{:S(2)}, u32[]{:S(2)}) %collective-permute-start) | collective-permute-done | bytes 96 | tf_op jit(solution)/shard_map/ppermute | solution.py:171
  39.7 0.7 pad_add_fusion.1
  40.4 1.2 fusion.40.limit_ref
  41.6 2.4 %pad_maximum_fusion.cache_ref = bf16[32,128,256]{2,1,0:T(8,128)(2,1)} fusion(bf16[8,128,256]{2,1,0:T(8,128)(2,1)S(1)} %collective-permute-done.5, bf16[8,128,256]{2,1,0:T(8,128)(2,1)S(1)} %collective-permute-done.4, bf16[8,128,256]{2,1,0:T(8,128)(2,1)} %collective-permute-done.3, bf16[8,128,128]{2,1,0:T(8,128)(2,1)S(1)} %get-tuple-element.3, ...), kind=kLoop, calls=%fused_computation.16 | loop fusion | flops 10485760 | bytes 4194304 | tf_op jit(solution)/shard_map/concatenate | solution.py:212
  44.0 2.2 fusion.2
  46.3 2.6 %bitcast_convert_fusion = (f32[256,1,128]{2,0,1:T(8,128)S(1)}, bf16[256,128]{1,0:T(8,128)(2,1)S(1)}) fusion(bf16[4096,128]{1,0:T(8,128)(2,1)S(1)} %copy-done, bf16[256,4096]{1,0:T(8,128)(2,1)} %all-gather.3.cloned.1.call-done, f32[4096]{0:T(1024)S(1)} %convert_element_type.72, f32[256]{0:T(256)S(1)} %add_rsqrt_fusion.1), kind=kOutput, calls=%fused_computation.52 | convolution fusion | flops 272695296 | bytes 3359744 | tf_op jit(solution)/shard_map/dot_general | solution.py:217
  48.9 1.3 collective-permute-start.8
  50.2 0.7 collective-permute-start.7
  50.8 2.2 collective-permute-start.6
  53.0 0.7 collective-permute-start.9
  53.7 1.3 fusion.14
  55.0 0.2 reshape.193
  55.2 0.6 fusion.37
  55.8 0.3 fusion.42
  56.1 0.1 subtract_convert_fusion
  56.2 0.9 pad_maximum_fusion.2
  57.1 2.0 fusion.35
  59.1 0.6 fusion.39
  59.7 0.7 pad_maximum_fusion.3.nk_ref
  60.4 19.0 %shard_map.176 = bf16[1024,128]{1,0:T(8,128)(2,1)} custom-call(s32[32]{0:T(128)} %fusion.40.limit_ref, s32[1]{0:T(128)} %dynamic_slice.22.span_ref, bf16[1024,128]{1,0:T(8,128)(2,1)} %bitcast.50, bf16[32,128,256]{2,1,0:T(8,128)(2,1)} %pad_maximum_fusion.cache_ref, bf16[256,128]{1,0:T(8,128)(2,1)} %pad_maximum_fusion.3.nk_ref, ...), custom_call_target="tpu_custom_call" | custom-call | tf_op jit(solution)/shard_map/pallas_call | solution.py:116
  79.4 1.1 copy.25
  80.5 4.8 %fusion.1 = bf16[4096,256]{0,1:T(8,128)(2,1)} fusion(bf16[256,512]{0,1:T(8,128)(2,1)S(1)} %bitcast.52, bf16[512,4096]{1,0:T(8,128)(2,1)} %param.22), kind=kOutput, calls=%fused_computation.7 | convolution fusion | flops 1074790400 | bytes 6553600 | tf_op jit(solution)/shard_map/dot_general | solution.py:40
  85.4 40.4 %reduce-scatter.3.cloned.1.call-done = bf16[512,256]{0,1:T(8,128)(2,1)} async-done(((bf16[4096,256]{0,1:T(8,128)(2,1)}), bf16[512,256]{0,1:T(8,128)(2,1)}) %reduce-scatter.3.cloned.1.call-update) | async-done | bytes 262160 | tf_op jit(solution)/shard_map/reduce_scatter | solution.py:263
  125.9 1.7 fusion.17
  127.6 0.2 reduce-scatter.5.cloned.1.call-start
  127.9 28.1 %all-gather.5.cloned.1.call-done = bf16[256,4096]{1,0:T(8,128)(2,1)} async-done(((bf16[256,512]{1,0:T(8,128)(2,1)}), bf16[256,4096]{1,0:T(8,128)(2,1)}) %all-gather.5.cloned.1.call-update) | async-done | bytes 2097168 | tf_op jit(solution)/shard_map/all_gather | solution.py:267
  156.0 2.1 fusion.5
  158.1 9.3 %fusion.11 = f32[256,1376]{0,1:T(8,128)} fusion(bf16[4096,1376]{0,1:T(8,128)(2,1)} %param.23, bf16[256,4096]{1,0:T(8,128)(2,1)} %all-gather.5.cloned.1.call-done, f32[4096]{0:T(1024)S(1)} %convert_element_type.81, f32[256]{0:T(256)S(1)} %add_rsqrt_fusion), kind=kOutput, calls=%fused_computation.18 | convolution fusion | flops 2889875456 | bytes 14795776 | tf_op jit(solution)/shard_map/dot_general | solution.py:269
  167.4 21.5 %fusion = bf16[4096,256]{0,1:T(8,128)(2,1)} fusion(bf16[1376,4096]{1,0:T(8,128)(2,1)} %param.25, bf16[4096,1376]{0,1:T(8,128)(2,1)} %param.24, f32[256,1376]{0,1:T(8,128)} %fusion.11, bf16[256,4096]{1,0:T(8,128)(2,1)S(1)} %copy-done.3, f32[4096]{0:T(1024)S(1)} %convert_element_type.81, f32[256]{0:T(256)S(1)} %add_rsqrt_fusion), kind=kOutput, calls=%fused_computation.6 | convolution fusion | flops 5778718720 | bytes 28165120 | tf_op jit(solution)/shard_map/dot_general | solution.py:40
  188.9 35.5 %reduce-scatter.5.cloned.1.call-done = bf16[512,256]{0,1:T(8,128)(2,1)} async-done(((bf16[4096,256]{0,1:T(8,128)(2,1)}), bf16[512,256]{0,1:T(8,128)(2,1)}) %reduce-scatter.5.cloned.1.call-update) | async-done | bytes 262160 | tf_op jit(solution)/shard_map/reduce_scatter | solution.py:272
  224.3 1.8 fusion.18
  (35 shorter events, 0.3 us)
Async XLA Ops:
  7.2 39.1 %copy-start = (bf16[4096,128]{1,0:T(8,128)(2,1)S(1)}, bf16[4096,128]{1,0:T(8,128)(2,1)}, u32[]{:S(2)}) copy-start(bf16[4096,128]{1,0:T(8,128)(2,1)} %param.21) | copy-start | bytes 3145732
  7.2 36.8 %all-gather.3.cloned.1.call-start = ((), (), s32[]{:S(2)}) async-start(), calls=%async_computation.2 | async-start | bytes 2359296 | tf_op jit(solution)/shard_map/all_gather | solution.py:215
  7.9 118.0 %reduce-scatter.3.cloned.1.call-start = ((), (), s32[]{:S(2)}) async-start(), calls=%async_computation.3 | async-start | bytes 2359296 | tf_op jit(solution)/shard_map/reduce_scatter | solution.py:263
  8.6 16.9 %collective-permute-start.2 = (s32[2,8]{1,0:T(2,128)S(1)}, s32[2,8]{1,0:T(2,128)S(1)}, u32[]{:S(2)}, u32[]{:S(2)}) collective-permute-start(s32[2,8]{1,0:T(2,128)S(1)} %pad_add_fusion), channel_id=1, source_target_pairs={{0,24},{8,0},{16,8},{24,16},{1,25},{9,1},{17,9},{25,17},{2,26},{10... | collective-permute-start | bytes 200 | tf_op jit(solution)/shard_map/ppermute | solution.py:171
  12.5 13.0 %collective-permute-start.1 = (s32[2,8]{1,0:T(2,128)S(1)}, s32[2,8]{1,0:T(2,128)S(1)}, u32[]{:S(2)}, u32[]{:S(2)}) collective-permute-start(s32[2,8]{1,0:T(2,128)S(1)} %pad_add_fusion), channel_id=1, source_target_pairs={{0,16},{8,24},{16,0},{24,8},{1,17},{9,25},{17,1},{25,9},{2,18},{10... | collective-permute-start | bytes 200 | tf_op jit(solution)/shard_map/ppermute | solution.py:171
  14.2 27.4 %collective-permute-start.5 = (bf16[8,128,256]{2,1,0:T(8,128)(2,1)S(1)}, bf16[8,128,256]{2,1,0:T(8,128)(2,1)S(1)}, u32[]{:S(2)}, u32[]{:S(2)}) collective-permute-start(bf16[8,128,256]{2,1,0:T(8,128)(2,1)S(1)} %pad_maximum_fusion.1), channel_id=1, source_target_pairs={{0,24},{8,0},{16,8},{24,16},{1,25},{9,1},{17,9},{25,17},{2,26},{10... | collective-permute-start | bytes 1572872 | tf_op jit(solution)/shard_map/ppermute | solution.py:171
  14.3 27.3 %collective-permute-start.4 = (bf16[8,128,256]{2,1,0:T(8,128)(2,1)S(1)}, bf16[8,128,256]{2,1,0:T(8,128)(2,1)S(1)}, u32[]{:S(2)}, u32[]{:S(2)}) collective-permute-start(bf16[8,128,256]{2,1,0:T(8,128)(2,1)S(1)} %pad_maximum_fusion.1), channel_id=1, source_target_pairs={{0,16},{8,24},{16,0},{24,8},{1,17},{9,25},{17,1},{25,9},{2,18},{10... | collective-permute-start | bytes 1572872 | tf_op jit(solution)/shard_map/ppermute | solution.py:171
  16.3 25.3 %collective-permute-start.3 = (bf16[8,128,256]{2,1,0:T(8,128)(2,1)S(1)}, bf16[8,128,256]{2,1,0:T(8,128)(2,1)}, u32[]{:S(2)}, u32[]{:S(2)}) collective-permute-start(bf16[8,128,256]{2,1,0:T(8,128)(2,1)S(1)} %pad_maximum_fusion.1), channel_id=1, source_target_pairs={{0,8},{8,16},{16,24},{24,0},{1,9},{9,17},{17,25},{25,1},{2,10},{10... | collective-permute-start | bytes 1572872 | tf_op jit(solution)/shard_map/ppermute | solution.py:171
  25.5 14.2 %collective-permute-start = (s32[2,8]{1,0:T(2,128)S(1)}, s32[2,8]{1,0:T(2,128)S(1)}, u32[]{:S(2)}, u32[]{:S(2)}) collective-permute-start(s32[2,8]{1,0:T(2,128)S(1)} %pad_add_fusion), channel_id=1, source_target_pairs={{0,8},{8,16},{16,24},{24,0},{1,9},{9,17},{17,25},{25,1},{2,10},{10... | collective-permute-start | bytes 200 | tf_op jit(solution)/shard_map/ppermute | solution.py:171
  44.0 9.7 %copy-start.2 = (bf16[256,4096]{1,0:T(8,128)(2,1)S(1)}, bf16[256,4096]{1,0:T(8,128)(2,1)}, u32[]{:S(2)}) copy-start(bf16[256,4096]{1,0:T(8,128)(2,1)} %all-gather.3.cloned.1.call-done) | copy-start | bytes 6291460
  44.0 9.7 %copy-start.6 = (bf16[4096,512]{1,0:T(8,128)(2,1)S(1)}, bf16[4096,512]{1,0:T(8,128)(2,1)}, u32[]{:S(2)}) copy-start(bf16[4096,512]{1,0:T(8,128)(2,1)} %param.20) | copy-start | bytes 12582916
  48.9 8.2 %collective-permute-start.8 = (bf16[256,128]{1,0:T(8,128)(2,1)S(1)}, bf16[256,128]{1,0:T(8,128)(2,1)S(1)}, u32[]{:S(2)}, u32[]{:S(2)}) collective-permute-start(bf16[256,128]{1,0:T(8,128)(2,1)S(1)} %get-tuple-element.18), channel_id=1, source_target_pairs={{4,0},{5,2},{6,4},{7,6},{12,8},{13,10},{14,12},{15,14},{20,16},{21... | collective-permute-start | bytes 196616 | tf_op jit(solution)/shard_map/ppermute | solution.py:226
  50.2 6.9 %collective-permute-start.7 = (bf16[256,128]{1,0:T(8,128)(2,1)S(1)}, bf16[256,128]{1,0:T(8,128)(2,1)S(1)}, u32[]{:S(2)}, u32[]{:S(2)}) collective-permute-start(bf16[256,128]{1,0:T(8,128)(2,1)S(1)} %get-tuple-element.18), channel_id=1, source_target_pairs={{1,3},{2,5},{3,7},{9,11},{10,13},{11,15},{17,19},{18,21},{19,23},{... | collective-permute-start | bytes 196616 | tf_op jit(solution)/shard_map/ppermute | solution.py:226
  50.8 6.3 %collective-permute-start.6 = (bf16[256,128]{1,0:T(8,128)(2,1)S(1)}, bf16[256,128]{1,0:T(8,128)(2,1)S(1)}, u32[]{:S(2)}, u32[]{:S(2)}) collective-permute-start(bf16[256,128]{1,0:T(8,128)(2,1)S(1)} %get-tuple-element.18), channel_id=1, source_target_pairs={{0,1},{1,2},{2,4},{3,6},{8,9},{9,10},{10,12},{11,14},{16,17},{17,1... | collective-permute-start | bytes 196616 | tf_op jit(solution)/shard_map/ppermute | solution.py:226
  53.0 4.1 %collective-permute-start.9 = (bf16[256,128]{1,0:T(8,128)(2,1)S(1)}, bf16[256,128]{1,0:T(8,128)(2,1)S(1)}, u32[]{:S(2)}, u32[]{:S(2)}) collective-permute-start(bf16[256,128]{1,0:T(8,128)(2,1)S(1)} %get-tuple-element.18), channel_id=1, source_target_pairs={{4,1},{5,3},{6,5},{12,9},{13,11},{14,13},{20,17},{21,19},{22,21},{... | collective-permute-start | bytes 196616 | tf_op jit(solution)/shard_map/ppermute | solution.py:226
  80.5 45.4 %copy-start.4 = (bf16[256,512]{1,0:T(8,128)(2,1)S(1)}, bf16[256,512]{1,0:T(8,128)(2,1)}, u32[]{:S(2)}) copy-start(bf16[256,512]{1,0:T(8,128)(2,1)} %param.17) | copy-start | bytes 786436
  80.5 47.3 %copy-start.5 = (bf16[4096]{0:T(1024)(128)(2,1)S(1)}, bf16[4096]{0:T(1024)(128)(2,1)}, u32[]{:S(2)}) copy-start(bf16[4096]{0:T(1024)(128)(2,1)} %param.19) | copy-start | bytes 24580
  85.4 70.6 %all-gather.5.cloned.1.call-start = ((), (), s32[]{:S(2)}) async-start(), calls=%async_computation.4 | async-start | bytes 2359296 | tf_op jit(solution)/shard_map/all_gather | solution.py:267
  127.6 96.7 %reduce-scatter.5.cloned.1.call-start = ((), (), s32[]{:S(2)}) async-start(), calls=%async_computation.5 | async-start | bytes 2359296 | tf_op jit(solution)/shard_map/reduce_scatter | solution.py:272
  158.0 9.3 %copy-start.3 = (bf16[256,4096]{1,0:T(8,128)(2,1)S(1)}, bf16[256,4096]{1,0:T(8,128)(2,1)}, u32[]{:S(2)}) copy-start(bf16[256,4096]{1,0:T(8,128)(2,1)} %all-gather.5.cloned.1.call-done) | copy-start | bytes 6291460
  167.4 57.0 %copy-start.1 = (bf16[256,512]{1,0:T(8,128)(2,1)S(1)}, bf16[256,512]{1,0:T(8,128)(2,1)}, u32[]{:S(2)}) copy-start(bf16[256,512]{1,0:T(8,128)(2,1)} %fusion.17) | copy-start | bytes 786436
Sparse Core Ops, SparseCore 0:
  9.6 31.8 all-gather.2
  85.5 40.3 reduce-scatter.2
  128.1 27.8 all-gather.4
  189.0 35.2 reduce-scatter.4

commit v6 on v5

--- a/solution.py
+++ b/solution.py
@@ -42,54 +42,52 @@
     )
 
 
-def attn_kernel(limit_ref, span_ref, q_ref, cache_ref, nk_ref, nv_ref, o_ref, m_scr, t_scr, acc_scr):
+def attn_kernel(limit_ref, span_ref, q_ref, cache_ref, bias_ref, nk_ref, nv_ref, o_ref, top_scr, tot_scr, acc_scr):
     slots = cache_ref.shape[0]
     span_size = nk_ref.shape[0]
     heads = q_ref.shape[0] // span_size
     scale = HD ** (-0.5)
     q_all = q_ref[...]
-    col = lax.broadcasted_iota(jnp.int32, (1, BLK), 1)
     row_i = lax.broadcasted_iota(jnp.int32, (span_size, span_size), 0)
     col_j = lax.broadcasted_iota(jnp.int32, (span_size, span_size), 1)
     new_ok = (col_j <= row_i) & (col_j < span_ref[0])
     dims = (((1,), (1,)), ((), ()))
 
-    def cache_scores(s):
-        keys = cache_ref[s, :, :HD]
-        return lax.dot_general(q_all, keys, dims, preferred_element_type=jnp.float32) * scale
-
-    def new_scores(h):
+    def cache_raw(s):
+        return lax.dot_general(q_all, cache_ref[s, :, :HD], dims, preferred_element_type=jnp.float32)
+
+    def new_raw(h):
         rows = q_ref[h * span_size : (h + 1) * span_size, :]
-        return lax.dot_general(rows, nk_ref[...], dims, preferred_element_type=jnp.float32) * scale
-
-    m_scr[...] = jnp.full(m_scr.shape, NEG, jnp.float32)
+        return lax.dot_general(rows, nk_ref[...], dims, preferred_element_type=jnp.float32)
+
+    top_scr[...] = jnp.full(top_scr.shape, NEG, jnp.float32)
 
     def max_step(s, carry):
-        lim = limit_ref[s]
-
-        @pl.when(lim > 0)
+        @pl.when(limit_ref[s] > 0)
         def _():
-            sc = jnp.where(col < lim, cache_scores(s), NEG)
-            m_scr[...] = jnp.maximum(m_scr[...], jnp.max(sc, axis=1, keepdims=True))
+            top_scr[...] = jnp.maximum(top_scr[...], cache_raw(s) + bias_ref[pl.ds(s, 1), :])
 
         return carry
 
     lax.fori_loop(0, slots, max_step, 0)
+    peaks = []
     for h in range(heads):
         part = slice(h * span_size, (h + 1) * span_size)
-        sc = jnp.where(new_ok, new_scores(h), NEG)
-        m_scr[part, :] = jnp.maximum(m_scr[part, :], jnp.max(sc, axis=1, keepdims=True))
-
-    t_scr[...] = jnp.zeros(t_scr.shape, jnp.float32)
+        raw_top = jnp.maximum(
+            jnp.max(top_scr[part, :], axis=1, keepdims=True),
+            jnp.max(jnp.where(new_ok, new_raw(h), NEG), axis=1, keepdims=True),
+        )
+        peaks.append(raw_top * scale)
+    peak = jnp.concatenate(peaks, axis=0)
+
+    tot_scr[...] = jnp.zeros(tot_scr.shape, jnp.float32)
     acc_scr[...] = jnp.zeros(acc_scr.shape, jnp.float32)
 
     def sum_step(s, carry):
-        lim = limit_ref[s]
-
-        @pl.when(lim > 0)
+        @pl.when(limit_ref[s] > 0)
         def _():
-            w = jnp.where(col < lim, jnp.exp(cache_scores(s) - m_scr[...]), 0.0)
-            t_scr[...] += jnp.sum(w, axis=1, keepdims=True)
+            w = jnp.exp(cache_raw(s) * scale + bias_ref[pl.ds(s, 1), :] - peak)
+            tot_scr[...] += w
             acc_scr[...] += jnp.dot(
                 w.astype(jnp.bfloat16), cache_ref[s, :, HD:], preferred_element_type=jnp.float32
             )
@@ -99,16 +97,19 @@
     lax.fori_loop(0, slots, sum_step, 0)
     for h in range(heads):
         part = slice(h * span_size, (h + 1) * span_size)
-        w = jnp.where(new_ok, jnp.exp(new_scores(h) - m_scr[part, :]), 0.0)
-        t_scr[part, :] += jnp.sum(w, axis=1, keepdims=True)
-        acc_scr[part, :] += jnp.dot(
+        w = jnp.where(new_ok, jnp.exp(new_raw(h) * scale - peak[part, :]), 0.0)
+        total = jnp.sum(tot_scr[part, :], axis=1, keepdims=True) + jnp.sum(w, axis=1, keepdims=True)
+        summed = acc_scr[part, :] + jnp.dot(
             w.astype(jnp.bfloat16), nv_ref[...], preferred_element_type=jnp.float32
         )
-    o_ref[...] = (acc_scr[...] / t_scr[...]).astype(o_ref.dtype)
+        o_ref[part, :] = (summed / total).astype(o_ref.dtype)
 
 
 def local_attention(limit, span, q_rows, cache_all, new_keys, new_vals):
     rows = q_rows.shape[0]
+    bias = jnp.where(
+        jnp.arange(BLK, dtype=jnp.int32)[None, :] < limit[:, None], 0.0, NEG
+    ).astype(jnp.float32)
 
     def whole(shape):
         return pl.BlockSpec(shape, lambda i, *_: (0,) * len(shape))
@@ -122,17 +123,18 @@
             in_specs=[
                 whole(q_rows.shape),
                 whole(cache_all.shape),
+                whole(bias.shape),
                 whole(new_keys.shape),
                 whole(new_vals.shape),
             ],
             out_specs=whole((rows, HD)),
             scratch_shapes=[
-                pltpu.VMEM((rows, 1), jnp.float32),
-                pltpu.VMEM((rows, 1), jnp.float32),
+                pltpu.VMEM((rows, BLK), jnp.float32),
+                pltpu.VMEM((rows, BLK), jnp.float32),
                 pltpu.VMEM((rows, HD), jnp.float32),
             ],
         ),
-    )(limit, span, q_rows, cache_all, new_keys, new_vals)
+    )(limit, span, q_rows, cache_all, bias, new_keys, new_vals)
 
 
 def kv_routes(tp_count, kv_width):

time: 233 us -> 229 us (0.983)
  Pallas kernels: 19 us -> 15.8 us
  waiting for transfers between devices: 119 us -> 116 us
    pallas_call x1, Pallas kernels: 19 us -> 15.8 us  [local_attention(): pl.pallas_call(attn_kernel, out_shape=jax.ShapeDtypeStruct((rows, HD), jn...]
  transfers between devices with their start and end apart: 14 -> 14, of which waited for: 4 -> 5; matrix products, arithmetic and copies ran while one was open for 7% -> 7% of each run, Pallas kernels for 0% -> 0%
where the time goes in v6:
time: 229 us; the launch traced here: 228 us
  waiting for transfers between devices  116 us (51%)
  matrix products  39.5 us (17%)
  other arithmetic  19.5 us (9%)
  Pallas kernels  15.8 us (7%)
  starting transfers between devices  14.8 us (6%)
  between operations  14 us (6%)
  local copies, waits for them, and re-layouts  7.8 us (3%)
    reduce_scatter x1, waiting for transfers between devices, per_device(): lax.psum_scatter(column_term(attn_rows, w_out).astype(jnp.bfloat16), 'tp'...  39.7 us
    reduce_scatter x1, waiting for transfers between devices, per_device(): lax.psum_scatter(column_term(hidden, w_down).astype(jnp.bfloat16), 'tp',...  35.5 us
    all_gather x1, waiting for transfers between devices, per_device(): full_mid = lax.all_gather(mid, 'tp', axis=1, tiled=True)  28 us
    dot_general x2, matrix products, column_term(): lax.dot_general(weight, rows, (((0,), (1,)), ((), ())), preferred_element...  26.3 us
    pallas_call x1, Pallas kernels, local_attention(): pl.pallas_call(attn_kernel, out_shape=jax.ShapeDtypeStruct((rows, HD), jn...  15.8 us
    ppermute x6, waiting for transfers between devices, gather_ctx(): parts.append(lax.ppermute(value, 'ctx', pairs))  12.5 us
    dot_general x1, matrix products, per_device(): gate = jnp.dot(x_two, w_gate, preferred_element_type=jnp.float32)  9.3 us
    ppermute x6, starting transfers between devices, gather_ctx(): parts.append(lax.ppermute(value, 'ctx', pairs))  8.9 us
  transfers between devices with their start and end apart: 14, of which 5 were waited for; matrix products, arithmetic and copies ran while one was open for 7% of the time, Pallas kernels for 0%

profile of v6, /device:TPU:0, one launch (start us, length us, event | category | flops | bytes accessed | tf_op | source)
XLA Modules:
  0.0 227.8 jit_solution(13275099356932954659)
XLA Ops:
  7.2 0.7 all-gather.3.cloned.1.call-update
  8.0 0.7 pad_add_fusion
  8.6 3.9 %collective-permute-start.2 = (s32[2,8]{1,0:T(2,128)S(1)}, s32[2,8]{1,0:T(2,128)S(1)}, u32[]{:S(2)}, u32[]{:S(2)}) collective-permute-start(s32[2,8]{1,0:T(2,128)S(1)} %pad_add_fusion), channel_id=1, source_target_pairs={{0,24},{8,0},{16,8},{24,16},{1,25},{9,1},{17,9},{25,17},{2,26},{10... | collective-permute-start | bytes 200 | tf_op jit(solution)/shard_map/ppermute | solution.py:173
  12.5 0.5 collective-permute-start.1
  13.0 0.6 collective-permute-start
  13.6 1.1 constant_dynamic-slice_fusion.1
  14.8 2.4 %collective-permute-start.5 = (bf16[8,128,256]{2,1,0:T(8,128)(2,1)S(1)}, bf16[8,128,256]{2,1,0:T(8,128)(2,1)S(1)}, u32[]{:S(2)}, u32[]{:S(2)}) collective-permute-start(bf16[8,128,256]{2,1,0:T(8,128)(2,1)S(1)} %pad_maximum_fusion.1), channel_id=1, source_target_pairs={{0,24},{8,0},{16,8},{24,16},{1,25},{9,1},{17,9},{25,17},{2,26},{10... | collective-permute-start | bytes 1572872 | tf_op jit(solution)/shard_map/ppermute | solution.py:173
  17.2 1.5 collective-permute-start.4
  18.7 1.3 dynamic_slice.22.span_ref
  20.0 1.2 dynamic_slice.23
  21.2 1.3 dynamic_slice.27
  22.5 1.2 dynamic_slice.26
  23.8 0.6 iota_compare_fusion.1
  24.4 0.7 add_convert_fusion.1
  25.1 0.5 multiply_cosine_fusion.1
  25.6 0.7 convert_element_type.72
  26.4 0.8 pad_add_fusion.1
  27.1 0.7 fusion.41.limit_ref
  27.8 0.7 fusion.40.bias_ref
  28.5 1.1 collective-permute-done.5
  29.6 11.4 %collective-permute-done.4 = bf16[8,128,256]{2,1,0:T(8,128)(2,1)S(1)} collective-permute-done((bf16[8,128,256]{2,1,0:T(8,128)(2,1)S(1)}, bf16[8,128,256]{2,1,0:T(8,128)(2,1)S(1)}, u32[]{:S(2)}, u32[]{:S(2)}) %collective-permute-start.4) | collective-permute-done | bytes 524320 | tf_op jit(solution)/shard_map/ppermute | solution.py:173
  41.0 1.5 pad_maximum_fusion.cache_ref
  42.4 2.2 fusion.2
  44.7 2.6 %bitcast_convert_fusion = (f32[256,1,128]{2,0,1:T(8,128)S(1)}, bf16[256,128]{1,0:T(8,128)(2,1)S(1)}) fusion(bf16[4096,128]{1,0:T(8,128)(2,1)S(1)} %copy-done, bf16[256,4096]{1,0:T(8,128)(2,1)} %all-gather.3.cloned.1.call-done, f32[4096]{0:T(1024)S(1)} %convert_element_type.72, f32[256]{0:T(256)S(1)} %add_rsqrt_fusion.1), kind=kOutput, calls=%fused_computation.52 | convolution fusion | flops 272695296 | bytes 3359744 | tf_op jit(solution)/shard_map/dot_general | solution.py:219
  47.3 1.3 collective-permute-start.8
  48.6 0.7 collective-permute-start.7
  49.3 3.0 %collective-permute-start.6 = (bf16[256,128]{1,0:T(8,128)(2,1)S(1)}, bf16[256,128]{1,0:T(8,128)(2,1)S(1)}, u32[]{:S(2)}, u32[]{:S(2)}) collective-permute-start(bf16[256,128]{1,0:T(8,128)(2,1)S(1)} %get-tuple-element.18), channel_id=1, source_target_pairs={{0,1},{1,2},{2,4},{3,6},{8,9},{9,10},{10,12},{11,14},{16,17},{17,1... | collective-permute-start | bytes 196616 | tf_op jit(solution)/shard_map/ppermute | solution.py:228
  52.3 0.7 collective-permute-start.9
  53.0 1.3 fusion.14
  54.3 0.2 reshape.206
  54.4 0.6 fusion.37
  55.0 0.3 fusion.43
  55.5 0.9 pad_maximum_fusion.2
  56.4 2.0 fusion.35
  58.4 0.6 fusion.39
  59.0 0.7 pad_maximum_fusion.3.nk_ref
  59.7 15.8 %shard_map.176 = bf16[1024,128]{1,0:T(8,128)(2,1)} custom-call(s32[32]{0:T(128)} %copy-done.6, s32[1]{0:T(128)} %dynamic_slice.22.span_ref, bf16[1024,128]{1,0:T(8,128)(2,1)} %bitcast.50, bf16[32,128,256]{2,1,0:T(8,128)(2,1)} %pad_maximum_fusion.cache_ref, f32[32,128]{1,0:T(8,128)} %fusion.40.bias_ref, bf16[256,128]{1,0:T(8,128)(2,1)} %pad_maximum_fusion.3.nk_ref, ...), custom_call_target="tpu_custom_call" | custom-call | tf_op jit(solution)/shard_map/pallas_call | solution.py:117
  75.4 1.1 copy.25
  76.6 4.8 %fusion.1 = bf16[4096,256]{0,1:T(8,128)(2,1)} fusion(bf16[256,512]{0,1:T(8,128)(2,1)S(1)} %bitcast.52, bf16[512,4096]{1,0:T(8,128)(2,1)} %param.22), kind=kOutput, calls=%fused_computation.7 | convolution fusion | flops 1074790400 | bytes 6553600 | tf_op jit(solution)/shard_map/dot_general | solution.py:40
  81.5 39.7 %reduce-scatter.3.cloned.1.call-done = bf16[512,256]{0,1:T(8,128)(2,1)} async-done(((bf16[4096,256]{0,1:T(8,128)(2,1)}), bf16[512,256]{0,1:T(8,128)(2,1)}) %reduce-scatter.3.cloned.1.call-update) | async-done | bytes 262160 | tf_op jit(solution)/shard_map/reduce_scatter | solution.py:265
  121.1 1.7 fusion.17
  122.9 0.2 reduce-scatter.5.cloned.1.call-start
  123.1 28.0 %all-gather.5.cloned.1.call-done = bf16[256,4096]{1,0:T(8,128)(2,1)} async-done(((bf16[256,512]{1,0:T(8,128)(2,1)}), bf16[256,4096]{1,0:T(8,128)(2,1)}) %all-gather.5.cloned.1.call-update) | async-done | bytes 2097168 | tf_op jit(solution)/shard_map/all_gather | solution.py:269
  151.1 2.1 fusion.5
  153.2 9.3 %fusion.11 = f32[256,1376]{0,1:T(8,128)} fusion(bf16[4096,1376]{0,1:T(8,128)(2,1)} %param.23, bf16[256,4096]{1,0:T(8,128)(2,1)} %all-gather.5.cloned.1.call-done, f32[4096]{0:T(1024)S(1)} %convert_element_type.81, f32[256]{0:T(256)S(1)} %add_rsqrt_fusion), kind=kOutput, calls=%fused_computation.18 | convolution fusion | flops 2889875456 | bytes 14795776 | tf_op jit(solution)/shard_map/dot_general | solution.py:271
  162.5 21.5 %fusion = bf16[4096,256]{0,1:T(8,128)(2,1)} fusion(bf16[1376,4096]{1,0:T(8,128)(2,1)} %param.25, bf16[4096,1376]{0,1:T(8,128)(2,1)} %param.24, f32[256,1376]{0,1:T(8,128)} %fusion.11, bf16[256,4096]{1,0:T(8,128)(2,1)S(1)} %copy-done.3, f32[4096]{0:T(1024)S(1)} %convert_element_type.81, f32[256]{0:T(256)S(1)} %add_rsqrt_fusion), kind=kOutput, calls=%fused_computation.6 | convolution fusion | flops 5778718720 | bytes 28165120 | tf_op jit(solution)/shard_map/dot_general | solution.py:40
  184.0 35.5 %reduce-scatter.5.cloned.1.call-done = bf16[512,256]{0,1:T(8,128)(2,1)} async-done(((bf16[4096,256]{0,1:T(8,128)(2,1)}), bf16[512,256]{0,1:T(8,128)(2,1)}) %reduce-scatter.5.cloned.1.call-update) | async-done | bytes 262160 | tf_op jit(solution)/shard_map/reduce_scatter | solution.py:274
  219.5 1.8 fusion.18
  (38 shorter events, 0.5 us)
Async XLA Ops:
  7.2 37.5 %copy-start = (bf16[4096,128]{1,0:T(8,128)(2,1)S(1)}, bf16[4096,128]{1,0:T(8,128)(2,1)}, u32[]{:S(2)}) copy-start(bf16[4096,128]{1,0:T(8,128)(2,1)} %param.21) | copy-start | bytes 3145732
  7.2 35.3 %all-gather.3.cloned.1.call-start = ((), (), s32[]{:S(2)}) async-start(), calls=%async_computation.2 | async-start | bytes 2359296 | tf_op jit(solution)/shard_map/all_gather | solution.py:217
  7.9 113.2 %reduce-scatter.3.cloned.1.call-start = ((), (), s32[]{:S(2)}) async-start(), calls=%async_computation.3 | async-start | bytes 2359296 | tf_op jit(solution)/shard_map/reduce_scatter | solution.py:265
  8.6 17.7 %collective-permute-start.2 = (s32[2,8]{1,0:T(2,128)S(1)}, s32[2,8]{1,0:T(2,128)S(1)}, u32[]{:S(2)}, u32[]{:S(2)}) collective-permute-start(s32[2,8]{1,0:T(2,128)S(1)} %pad_add_fusion), channel_id=1, source_target_pairs={{0,24},{8,0},{16,8},{24,16},{1,25},{9,1},{17,9},{25,17},{2,26},{10... | collective-permute-start | bytes 200 | tf_op jit(solution)/shard_map/ppermute | solution.py:173
  12.5 13.8 %collective-permute-start.1 = (s32[2,8]{1,0:T(2,128)S(1)}, s32[2,8]{1,0:T(2,128)S(1)}, u32[]{:S(2)}, u32[]{:S(2)}) collective-permute-start(s32[2,8]{1,0:T(2,128)S(1)} %pad_add_fusion), channel_id=1, source_target_pairs={{0,16},{8,24},{16,0},{24,8},{1,17},{9,25},{17,1},{25,9},{2,18},{10... | collective-permute-start | bytes 200 | tf_op jit(solution)/shard_map/ppermute | solution.py:173
  13.0 13.3 %collective-permute-start = (s32[2,8]{1,0:T(2,128)S(1)}, s32[2,8]{1,0:T(2,128)S(1)}, u32[]{:S(2)}, u32[]{:S(2)}) collective-permute-start(s32[2,8]{1,0:T(2,128)S(1)} %pad_add_fusion), channel_id=1, source_target_pairs={{0,8},{8,16},{16,24},{24,0},{1,9},{9,17},{17,25},{25,1},{2,10},{10... | collective-permute-start | bytes 200 | tf_op jit(solution)/shard_map/ppermute | solution.py:173
  14.8 14.8 %collective-permute-start.5 = (bf16[8,128,256]{2,1,0:T(8,128)(2,1)S(1)}, bf16[8,128,256]{2,1,0:T(8,128)(2,1)S(1)}, u32[]{:S(2)}, u32[]{:S(2)}) collective-permute-start(bf16[8,128,256]{2,1,0:T(8,128)(2,1)S(1)} %pad_maximum_fusion.1), channel_id=1, source_target_pairs={{0,24},{8,0},{16,8},{24,16},{1,25},{9,1},{17,9},{25,17},{2,26},{10... | collective-permute-start | bytes 1572872 | tf_op jit(solution)/shard_map/ppermute | solution.py:173
  17.2 23.8 %collective-permute-start.4 = (bf16[8,128,256]{2,1,0:T(8,128)(2,1)S(1)}, bf16[8,128,256]{2,1,0:T(8,128)(2,1)S(1)}, u32[]{:S(2)}, u32[]{:S(2)}) collective-permute-start(bf16[8,128,256]{2,1,0:T(8,128)(2,1)S(1)} %pad_maximum_fusion.1), channel_id=1, source_target_pairs={{0,16},{8,24},{16,0},{24,8},{1,17},{9,25},{17,1},{25,9},{2,18},{10... | collective-permute-start | bytes 1572872 | tf_op jit(solution)/shard_map/ppermute | solution.py:173
  26.4 14.6 %collective-permute-start.3 = (bf16[8,128,256]{2,1,0:T(8,128)(2,1)S(1)}, bf16[8,128,256]{2,1,0:T(8,128)(2,1)S(1)}, u32[]{:S(2)}, u32[]{:S(2)}) collective-permute-start(bf16[8,128,256]{2,1,0:T(8,128)(2,1)S(1)} %pad_maximum_fusion.1), channel_id=1, source_target_pairs={{0,8},{8,16},{16,24},{24,0},{1,9},{9,17},{17,25},{25,1},{2,10},{10... | collective-permute-start | bytes 1572872 | tf_op jit(solution)/shard_map/ppermute | solution.py:173
  27.8 19.5 %copy-start.6 = (s32[32]{0:T(128)}, s32[32]{0:T(128)S(1)}, u32[]{:S(2)}) copy-start(s32[32]{0:T(128)S(1)} %fusion.41.limit_ref) | copy-start | bytes 388
  42.4 10.5 %copy-start.2 = (bf16[256,4096]{1,0:T(8,128)(2,1)S(1)}, bf16[256,4096]{1,0:T(8,128)(2,1)}, u32[]{:S(2)}) copy-start(bf16[256,4096]{1,0:T(8,128)(2,1)} %all-gather.3.cloned.1.call-done) | copy-start | bytes 6291460
  42.4 10.5 %copy-start.7 = (bf16[4096,512]{1,0:T(8,128)(2,1)S(1)}, bf16[4096,512]{1,0:T(8,128)(2,1)}, u32[]{:S(2)}) copy-start(bf16[4096,512]{1,0:T(8,128)(2,1)} %param.20) | copy-start | bytes 12582916
  47.3 9.1 %collective-permute-start.8 = (bf16[256,128]{1,0:T(8,128)(2,1)S(1)}, bf16[256,128]{1,0:T(8,128)(2,1)S(1)}, u32[]{:S(2)}, u32[]{:S(2)}) collective-permute-start(bf16[256,128]{1,0:T(8,128)(2,1)S(1)} %get-tuple-element.18), channel_id=1, source_target_pairs={{4,0},{5,2},{6,4},{7,6},{12,8},{13,10},{14,12},{15,14},{20,16},{21... | collective-permute-start | bytes 196616 | tf_op jit(solution)/shard_map/ppermute | solution.py:228
  48.6 7.8 %collective-permute-start.7 = (bf16[256,128]{1,0:T(8,128)(2,1)S(1)}, bf16[256,128]{1,0:T(8,128)(2,1)S(1)}, u32[]{:S(2)}, u32[]{:S(2)}) collective-permute-start(bf16[256,128]{1,0:T(8,128)(2,1)S(1)} %get-tuple-element.18), channel_id=1, source_target_pairs={{1,3},{2,5},{3,7},{9,11},{10,13},{11,15},{17,19},{18,21},{19,23},{... | collective-permute-start | bytes 196616 | tf_op jit(solution)/shard_map/ppermute | solution.py:228
  49.3 7.1 %collective-permute-start.6 = (bf16[256,128]{1,0:T(8,128)(2,1)S(1)}, bf16[256,128]{1,0:T(8,128)(2,1)S(1)}, u32[]{:S(2)}, u32[]{:S(2)}) collective-permute-start(bf16[256,128]{1,0:T(8,128)(2,1)S(1)} %get-tuple-element.18), channel_id=1, source_target_pairs={{0,1},{1,2},{2,4},{3,6},{8,9},{9,10},{10,12},{11,14},{16,17},{17,1... | collective-permute-start | bytes 196616 | tf_op jit(solution)/shard_map/ppermute | solution.py:228
  52.3 4.1 %collective-permute-start.9 = (bf16[256,128]{1,0:T(8,128)(2,1)S(1)}, bf16[256,128]{1,0:T(8,128)(2,1)S(1)}, u32[]{:S(2)}, u32[]{:S(2)}) collective-permute-start(bf16[256,128]{1,0:T(8,128)(2,1)S(1)} %get-tuple-element.18), channel_id=1, source_target_pairs={{4,1},{5,3},{6,5},{12,9},{13,11},{14,13},{20,17},{21,19},{22,21},{... | collective-permute-start | bytes 196616 | tf_op jit(solution)/shard_map/ppermute | solution.py:228
  76.5 44.6 %copy-start.4 = (bf16[256,512]{1,0:T(8,128)(2,1)S(1)}, bf16[256,512]{1,0:T(8,128)(2,1)}, u32[]{:S(2)}) copy-start(bf16[256,512]{1,0:T(8,128)(2,1)} %param.17) | copy-start | bytes 786436
  76.5 46.6 %copy-start.5 = (bf16[4096]{0:T(1024)(128)(2,1)S(1)}, bf16[4096]{0:T(1024)(128)(2,1)}, u32[]{:S(2)}) copy-start(bf16[4096]{0:T(1024)(128)(2,1)} %param.19) | copy-start | bytes 24580
  81.4 69.7 %all-gather.5.cloned.1.call-start = ((), (), s32[]{:S(2)}) async-start(), calls=%async_computation.4 | async-start | bytes 2359296 | tf_op jit(solution)/shard_map/all_gather | solution.py:269
  122.9 96.6 %reduce-scatter.5.cloned.1.call-start = ((), (), s32[]{:S(2)}) async-start(), calls=%async_computation.5 | async-start | bytes 2359296 | tf_op jit(solution)/shard_map/reduce_scatter | solution.py:274
  153.2 9.3 %copy-start.3 = (bf16[256,4096]{1,0:T(8,128)(2,1)S(1)}, bf16[256,4096]{1,0:T(8,128)(2,1)}, u32[]{:S(2)}) copy-start(bf16[256,4096]{1,0:T(8,128)(2,1)} %all-gather.5.cloned.1.call-done) | copy-start | bytes 6291460
  162.5 57.0 %copy-start.1 = (bf16[256,512]{1,0:T(8,128)(2,1)S(1)}, bf16[256,512]{1,0:T(8,128)(2,1)}, u32[]{:S(2)}) copy-start(bf16[256,512]{1,0:T(8,128)(2,1)} %fusion.17) | copy-start | bytes 786436
Sparse Core Ops, SparseCore 0:
  9.6 31.7 all-gather.2
  81.5 39.5 reduce-scatter.2
  123.3 27.7 all-gather.4
  184.1 35.3 reduce-scatter.4

commit v7 on v6

--- a/solution.py
+++ b/solution.py
@@ -1,3 +1,5 @@
+import functools
+
 import jax
 import jax.numpy as jnp
 from jax import lax
@@ -135,6 +137,60 @@
             ],
         ),
     )(limit, span, q_rows, cache_all, bias, new_keys, new_vals)
+
+
+def ffn_kernel(first, x_ref, wg_ref, wu_ref, wd_ref, o_ref, g_acc, u_acc, h_scr):
+    step = pl.program_id(0)
+
+    @pl.when(step == 0)
+    def _():
+        g_acc[...] = jnp.zeros(g_acc.shape, jnp.float32)
+        u_acc[...] = jnp.zeros(u_acc.shape, jnp.float32)
+
+    @pl.when(step < first)
+    def _():
+        x = x_ref[...]
+        dims = (((1,), (1,)), ((), ()))
+        g_acc[...] += lax.dot_general(x, wg_ref[...], dims, preferred_element_type=jnp.float32)
+        u_acc[...] += lax.dot_general(x, wu_ref[...], dims, preferred_element_type=jnp.float32)
+
+    @pl.when(step == first - 1)
+    def _():
+        g = g_acc[...]
+        h_scr[...] = (g / (1.0 + jnp.exp(-g)) * u_acc[...]).astype(h_scr.dtype)
+
+    @pl.when(step >= first)
+    def _():
+        o_ref[...] = jnp.dot(h_scr[...], wd_ref[...], preferred_element_type=jnp.float32).astype(
+            o_ref.dtype
+        )
+
+
+def feed_forward(x_two, w_gate, w_up, w_down):
+    rows, width = x_two.shape
+    units = w_gate.shape[1]
+    chunk = 1024 if width % 1024 == 0 else width
+    first = width // chunk
+    outs = w_down.shape[1] // chunk
+    last = first - 1
+    return pl.pallas_call(
+        functools.partial(ffn_kernel, first),
+        out_shape=jax.ShapeDtypeStruct((rows, w_down.shape[1]), jnp.bfloat16),
+        grid=(first + outs,),
+        in_specs=[
+            pl.BlockSpec((rows, chunk), lambda i: (0, jnp.minimum(i, last))),
+            pl.BlockSpec((units, chunk), lambda i: (0, jnp.minimum(i, last))),
+            pl.BlockSpec((units, chunk), lambda i: (0, jnp.minimum(i, last))),
+            pl.BlockSpec((units, chunk), lambda i: (0, jnp.maximum(i - first, 0))),
+        ],
+        out_specs=pl.BlockSpec((rows, chunk), lambda i: (0, jnp.maximum(i - first, 0))),
+        scratch_shapes=[
+            pltpu.VMEM((rows, units), jnp.float32),
+            pltpu.VMEM((rows, units), jnp.float32),
+            pltpu.VMEM((rows, units), jnp.bfloat16),
+        ],
+        compiler_params=pltpu.CompilerParams(dimension_semantics=("arbitrary",)),
+    )(x_two, w_gate.T, w_up.T, w_down)
 
 
 def kv_routes(tp_count, kv_width):
@@ -268,13 +324,10 @@
     mid = (resid.astype(jnp.float32) + head_sum.T).astype(jnp.bfloat16)
     full_mid = lax.all_gather(mid, "tp", axis=1, tiled=True)
     x_two = rms_norm(full_mid, mlp_gain)
-    gate = jnp.dot(x_two, w_gate, preferred_element_type=jnp.float32)
-    up_part = jnp.dot(x_two, w_up, preferred_element_type=jnp.float32)
-    hidden = (jax.nn.silu(gate) * up_part).astype(jnp.bfloat16)
     down_sum = lax.psum_scatter(
-        column_term(hidden, w_down).astype(jnp.bfloat16), "tp", scatter_dimension=0, tiled=True
+        feed_forward(x_two, w_gate, w_up, w_down), "tp", scatter_dimension=1, tiled=True
     ).astype(jnp.float32)
-    layer_out = (mid.astype(jnp.float32) + down_sum.T).astype(jnp.bfloat16)
+    layer_out = (mid.astype(jnp.float32) + down_sum).astype(jnp.bfloat16)
     layer_out = jnp.where(live_rows[:, None], layer_out, jnp.zeros_like(layer_out))
     return (layer_out, new_kv)
 

time: 229 us -> 221 us (0.965)
  matrix products: 39.5 us -> 8.72 us
  Pallas kernels: 15.8 us -> 28.4 us
  waiting for transfers between devices: 116 us -> 124 us
  other arithmetic: 19.5 us -> 23.1 us
    dot_general x2 -> x1, matrix products: 26.3 us -> 4.84 us  [column_term(): lax.dot_general(weight, rows, (((0,), (1,)), ((), ())), preferred_element...]
    pallas_call x0 -> x1, Pallas kernels: none -> 19.6 us  [feed_forward(): pl.pallas_call(functools.partial(ffn_kernel, first), out_shape=jax.ShapeD...]
    dot_general x1 -> x0, matrix products: 9.3 us -> none  [per_device(): gate = jnp.dot(x_two, w_gate, preferred_element_type=jnp.float32)]
    reduce_scatter x1, waiting for transfers between devices: 39.7 us -> 47.5 us  [per_device(): lax.psum_scatter(column_term(attn_rows, w_out).astype(jnp.bfloat16), 'tp'...]
    pallas_call x1, Pallas kernels: 15.8 us -> 8.82 us  [local_attention(): pl.pallas_call(attn_kernel, out_shape=jax.ShapeDtypeStruct((rows, HD), jn...]
    convert_element_type x2 -> x3, other arithmetic: 0.72 us -> 4.27 us  [rms_norm(): return (wide * factor * gain.astype(jnp.float32)).astype(jnp.bfloat16)]
where the time goes in v7:
time: 221 us
  waiting for transfers between devices  124 us (56%)
  Pallas kernels  28.4 us (13%)
  other arithmetic  23.1 us (10%)
  starting transfers between devices  14.9 us (7%)
  between operations  14 us (6%)
  matrix products  8.72 us (4%)
  local copies, waits for them, and re-layouts  7.81 us (4%)
    reduce_scatter x1, waiting for transfers between devices, per_device(): lax.psum_scatter(column_term(attn_rows, w_out).astype(jnp.bfloat16), 'tp'...  47.5 us
    reduce_scatter x1, waiting for transfers between devices, per_device(): lax.psum_scatter(feed_forward(x_two, w_gate, w_up, w_down), 'tp', scatter...  35.5 us
    all_gather x1, waiting for transfers between devices, per_device(): full_mid = lax.all_gather(mid, 'tp', axis=1, tiled=True)  28 us
    pallas_call x1, Pallas kernels, feed_forward(): pl.pallas_call(functools.partial(ffn_kernel, first), out_shape=jax.ShapeD...  19.6 us
    ppermute x6, waiting for transfers between devices, gather_ctx(): parts.append(lax.ppermute(value, 'ctx', pairs))  12.5 us
    ppermute x6, starting transfers between devices, gather_ctx(): parts.append(lax.ppermute(value, 'ctx', pairs))  8.9 us
    pallas_call x1, Pallas kernels, local_attention(): pl.pallas_call(attn_kernel, out_shape=jax.ShapeDtypeStruct((rows, HD), jn...  8.82 us
    ppermute x4, starting transfers between devices, per_device(): got = got + lax.ppermute(kv_piece, 'tp', pairs)  5.65 us
  transfers between devices with their start and end apart: 14, of which 5 were waited for; matrix products, arithmetic and copies ran while one was open for 7% of the time, Pallas kernels for 0%

profile of v7, /device:TPU:0, one launch (start us, length us, event | category | flops | bytes accessed | tf_op | source)
XLA Modules:
  0.0 221.1 jit_solution(11395634326456949604)
XLA Ops:
  7.2 0.7 all-gather.3.cloned.1.call-update
  8.0 0.7 pad_add_fusion
  8.6 3.9 %collective-permute-start.2 = (s32[2,8]{1,0:T(2,128)S(1)}, s32[2,8]{1,0:T(2,128)S(1)}, u32[]{:S(2)}, u32[]{:S(2)}) collective-permute-start(s32[2,8]{1,0:T(2,128)S(1)} %pad_add_fusion), channel_id=1, source_target_pairs={{0,24},{8,0},{16,8},{24,16},{1,25},{9,1},{17,9},{25,17},{2,26},{10... | collective-permute-start | bytes 200 | tf_op jit(solution)/shard_map/ppermute | solution.py:229
  12.5 0.5 collective-permute-start.1
  13.0 0.6 collective-permute-start
  13.6 1.1 constant_dynamic-slice_fusion.1
  14.8 2.4 %collective-permute-start.5 = (bf16[8,128,256]{2,1,0:T(8,128)(2,1)S(1)}, bf16[8,128,256]{2,1,0:T(8,128)(2,1)S(1)}, u32[]{:S(2)}, u32[]{:S(2)}) collective-permute-start(bf16[8,128,256]{2,1,0:T(8,128)(2,1)S(1)} %pad_maximum_fusion.1), channel_id=1, source_target_pairs={{0,24},{8,0},{16,8},{24,16},{1,25},{9,1},{17,9},{25,17},{2,26},{10... | collective-permute-start | bytes 1572872 | tf_op jit(solution)/shard_map/ppermute | solution.py:229
  17.2 1.5 collective-permute-start.4
  18.7 1.3 dynamic_slice.22.span_ref
  20.0 1.2 dynamic_slice.23
  21.2 1.3 dynamic_slice.27
  22.5 1.3 dynamic_slice.26
  23.8 0.6 iota_compare_fusion.1
  24.4 0.7 add_convert_fusion.2
  25.1 0.5 multiply_cosine_fusion.1
  25.6 0.7 convert_element_type.65
  26.4 0.8 pad_add_fusion.1
  27.1 0.7 fusion.34.limit_ref
  27.8 0.7 fusion.33.bias_ref
  28.5 1.1 collective-permute-done.5
  29.6 11.4 %collective-permute-done.4 = bf16[8,128,256]{2,1,0:T(8,128)(2,1)S(1)} collective-permute-done((bf16[8,128,256]{2,1,0:T(8,128)(2,1)S(1)}, bf16[8,128,256]{2,1,0:T(8,128)(2,1)S(1)}, u32[]{:S(2)}, u32[]{:S(2)}) %collective-permute-start.4) | collective-permute-done | bytes 524320 | tf_op jit(solution)/shard_map/ppermute | solution.py:229
  41.0 1.4 pad_maximum_fusion.cache_ref
  42.4 2.2 %fusion.1 = f32[256]{0:T(256)S(1)} fusion(bf16[256,4096]{1,0:T(8,128)(2,1)} %all-gather.3.cloned.1.call-done), kind=kLoop, calls=%fused_computation.6 | loop fusion | flops 3145472 | bytes 2098176 | tf_op jit(solution)/shard_map/reduce_sum | solution.py:23
  44.6 2.6 %bitcast_convert_fusion = (f32[256,1,128]{2,0,1:T(8,128)S(1)}, bf16[256,128]{1,0:T(8,128)(2,1)S(1)}) fusion(bf16[4096,128]{1,0:T(8,128)(2,1)S(1)} %copy-done, bf16[256,4096]{1,0:T(8,128)(2,1)} %all-gather.3.cloned.1.call-done, f32[4096]{0:T(1024)S(1)} %convert_element_type.65, f32[256]{0:T(256)S(1)} %add_rsqrt_fusion.1), kind=kOutput, calls=%fused_computation.46 | convolution fusion | flops 272695296 | bytes 3359744 | tf_op jit(solution)/shard_map/dot_general | solution.py:275
  47.3 1.3 collective-permute-start.8
  48.6 0.7 collective-permute-start.7
  49.2 3.0 %collective-permute-start.6 = (bf16[256,128]{1,0:T(8,128)(2,1)S(1)}, bf16[256,128]{1,0:T(8,128)(2,1)S(1)}, u32[]{:S(2)}, u32[]{:S(2)}) collective-permute-start(bf16[256,128]{1,0:T(8,128)(2,1)S(1)} %get-tuple-element.18), channel_id=1, source_target_pairs={{0,1},{1,2},{2,4},{3,6},{8,9},{9,10},{10,12},{11,14},{16,17},{17,1... | collective-permute-start | bytes 196616 | tf_op jit(solution)/shard_map/ppermute | solution.py:284
  52.3 0.7 collective-permute-start.9
  53.0 1.3 fusion.8
  54.3 0.2 reshape.206
  54.4 0.6 fusion.30
  55.0 0.3 fusion.35
  55.5 0.9 pad_maximum_fusion.2
  56.4 2.1 fusion.28
  58.4 0.6 fusion.32
  59.0 0.7 pad_maximum_fusion.3.nk_ref
  59.7 8.8 %shard_map.176 = bf16[1024,128]{1,0:T(8,128)(2,1)} custom-call(s32[32]{0:T(128)} %copy-done.5, s32[1]{0:T(128)} %dynamic_slice.22.span_ref, bf16[1024,128]{1,0:T(8,128)(2,1)} %bitcast.43, bf16[32,128,256]{2,1,0:T(8,128)(2,1)} %pad_maximum_fusion.cache_ref, f32[32,128]{1,0:T(8,128)} %fusion.33.bias_ref, bf16[256,128]{1,0:T(8,128)(2,1)} %pad_maximum_fusion.3.nk_ref, ...), custom_call_target="tpu_custom_call" | custom-call | tf_op jit(solution)/shard_map/pallas_call | solution.py:119
  68.6 1.1 copy.25
  69.7 4.8 %fusion = bf16[4096,256]{0,1:T(8,128)(2,1)} fusion(bf16[256,512]{0,1:T(8,128)(2,1)S(1)} %bitcast.45, bf16[512,4096]{1,0:T(8,128)(2,1)} %param.22), kind=kOutput, calls=%fused_computation.5 | convolution fusion | flops 1074790400 | bytes 6553600 | tf_op jit(solution)/shard_map/dot_general | solution.py:42
  74.6 47.5 %reduce-scatter.3.cloned.1.call-done = bf16[512,256]{0,1:T(8,128)(2,1)} async-done(((bf16[4096,256]{0,1:T(8,128)(2,1)}), bf16[512,256]{0,1:T(8,128)(2,1)}) %reduce-scatter.3.cloned.1.call-update) | async-done | bytes 262160 | tf_op jit(solution)/shard_map/reduce_scatter | solution.py:321
  122.1 1.7 fusion.10
  123.8 0.2 reduce-scatter.5.cloned.1.call-start
  124.1 28.0 %all-gather.5.cloned.1.call-done = bf16[256,4096]{1,0:T(8,128)(2,1)} async-done(((bf16[256,512]{1,0:T(8,128)(2,1)}), bf16[256,4096]{1,0:T(8,128)(2,1)}) %all-gather.5.cloned.1.call-update) | async-done | bytes 2097168 | tf_op jit(solution)/shard_map/all_gather | solution.py:325
  152.1 2.1 fusion.4
  154.2 3.6 %fusion.6.x_ref = bf16[256,4096]{1,0:T(8,128)(2,1)} fusion(bf16[256,4096]{1,0:T(8,128)(2,1)} %all-gather.5.cloned.1.call-done, f32[4096]{0:T(1024)S(1)} %convert_element_type.74, f32[256]{0:T(256)S(1)} %add_rsqrt_fusion), kind=kLoop, calls=%fused_computation.11 | loop fusion | flops 4194304 | bytes 4211712 | tf_op jit(solution)/shard_map/convert_element_type | solution.py:24
  157.8 19.6 %shard_map.177 = bf16[256,4096]{1,0:T(8,128)(2,1)} custom-call(bf16[256,4096]{1,0:T(8,128)(2,1)} %fusion.6.x_ref, bf16[1376,4096]{1,0:T(8,128)(2,1)} %bitcast.41, bf16[1376,4096]{1,0:T(8,128)(2,1)} %bitcast.42, bf16[1376,4096]{1,0:T(8,128)(2,1)} %wd_ref.1), custom_call_target="tpu_custom_call" | custom-call | tf_op jit(solution)/shard_map/pallas_call | solution.py:176
  177.4 35.5 %reduce-scatter.5.cloned.1.call-done = bf16[256,512]{1,0:T(8,128)(2,1)} async-done(((bf16[256,4096]{1,0:T(8,128)(2,1)}), bf16[256,512]{1,0:T(8,128)(2,1)}) %reduce-scatter.5.cloned.1.call-update) | async-done | bytes 262160 | tf_op jit(solution)/shard_map/reduce_scatter | solution.py:327
  212.8 1.8 fusion.11
  (36 shorter events, 0.5 us)
Async XLA Ops:
  7.2 37.5 %copy-start = (bf16[4096,128]{1,0:T(8,128)(2,1)S(1)}, bf16[4096,128]{1,0:T(8,128)(2,1)}, u32[]{:S(2)}) copy-start(bf16[4096,128]{1,0:T(8,128)(2,1)} %param.21) | copy-start | bytes 3145732
  7.2 35.2 %all-gather.3.cloned.1.call-start = ((), (), s32[]{:S(2)}) async-start(), calls=%async_computation.2 | async-start | bytes 2359296 | tf_op jit(solution)/shard_map/all_gather | solution.py:273
  7.9 114.2 %reduce-scatter.3.cloned.1.call-start = ((), (), s32[]{:S(2)}) async-start(), calls=%async_computation.3 | async-start | bytes 2359296 | tf_op jit(solution)/shard_map/reduce_scatter | solution.py:321
  8.6 17.7 %collective-permute-start.2 = (s32[2,8]{1,0:T(2,128)S(1)}, s32[2,8]{1,0:T(2,128)S(1)}, u32[]{:S(2)}, u32[]{:S(2)}) collective-permute-start(s32[2,8]{1,0:T(2,128)S(1)} %pad_add_fusion), channel_id=1, source_target_pairs={{0,24},{8,0},{16,8},{24,16},{1,25},{9,1},{17,9},{25,17},{2,26},{10... | collective-permute-start | bytes 200 | tf_op jit(solution)/shard_map/ppermute | solution.py:229
  12.5 13.8 %collective-permute-start.1 = (s32[2,8]{1,0:T(2,128)S(1)}, s32[2,8]{1,0:T(2,128)S(1)}, u32[]{:S(2)}, u32[]{:S(2)}) collective-permute-start(s32[2,8]{1,0:T(2,128)S(1)} %pad_add_fusion), channel_id=1, source_target_pairs={{0,16},{8,24},{16,0},{24,8},{1,17},{9,25},{17,1},{25,9},{2,18},{10... | collective-permute-start | bytes 200 | tf_op jit(solution)/shard_map/ppermute | solution.py:229
  13.0 13.3 %collective-permute-start = (s32[2,8]{1,0:T(2,128)S(1)}, s32[2,8]{1,0:T(2,128)S(1)}, u32[]{:S(2)}, u32[]{:S(2)}) collective-permute-start(s32[2,8]{1,0:T(2,128)S(1)} %pad_add_fusion), channel_id=1, source_target_pairs={{0,8},{8,16},{16,24},{24,0},{1,9},{9,17},{17,25},{25,1},{2,10},{10... | collective-permute-start | bytes 200 | tf_op jit(solution)/shard_map/ppermute | solution.py:229
  14.8 14.8 %collective-permute-start.5 = (bf16[8,128,256]{2,1,0:T(8,128)(2,1)S(1)}, bf16[8,128,256]{2,1,0:T(8,128)(2,1)S(1)}, u32[]{:S(2)}, u32[]{:S(2)}) collective-permute-start(bf16[8,128,256]{2,1,0:T(8,128)(2,1)S(1)} %pad_maximum_fusion.1), channel_id=1, source_target_pairs={{0,24},{8,0},{16,8},{24,16},{1,25},{9,1},{17,9},{25,17},{2,26},{10... | collective-permute-start | bytes 1572872 | tf_op jit(solution)/shard_map/ppermute | solution.py:229
  17.2 23.8 %collective-permute-start.4 = (bf16[8,128,256]{2,1,0:T(8,128)(2,1)S(1)}, bf16[8,128,256]{2,1,0:T(8,128)(2,1)S(1)}, u32[]{:S(2)}, u32[]{:S(2)}) collective-permute-start(bf16[8,128,256]{2,1,0:T(8,128)(2,1)S(1)} %pad_maximum_fusion.1), channel_id=1, source_target_pairs={{0,16},{8,24},{16,0},{24,8},{1,17},{9,25},{17,1},{25,9},{2,18},{10... | collective-permute-start | bytes 1572872 | tf_op jit(solution)/shard_map/ppermute | solution.py:229
  26.4 14.6 %collective-permute-start.3 = (bf16[8,128,256]{2,1,0:T(8,128)(2,1)S(1)}, bf16[8,128,256]{2,1,0:T(8,128)(2,1)S(1)}, u32[]{:S(2)}, u32[]{:S(2)}) collective-permute-start(bf16[8,128,256]{2,1,0:T(8,128)(2,1)S(1)} %pad_maximum_fusion.1), channel_id=1, source_target_pairs={{0,8},{8,16},{16,24},{24,0},{1,9},{9,17},{17,25},{25,1},{2,10},{10... | collective-permute-start | bytes 1572872 | tf_op jit(solution)/shard_map/ppermute | solution.py:229
  27.8 19.5 %copy-start.5 = (s32[32]{0:T(128)}, s32[32]{0:T(128)S(1)}, u32[]{:S(2)}) copy-start(s32[32]{0:T(128)S(1)} %fusion.34.limit_ref) | copy-start | bytes 388
  42.4 10.6 %copy-start.2 = (bf16[256,4096]{1,0:T(8,128)(2,1)S(1)}, bf16[256,4096]{1,0:T(8,128)(2,1)}, u32[]{:S(2)}) copy-start(bf16[256,4096]{1,0:T(8,128)(2,1)} %all-gather.3.cloned.1.call-done) | copy-start | bytes 6291460
  42.4 10.6 %copy-start.6 = (bf16[4096,512]{1,0:T(8,128)(2,1)S(1)}, bf16[4096,512]{1,0:T(8,128)(2,1)}, u32[]{:S(2)}) copy-start(bf16[4096,512]{1,0:T(8,128)(2,1)} %param.20) | copy-start | bytes 12582916
  47.3 9.1 %collective-permute-start.8 = (bf16[256,128]{1,0:T(8,128)(2,1)S(1)}, bf16[256,128]{1,0:T(8,128)(2,1)S(1)}, u32[]{:S(2)}, u32[]{:S(2)}) collective-permute-start(bf16[256,128]{1,0:T(8,128)(2,1)S(1)} %get-tuple-element.18), channel_id=1, source_target_pairs={{4,0},{5,2},{6,4},{7,6},{12,8},{13,10},{14,12},{15,14},{20,16},{21... | collective-permute-start | bytes 196616 | tf_op jit(solution)/shard_map/ppermute | solution.py:284
  48.6 7.8 %collective-permute-start.7 = (bf16[256,128]{1,0:T(8,128)(2,1)S(1)}, bf16[256,128]{1,0:T(8,128)(2,1)S(1)}, u32[]{:S(2)}, u32[]{:S(2)}) collective-permute-start(bf16[256,128]{1,0:T(8,128)(2,1)S(1)} %get-tuple-element.18), channel_id=1, source_target_pairs={{1,3},{2,5},{3,7},{9,11},{10,13},{11,15},{17,19},{18,21},{19,23},{... | collective-permute-start | bytes 196616 | tf_op jit(solution)/shard_map/ppermute | solution.py:284
  49.2 7.1 %collective-permute-start.6 = (bf16[256,128]{1,0:T(8,128)(2,1)S(1)}, bf16[256,128]{1,0:T(8,128)(2,1)S(1)}, u32[]{:S(2)}, u32[]{:S(2)}) collective-permute-start(bf16[256,128]{1,0:T(8,128)(2,1)S(1)} %get-tuple-element.18), channel_id=1, source_target_pairs={{0,1},{1,2},{2,4},{3,6},{8,9},{9,10},{10,12},{11,14},{16,17},{17,1... | collective-permute-start | bytes 196616 | tf_op jit(solution)/shard_map/ppermute | solution.py:284
  52.3 4.1 %collective-permute-start.9 = (bf16[256,128]{1,0:T(8,128)(2,1)S(1)}, bf16[256,128]{1,0:T(8,128)(2,1)S(1)}, u32[]{:S(2)}, u32[]{:S(2)}) collective-permute-start(bf16[256,128]{1,0:T(8,128)(2,1)S(1)} %get-tuple-element.18), channel_id=1, source_target_pairs={{4,1},{5,3},{6,5},{12,9},{13,11},{14,13},{20,17},{21,19},{22,21},{... | collective-permute-start | bytes 196616 | tf_op jit(solution)/shard_map/ppermute | solution.py:284
  69.7 52.4 %copy-start.3 = (bf16[256,512]{1,0:T(8,128)(2,1)S(1)}, bf16[256,512]{1,0:T(8,128)(2,1)}, u32[]{:S(2)}) copy-start(bf16[256,512]{1,0:T(8,128)(2,1)} %param.17) | copy-start | bytes 786436
  69.7 54.4 %copy-start.4 = (bf16[4096]{0:T(1024)(128)(2,1)S(1)}, bf16[4096]{0:T(1024)(128)(2,1)}, u32[]{:S(2)}) copy-start(bf16[4096]{0:T(1024)(128)(2,1)} %param.19) | copy-start | bytes 24580
  74.5 77.6 %all-gather.5.cloned.1.call-start = ((), (), s32[]{:S(2)}) async-start(), calls=%async_computation.4 | async-start | bytes 2359296 | tf_op jit(solution)/shard_map/all_gather | solution.py:325
  123.8 89.0 %reduce-scatter.5.cloned.1.call-start = ((), (), s32[]{:S(2)}) async-start(), calls=%async_computation.5 | async-start | bytes 2359296 | tf_op jit(solution)/shard_map/reduce_scatter | solution.py:327
  157.8 55.1 %copy-start.1 = (bf16[256,512]{1,0:T(8,128)(2,1)S(1)}, bf16[256,512]{1,0:T(8,128)(2,1)}, u32[]{:S(2)}) copy-start(bf16[256,512]{1,0:T(8,128)(2,1)} %fusion.10) | copy-start | bytes 786436
Sparse Core Ops, SparseCore 0:
  9.6 31.7 all-gather.2
  74.7 47.3 reduce-scatter.2
  124.3 27.8 all-gather.4
  177.5 35.2 reduce-scatter.4

commit v8 on v7

--- a/solution.py
+++ b/solution.py
@@ -139,17 +139,21 @@
     )(limit, span, q_rows, cache_all, bias, new_keys, new_vals)
 
 
-def ffn_kernel(first, x_ref, wg_ref, wu_ref, wd_ref, o_ref, g_acc, u_acc, h_scr):
+def ffn_kernel(first, chunk, x_ref, gain_ref, wg_ref, wu_ref, wd_ref, o_ref, f_scr, g_acc, u_acc, h_scr):
     step = pl.program_id(0)
 
     @pl.when(step == 0)
     def _():
+        wide = x_ref[...].astype(jnp.float32)
+        f_scr[...] = lax.rsqrt(jnp.sum(wide * wide, axis=1, keepdims=True) / x_ref.shape[1] + EPS)
         g_acc[...] = jnp.zeros(g_acc.shape, jnp.float32)
         u_acc[...] = jnp.zeros(u_acc.shape, jnp.float32)
 
     @pl.when(step < first)
     def _():
-        x = x_ref[...]
+        start = pl.multiple_of(jnp.minimum(step, first - 1) * chunk, chunk)
+        part = x_ref[:, pl.ds(start, chunk)].astype(jnp.float32)
+        x = (part * f_scr[...] * gain_ref[:, pl.ds(start, chunk)]).astype(jnp.bfloat16)
         dims = (((1,), (1,)), ((), ()))
         g_acc[...] += lax.dot_general(x, wg_ref[...], dims, preferred_element_type=jnp.float32)
         u_acc[...] += lax.dot_general(x, wu_ref[...], dims, preferred_element_type=jnp.float32)
@@ -166,31 +170,33 @@
         )
 
 
-def feed_forward(x_two, w_gate, w_up, w_down):
-    rows, width = x_two.shape
+def feed_forward(full_mid, gain, w_gate, w_up, w_down):
+    rows, width = full_mid.shape
     units = w_gate.shape[1]
     chunk = 1024 if width % 1024 == 0 else width
     first = width // chunk
     outs = w_down.shape[1] // chunk
     last = first - 1
     return pl.pallas_call(
-        functools.partial(ffn_kernel, first),
+        functools.partial(ffn_kernel, first, chunk),
         out_shape=jax.ShapeDtypeStruct((rows, w_down.shape[1]), jnp.bfloat16),
         grid=(first + outs,),
         in_specs=[
-            pl.BlockSpec((rows, chunk), lambda i: (0, jnp.minimum(i, last))),
+            pl.BlockSpec((rows, width), lambda i: (0, 0)),
+            pl.BlockSpec((1, width), lambda i: (0, 0)),
             pl.BlockSpec((units, chunk), lambda i: (0, jnp.minimum(i, last))),
             pl.BlockSpec((units, chunk), lambda i: (0, jnp.minimum(i, last))),
             pl.BlockSpec((units, chunk), lambda i: (0, jnp.maximum(i - first, 0))),
         ],
         out_specs=pl.BlockSpec((rows, chunk), lambda i: (0, jnp.maximum(i - first, 0))),
         scratch_shapes=[
+            pltpu.VMEM((rows, 1), jnp.float32),
             pltpu.VMEM((rows, units), jnp.float32),
             pltpu.VMEM((rows, units), jnp.float32),
             pltpu.VMEM((rows, units), jnp.bfloat16),
         ],
         compiler_params=pltpu.CompilerParams(dimension_semantics=("arbitrary",)),
-    )(x_two, w_gate.T, w_up.T, w_down)
+    )(full_mid, gain.astype(jnp.float32).reshape(1, width), w_gate.T, w_up.T, w_down)
 
 
 def kv_routes(tp_count, kv_width):
@@ -323,9 +329,8 @@
     ).astype(jnp.float32)
     mid = (resid.astype(jnp.float32) + head_sum.T).astype(jnp.bfloat16)
     full_mid = lax.all_gather(mid, "tp", axis=1, tiled=True)
-    x_two = rms_norm(full_mid, mlp_gain)
     down_sum = lax.psum_scatter(
-        feed_forward(x_two, w_gate, w_up, w_down), "tp", scatter_dimension=1, tiled=True
+        feed_forward(full_mid, mlp_gain, w_gate, w_up, w_down), "tp", scatter_dimension=1, tiled=True
     ).astype(jnp.float32)
     layer_out = (mid.astype(jnp.float32) + down_sum).astype(jnp.bfloat16)
     layer_out = jnp.where(live_rows[:, None], layer_out, jnp.zeros_like(layer_out))

time: 221 us -> 217 us (0.982)
  other arithmetic: 23.1 us -> 18 us
    convert_element_type x3 -> x1, other arithmetic: 4.27 us -> 0.7 us  [rms_norm(): return (wide * factor * gain.astype(jnp.float32)).astype(jnp.bfloat16)]
  transfers between devices with their start and end apart: 14 -> 14, of which waited for: 5 -> 5; matrix products, arithmetic and copies ran while one was open for 7% -> 8% of each run, Pallas kernels for 0% -> 0%
where the time goes in v8:
time: 217 us
  waiting for transfers between devices  125 us (58%)
  Pallas kernels  29 us (13%)
  other arithmetic  18 us (8%)
  starting transfers between devices  14.9 us (7%)
  between operations  14 us (6%)
  matrix products  8.73 us (4%)
  local copies, waits for them, and re-layouts  7.78 us (4%)
    reduce_scatter x1, waiting for transfers between devices, per_device(): lax.psum_scatter(column_term(attn_rows, w_out).astype(jnp.bfloat16), 'tp'...  48.9 us
    reduce_scatter x1, waiting for transfers between devices, per_device(): lax.psum_scatter(feed_forward(full_mid, mlp_gain, w_gate, w_up, w_down),...  35.4 us
    all_gather x1, waiting for transfers between devices, per_device(): full_mid = lax.all_gather(mid, 'tp', axis=1, tiled=True)  27.1 us
    pallas_call x1, Pallas kernels, feed_forward(): pl.pallas_call(functools.partial(ffn_kernel, first, chunk), out_shape=jax...  21.3 us
    ppermute x6, waiting for transfers between devices, gather_ctx(): parts.append(lax.ppermute(value, 'ctx', pairs))  12.5 us
    ppermute x6, starting transfers between devices, gather_ctx(): parts.append(lax.ppermute(value, 'ctx', pairs))  8.9 us
    pallas_call x1, Pallas kernels, local_attention(): pl.pallas_call(attn_kernel, out_shape=jax.ShapeDtypeStruct((rows, HD), jn...  7.62 us
    ppermute x4, starting transfers between devices, per_device(): got = got + lax.ppermute(kv_piece, 'tp', pairs)  5.61 us
  transfers between devices with their start and end apart: 14, of which 5 were waited for; matrix products, arithmetic and copies ran while one was open for 8% of the time, Pallas kernels for 0%

profile of v8, /device:TPU:0, one launch (start us, length us, event | category | flops | bytes accessed | tf_op | source)
XLA Modules:
  0.0 216.9 jit_solution(4353490783195575234)
XLA Ops:
  7.2 0.7 all-gather.3.cloned.1.call-update
  8.0 0.7 pad_add_fusion
  8.6 3.9 %collective-permute-start.2 = (s32[2,8]{1,0:T(2,128)S(1)}, s32[2,8]{1,0:T(2,128)S(1)}, u32[]{:S(2)}, u32[]{:S(2)}) collective-permute-start(s32[2,8]{1,0:T(2,128)S(1)} %pad_add_fusion), channel_id=1, source_target_pairs={{0,24},{8,0},{16,8},{24,16},{1,25},{9,1},{17,9},{25,17},{2,26},{10... | collective-permute-start | bytes 200 | tf_op jit(solution)/shard_map/ppermute | solution.py:235
  12.5 0.5 collective-permute-start.1
  13.0 0.6 collective-permute-start
  13.6 1.1 constant_dynamic-slice_fusion.1
  14.8 2.4 %collective-permute-start.5 = (bf16[8,128,256]{2,1,0:T(8,128)(2,1)S(1)}, bf16[8,128,256]{2,1,0:T(8,128)(2,1)S(1)}, u32[]{:S(2)}, u32[]{:S(2)}) collective-permute-start(bf16[8,128,256]{2,1,0:T(8,128)(2,1)S(1)} %pad_maximum_fusion.1), channel_id=1, source_target_pairs={{0,24},{8,0},{16,8},{24,16},{1,25},{9,1},{17,9},{25,17},{2,26},{10... | collective-permute-start | bytes 1572872 | tf_op jit(solution)/shard_map/ppermute | solution.py:235
  17.2 1.5 collective-permute-start.4
  18.7 1.3 dynamic_slice.22.span_ref
  20.0 1.2 dynamic_slice.23
  21.2 1.2 dynamic_slice.27
  22.5 1.3 dynamic_slice.26
  23.8 0.7 iota_compare_fusion.1
  24.5 0.7 add_convert_fusion.2
  25.1 0.5 multiply_cosine_fusion.1
  25.7 0.7 convert_element_type.57
  26.4 0.8 pad_add_fusion.1
  27.1 0.7 fusion.31.limit_ref
  27.8 0.7 fusion.30.bias_ref
  28.5 1.1 collective-permute-done.5
  29.6 11.4 %collective-permute-done.4 = bf16[8,128,256]{2,1,0:T(8,128)(2,1)S(1)} collective-permute-done((bf16[8,128,256]{2,1,0:T(8,128)(2,1)S(1)}, bf16[8,128,256]{2,1,0:T(8,128)(2,1)S(1)}, u32[]{:S(2)}, u32[]{:S(2)}) %collective-permute-start.4) | collective-permute-done | bytes 524320 | tf_op jit(solution)/shard_map/ppermute | solution.py:235
  41.0 1.5 pad_maximum_fusion.cache_ref
  42.4 2.2 %fusion.1 = f32[256]{0:T(256)S(1)} fusion(bf16[256,4096]{1,0:T(8,128)(2,1)} %all-gather.3.cloned.1.call-done), kind=kLoop, calls=%fused_computation.4 | loop fusion | flops 3145472 | bytes 2098176 | tf_op jit(solution)/shard_map/reduce_sum | solution.py:23
  44.7 2.6 %bitcast_convert_fusion = (f32[256,1,128]{2,0,1:T(8,128)S(1)}, bf16[256,128]{1,0:T(8,128)(2,1)S(1)}) fusion(bf16[4096,128]{1,0:T(8,128)(2,1)S(1)} %copy-done, bf16[256,4096]{1,0:T(8,128)(2,1)} %all-gather.3.cloned.1.call-done, f32[4096]{0:T(1024)S(1)} %convert_element_type.57, f32[256]{0:T(256)S(1)} %add_rsqrt_fusion), kind=kOutput, calls=%fused_computation.41 | convolution fusion | flops 272695296 | bytes 3359744 | tf_op jit(solution)/shard_map/dot_general | solution.py:281
  47.3 1.3 collective-permute-start.8
  48.6 0.7 collective-permute-start.7
  49.3 3.0 %collective-permute-start.6 = (bf16[256,128]{1,0:T(8,128)(2,1)S(1)}, bf16[256,128]{1,0:T(8,128)(2,1)S(1)}, u32[]{:S(2)}, u32[]{:S(2)}) collective-permute-start(bf16[256,128]{1,0:T(8,128)(2,1)S(1)} %get-tuple-element.18), channel_id=1, source_target_pairs={{0,1},{1,2},{2,4},{3,6},{8,9},{9,10},{10,12},{11,14},{16,17},{17,1... | collective-permute-start | bytes 196616 | tf_op jit(solution)/shard_map/ppermute | solution.py:290
  52.3 0.7 collective-permute-start.9
  53.0 1.3 fusion.5
  54.3 0.2 reshape.202
  54.4 0.6 fusion.27
  55.0 0.3 fusion.32
  55.4 0.1 subtract_convert_fusion
  55.5 0.9 pad_maximum_fusion.2
  56.4 1.9 fusion.25
  58.3 0.6 fusion.29
  58.9 0.7 pad_maximum_fusion.3.nk_ref
  59.6 7.6 %shard_map.176 = bf16[1024,128]{1,0:T(8,128)(2,1)} custom-call(s32[32]{0:T(128)} %copy-done.5, s32[1]{0:T(128)} %dynamic_slice.22.span_ref, bf16[1024,128]{1,0:T(8,128)(2,1)} %bitcast.44, bf16[32,128,256]{2,1,0:T(8,128)(2,1)} %pad_maximum_fusion.cache_ref, f32[32,128]{1,0:T(8,128)} %fusion.30.bias_ref, bf16[256,128]{1,0:T(8,128)(2,1)} %pad_maximum_fusion.3.nk_ref, ...), custom_call_target="tpu_custom_call" | custom-call | tf_op jit(solution)/shard_map/pallas_call | solution.py:119
  67.2 1.1 copy.25
  68.3 4.9 %fusion = bf16[4096,256]{0,1:T(8,128)(2,1)} fusion(bf16[256,512]{0,1:T(8,128)(2,1)S(1)} %bitcast.46, bf16[512,4096]{1,0:T(8,128)(2,1)} %param.22), kind=kOutput, calls=%fused_computation.3 | convolution fusion | flops 1074790400 | bytes 6553600 | tf_op jit(solution)/shard_map/dot_general | solution.py:42
  73.3 48.9 %reduce-scatter.3.cloned.1.call-done = bf16[512,256]{0,1:T(8,128)(2,1)} async-done(((bf16[4096,256]{0,1:T(8,128)(2,1)}), bf16[512,256]{0,1:T(8,128)(2,1)}) %reduce-scatter.3.cloned.1.call-update) | async-done | bytes 262160 | tf_op jit(solution)/shard_map/reduce_scatter | solution.py:327
  122.2 1.7 fusion.7
  123.9 0.2 reduce-scatter.5.cloned.1.call-start
  124.2 0.6 reshape.214
  124.8 27.1 %all-gather.5.cloned.1.call-done.x_ref = bf16[256,4096]{1,0:T(8,128)(2,1)} async-done(((bf16[256,512]{1,0:T(8,128)(2,1)}), bf16[256,4096]{1,0:T(8,128)(2,1)}) %all-gather.5.cloned.1.call-update) | async-done | bytes 2097168 | tf_op jit(solution)/shard_map/all_gather | solution.py:331
  151.9 21.3 %shard_map.177 = bf16[256,4096]{1,0:T(8,128)(2,1)} custom-call(bf16[256,4096]{1,0:T(8,128)(2,1)} %all-gather.5.cloned.1.call-done.x_ref, f32[1,4096]{1,0:T(1,128)} %bitcast.47, bf16[1376,4096]{1,0:T(8,128)(2,1)} %bitcast.42, bf16[1376,4096]{1,0:T(8,128)(2,1)} %bitcast.43, bf16[1376,4096]{1,0:T(8,128)(2,1)} %wd_ref.1), custom_call_target="tpu_custom_call" | custom-call | tf_op jit(solution)/shard_map/pallas_call | solution.py:180
  173.3 35.4 %reduce-scatter.5.cloned.1.call-done = bf16[256,512]{1,0:T(8,128)(2,1)} async-done(((bf16[256,4096]{1,0:T(8,128)(2,1)}), bf16[256,512]{1,0:T(8,128)(2,1)}) %reduce-scatter.5.cloned.1.call-update) | async-done | bytes 262160 | tf_op jit(solution)/shard_map/reduce_scatter | solution.py:332
  208.7 1.8 fusion.8
  (33 shorter events, 0.3 us)
Async XLA Ops:
  7.2 37.5 %copy-start = (bf16[4096,128]{1,0:T(8,128)(2,1)S(1)}, bf16[4096,128]{1,0:T(8,128)(2,1)}, u32[]{:S(2)}) copy-start(bf16[4096,128]{1,0:T(8,128)(2,1)} %param.21) | copy-start | bytes 3145732
  7.2 35.2 %all-gather.3.cloned.1.call-start = ((), (), s32[]{:S(2)}) async-start(), calls=%async_computation.2 | async-start | bytes 2359296 | tf_op jit(solution)/shard_map/all_gather | solution.py:279
  7.9 114.3 %reduce-scatter.3.cloned.1.call-start = ((), (), s32[]{:S(2)}) async-start(), calls=%async_computation.3 | async-start | bytes 2359296 | tf_op jit(solution)/shard_map/reduce_scatter | solution.py:327
  8.6 17.7 %collective-permute-start.2 = (s32[2,8]{1,0:T(2,128)S(1)}, s32[2,8]{1,0:T(2,128)S(1)}, u32[]{:S(2)}, u32[]{:S(2)}) collective-permute-start(s32[2,8]{1,0:T(2,128)S(1)} %pad_add_fusion), channel_id=1, source_target_pairs={{0,24},{8,0},{16,8},{24,16},{1,25},{9,1},{17,9},{25,17},{2,26},{10... | collective-permute-start | bytes 200 | tf_op jit(solution)/shard_map/ppermute | solution.py:235
  12.5 13.8 %collective-permute-start.1 = (s32[2,8]{1,0:T(2,128)S(1)}, s32[2,8]{1,0:T(2,128)S(1)}, u32[]{:S(2)}, u32[]{:S(2)}) collective-permute-start(s32[2,8]{1,0:T(2,128)S(1)} %pad_add_fusion), channel_id=1, source_target_pairs={{0,16},{8,24},{16,0},{24,8},{1,17},{9,25},{17,1},{25,9},{2,18},{10... | collective-permute-start | bytes 200 | tf_op jit(solution)/shard_map/ppermute | solution.py:235
  13.0 13.3 %collective-permute-start = (s32[2,8]{1,0:T(2,128)S(1)}, s32[2,8]{1,0:T(2,128)S(1)}, u32[]{:S(2)}, u32[]{:S(2)}) collective-permute-start(s32[2,8]{1,0:T(2,128)S(1)} %pad_add_fusion), channel_id=1, source_target_pairs={{0,8},{8,16},{16,24},{24,0},{1,9},{9,17},{17,25},{25,1},{2,10},{10... | collective-permute-start | bytes 200 | tf_op jit(solution)/shard_map/ppermute | solution.py:235
  14.8 14.8 %collective-permute-start.5 = (bf16[8,128,256]{2,1,0:T(8,128)(2,1)S(1)}, bf16[8,128,256]{2,1,0:T(8,128)(2,1)S(1)}, u32[]{:S(2)}, u32[]{:S(2)}) collective-permute-start(bf16[8,128,256]{2,1,0:T(8,128)(2,1)S(1)} %pad_maximum_fusion.1), channel_id=1, source_target_pairs={{0,24},{8,0},{16,8},{24,16},{1,25},{9,1},{17,9},{25,17},{2,26},{10... | collective-permute-start | bytes 1572872 | tf_op jit(solution)/shard_map/ppermute | solution.py:235
  17.2 23.8 %collective-permute-start.4 = (bf16[8,128,256]{2,1,0:T(8,128)(2,1)S(1)}, bf16[8,128,256]{2,1,0:T(8,128)(2,1)S(1)}, u32[]{:S(2)}, u32[]{:S(2)}) collective-permute-start(bf16[8,128,256]{2,1,0:T(8,128)(2,1)S(1)} %pad_maximum_fusion.1), channel_id=1, source_target_pairs={{0,16},{8,24},{16,0},{24,8},{1,17},{9,25},{17,1},{25,9},{2,18},{10... | collective-permute-start | bytes 1572872 | tf_op jit(solution)/shard_map/ppermute | solution.py:235
  26.4 14.6 %collective-permute-start.3 = (bf16[8,128,256]{2,1,0:T(8,128)(2,1)S(1)}, bf16[8,128,256]{2,1,0:T(8,128)(2,1)S(1)}, u32[]{:S(2)}, u32[]{:S(2)}) collective-permute-start(bf16[8,128,256]{2,1,0:T(8,128)(2,1)S(1)} %pad_maximum_fusion.1), channel_id=1, source_target_pairs={{0,8},{8,16},{16,24},{24,0},{1,9},{9,17},{17,25},{25,1},{2,10},{10... | collective-permute-start | bytes 1572872 | tf_op jit(solution)/shard_map/ppermute | solution.py:235
  27.8 19.5 %copy-start.5 = (s32[32]{0:T(128)}, s32[32]{0:T(128)S(1)}, u32[]{:S(2)}) copy-start(s32[32]{0:T(128)S(1)} %fusion.31.limit_ref) | copy-start | bytes 388
  42.4 10.5 %copy-start.2 = (bf16[256,4096]{1,0:T(8,128)(2,1)S(1)}, bf16[256,4096]{1,0:T(8,128)(2,1)}, u32[]{:S(2)}) copy-start(bf16[256,4096]{1,0:T(8,128)(2,1)} %all-gather.3.cloned.1.call-done) | copy-start | bytes 6291460
  42.4 10.5 %copy-start.6 = (bf16[4096,512]{1,0:T(8,128)(2,1)S(1)}, bf16[4096,512]{1,0:T(8,128)(2,1)}, u32[]{:S(2)}) copy-start(bf16[4096,512]{1,0:T(8,128)(2,1)} %param.20) | copy-start | bytes 12582916
  47.3 9.1 %collective-permute-start.8 = (bf16[256,128]{1,0:T(8,128)(2,1)S(1)}, bf16[256,128]{1,0:T(8,128)(2,1)S(1)}, u32[]{:S(2)}, u32[]{:S(2)}) collective-permute-start(bf16[256,128]{1,0:T(8,128)(2,1)S(1)} %get-tuple-element.18), channel_id=1, source_target_pairs={{4,0},{5,2},{6,4},{7,6},{12,8},{13,10},{14,12},{15,14},{20,16},{21... | collective-permute-start | bytes 196616 | tf_op jit(solution)/shard_map/ppermute | solution.py:290
  48.6 7.8 %collective-permute-start.7 = (bf16[256,128]{1,0:T(8,128)(2,1)S(1)}, bf16[256,128]{1,0:T(8,128)(2,1)S(1)}, u32[]{:S(2)}, u32[]{:S(2)}) collective-permute-start(bf16[256,128]{1,0:T(8,128)(2,1)S(1)} %get-tuple-element.18), channel_id=1, source_target_pairs={{1,3},{2,5},{3,7},{9,11},{10,13},{11,15},{17,19},{18,21},{19,23},{... | collective-permute-start | bytes 196616 | tf_op jit(solution)/shard_map/ppermute | solution.py:290
  49.3 7.1 %collective-permute-start.6 = (bf16[256,128]{1,0:T(8,128)(2,1)S(1)}, bf16[256,128]{1,0:T(8,128)(2,1)S(1)}, u32[]{:S(2)}, u32[]{:S(2)}) collective-permute-start(bf16[256,128]{1,0:T(8,128)(2,1)S(1)} %get-tuple-element.18), channel_id=1, source_target_pairs={{0,1},{1,2},{2,4},{3,6},{8,9},{9,10},{10,12},{11,14},{16,17},{17,1... | collective-permute-start | bytes 196616 | tf_op jit(solution)/shard_map/ppermute | solution.py:290
  52.3 4.1 %collective-permute-start.9 = (bf16[256,128]{1,0:T(8,128)(2,1)S(1)}, bf16[256,128]{1,0:T(8,128)(2,1)S(1)}, u32[]{:S(2)}, u32[]{:S(2)}) collective-permute-start(bf16[256,128]{1,0:T(8,128)(2,1)S(1)} %get-tuple-element.18), channel_id=1, source_target_pairs={{4,1},{5,3},{6,5},{12,9},{13,11},{14,13},{20,17},{21,19},{22,21},{... | collective-permute-start | bytes 196616 | tf_op jit(solution)/shard_map/ppermute | solution.py:290
  68.3 53.9 %copy-start.3 = (bf16[256,512]{1,0:T(8,128)(2,1)S(1)}, bf16[256,512]{1,0:T(8,128)(2,1)}, u32[]{:S(2)}) copy-start(bf16[256,512]{1,0:T(8,128)(2,1)} %param.17) | copy-start | bytes 786436
  68.3 55.8 %copy-start.4 = (bf16[4096]{0:T(1024)(128)(2,1)S(1)}, bf16[4096]{0:T(1024)(128)(2,1)}, u32[]{:S(2)}) copy-start(bf16[4096]{0:T(1024)(128)(2,1)} %param.19) | copy-start | bytes 24580
  73.2 78.7 %all-gather.5.cloned.1.call-start = ((), (), s32[]{:S(2)}) async-start(), calls=%async_computation.4 | async-start | bytes 2359296 | tf_op jit(solution)/shard_map/all_gather | solution.py:331
  123.9 84.7 %reduce-scatter.5.cloned.1.call-start = ((), (), s32[]{:S(2)}) async-start(), calls=%async_computation.5 | async-start | bytes 2359296 | tf_op jit(solution)/shard_map/reduce_scatter | solution.py:332
  151.9 56.8 %copy-start.1 = (bf16[256,512]{1,0:T(8,128)(2,1)S(1)}, bf16[256,512]{1,0:T(8,128)(2,1)}, u32[]{:S(2)}) copy-start(bf16[256,512]{1,0:T(8,128)(2,1)} %fusion.7) | copy-start | bytes 786436
Sparse Core Ops, SparseCore 0:
  9.6 31.7 all-gather.2
  73.3 48.8 reduce-scatter.2
  124.4 27.4 all-gather.4
  173.4 35.2 reduce-scatter.4

commit v9 on v8

--- a/solution.py
+++ b/solution.py
@@ -44,7 +44,9 @@
     )
 
 
-def attn_kernel(limit_ref, span_ref, q_ref, cache_ref, bias_ref, nk_ref, nv_ref, o_ref, top_scr, tot_scr, acc_scr):
+def attn_kernel(
+    limit_ref, span_ref, q_ref, cache_ref, bias_ref, nk_ref, nv_ref, wo_ref, o_ref, top_scr, tot_scr, acc_scr, out_scr
+):
     slots = cache_ref.shape[0]
     span_size = nk_ref.shape[0]
     heads = q_ref.shape[0] // span_size
@@ -104,11 +106,19 @@
         summed = acc_scr[part, :] + jnp.dot(
             w.astype(jnp.bfloat16), nv_ref[...], preferred_element_type=jnp.float32
         )
-        o_ref[part, :] = (summed / total).astype(o_ref.dtype)
-
-
-def local_attention(limit, span, q_rows, cache_all, new_keys, new_vals):
+        head_out = (summed / total).astype(jnp.bfloat16)
+        term = jnp.dot(head_out, wo_ref[h * HD : (h + 1) * HD, :], preferred_element_type=jnp.float32)
+        if h == 0:
+            out_scr[...] = term
+        else:
+            out_scr[...] += term
+    o_ref[...] = out_scr[...].astype(o_ref.dtype)
+
+
+def local_attention(limit, span, q_rows, cache_all, new_keys, new_vals, w_out):
     rows = q_rows.shape[0]
+    span_size = new_keys.shape[0]
+    width = w_out.shape[1]
     bias = jnp.where(
         jnp.arange(BLK, dtype=jnp.int32)[None, :] < limit[:, None], 0.0, NEG
     ).astype(jnp.float32)
@@ -118,7 +128,7 @@
 
     return pl.pallas_call(
         attn_kernel,
-        out_shape=jax.ShapeDtypeStruct((rows, HD), jnp.bfloat16),
+        out_shape=jax.ShapeDtypeStruct((span_size, width), jnp.bfloat16),
         grid_spec=pltpu.PrefetchScalarGridSpec(
             num_scalar_prefetch=2,
             grid=(1,),
@@ -128,15 +138,17 @@
                 whole(bias.shape),
                 whole(new_keys.shape),
                 whole(new_vals.shape),
+                whole(w_out.shape),
             ],
-            out_specs=whole((rows, HD)),
+            out_specs=whole((span_size, width)),
             scratch_shapes=[
                 pltpu.VMEM((rows, BLK), jnp.float32),
                 pltpu.VMEM((rows, BLK), jnp.float32),
                 pltpu.VMEM((rows, HD), jnp.float32),
+                pltpu.VMEM((span_size, width), jnp.float32),
             ],
         ),
-    )(limit, span, q_rows, cache_all, bias, new_keys, new_vals)
+    )(limit, span, q_rows, cache_all, bias, new_keys, new_vals, w_out)
 
 
 def ffn_kernel(first, chunk, x_ref, gain_ref, wg_ref, wu_ref, wd_ref, o_ref, f_scr, g_acc, u_acc, h_scr):
@@ -318,16 +330,11 @@
         meta_all[0] == ctx_rank, jnp.clip(my_len - meta_all[1] * BLK, 0, BLK), 0
     ).astype(jnp.int32)
     q_rows = query.transpose(1, 0, 2).reshape(heads_dev * span_size, HD)
-    attn_heads = local_attention(
-        limit, my_span.reshape(1).astype(jnp.int32), q_rows, cache_all, new_keys, new_vals
-    )
-    attn_rows = (
-        attn_heads.reshape(heads_dev, span_size, HD).transpose(1, 0, 2).reshape(span_size, q_cols)
-    )
-    head_sum = lax.psum_scatter(
-        column_term(attn_rows, w_out).astype(jnp.bfloat16), "tp", scatter_dimension=0, tiled=True
-    ).astype(jnp.float32)
-    mid = (resid.astype(jnp.float32) + head_sum.T).astype(jnp.bfloat16)
+    head_term = local_attention(
+        limit, my_span.reshape(1).astype(jnp.int32), q_rows, cache_all, new_keys, new_vals, w_out
+    )
+    head_sum = lax.psum_scatter(head_term, "tp", scatter_dimension=1, tiled=True).astype(jnp.float32)
+    mid = (resid.astype(jnp.float32) + head_sum).astype(jnp.bfloat16)
     full_mid = lax.all_gather(mid, "tp", axis=1, tiled=True)
     down_sum = lax.psum_scatter(
         feed_forward(full_mid, mlp_gain, w_gate, w_up, w_down), "tp", scatter_dimension=1, tiled=True

time: 217 us -> 216 us (level)
  Pallas kernels: 29 us -> 34.3 us
  matrix products: 8.73 us -> 3.88 us
    pallas_call x1, Pallas kernels: 7.62 us -> 13 us  [local_attention(): pl.pallas_call(attn_kernel, out_shape=jax.ShapeDtypeStruct((span_size, wi...]
    dot_general x1 -> x0, matrix products: 4.85 us -> none  [column_term(): lax.dot_general(weight, rows, (((0,), (1,)), ((), ())), preferred_element...]
where the time goes in v9:
time: 216 us
  waiting for transfers between devices  124 us (57%)
  Pallas kernels  34.3 us (16%)
  other arithmetic  18.1 us (8%)
  starting transfers between devices  14.9 us (7%)
  between operations  14 us (6%)
  local copies, waits for them, and re-layouts  6.73 us (3%)
  matrix products  3.88 us (2%)
    reduce_scatter x1, waiting for transfers between devices, per_device(): lax.psum_scatter(head_term, 'tp', scatter_dimension=1, tiled=True)  48.2 us
    reduce_scatter x1, waiting for transfers between devices, per_device(): lax.psum_scatter(feed_forward(full_mid, mlp_gain, w_gate, w_up, w_down),...  35.5 us
    all_gather x1, waiting for transfers between devices, per_device(): full_mid = lax.all_gather(mid, 'tp', axis=1, tiled=True)  27.3 us
    pallas_call x1, Pallas kernels, feed_forward(): pl.pallas_call(functools.partial(ffn_kernel, first, chunk), out_shape=jax...  21.3 us
    pallas_call x1, Pallas kernels, local_attention(): pl.pallas_call(attn_kernel, out_shape=jax.ShapeDtypeStruct((span_size, wi...  13 us
    ppermute x6, waiting for transfers between devices, gather_ctx(): parts.append(lax.ppermute(value, 'ctx', pairs))  12.5 us
    ppermute x6, starting transfers between devices, gather_ctx(): parts.append(lax.ppermute(value, 'ctx', pairs))  8.9 us
    ppermute x4, starting transfers between devices, per_device(): got = got + lax.ppermute(kv_piece, 'tp', pairs)  5.61 us
  transfers between devices with their start and end apart: 14, of which 5 were waited for; matrix products, arithmetic and copies ran while one was open for 8% of the time, Pallas kernels for 0%

profile of v9, /device:TPU:0, one launch (start us, length us, event | category | flops | bytes accessed | tf_op | source)
XLA Modules:
  0.0 216.0 jit_solution(15516029766442463938)
XLA Ops:
  7.2 0.7 all-gather.3.cloned.1.call-update
  8.0 0.7 pad_add_fusion
  8.6 3.9 %collective-permute-start.2 = (s32[2,8]{1,0:T(2,128)S(1)}, s32[2,8]{1,0:T(2,128)S(1)}, u32[]{:S(2)}, u32[]{:S(2)}) collective-permute-start(s32[2,8]{1,0:T(2,128)S(1)} %pad_add_fusion), channel_id=1, source_target_pairs={{0,24},{8,0},{16,8},{24,16},{1,25},{9,1},{17,9},{25,17},{2,26},{10... | collective-permute-start | bytes 200 | tf_op jit(solution)/shard_map/ppermute | solution.py:247
  12.5 0.5 collective-permute-start.1
  13.0 0.6 collective-permute-start
  13.6 1.1 constant_dynamic-slice_fusion.1
  14.7 0.1 pad_maximum_fusion.1
  14.8 2.4 %collective-permute-start.5 = (bf16[8,128,256]{2,1,0:T(8,128)(2,1)S(1)}, bf16[8,128,256]{2,1,0:T(8,128)(2,1)S(1)}, u32[]{:S(2)}, u32[]{:S(2)}) collective-permute-start(bf16[8,128,256]{2,1,0:T(8,128)(2,1)S(1)} %pad_maximum_fusion.1), channel_id=1, source_target_pairs={{0,24},{8,0},{16,8},{24,16},{1,25},{9,1},{17,9},{25,17},{2,26},{10... | collective-permute-start | bytes 1572872 | tf_op jit(solution)/shard_map/ppermute | solution.py:247
  17.2 1.5 collective-permute-start.4
  18.7 1.3 dynamic_slice.22.span_ref
  20.0 1.2 dynamic_slice.23
  21.2 1.3 dynamic_slice.27
  22.5 1.3 dynamic_slice.26
  23.8 0.6 iota_compare_fusion.1
  24.5 0.7 add_convert_fusion.3
  25.1 0.5 multiply_cosine_fusion.1
  25.7 0.7 convert_element_type.53
  26.4 0.8 pad_add_fusion.1
  27.1 0.7 fusion.29.limit_ref
  27.8 0.7 fusion.28.bias_ref
  28.5 1.1 collective-permute-done.5
  29.6 11.4 %collective-permute-done.4 = bf16[8,128,256]{2,1,0:T(8,128)(2,1)S(1)} collective-permute-done((bf16[8,128,256]{2,1,0:T(8,128)(2,1)S(1)}, bf16[8,128,256]{2,1,0:T(8,128)(2,1)S(1)}, u32[]{:S(2)}, u32[]{:S(2)}) %collective-permute-start.4) | collective-permute-done | bytes 524320 | tf_op jit(solution)/shard_map/ppermute | solution.py:247
  41.0 1.5 pad_maximum_fusion.cache_ref
  42.4 2.2 %fusion = f32[256]{0:T(256)S(1)} fusion(bf16[256,4096]{1,0:T(8,128)(2,1)} %all-gather.3.cloned.1.call-done), kind=kLoop, calls=%fused_computation.2 | loop fusion | flops 3145472 | bytes 2098176 | tf_op jit(solution)/shard_map/reduce_sum | solution.py:23
  44.7 2.6 %bitcast_convert_fusion = (f32[256,1,128]{2,0,1:T(8,128)S(1)}, bf16[256,128]{1,0:T(8,128)(2,1)S(1)}) fusion(bf16[4096,128]{1,0:T(8,128)(2,1)S(1)} %copy-done, bf16[256,4096]{1,0:T(8,128)(2,1)} %all-gather.3.cloned.1.call-done, f32[4096]{0:T(1024)S(1)} %convert_element_type.53, f32[256]{0:T(256)S(1)} %add_rsqrt_fusion), kind=kOutput, calls=%fused_computation.38 | convolution fusion | flops 272695296 | bytes 3359744 | tf_op jit(solution)/shard_map/dot_general | solution.py:293
  47.3 1.3 collective-permute-start.8
  48.6 0.7 collective-permute-start.7
  49.3 3.0 %collective-permute-start.6 = (bf16[256,128]{1,0:T(8,128)(2,1)S(1)}, bf16[256,128]{1,0:T(8,128)(2,1)S(1)}, u32[]{:S(2)}, u32[]{:S(2)}) collective-permute-start(bf16[256,128]{1,0:T(8,128)(2,1)S(1)} %get-tuple-element.18), channel_id=1, source_target_pairs={{0,1},{1,2},{2,4},{3,6},{8,9},{9,10},{10,12},{11,14},{16,17},{17,1... | collective-permute-start | bytes 196616 | tf_op jit(solution)/shard_map/ppermute | solution.py:302
  52.3 0.7 collective-permute-start.9
  53.0 1.3 fusion.4
  54.3 0.2 reshape.196
  54.4 0.6 fusion.25
  55.0 0.3 fusion.30
  55.4 0.1 subtract_convert_fusion
  55.5 0.9 pad_maximum_fusion.2
  56.4 2.1 fusion.23
  58.4 0.6 fusion.27
  59.0 0.7 pad_maximum_fusion.3.nk_ref
  59.8 13.0 %shard_map.176 = bf16[256,4096]{1,0:T(8,128)(2,1)} custom-call(s32[32]{0:T(128)} %copy-done.5, s32[1]{0:T(128)} %dynamic_slice.22.span_ref, bf16[1024,128]{1,0:T(8,128)(2,1)} %bitcast.32, bf16[32,128,256]{2,1,0:T(8,128)(2,1)} %pad_maximum_fusion.cache_ref, f32[32,128]{1,0:T(8,128)} %fusion.28.bias_ref, bf16[256,128]{1,0:T(8,128)(2,1)} %pad_maximum_fusion.3.nk_ref, ...), custom_call_target="tpu_custom_call" | custom-call | tf_op jit(solution)/shard_map/pallas_call | solution.py:129
  72.8 0.0 all-gather.5.cloned.1.call-start
  72.8 48.2 %reduce-scatter.3.cloned.1.call-done = bf16[256,512]{1,0:T(8,128)(2,1)} async-done(((bf16[256,4096]{1,0:T(8,128)(2,1)}), bf16[256,512]{1,0:T(8,128)(2,1)}) %reduce-scatter.3.cloned.1.call-update) | async-done | bytes 262160 | tf_op jit(solution)/shard_map/reduce_scatter | solution.py:336
  121.0 1.7 add_convert_fusion.1
  122.7 0.2 reduce-scatter.5.cloned.1.call-start
  123.0 0.6 reshape.206
  123.6 27.3 %all-gather.5.cloned.1.call-done.x_ref = bf16[256,4096]{1,0:T(8,128)(2,1)} async-done(((bf16[256,512]{1,0:T(8,128)(2,1)}), bf16[256,4096]{1,0:T(8,128)(2,1)}) %all-gather.5.cloned.1.call-update) | async-done | bytes 2097168 | tf_op jit(solution)/shard_map/all_gather | solution.py:338
  150.9 21.3 %shard_map.177 = bf16[256,4096]{1,0:T(8,128)(2,1)} custom-call(bf16[256,4096]{1,0:T(8,128)(2,1)} %all-gather.5.cloned.1.call-done.x_ref, f32[1,4096]{1,0:T(1,128)} %bitcast.33, bf16[1376,4096]{1,0:T(8,128)(2,1)} %bitcast.30, bf16[1376,4096]{1,0:T(8,128)(2,1)} %bitcast.31, bf16[1376,4096]{1,0:T(8,128)(2,1)} %wd_ref.1), custom_call_target="tpu_custom_call" | custom-call | tf_op jit(solution)/shard_map/pallas_call | solution.py:192
  172.3 35.5 %reduce-scatter.5.cloned.1.call-done = bf16[256,512]{1,0:T(8,128)(2,1)} async-done(((bf16[256,4096]{1,0:T(8,128)(2,1)}), bf16[256,512]{1,0:T(8,128)(2,1)}) %reduce-scatter.5.cloned.1.call-update) | async-done | bytes 262160 | tf_op jit(solution)/shard_map/reduce_scatter | solution.py:339
  207.8 1.8 fusion.6
  (31 shorter events, 0.2 us)
Async XLA Ops:
  7.2 37.5 %copy-start = (bf16[4096,128]{1,0:T(8,128)(2,1)S(1)}, bf16[4096,128]{1,0:T(8,128)(2,1)}, u32[]{:S(2)}) copy-start(bf16[4096,128]{1,0:T(8,128)(2,1)} %param.21) | copy-start | bytes 3145732
  7.2 35.2 %all-gather.3.cloned.1.call-start = ((), (), s32[]{:S(2)}) async-start(), calls=%async_computation.2 | async-start | bytes 2359296 | tf_op jit(solution)/shard_map/all_gather | solution.py:291
  7.9 113.1 %reduce-scatter.3.cloned.1.call-start = ((), (), s32[]{:S(2)}) async-start(), calls=%async_computation.3 | async-start | bytes 2359296 | tf_op jit(solution)/shard_map/reduce_scatter | solution.py:336
  8.6 17.7 %collective-permute-start.2 = (s32[2,8]{1,0:T(2,128)S(1)}, s32[2,8]{1,0:T(2,128)S(1)}, u32[]{:S(2)}, u32[]{:S(2)}) collective-permute-start(s32[2,8]{1,0:T(2,128)S(1)} %pad_add_fusion), channel_id=1, source_target_pairs={{0,24},{8,0},{16,8},{24,16},{1,25},{9,1},{17,9},{25,17},{2,26},{10... | collective-permute-start | bytes 200 | tf_op jit(solution)/shard_map/ppermute | solution.py:247
  12.5 13.8 %collective-permute-start.1 = (s32[2,8]{1,0:T(2,128)S(1)}, s32[2,8]{1,0:T(2,128)S(1)}, u32[]{:S(2)}, u32[]{:S(2)}) collective-permute-start(s32[2,8]{1,0:T(2,128)S(1)} %pad_add_fusion), channel_id=1, source_target_pairs={{0,16},{8,24},{16,0},{24,8},{1,17},{9,25},{17,1},{25,9},{2,18},{10... | collective-permute-start | bytes 200 | tf_op jit(solution)/shard_map/ppermute | solution.py:247
  13.0 13.3 %collective-permute-start = (s32[2,8]{1,0:T(2,128)S(1)}, s32[2,8]{1,0:T(2,128)S(1)}, u32[]{:S(2)}, u32[]{:S(2)}) collective-permute-start(s32[2,8]{1,0:T(2,128)S(1)} %pad_add_fusion), channel_id=1, source_target_pairs={{0,8},{8,16},{16,24},{24,0},{1,9},{9,17},{17,25},{25,1},{2,10},{10... | collective-permute-start | bytes 200 | tf_op jit(solution)/shard_map/ppermute | solution.py:247
  14.8 14.8 %collective-permute-start.5 = (bf16[8,128,256]{2,1,0:T(8,128)(2,1)S(1)}, bf16[8,128,256]{2,1,0:T(8,128)(2,1)S(1)}, u32[]{:S(2)}, u32[]{:S(2)}) collective-permute-start(bf16[8,128,256]{2,1,0:T(8,128)(2,1)S(1)} %pad_maximum_fusion.1), channel_id=1, source_target_pairs={{0,24},{8,0},{16,8},{24,16},{1,25},{9,1},{17,9},{25,17},{2,26},{10... | collective-permute-start | bytes 1572872 | tf_op jit(solution)/shard_map/ppermute | solution.py:247
  17.2 23.8 %collective-permute-start.4 = (bf16[8,128,256]{2,1,0:T(8,128)(2,1)S(1)}, bf16[8,128,256]{2,1,0:T(8,128)(2,1)S(1)}, u32[]{:S(2)}, u32[]{:S(2)}) collective-permute-start(bf16[8,128,256]{2,1,0:T(8,128)(2,1)S(1)} %pad_maximum_fusion.1), channel_id=1, source_target_pairs={{0,16},{8,24},{16,0},{24,8},{1,17},{9,25},{17,1},{25,9},{2,18},{10... | collective-permute-start | bytes 1572872 | tf_op jit(solution)/shard_map/ppermute | solution.py:247
  26.4 14.6 %collective-permute-start.3 = (bf16[8,128,256]{2,1,0:T(8,128)(2,1)S(1)}, bf16[8,128,256]{2,1,0:T(8,128)(2,1)S(1)}, u32[]{:S(2)}, u32[]{:S(2)}) collective-permute-start(bf16[8,128,256]{2,1,0:T(8,128)(2,1)S(1)} %pad_maximum_fusion.1), channel_id=1, source_target_pairs={{0,8},{8,16},{16,24},{24,0},{1,9},{9,17},{17,25},{25,1},{2,10},{10... | collective-permute-start | bytes 1572872 | tf_op jit(solution)/shard_map/ppermute | solution.py:247
  27.8 19.5 %copy-start.5 = (s32[32]{0:T(128)}, s32[32]{0:T(128)S(1)}, u32[]{:S(2)}) copy-start(s32[32]{0:T(128)S(1)} %fusion.29.limit_ref) | copy-start | bytes 388
  42.4 10.5 %copy-start.2 = (bf16[256,4096]{1,0:T(8,128)(2,1)S(1)}, bf16[256,4096]{1,0:T(8,128)(2,1)}, u32[]{:S(2)}) copy-start(bf16[256,4096]{1,0:T(8,128)(2,1)} %all-gather.3.cloned.1.call-done) | copy-start | bytes 6291460
  42.4 10.5 %copy-start.6 = (bf16[4096,512]{1,0:T(8,128)(2,1)S(1)}, bf16[4096,512]{1,0:T(8,128)(2,1)}, u32[]{:S(2)}) copy-start(bf16[4096,512]{1,0:T(8,128)(2,1)} %param.20) | copy-start | bytes 12582916
  47.3 9.1 %collective-permute-start.8 = (bf16[256,128]{1,0:T(8,128)(2,1)S(1)}, bf16[256,128]{1,0:T(8,128)(2,1)S(1)}, u32[]{:S(2)}, u32[]{:S(2)}) collective-permute-start(bf16[256,128]{1,0:T(8,128)(2,1)S(1)} %get-tuple-element.18), channel_id=1, source_target_pairs={{4,0},{5,2},{6,4},{7,6},{12,8},{13,10},{14,12},{15,14},{20,16},{21... | collective-permute-start | bytes 196616 | tf_op jit(solution)/shard_map/ppermute | solution.py:302
  48.6 7.8 %collective-permute-start.7 = (bf16[256,128]{1,0:T(8,128)(2,1)S(1)}, bf16[256,128]{1,0:T(8,128)(2,1)S(1)}, u32[]{:S(2)}, u32[]{:S(2)}) collective-permute-start(bf16[256,128]{1,0:T(8,128)(2,1)S(1)} %get-tuple-element.18), channel_id=1, source_target_pairs={{1,3},{2,5},{3,7},{9,11},{10,13},{11,15},{17,19},{18,21},{19,23},{... | collective-permute-start | bytes 196616 | tf_op jit(solution)/shard_map/ppermute | solution.py:302
  49.3 7.1 %collective-permute-start.6 = (bf16[256,128]{1,0:T(8,128)(2,1)S(1)}, bf16[256,128]{1,0:T(8,128)(2,1)S(1)}, u32[]{:S(2)}, u32[]{:S(2)}) collective-permute-start(bf16[256,128]{1,0:T(8,128)(2,1)S(1)} %get-tuple-element.18), channel_id=1, source_target_pairs={{0,1},{1,2},{2,4},{3,6},{8,9},{9,10},{10,12},{11,14},{16,17},{17,1... | collective-permute-start | bytes 196616 | tf_op jit(solution)/shard_map/ppermute | solution.py:302
  52.3 4.1 %collective-permute-start.9 = (bf16[256,128]{1,0:T(8,128)(2,1)S(1)}, bf16[256,128]{1,0:T(8,128)(2,1)S(1)}, u32[]{:S(2)}, u32[]{:S(2)}) collective-permute-start(bf16[256,128]{1,0:T(8,128)(2,1)S(1)} %get-tuple-element.18), channel_id=1, source_target_pairs={{4,1},{5,3},{6,5},{12,9},{13,11},{14,13},{20,17},{21,19},{22,21},{... | collective-permute-start | bytes 196616 | tf_op jit(solution)/shard_map/ppermute | solution.py:302
  59.7 61.2 %copy-start.3 = (bf16[256,512]{1,0:T(8,128)(2,1)S(1)}, bf16[256,512]{1,0:T(8,128)(2,1)}, u32[]{:S(2)}) copy-start(bf16[256,512]{1,0:T(8,128)(2,1)} %param.17) | copy-start | bytes 786436
  59.8 63.2 %copy-start.4 = (bf16[4096]{0:T(1024)(128)(2,1)S(1)}, bf16[4096]{0:T(1024)(128)(2,1)}, u32[]{:S(2)}) copy-start(bf16[4096]{0:T(1024)(128)(2,1)} %param.19) | copy-start | bytes 24580
  72.8 78.1 %all-gather.5.cloned.1.call-start = ((), (), s32[]{:S(2)}) async-start(), calls=%async_computation.4 | async-start | bytes 2359296 | tf_op jit(solution)/shard_map/all_gather | solution.py:338
  122.7 85.0 %reduce-scatter.5.cloned.1.call-start = ((), (), s32[]{:S(2)}) async-start(), calls=%async_computation.5 | async-start | bytes 2359296 | tf_op jit(solution)/shard_map/reduce_scatter | solution.py:339
  150.9 56.8 %copy-start.1 = (bf16[256,512]{1,0:T(8,128)(2,1)S(1)}, bf16[256,512]{1,0:T(8,128)(2,1)}, u32[]{:S(2)}) copy-start(bf16[256,512]{1,0:T(8,128)(2,1)} %add_convert_fusion.1) | copy-start | bytes 786436
Sparse Core Ops, SparseCore 0:
  9.6 31.7 all-gather.2
  72.9 48.0 reduce-scatter.2
  123.2 27.6 all-gather.4
  172.4 35.3 reduce-scatter.4

commit v10 on v9

--- a/solution.py
+++ b/solution.py
@@ -45,12 +45,15 @@
 
 
 def attn_kernel(
-    limit_ref, span_ref, q_ref, cache_ref, bias_ref, nk_ref, nv_ref, wo_ref, o_ref, top_scr, tot_scr, acc_scr, out_scr
+    limit_ref, span_ref, q_ref, cache_ref, bias_ref, nk_ref, nv_ref, wo_hbm, o_ref,
+    top_scr, tot_scr, acc_scr, out_scr, wo_ref, wo_sem
 ):
     slots = cache_ref.shape[0]
     span_size = nk_ref.shape[0]
     heads = q_ref.shape[0] // span_size
     scale = HD ** (-0.5)
+    wo_copy = pltpu.make_async_copy(wo_hbm, wo_ref, wo_sem)
+    wo_copy.start()
     q_all = q_ref[...]
     row_i = lax.broadcasted_iota(jnp.int32, (span_size, span_size), 0)
     col_j = lax.broadcasted_iota(jnp.int32, (span_size, span_size), 1)
@@ -99,6 +102,7 @@
         return carry
 
     lax.fori_loop(0, slots, sum_step, 0)
+    wo_copy.wait()
     for h in range(heads):
         part = slice(h * span_size, (h + 1) * span_size)
         w = jnp.where(new_ok, jnp.exp(new_raw(h) * scale - peak[part, :]), 0.0)
@@ -138,7 +142,7 @@
                 whole(bias.shape),
                 whole(new_keys.shape),
                 whole(new_vals.shape),
-                whole(w_out.shape),
+                pl.BlockSpec(memory_space=pl.ANY),
             ],
             out_specs=whole((span_size, width)),
             scratch_shapes=[
@@ -146,6 +150,8 @@
                 pltpu.VMEM((rows, BLK), jnp.float32),
                 pltpu.VMEM((rows, HD), jnp.float32),
                 pltpu.VMEM((span_size, width), jnp.float32),
+                pltpu.VMEM(w_out.shape, w_out.dtype),
+                pltpu.SemaphoreType.DMA(()),
             ],
         ),
     )(limit, span, q_rows, cache_all, bias, new_keys, new_vals, w_out)

time: 216 us -> 214 us (level)
  no operation moved by 1% of the time
where the time goes in v10:
time: 214 us
  waiting for transfers between devices  124 us (58%)
  Pallas kernels  32.3 us (15%)
  other arithmetic  18.1 us (8%)
  starting transfers between devices  14.9 us (7%)
  between operations  14 us (7%)
  local copies, waits for them, and re-layouts  6.73 us (3%)
  matrix products  3.88 us (2%)
    reduce_scatter x1, waiting for transfers between devices, per_device(): lax.psum_scatter(head_term, 'tp', scatter_dimension=1, tiled=True)  47.7 us
    reduce_scatter x1, waiting for transfers between devices, per_device(): lax.psum_scatter(feed_forward(full_mid, mlp_gain, w_gate, w_up, w_down),...  35.4 us
    all_gather x1, waiting for transfers between devices, per_device(): full_mid = lax.all_gather(mid, 'tp', axis=1, tiled=True)  27.4 us
    pallas_call x1, Pallas kernels, feed_forward(): pl.pallas_call(functools.partial(ffn_kernel, first, chunk), out_shape=jax...  21.3 us
    ppermute x6, waiting for transfers between devices, gather_ctx(): parts.append(lax.ppermute(value, 'ctx', pairs))  12.5 us
    pallas_call x1, Pallas kernels, local_attention(): pl.pallas_call(attn_kernel, out_shape=jax.ShapeDtypeStruct((span_size, wi...  11 us
    ppermute x6, starting transfers between devices, gather_ctx(): parts.append(lax.ppermute(value, 'ctx', pairs))  8.9 us
    ppermute x4, starting transfers between devices, per_device(): got = got + lax.ppermute(kv_piece, 'tp', pairs)  5.61 us
  transfers between devices with their start and end apart: 14, of which 5 were waited for; matrix products, arithmetic and copies ran while one was open for 8% of the time, Pallas kernels for 0%

profile of v10, /device:TPU:0, one launch (start us, length us, event | category | flops | bytes accessed | tf_op | source)
XLA Modules:
  0.0 213.6 jit_solution(3836496931432823078)
XLA Ops:
  7.2 0.7 all-gather.3.cloned.1.call-update
  8.0 0.7 pad_add_fusion
  8.6 3.9 %collective-permute-start.2 = (s32[2,8]{1,0:T(2,128)S(1)}, s32[2,8]{1,0:T(2,128)S(1)}, u32[]{:S(2)}, u32[]{:S(2)}) collective-permute-start(s32[2,8]{1,0:T(2,128)S(1)} %pad_add_fusion), channel_id=1, source_target_pairs={{0,24},{8,0},{16,8},{24,16},{1,25},{9,1},{17,9},{25,17},{2,26},{10... | collective-permute-start | bytes 200 | tf_op jit(solution)/shard_map/ppermute | solution.py:253
  12.5 0.5 collective-permute-start.1
  13.0 0.6 collective-permute-start
  13.6 1.1 constant_dynamic-slice_fusion.1
  14.7 0.1 pad_maximum_fusion.1
  14.8 2.4 %collective-permute-start.5 = (bf16[8,128,256]{2,1,0:T(8,128)(2,1)S(1)}, bf16[8,128,256]{2,1,0:T(8,128)(2,1)S(1)}, u32[]{:S(2)}, u32[]{:S(2)}) collective-permute-start(bf16[8,128,256]{2,1,0:T(8,128)(2,1)S(1)} %pad_maximum_fusion.1), channel_id=1, source_target_pairs={{0,24},{8,0},{16,8},{24,16},{1,25},{9,1},{17,9},{25,17},{2,26},{10... | collective-permute-start | bytes 1572872 | tf_op jit(solution)/shard_map/ppermute | solution.py:253
  17.2 1.5 collective-permute-start.4
  18.7 1.3 dynamic_slice.22.span_ref
  20.0 1.2 dynamic_slice.23
  21.2 1.3 dynamic_slice.27
  22.5 1.3 dynamic_slice.26
  23.8 0.6 iota_compare_fusion.1
  24.5 0.7 add_convert_fusion.3
  25.1 0.5 multiply_cosine_fusion.1
  25.7 0.7 convert_element_type.53
  26.4 0.8 pad_add_fusion.1
  27.1 0.7 fusion.29.limit_ref
  27.8 0.7 fusion.28.bias_ref
  28.5 1.1 collective-permute-done.5
  29.6 11.4 %collective-permute-done.4 = bf16[8,128,256]{2,1,0:T(8,128)(2,1)S(1)} collective-permute-done((bf16[8,128,256]{2,1,0:T(8,128)(2,1)S(1)}, bf16[8,128,256]{2,1,0:T(8,128)(2,1)S(1)}, u32[]{:S(2)}, u32[]{:S(2)}) %collective-permute-start.4) | collective-permute-done | bytes 524320 | tf_op jit(solution)/shard_map/ppermute | solution.py:253
  41.0 1.5 pad_maximum_fusion.cache_ref
  42.4 2.2 %fusion = f32[256]{0:T(256)S(1)} fusion(bf16[256,4096]{1,0:T(8,128)(2,1)} %all-gather.3.cloned.1.call-done), kind=kLoop, calls=%fused_computation.2 | loop fusion | flops 3145472 | bytes 2098176 | tf_op jit(solution)/shard_map/reduce_sum | solution.py:23
  44.7 2.6 %bitcast_convert_fusion = (f32[256,1,128]{2,0,1:T(8,128)S(1)}, bf16[256,128]{1,0:T(8,128)(2,1)S(1)}) fusion(bf16[4096,128]{1,0:T(8,128)(2,1)S(1)} %copy-done, bf16[256,4096]{1,0:T(8,128)(2,1)} %all-gather.3.cloned.1.call-done, f32[4096]{0:T(1024)S(1)} %convert_element_type.53, f32[256]{0:T(256)S(1)} %add_rsqrt_fusion), kind=kOutput, calls=%fused_computation.38 | convolution fusion | flops 272695296 | bytes 3359744 | tf_op jit(solution)/shard_map/dot_general | solution.py:299
  47.3 1.3 collective-permute-start.8
  48.6 0.7 collective-permute-start.7
  49.3 3.0 %collective-permute-start.6 = (bf16[256,128]{1,0:T(8,128)(2,1)S(1)}, bf16[256,128]{1,0:T(8,128)(2,1)S(1)}, u32[]{:S(2)}, u32[]{:S(2)}) collective-permute-start(bf16[256,128]{1,0:T(8,128)(2,1)S(1)} %get-tuple-element.18), channel_id=1, source_target_pairs={{0,1},{1,2},{2,4},{3,6},{8,9},{9,10},{10,12},{11,14},{16,17},{17,1... | collective-permute-start | bytes 196616 | tf_op jit(solution)/shard_map/ppermute | solution.py:308
  52.3 0.7 collective-permute-start.9
  53.0 1.3 fusion.4
  54.3 0.2 reshape.196
  54.4 0.6 fusion.25
  55.0 0.3 fusion.30
  55.4 0.1 subtract_convert_fusion
  55.5 0.9 pad_maximum_fusion.2
  56.4 2.1 fusion.23
  58.4 0.6 fusion.27
  59.0 0.7 pad_maximum_fusion.3.nk_ref
  59.8 11.0 %shard_map.176 = bf16[256,4096]{1,0:T(8,128)(2,1)} custom-call(s32[32]{0:T(128)} %copy-done.5, s32[1]{0:T(128)} %dynamic_slice.22.span_ref, bf16[1024,128]{1,0:T(8,128)(2,1)} %bitcast.32, bf16[32,128,256]{2,1,0:T(8,128)(2,1)} %pad_maximum_fusion.cache_ref, f32[32,128]{1,0:T(8,128)} %fusion.28.bias_ref, bf16[256,128]{1,0:T(8,128)(2,1)} %pad_maximum_fusion.3.nk_ref, ...), custom_call_target="tpu_custom_call" | custom-call | tf_op jit(solution)/shard_map/pallas_call | solution.py:133
  70.8 0.0 all-gather.5.cloned.1.call-start
  70.8 47.7 %reduce-scatter.3.cloned.1.call-done = bf16[256,512]{1,0:T(8,128)(2,1)} async-done(((bf16[256,4096]{1,0:T(8,128)(2,1)}), bf16[256,512]{1,0:T(8,128)(2,1)}) %reduce-scatter.3.cloned.1.call-update) | async-done | bytes 262160 | tf_op jit(solution)/shard_map/reduce_scatter | solution.py:342
  118.5 1.7 add_convert_fusion.1
  120.3 0.2 reduce-scatter.5.cloned.1.call-start
  120.5 0.6 reshape.206
  121.1 27.4 %all-gather.5.cloned.1.call-done.x_ref = bf16[256,4096]{1,0:T(8,128)(2,1)} async-done(((bf16[256,512]{1,0:T(8,128)(2,1)}), bf16[256,4096]{1,0:T(8,128)(2,1)}) %all-gather.5.cloned.1.call-update) | async-done | bytes 2097168 | tf_op jit(solution)/shard_map/all_gather | solution.py:344
  148.5 21.3 %shard_map.177 = bf16[256,4096]{1,0:T(8,128)(2,1)} custom-call(bf16[256,4096]{1,0:T(8,128)(2,1)} %all-gather.5.cloned.1.call-done.x_ref, f32[1,4096]{1,0:T(1,128)} %bitcast.33, bf16[1376,4096]{1,0:T(8,128)(2,1)} %bitcast.30, bf16[1376,4096]{1,0:T(8,128)(2,1)} %bitcast.31, bf16[1376,4096]{1,0:T(8,128)(2,1)} %wd_ref.1), custom_call_target="tpu_custom_call" | custom-call | tf_op jit(solution)/shard_map/pallas_call | solution.py:198
  169.9 35.4 %reduce-scatter.5.cloned.1.call-done = bf16[256,512]{1,0:T(8,128)(2,1)} async-done(((bf16[256,4096]{1,0:T(8,128)(2,1)}), bf16[256,512]{1,0:T(8,128)(2,1)}) %reduce-scatter.5.cloned.1.call-update) | async-done | bytes 262160 | tf_op jit(solution)/shard_map/reduce_scatter | solution.py:345
  205.3 1.8 fusion.6
  (31 shorter events, 0.2 us)
Async XLA Ops:
  7.2 37.5 %copy-start = (bf16[4096,128]{1,0:T(8,128)(2,1)S(1)}, bf16[4096,128]{1,0:T(8,128)(2,1)}, u32[]{:S(2)}) copy-start(bf16[4096,128]{1,0:T(8,128)(2,1)} %param.21) | copy-start | bytes 3145732
  7.2 35.2 %all-gather.3.cloned.1.call-start = ((), (), s32[]{:S(2)}) async-start(), calls=%async_computation.2 | async-start | bytes 2359296 | tf_op jit(solution)/shard_map/all_gather | solution.py:297
  7.9 110.6 %reduce-scatter.3.cloned.1.call-start = ((), (), s32[]{:S(2)}) async-start(), calls=%async_computation.3 | async-start | bytes 2359296 | tf_op jit(solution)/shard_map/reduce_scatter | solution.py:342
  8.6 17.7 %collective-permute-start.2 = (s32[2,8]{1,0:T(2,128)S(1)}, s32[2,8]{1,0:T(2,128)S(1)}, u32[]{:S(2)}, u32[]{:S(2)}) collective-permute-start(s32[2,8]{1,0:T(2,128)S(1)} %pad_add_fusion), channel_id=1, source_target_pairs={{0,24},{8,0},{16,8},{24,16},{1,25},{9,1},{17,9},{25,17},{2,26},{10... | collective-permute-start | bytes 200 | tf_op jit(solution)/shard_map/ppermute | solution.py:253
  12.5 13.8 %collective-permute-start.1 = (s32[2,8]{1,0:T(2,128)S(1)}, s32[2,8]{1,0:T(2,128)S(1)}, u32[]{:S(2)}, u32[]{:S(2)}) collective-permute-start(s32[2,8]{1,0:T(2,128)S(1)} %pad_add_fusion), channel_id=1, source_target_pairs={{0,16},{8,24},{16,0},{24,8},{1,17},{9,25},{17,1},{25,9},{2,18},{10... | collective-permute-start | bytes 200 | tf_op jit(solution)/shard_map/ppermute | solution.py:253
  13.0 13.3 %collective-permute-start = (s32[2,8]{1,0:T(2,128)S(1)}, s32[2,8]{1,0:T(2,128)S(1)}, u32[]{:S(2)}, u32[]{:S(2)}) collective-permute-start(s32[2,8]{1,0:T(2,128)S(1)} %pad_add_fusion), channel_id=1, source_target_pairs={{0,8},{8,16},{16,24},{24,0},{1,9},{9,17},{17,25},{25,1},{2,10},{10... | collective-permute-start | bytes 200 | tf_op jit(solution)/shard_map/ppermute | solution.py:253
  14.8 14.8 %collective-permute-start.5 = (bf16[8,128,256]{2,1,0:T(8,128)(2,1)S(1)}, bf16[8,128,256]{2,1,0:T(8,128)(2,1)S(1)}, u32[]{:S(2)}, u32[]{:S(2)}) collective-permute-start(bf16[8,128,256]{2,1,0:T(8,128)(2,1)S(1)} %pad_maximum_fusion.1), channel_id=1, source_target_pairs={{0,24},{8,0},{16,8},{24,16},{1,25},{9,1},{17,9},{25,17},{2,26},{10... | collective-permute-start | bytes 1572872 | tf_op jit(solution)/shard_map/ppermute | solution.py:253
  17.2 23.8 %collective-permute-start.4 = (bf16[8,128,256]{2,1,0:T(8,128)(2,1)S(1)}, bf16[8,128,256]{2,1,0:T(8,128)(2,1)S(1)}, u32[]{:S(2)}, u32[]{:S(2)}) collective-permute-start(bf16[8,128,256]{2,1,0:T(8,128)(2,1)S(1)} %pad_maximum_fusion.1), channel_id=1, source_target_pairs={{0,16},{8,24},{16,0},{24,8},{1,17},{9,25},{17,1},{25,9},{2,18},{10... | collective-permute-start | bytes 1572872 | tf_op jit(solution)/shard_map/ppermute | solution.py:253
  26.4 14.6 %collective-permute-start.3 = (bf16[8,128,256]{2,1,0:T(8,128)(2,1)S(1)}, bf16[8,128,256]{2,1,0:T(8,128)(2,1)S(1)}, u32[]{:S(2)}, u32[]{:S(2)}) collective-permute-start(bf16[8,128,256]{2,1,0:T(8,128)(2,1)S(1)} %pad_maximum_fusion.1), channel_id=1, source_target_pairs={{0,8},{8,16},{16,24},{24,0},{1,9},{9,17},{17,25},{25,1},{2,10},{10... | collective-permute-start | bytes 1572872 | tf_op jit(solution)/shard_map/ppermute | solution.py:253
  27.8 19.5 %copy-start.5 = (s32[32]{0:T(128)}, s32[32]{0:T(128)S(1)}, u32[]{:S(2)}) copy-start(s32[32]{0:T(128)S(1)} %fusion.29.limit_ref) | copy-start | bytes 388
  42.4 10.5 %copy-start.2 = (bf16[256,4096]{1,0:T(8,128)(2,1)S(1)}, bf16[256,4096]{1,0:T(8,128)(2,1)}, u32[]{:S(2)}) copy-start(bf16[256,4096]{1,0:T(8,128)(2,1)} %all-gather.3.cloned.1.call-done) | copy-start | bytes 6291460
  42.4 10.5 %copy-start.6 = (bf16[4096,512]{1,0:T(8,128)(2,1)S(1)}, bf16[4096,512]{1,0:T(8,128)(2,1)}, u32[]{:S(2)}) copy-start(bf16[4096,512]{1,0:T(8,128)(2,1)} %param.20) | copy-start | bytes 12582916
  47.3 9.1 %collective-permute-start.8 = (bf16[256,128]{1,0:T(8,128)(2,1)S(1)}, bf16[256,128]{1,0:T(8,128)(2,1)S(1)}, u32[]{:S(2)}, u32[]{:S(2)}) collective-permute-start(bf16[256,128]{1,0:T(8,128)(2,1)S(1)} %get-tuple-element.18), channel_id=1, source_target_pairs={{4,0},{5,2},{6,4},{7,6},{12,8},{13,10},{14,12},{15,14},{20,16},{21... | collective-permute-start | bytes 196616 | tf_op jit(solution)/shard_map/ppermute | solution.py:308
  48.6 7.8 %collective-permute-start.7 = (bf16[256,128]{1,0:T(8,128)(2,1)S(1)}, bf16[256,128]{1,0:T(8,128)(2,1)S(1)}, u32[]{:S(2)}, u32[]{:S(2)}) collective-permute-start(bf16[256,128]{1,0:T(8,128)(2,1)S(1)} %get-tuple-element.18), channel_id=1, source_target_pairs={{1,3},{2,5},{3,7},{9,11},{10,13},{11,15},{17,19},{18,21},{19,23},{... | collective-permute-start | bytes 196616 | tf_op jit(solution)/shard_map/ppermute | solution.py:308
  49.3 7.1 %collective-permute-start.6 = (bf16[256,128]{1,0:T(8,128)(2,1)S(1)}, bf16[256,128]{1,0:T(8,128)(2,1)S(1)}, u32[]{:S(2)}, u32[]{:S(2)}) collective-permute-start(bf16[256,128]{1,0:T(8,128)(2,1)S(1)} %get-tuple-element.18), channel_id=1, source_target_pairs={{0,1},{1,2},{2,4},{3,6},{8,9},{9,10},{10,12},{11,14},{16,17},{17,1... | collective-permute-start | bytes 196616 | tf_op jit(solution)/shard_map/ppermute | solution.py:308
  52.3 4.1 %collective-permute-start.9 = (bf16[256,128]{1,0:T(8,128)(2,1)S(1)}, bf16[256,128]{1,0:T(8,128)(2,1)S(1)}, u32[]{:S(2)}, u32[]{:S(2)}) collective-permute-start(bf16[256,128]{1,0:T(8,128)(2,1)S(1)} %get-tuple-element.18), channel_id=1, source_target_pairs={{4,1},{5,3},{6,5},{12,9},{13,11},{14,13},{20,17},{21,19},{22,21},{... | collective-permute-start | bytes 196616 | tf_op jit(solution)/shard_map/ppermute | solution.py:308
  59.7 58.8 %copy-start.3 = (bf16[256,512]{1,0:T(8,128)(2,1)S(1)}, bf16[256,512]{1,0:T(8,128)(2,1)}, u32[]{:S(2)}) copy-start(bf16[256,512]{1,0:T(8,128)(2,1)} %param.17) | copy-start | bytes 786436
  59.8 60.7 %copy-start.4 = (bf16[4096]{0:T(1024)(128)(2,1)S(1)}, bf16[4096]{0:T(1024)(128)(2,1)}, u32[]{:S(2)}) copy-start(bf16[4096]{0:T(1024)(128)(2,1)} %param.19) | copy-start | bytes 24580
  70.8 77.8 %all-gather.5.cloned.1.call-start = ((), (), s32[]{:S(2)}) async-start(), calls=%async_computation.4 | async-start | bytes 2359296 | tf_op jit(solution)/shard_map/all_gather | solution.py:344
  120.3 85.0 %reduce-scatter.5.cloned.1.call-start = ((), (), s32[]{:S(2)}) async-start(), calls=%async_computation.5 | async-start | bytes 2359296 | tf_op jit(solution)/shard_map/reduce_scatter | solution.py:345
  148.5 56.7 %copy-start.1 = (bf16[256,512]{1,0:T(8,128)(2,1)S(1)}, bf16[256,512]{1,0:T(8,128)(2,1)}, u32[]{:S(2)}) copy-start(bf16[256,512]{1,0:T(8,128)(2,1)} %add_convert_fusion.1) | copy-start | bytes 786436
Sparse Core Ops, SparseCore 0:
  9.6 31.7 all-gather.2
  70.9 47.5 reduce-scatter.2
  120.7 27.7 all-gather.4
  170.0 35.2 reduce-scatter.4

commit v11 on v10

--- a/solution.py
+++ b/solution.py
@@ -228,22 +228,24 @@
         own_head = dev * kv_width // HD
         own = [own_head * per_head + u for u in range(per_head)] if own_head < KVH else [dev] * per_head
         needs.append(keys + vals + own)
-    rounds = []
-    for entry in range(len(needs[0])):
-        sets = []
+    entries = len(needs[0])
+    colours = []
+    slot = [[-1] * tp_count for _ in range(entries)]
+    for entry in range(entries):
         for dev in range(tp_count):
             src = needs[dev][entry]
             if src == dev:
                 continue
-            for pairs in sets:
-                if all(a != src for a, _ in pairs):
+            for index, pairs in enumerate(colours):
+                if all(a != src and b != dev for a, b in pairs):
                     pairs.append((src, dev))
                     break
             else:
-                sets.append([(src, dev)])
-        rounds.append(sets)
-    selfs = [[needs[dev][entry] == dev for dev in range(tp_count)] for entry in range(len(needs[0]))]
-    return per_head, rounds, selfs
+                index = len(colours)
+                colours.append([(src, dev)])
+            slot[entry][dev] = index
+    selfs = [[needs[dev][entry] == dev for dev in range(tp_count)] for entry in range(entries)]
+    return per_head, colours, slot, selfs
 
 
 def gather_ctx(value, count):
@@ -299,13 +301,15 @@
     kv_piece = jnp.dot(x_norm, w_kv, preferred_element_type=jnp.float32).astype(jnp.bfloat16)
     kv_width = kv_piece.shape[1]
     tp_count = lax.axis_size("tp")
-    per_head, rounds, selfs = kv_routes(tp_count, kv_width)
+    per_head, colours, slot, selfs = kv_routes(tp_count, kv_width)
+    received = [lax.ppermute(kv_piece, "tp", pairs) for pairs in colours]
+    zeros = jnp.zeros_like(kv_piece)
     blocks = []
-    for entry, sets in enumerate(rounds):
-        is_self = jnp.asarray(selfs[entry])[tp_rank]
-        got = jnp.where(is_self, kv_piece, jnp.zeros_like(kv_piece))
-        for pairs in sets:
-            got = got + lax.ppermute(kv_piece, "tp", pairs)
+    for entry in range(len(slot)):
+        got = jnp.where(jnp.asarray(selfs[entry])[tp_rank], kv_piece, zeros)
+        for index, value in enumerate(received):
+            hit = jnp.asarray([slot[entry][dev] == index for dev in range(tp_count)])[tp_rank]
+            got = got + jnp.where(hit, value, zeros)
         blocks.append(got)
 
     def head_of(parts):

time: 214 us -> 214 us (level)
  local copies, waits for them, and re-layouts: 6.73 us -> 10.5 us
  starting transfers between devices: 14.9 us -> 11.9 us
  waiting for transfers between devices: 124 us -> 121 us
    reduce_scatter x1, waiting for transfers between devices: 47.7 us -> 43.5 us  [per_device(): lax.psum_scatter(head_term, 'tp', scatter_dimension=1, tiled=True)]
    add x0 -> x1, other arithmetic: none -> 3.84 us  [per_device(): got = got + jnp.where(hit, value, zeros)]
    dynamic_slice x2 -> x5, local copies, waits for them, and re-layouts: 2.6 us -> 6.35 us  [the longest x3 3.82 us: per_device(): jnp.asarray([slot[entry][dev] == index for dev in range(tp_count)])[tp_rank]]
    ppermute x4 -> x2, waiting for transfers between devices: 0.01 us -> 3.17 us  [per_device(): received = [lax.ppermute(kv_piece, 'tp', pairs) for pairs in colours]]
    ppermute x4 -> x2, starting transfers between devices: 5.61 us -> 2.62 us  [per_device(): received = [lax.ppermute(kv_piece, 'tp', pairs) for pairs in colours]]
  transfers between devices with their start and end apart: 14 -> 12, of which waited for: 5 -> 5; matrix products, arithmetic and copies ran while one was open for 8% -> 10% of each run, Pallas kernels for 0% -> 0%
where the time goes in v11:
time: 214 us; the launch traced here: 213 us
  waiting for transfers between devices  121 us (57%)
  Pallas kernels  31.7 us (15%)
  other arithmetic  19.7 us (9%)
  between operations  14 us (7%)
  starting transfers between devices  11.9 us (6%)
  local copies, waits for them, and re-layouts  10.5 us (5%)
  matrix products  3.88 us (2%)
    reduce_scatter x1, waiting for transfers between devices, per_device(): lax.psum_scatter(head_term, 'tp', scatter_dimension=1, tiled=True)  43.5 us
    reduce_scatter x1, waiting for transfers between devices, per_device(): lax.psum_scatter(feed_forward(full_mid, mlp_gain, w_gate, w_up, w_down),...  35.4 us
    all_gather x1, waiting for transfers between devices, per_device(): full_mid = lax.all_gather(mid, 'tp', axis=1, tiled=True)  27.5 us
    pallas_call x1, Pallas kernels, feed_forward(): pl.pallas_call(functools.partial(ffn_kernel, first, chunk), out_shape=jax...  21.4 us
    ppermute x6, waiting for transfers between devices, gather_ctx(): parts.append(lax.ppermute(value, 'ctx', pairs))  11 us
    pallas_call x1, Pallas kernels, local_attention(): pl.pallas_call(attn_kernel, out_shape=jax.ShapeDtypeStruct((span_size, wi...  10.3 us
    ppermute x6, starting transfers between devices, gather_ctx(): parts.append(lax.ppermute(value, 'ctx', pairs))  8.9 us
  transfers between devices with their start and end apart: 12, of which 5 were waited for; matrix products, arithmetic and copies ran while one was open for 10% of the time, Pallas kernels for 0%

profile of v11, /device:TPU:0, one launch (start us, length us, event | category | flops | bytes accessed | tf_op | source)
XLA Modules:
  0.0 213.0 jit_solution(10012342050022420915)
XLA Ops:
  7.2 0.7 all-gather.3.cloned.1.call-update
  8.0 0.7 pad_add_fusion
  8.6 3.9 %collective-permute-start.2 = (s32[2,8]{1,0:T(2,128)S(1)}, s32[2,8]{1,0:T(2,128)S(1)}, u32[]{:S(2)}, u32[]{:S(2)}) collective-permute-start(s32[2,8]{1,0:T(2,128)S(1)} %pad_add_fusion), channel_id=1, source_target_pairs={{0,24},{8,0},{16,8},{24,16},{1,25},{9,1},{17,9},{25,17},{2,26},{10... | collective-permute-start | bytes 200 | tf_op jit(solution)/shard_map/ppermute | solution.py:255
  12.5 0.5 collective-permute-start.1
  13.0 0.6 collective-permute-start
  13.6 1.1 constant_dynamic-slice_fusion.1
  14.7 0.1 pad_maximum_fusion.1
  14.8 2.4 %collective-permute-start.5 = (bf16[8,128,256]{2,1,0:T(8,128)(2,1)S(1)}, bf16[8,128,256]{2,1,0:T(8,128)(2,1)S(1)}, u32[]{:S(2)}, u32[]{:S(2)}) collective-permute-start(bf16[8,128,256]{2,1,0:T(8,128)(2,1)S(1)} %pad_maximum_fusion.1), channel_id=1, source_target_pairs={{0,24},{8,0},{16,8},{24,16},{1,25},{9,1},{17,9},{25,17},{2,26},{10... | collective-permute-start | bytes 1572872 | tf_op jit(solution)/shard_map/ppermute | solution.py:255
  17.2 1.5 collective-permute-start.4
  18.7 1.2 dynamic_slice.40.span_ref
  19.9 1.3 dynamic_slice.41
  21.2 1.3 dynamic_slice.48
  22.5 1.2 dynamic_slice.47
  23.7 1.3 dynamic_slice.46
  25.0 1.2 dynamic_slice.45
  26.2 1.3 dynamic_slice.44
  27.6 0.6 iota_compare_fusion.1
  28.1 0.7 add_convert_fusion.3
  28.8 0.5 multiply_cosine_fusion.1
  29.3 0.7 convert_element_type.53
  30.1 0.8 pad_add_fusion.1
  30.8 0.7 fusion.29.limit_ref
  31.5 0.7 fusion.28.bias_ref
  32.2 11.0 %collective-permute-done.3 = bf16[8,128,256]{2,1,0:T(8,128)(2,1)S(1)} collective-permute-done((bf16[8,128,256]{2,1,0:T(8,128)(2,1)S(1)}, bf16[8,128,256]{2,1,0:T(8,128)(2,1)S(1)}, u32[]{:S(2)}, u32[]{:S(2)}) %collective-permute-start.3) | collective-permute-done | bytes 524320 | tf_op jit(solution)/shard_map/ppermute | solution.py:255
  43.2 1.4 pad_maximum_fusion.cache_ref
  44.6 2.2 %fusion = f32[256]{0:T(256)S(1)} fusion(bf16[256,4096]{1,0:T(8,128)(2,1)} %all-gather.3.cloned.1.call-done), kind=kLoop, calls=%fused_computation.2 | loop fusion | flops 3145472 | bytes 2098176 | tf_op jit(solution)/shard_map/reduce_sum | solution.py:23
  46.9 2.6 %bitcast_convert_fusion = (f32[256,1,128]{2,0,1:T(8,128)S(1)}, bf16[256,128]{1,0:T(8,128)(2,1)S(1)}) fusion(bf16[4096,128]{1,0:T(8,128)(2,1)S(1)} %copy-done, bf16[256,4096]{1,0:T(8,128)(2,1)} %all-gather.3.cloned.1.call-done, f32[4096]{0:T(1024)S(1)} %convert_element_type.53, f32[256]{0:T(256)S(1)} %add_rsqrt_fusion), kind=kOutput, calls=%fused_computation.38 | convolution fusion | flops 272695296 | bytes 3359744 | tf_op jit(solution)/shard_map/dot_general | solution.py:301
  49.5 0.7 collective-permute-start.7
  50.2 2.0 collective-permute-start.6
  52.1 1.3 fusion.4
  53.4 0.2 reshape.196
  53.6 0.6 fusion.25
  54.2 0.3 fusion.30
  54.5 0.1 subtract_convert_fusion
  54.7 0.9 pad_maximum_fusion.2
  55.5 3.2 %collective-permute-done.6 = bf16[256,128]{1,0:T(8,128)(2,1)S(1)} collective-permute-done((bf16[256,128]{1,0:T(8,128)(2,1)S(1)}, bf16[256,128]{1,0:T(8,128)(2,1)S(1)}, u32[]{:S(2)}, u32[]{:S(2)}) %collective-permute-start.6) | collective-permute-done | bytes 65568 | tf_op jit(solution)/shard_map/ppermute | solution.py:305
  58.7 3.8 %select_add_fusion = (bf16[256,128]{1,0:T(8,128)(2,1)}, f32[256,1,128]{2,0,1:T(8,128)S(1)}, bf16[256,128]{1,0:T(8,128)(2,1)}) fusion(bf16[256,128]{1,0:T(8,128)(2,1)S(1)} %collective-permute-done.7, bf16[256,128]{1,0:T(8,128)(2,1)S(1)} %collective-permute-done.6, bf16[256,128]{1,0:T(8,128)(2,1)S(1)} %get-tuple-element.18, pred[]{:T(512)} %bitcast.15, ...), kind=kLoop, calls=%fused_computation.40 | loop fusion | flops 819200 | bytes 524550 | tf_op jit(solution)/shard_map/add | solution.py:312
  62.5 0.6 fusion.27
  63.1 0.7 pad_maximum_fusion.3.nk_ref
  63.9 10.3 %shard_map.230 = bf16[256,4096]{1,0:T(8,128)(2,1)} custom-call(s32[32]{0:T(128)} %copy-done.5, s32[1]{0:T(128)} %dynamic_slice.40.span_ref, bf16[1024,128]{1,0:T(8,128)(2,1)} %bitcast.35, bf16[32,128,256]{2,1,0:T(8,128)(2,1)} %pad_maximum_fusion.cache_ref, f32[32,128]{1,0:T(8,128)} %fusion.28.bias_ref, bf16[256,128]{1,0:T(8,128)(2,1)} %pad_maximum_fusion.3.nk_ref, ...), custom_call_target="tpu_custom_call" | custom-call | tf_op jit(solution)/shard_map/pallas_call | solution.py:133
  74.2 43.5 %reduce-scatter.3.cloned.1.call-done = bf16[256,512]{1,0:T(8,128)(2,1)} async-done(((bf16[256,4096]{1,0:T(8,128)(2,1)}), bf16[256,512]{1,0:T(8,128)(2,1)}) %reduce-scatter.3.cloned.1.call-update) | async-done | bytes 262160 | tf_op jit(solution)/shard_map/reduce_scatter | solution.py:346
  117.8 1.7 add_convert_fusion.1
  119.5 0.2 reduce-scatter.5.cloned.1.call-start
  119.8 0.6 reshape.206
  120.4 27.5 %all-gather.5.cloned.1.call-done.x_ref = bf16[256,4096]{1,0:T(8,128)(2,1)} async-done(((bf16[256,512]{1,0:T(8,128)(2,1)}), bf16[256,4096]{1,0:T(8,128)(2,1)}) %all-gather.5.cloned.1.call-update) | async-done | bytes 2097168 | tf_op jit(solution)/shard_map/all_gather | solution.py:348
  147.9 21.4 %shard_map.231 = bf16[256,4096]{1,0:T(8,128)(2,1)} custom-call(bf16[256,4096]{1,0:T(8,128)(2,1)} %all-gather.5.cloned.1.call-done.x_ref, f32[1,4096]{1,0:T(1,128)} %bitcast.36, bf16[1376,4096]{1,0:T(8,128)(2,1)} %bitcast.33, bf16[1376,4096]{1,0:T(8,128)(2,1)} %bitcast.34, bf16[1376,4096]{1,0:T(8,128)(2,1)} %wd_ref.1), custom_call_target="tpu_custom_call" | custom-call | tf_op jit(solution)/shard_map/pallas_call | solution.py:198
  169.3 35.4 %reduce-scatter.5.cloned.1.call-done = bf16[256,512]{1,0:T(8,128)(2,1)} async-done(((bf16[256,4096]{1,0:T(8,128)(2,1)}), bf16[256,512]{1,0:T(8,128)(2,1)}) %reduce-scatter.5.cloned.1.call-update) | async-done | bytes 262160 | tf_op jit(solution)/shard_map/reduce_scatter | solution.py:349
  204.7 1.8 fusion.6
  (30 shorter events, 0.2 us)
Async XLA Ops:
  7.2 39.7 %copy-start = (bf16[4096,128]{1,0:T(8,128)(2,1)S(1)}, bf16[4096,128]{1,0:T(8,128)(2,1)}, u32[]{:S(2)}) copy-start(bf16[4096,128]{1,0:T(8,128)(2,1)} %param.27) | copy-start | bytes 3145732
  7.2 37.4 %all-gather.3.cloned.1.call-start = ((), (), s32[]{:S(2)}) async-start(), calls=%async_computation.2 | async-start | bytes 2359296 | tf_op jit(solution)/shard_map/all_gather | solution.py:299
  7.9 109.9 %reduce-scatter.3.cloned.1.call-start = ((), (), s32[]{:S(2)}) async-start(), calls=%async_computation.3 | async-start | bytes 2359296 | tf_op jit(solution)/shard_map/reduce_scatter | solution.py:346
  8.6 21.4 %collective-permute-start.2 = (s32[2,8]{1,0:T(2,128)S(1)}, s32[2,8]{1,0:T(2,128)S(1)}, u32[]{:S(2)}, u32[]{:S(2)}) collective-permute-start(s32[2,8]{1,0:T(2,128)S(1)} %pad_add_fusion), channel_id=1, source_target_pairs={{0,24},{8,0},{16,8},{24,16},{1,25},{9,1},{17,9},{25,17},{2,26},{10... | collective-permute-start | bytes 200 | tf_op jit(solution)/shard_map/ppermute | solution.py:255
  12.5 17.5 %collective-permute-start.1 = (s32[2,8]{1,0:T(2,128)S(1)}, s32[2,8]{1,0:T(2,128)S(1)}, u32[]{:S(2)}, u32[]{:S(2)}) collective-permute-start(s32[2,8]{1,0:T(2,128)S(1)} %pad_add_fusion), channel_id=1, source_target_pairs={{0,16},{8,24},{16,0},{24,8},{1,17},{9,25},{17,1},{25,9},{2,18},{10... | collective-permute-start | bytes 200 | tf_op jit(solution)/shard_map/ppermute | solution.py:255
  13.0 17.0 %collective-permute-start = (s32[2,8]{1,0:T(2,128)S(1)}, s32[2,8]{1,0:T(2,128)S(1)}, u32[]{:S(2)}, u32[]{:S(2)}) collective-permute-start(s32[2,8]{1,0:T(2,128)S(1)} %pad_add_fusion), channel_id=1, source_target_pairs={{0,8},{8,16},{16,24},{24,0},{1,9},{9,17},{17,25},{25,1},{2,10},{10... | collective-permute-start | bytes 200 | tf_op jit(solution)/shard_map/ppermute | solution.py:255
  14.8 17.4 %collective-permute-start.5 = (bf16[8,128,256]{2,1,0:T(8,128)(2,1)S(1)}, bf16[8,128,256]{2,1,0:T(8,128)(2,1)S(1)}, u32[]{:S(2)}, u32[]{:S(2)}) collective-permute-start(bf16[8,128,256]{2,1,0:T(8,128)(2,1)S(1)} %pad_maximum_fusion.1), channel_id=1, source_target_pairs={{0,24},{8,0},{16,8},{24,16},{1,25},{9,1},{17,9},{25,17},{2,26},{10... | collective-permute-start | bytes 1572872 | tf_op jit(solution)/shard_map/ppermute | solution.py:255
  17.2 15.0 %collective-permute-start.4 = (bf16[8,128,256]{2,1,0:T(8,128)(2,1)S(1)}, bf16[8,128,256]{2,1,0:T(8,128)(2,1)S(1)}, u32[]{:S(2)}, u32[]{:S(2)}) collective-permute-start(bf16[8,128,256]{2,1,0:T(8,128)(2,1)S(1)} %pad_maximum_fusion.1), channel_id=1, source_target_pairs={{0,16},{8,24},{16,0},{24,8},{1,17},{9,25},{17,1},{25,9},{2,18},{10... | collective-permute-start | bytes 1572872 | tf_op jit(solution)/shard_map/ppermute | solution.py:255
  30.0 13.2 %collective-permute-start.3 = (bf16[8,128,256]{2,1,0:T(8,128)(2,1)S(1)}, bf16[8,128,256]{2,1,0:T(8,128)(2,1)S(1)}, u32[]{:S(2)}, u32[]{:S(2)}) collective-permute-start(bf16[8,128,256]{2,1,0:T(8,128)(2,1)S(1)} %pad_maximum_fusion.1), channel_id=1, source_target_pairs={{0,8},{8,16},{16,24},{24,0},{1,9},{9,17},{17,25},{25,1},{2,10},{10... | collective-permute-start | bytes 1572872 | tf_op jit(solution)/shard_map/ppermute | solution.py:255
  31.5 18.0 %copy-start.5 = (s32[32]{0:T(128)}, s32[32]{0:T(128)S(1)}, u32[]{:S(2)}) copy-start(s32[32]{0:T(128)S(1)} %fusion.29.limit_ref) | copy-start | bytes 388
  44.6 7.5 %copy-start.2 = (bf16[256,4096]{1,0:T(8,128)(2,1)S(1)}, bf16[256,4096]{1,0:T(8,128)(2,1)}, u32[]{:S(2)}) copy-start(bf16[256,4096]{1,0:T(8,128)(2,1)} %all-gather.3.cloned.1.call-done) | copy-start | bytes 6291460
  44.6 7.5 %copy-start.6 = (bf16[4096,512]{1,0:T(8,128)(2,1)S(1)}, bf16[4096,512]{1,0:T(8,128)(2,1)}, u32[]{:S(2)}) copy-start(bf16[4096,512]{1,0:T(8,128)(2,1)} %param.26) | copy-start | bytes 12582916
  49.5 6.1 %collective-permute-start.7 = (bf16[256,128]{1,0:T(8,128)(2,1)S(1)}, bf16[256,128]{1,0:T(8,128)(2,1)S(1)}, u32[]{:S(2)}, u32[]{:S(2)}) collective-permute-start(bf16[256,128]{1,0:T(8,128)(2,1)S(1)} %get-tuple-element.18), channel_id=1, source_target_pairs={{1,3},{2,5},{3,7},{4,1},{5,2},{6,4},{7,6},{9,11},{10,13},{11,15},{... | collective-permute-start | bytes 196616 | tf_op jit(solution)/shard_map/ppermute | solution.py:305
  50.2 8.6 %collective-permute-start.6 = (bf16[256,128]{1,0:T(8,128)(2,1)S(1)}, bf16[256,128]{1,0:T(8,128)(2,1)S(1)}, u32[]{:S(2)}, u32[]{:S(2)}) collective-permute-start(bf16[256,128]{1,0:T(8,128)(2,1)S(1)} %get-tuple-element.18), channel_id=1, source_target_pairs={{0,1},{1,2},{2,4},{3,6},{4,0},{5,3},{6,5},{8,9},{9,10},{10,12},{11... | collective-permute-start | bytes 196616 | tf_op jit(solution)/shard_map/ppermute | solution.py:305
  63.8 53.9 %copy-start.3 = (bf16[256,512]{1,0:T(8,128)(2,1)S(1)}, bf16[256,512]{1,0:T(8,128)(2,1)}, u32[]{:S(2)}) copy-start(bf16[256,512]{1,0:T(8,128)(2,1)} %param.23) | copy-start | bytes 786436
  63.8 55.9 %copy-start.4 = (bf16[4096]{0:T(1024)(128)(2,1)S(1)}, bf16[4096]{0:T(1024)(128)(2,1)}, u32[]{:S(2)}) copy-start(bf16[4096]{0:T(1024)(128)(2,1)} %param.25) | copy-start | bytes 24580
  74.2 73.7 %all-gather.5.cloned.1.call-start = ((), (), s32[]{:S(2)}) async-start(), calls=%async_computation.4 | async-start | bytes 2359296 | tf_op jit(solution)/shard_map/all_gather | solution.py:348
  119.5 85.2 %reduce-scatter.5.cloned.1.call-start = ((), (), s32[]{:S(2)}) async-start(), calls=%async_computation.5 | async-start | bytes 2359296 | tf_op jit(solution)/shard_map/reduce_scatter | solution.py:349
  147.9 56.8 %copy-start.1 = (bf16[256,512]{1,0:T(8,128)(2,1)S(1)}, bf16[256,512]{1,0:T(8,128)(2,1)}, u32[]{:S(2)}) copy-start(bf16[256,512]{1,0:T(8,128)(2,1)} %add_convert_fusion.1) | copy-start | bytes 786436
Sparse Core Ops, SparseCore 0:
  9.6 31.7 all-gather.2
  74.3 43.4 reduce-scatter.2
  120.0 27.8 all-gather.4
  169.4 35.2 reduce-scatter.4

commit v12 on v11

--- a/solution.py
+++ b/solution.py
@@ -70,7 +70,13 @@
     top_scr[...] = jnp.full(top_scr.shape, NEG, jnp.float32)
 
     def max_step(s, carry):
-        @pl.when(limit_ref[s] > 0)
+        lim = limit_ref[s]
+
+        @pl.when(lim == BLK)
+        def _():
+            top_scr[...] = jnp.maximum(top_scr[...], cache_raw(s))
+
+        @pl.when((lim > 0) & (lim < BLK))
         def _():
             top_scr[...] = jnp.maximum(top_scr[...], cache_raw(s) + bias_ref[pl.ds(s, 1), :])
 
@@ -90,14 +96,22 @@
     tot_scr[...] = jnp.zeros(tot_scr.shape, jnp.float32)
     acc_scr[...] = jnp.zeros(acc_scr.shape, jnp.float32)
 
+    def add_weights(s, w):
+        tot_scr[...] += w
+        acc_scr[...] += jnp.dot(
+            w.astype(jnp.bfloat16), cache_ref[s, :, HD:], preferred_element_type=jnp.float32
+        )
+
     def sum_step(s, carry):
-        @pl.when(limit_ref[s] > 0)
+        lim = limit_ref[s]
+
+        @pl.when(lim == BLK)
         def _():
-            w = jnp.exp(cache_raw(s) * scale + bias_ref[pl.ds(s, 1), :] - peak)
-            tot_scr[...] += w
-            acc_scr[...] += jnp.dot(
-                w.astype(jnp.bfloat16), cache_ref[s, :, HD:], preferred_element_type=jnp.float32
-            )
+            add_weights(s, jnp.exp(cache_raw(s) * scale - peak))
+
+        @pl.when((lim > 0) & (lim < BLK))
+        def _():
+            add_weights(s, jnp.exp(cache_raw(s) * scale + bias_ref[pl.ds(s, 1), :] - peak))
 
         return carry
 

time: 214 us -> 213 us (level)
  waiting for transfers between devices: 121 us -> 118 us
  Pallas kernels: 31.7 us -> 33.9 us
    reduce_scatter x1, waiting for transfers between devices: 43.5 us -> 40.6 us  [per_device(): lax.psum_scatter(head_term, 'tp', scatter_dimension=1, tiled=True)]
    pallas_call x1, Pallas kernels: 10.3 us -> 12.5 us  [local_attention(): pl.pallas_call(attn_kernel, out_shape=jax.ShapeDtypeStruct((span_size, wi...]
where the time goes in v12:
time: 213 us; the launch traced here: 212 us
  waiting for transfers between devices  118 us (55%)
  Pallas kernels  33.9 us (16%)
  other arithmetic  19.7 us (9%)
  between operations  14 us (7%)
  starting transfers between devices  11.9 us (6%)
  local copies, waits for them, and re-layouts  10.5 us (5%)
  matrix products  3.88 us (2%)
    reduce_scatter x1, waiting for transfers between devices, per_device(): lax.psum_scatter(head_term, 'tp', scatter_dimension=1, tiled=True)  40.6 us
    reduce_scatter x1, waiting for transfers between devices, per_device(): lax.psum_scatter(feed_forward(full_mid, mlp_gain, w_gate, w_up, w_down),...  35.4 us
    all_gather x1, waiting for transfers between devices, per_device(): full_mid = lax.all_gather(mid, 'tp', axis=1, tiled=True)  27.3 us
    pallas_call x1, Pallas kernels, feed_forward(): pl.pallas_call(functools.partial(ffn_kernel, first, chunk), out_shape=jax...  21.4 us
    pallas_call x1, Pallas kernels, local_attention(): pl.pallas_call(attn_kernel, out_shape=jax.ShapeDtypeStruct((span_size, wi...  12.5 us
    ppermute x6, waiting for transfers between devices, gather_ctx(): parts.append(lax.ppermute(value, 'ctx', pairs))  11 us
    ppermute x6, starting transfers between devices, gather_ctx(): parts.append(lax.ppermute(value, 'ctx', pairs))  8.9 us
  transfers between devices with their start and end apart: 12, of which 5 were waited for; matrix products, arithmetic and copies ran while one was open for 10% of the time, Pallas kernels for 0%

profile of v12, /device:TPU:0, one launch (start us, length us, event | category | flops | bytes accessed | tf_op | source)
XLA Modules:
  0.0 212.0 jit_solution(8575139857399703910)
XLA Ops:
  7.2 0.7 all-gather.3.cloned.1.call-update
  8.0 0.7 pad_add_fusion
  8.6 3.9 %collective-permute-start.2 = (s32[2,8]{1,0:T(2,128)S(1)}, s32[2,8]{1,0:T(2,128)S(1)}, u32[]{:S(2)}, u32[]{:S(2)}) collective-permute-start(s32[2,8]{1,0:T(2,128)S(1)} %pad_add_fusion), channel_id=1, source_target_pairs={{0,24},{8,0},{16,8},{24,16},{1,25},{9,1},{17,9},{25,17},{2,26},{10... | collective-permute-start | bytes 200 | tf_op jit(solution)/shard_map/ppermute | solution.py:269
  12.5 0.5 collective-permute-start.1
  13.0 0.6 collective-permute-start
  13.6 1.1 constant_dynamic-slice_fusion.1
  14.7 0.1 pad_maximum_fusion.1
  14.8 2.4 %collective-permute-start.5 = (bf16[8,128,256]{2,1,0:T(8,128)(2,1)S(1)}, bf16[8,128,256]{2,1,0:T(8,128)(2,1)S(1)}, u32[]{:S(2)}, u32[]{:S(2)}) collective-permute-start(bf16[8,128,256]{2,1,0:T(8,128)(2,1)S(1)} %pad_maximum_fusion.1), channel_id=1, source_target_pairs={{0,24},{8,0},{16,8},{24,16},{1,25},{9,1},{17,9},{25,17},{2,26},{10... | collective-permute-start | bytes 1572872 | tf_op jit(solution)/shard_map/ppermute | solution.py:269
  17.2 1.5 collective-permute-start.4
  18.7 1.2 dynamic_slice.40.span_ref
  19.9 1.3 dynamic_slice.41
  21.2 1.3 dynamic_slice.48
  22.5 1.2 dynamic_slice.47
  23.7 1.3 dynamic_slice.46
  25.0 1.2 dynamic_slice.45
  26.2 1.3 dynamic_slice.44
  27.6 0.6 iota_compare_fusion.1
  28.1 0.7 add_convert_fusion.3
  28.8 0.5 multiply_cosine_fusion.1
  29.3 0.7 convert_element_type.53
  30.1 0.8 pad_add_fusion.1
  30.8 0.7 fusion.29.limit_ref
  31.5 0.7 fusion.28.bias_ref
  32.2 11.0 %collective-permute-done.3 = bf16[8,128,256]{2,1,0:T(8,128)(2,1)S(1)} collective-permute-done((bf16[8,128,256]{2,1,0:T(8,128)(2,1)S(1)}, bf16[8,128,256]{2,1,0:T(8,128)(2,1)S(1)}, u32[]{:S(2)}, u32[]{:S(2)}) %collective-permute-start.3) | collective-permute-done | bytes 524320 | tf_op jit(solution)/shard_map/ppermute | solution.py:269
  43.2 1.4 pad_maximum_fusion.cache_ref
  44.6 2.2 %fusion = f32[256]{0:T(256)S(1)} fusion(bf16[256,4096]{1,0:T(8,128)(2,1)} %all-gather.3.cloned.1.call-done), kind=kLoop, calls=%fused_computation.2 | loop fusion | flops 3145472 | bytes 2098176 | tf_op jit(solution)/shard_map/reduce_sum | solution.py:23
  46.9 2.6 %bitcast_convert_fusion = (f32[256,1,128]{2,0,1:T(8,128)S(1)}, bf16[256,128]{1,0:T(8,128)(2,1)S(1)}) fusion(bf16[4096,128]{1,0:T(8,128)(2,1)S(1)} %copy-done, bf16[256,4096]{1,0:T(8,128)(2,1)} %all-gather.3.cloned.1.call-done, f32[4096]{0:T(1024)S(1)} %convert_element_type.53, f32[256]{0:T(256)S(1)} %add_rsqrt_fusion), kind=kOutput, calls=%fused_computation.38 | convolution fusion | flops 272695296 | bytes 3359744 | tf_op jit(solution)/shard_map/dot_general | solution.py:315
  49.5 0.7 collective-permute-start.7
  50.2 2.0 collective-permute-start.6
  52.1 1.3 fusion.4
  53.4 0.2 reshape.196
  53.6 0.6 fusion.25
  54.2 0.3 fusion.30
  54.5 0.1 subtract_convert_fusion
  54.7 0.9 pad_maximum_fusion.2
  55.5 3.2 %collective-permute-done.6 = bf16[256,128]{1,0:T(8,128)(2,1)S(1)} collective-permute-done((bf16[256,128]{1,0:T(8,128)(2,1)S(1)}, bf16[256,128]{1,0:T(8,128)(2,1)S(1)}, u32[]{:S(2)}, u32[]{:S(2)}) %collective-permute-start.6) | collective-permute-done | bytes 65568 | tf_op jit(solution)/shard_map/ppermute | solution.py:319
  58.7 3.8 %select_add_fusion = (bf16[256,128]{1,0:T(8,128)(2,1)}, f32[256,1,128]{2,0,1:T(8,128)S(1)}, bf16[256,128]{1,0:T(8,128)(2,1)}) fusion(bf16[256,128]{1,0:T(8,128)(2,1)S(1)} %collective-permute-done.7, bf16[256,128]{1,0:T(8,128)(2,1)S(1)} %collective-permute-done.6, bf16[256,128]{1,0:T(8,128)(2,1)S(1)} %get-tuple-element.18, pred[]{:T(512)} %bitcast.15, ...), kind=kLoop, calls=%fused_computation.40 | loop fusion | flops 819200 | bytes 524550 | tf_op jit(solution)/shard_map/add | solution.py:326
  62.5 0.6 fusion.27
  63.1 0.7 pad_maximum_fusion.3.nk_ref
  63.9 12.5 %shard_map.230 = bf16[256,4096]{1,0:T(8,128)(2,1)} custom-call(s32[32]{0:T(128)} %copy-done.5, s32[1]{0:T(128)} %dynamic_slice.40.span_ref, bf16[1024,128]{1,0:T(8,128)(2,1)} %bitcast.35, bf16[32,128,256]{2,1,0:T(8,128)(2,1)} %pad_maximum_fusion.cache_ref, f32[32,128]{1,0:T(8,128)} %fusion.28.bias_ref, bf16[256,128]{1,0:T(8,128)(2,1)} %pad_maximum_fusion.3.nk_ref, ...), custom_call_target="tpu_custom_call" | custom-call | tf_op jit(solution)/shard_map/pallas_call | solution.py:147
  76.5 40.6 %reduce-scatter.3.cloned.1.call-done = bf16[256,512]{1,0:T(8,128)(2,1)} async-done(((bf16[256,4096]{1,0:T(8,128)(2,1)}), bf16[256,512]{1,0:T(8,128)(2,1)}) %reduce-scatter.3.cloned.1.call-update) | async-done | bytes 262160 | tf_op jit(solution)/shard_map/reduce_scatter | solution.py:360
  117.0 1.7 add_convert_fusion.1
  118.8 0.2 reduce-scatter.5.cloned.1.call-start
  119.0 0.6 reshape.206
  119.6 27.3 %all-gather.5.cloned.1.call-done.x_ref = bf16[256,4096]{1,0:T(8,128)(2,1)} async-done(((bf16[256,512]{1,0:T(8,128)(2,1)}), bf16[256,4096]{1,0:T(8,128)(2,1)}) %all-gather.5.cloned.1.call-update) | async-done | bytes 2097168 | tf_op jit(solution)/shard_map/all_gather | solution.py:362
  146.9 21.4 %shard_map.231 = bf16[256,4096]{1,0:T(8,128)(2,1)} custom-call(bf16[256,4096]{1,0:T(8,128)(2,1)} %all-gather.5.cloned.1.call-done.x_ref, f32[1,4096]{1,0:T(1,128)} %bitcast.36, bf16[1376,4096]{1,0:T(8,128)(2,1)} %bitcast.33, bf16[1376,4096]{1,0:T(8,128)(2,1)} %bitcast.34, bf16[1376,4096]{1,0:T(8,128)(2,1)} %wd_ref.1), custom_call_target="tpu_custom_call" | custom-call | tf_op jit(solution)/shard_map/pallas_call | solution.py:212
  168.3 35.4 %reduce-scatter.5.cloned.1.call-done = bf16[256,512]{1,0:T(8,128)(2,1)} async-done(((bf16[256,4096]{1,0:T(8,128)(2,1)}), bf16[256,512]{1,0:T(8,128)(2,1)}) %reduce-scatter.5.cloned.1.call-update) | async-done | bytes 262160 | tf_op jit(solution)/shard_map/reduce_scatter | solution.py:363
  203.8 1.8 fusion.6
  (30 shorter events, 0.2 us)
Async XLA Ops:
  7.2 39.7 %copy-start = (bf16[4096,128]{1,0:T(8,128)(2,1)S(1)}, bf16[4096,128]{1,0:T(8,128)(2,1)}, u32[]{:S(2)}) copy-start(bf16[4096,128]{1,0:T(8,128)(2,1)} %param.27) | copy-start | bytes 3145732
  7.2 37.4 %all-gather.3.cloned.1.call-start = ((), (), s32[]{:S(2)}) async-start(), calls=%async_computation.2 | async-start | bytes 2359296 | tf_op jit(solution)/shard_map/all_gather | solution.py:313
  7.9 109.1 %reduce-scatter.3.cloned.1.call-start = ((), (), s32[]{:S(2)}) async-start(), calls=%async_computation.3 | async-start | bytes 2359296 | tf_op jit(solution)/shard_map/reduce_scatter | solution.py:360
  8.6 21.4 %collective-permute-start.2 = (s32[2,8]{1,0:T(2,128)S(1)}, s32[2,8]{1,0:T(2,128)S(1)}, u32[]{:S(2)}, u32[]{:S(2)}) collective-permute-start(s32[2,8]{1,0:T(2,128)S(1)} %pad_add_fusion), channel_id=1, source_target_pairs={{0,24},{8,0},{16,8},{24,16},{1,25},{9,1},{17,9},{25,17},{2,26},{10... | collective-permute-start | bytes 200 | tf_op jit(solution)/shard_map/ppermute | solution.py:269
  12.5 17.5 %collective-permute-start.1 = (s32[2,8]{1,0:T(2,128)S(1)}, s32[2,8]{1,0:T(2,128)S(1)}, u32[]{:S(2)}, u32[]{:S(2)}) collective-permute-start(s32[2,8]{1,0:T(2,128)S(1)} %pad_add_fusion), channel_id=1, source_target_pairs={{0,16},{8,24},{16,0},{24,8},{1,17},{9,25},{17,1},{25,9},{2,18},{10... | collective-permute-start | bytes 200 | tf_op jit(solution)/shard_map/ppermute | solution.py:269
  13.0 17.0 %collective-permute-start = (s32[2,8]{1,0:T(2,128)S(1)}, s32[2,8]{1,0:T(2,128)S(1)}, u32[]{:S(2)}, u32[]{:S(2)}) collective-permute-start(s32[2,8]{1,0:T(2,128)S(1)} %pad_add_fusion), channel_id=1, source_target_pairs={{0,8},{8,16},{16,24},{24,0},{1,9},{9,17},{17,25},{25,1},{2,10},{10... | collective-permute-start | bytes 200 | tf_op jit(solution)/shard_map/ppermute | solution.py:269
  14.8 17.4 %collective-permute-start.5 = (bf16[8,128,256]{2,1,0:T(8,128)(2,1)S(1)}, bf16[8,128,256]{2,1,0:T(8,128)(2,1)S(1)}, u32[]{:S(2)}, u32[]{:S(2)}) collective-permute-start(bf16[8,128,256]{2,1,0:T(8,128)(2,1)S(1)} %pad_maximum_fusion.1), channel_id=1, source_target_pairs={{0,24},{8,0},{16,8},{24,16},{1,25},{9,1},{17,9},{25,17},{2,26},{10... | collective-permute-start | bytes 1572872 | tf_op jit(solution)/shard_map/ppermute | solution.py:269
  17.2 15.0 %collective-permute-start.4 = (bf16[8,128,256]{2,1,0:T(8,128)(2,1)S(1)}, bf16[8,128,256]{2,1,0:T(8,128)(2,1)S(1)}, u32[]{:S(2)}, u32[]{:S(2)}) collective-permute-start(bf16[8,128,256]{2,1,0:T(8,128)(2,1)S(1)} %pad_maximum_fusion.1), channel_id=1, source_target_pairs={{0,16},{8,24},{16,0},{24,8},{1,17},{9,25},{17,1},{25,9},{2,18},{10... | collective-permute-start | bytes 1572872 | tf_op jit(solution)/shard_map/ppermute | solution.py:269
  30.0 13.2 %collective-permute-start.3 = (bf16[8,128,256]{2,1,0:T(8,128)(2,1)S(1)}, bf16[8,128,256]{2,1,0:T(8,128)(2,1)S(1)}, u32[]{:S(2)}, u32[]{:S(2)}) collective-permute-start(bf16[8,128,256]{2,1,0:T(8,128)(2,1)S(1)} %pad_maximum_fusion.1), channel_id=1, source_target_pairs={{0,8},{8,16},{16,24},{24,0},{1,9},{9,17},{17,25},{25,1},{2,10},{10... | collective-permute-start | bytes 1572872 | tf_op jit(solution)/shard_map/ppermute | solution.py:269
  31.5 18.0 %copy-start.5 = (s32[32]{0:T(128)}, s32[32]{0:T(128)S(1)}, u32[]{:S(2)}) copy-start(s32[32]{0:T(128)S(1)} %fusion.29.limit_ref) | copy-start | bytes 388
  44.6 7.5 %copy-start.2 = (bf16[256,4096]{1,0:T(8,128)(2,1)S(1)}, bf16[256,4096]{1,0:T(8,128)(2,1)}, u32[]{:S(2)}) copy-start(bf16[256,4096]{1,0:T(8,128)(2,1)} %all-gather.3.cloned.1.call-done) | copy-start | bytes 6291460
  44.6 7.5 %copy-start.6 = (bf16[4096,512]{1,0:T(8,128)(2,1)S(1)}, bf16[4096,512]{1,0:T(8,128)(2,1)}, u32[]{:S(2)}) copy-start(bf16[4096,512]{1,0:T(8,128)(2,1)} %param.26) | copy-start | bytes 12582916
  49.5 6.1 %collective-permute-start.7 = (bf16[256,128]{1,0:T(8,128)(2,1)S(1)}, bf16[256,128]{1,0:T(8,128)(2,1)S(1)}, u32[]{:S(2)}, u32[]{:S(2)}) collective-permute-start(bf16[256,128]{1,0:T(8,128)(2,1)S(1)} %get-tuple-element.18), channel_id=1, source_target_pairs={{1,3},{2,5},{3,7},{4,1},{5,2},{6,4},{7,6},{9,11},{10,13},{11,15},{... | collective-permute-start | bytes 196616 | tf_op jit(solution)/shard_map/ppermute | solution.py:319
  50.2 8.6 %collective-permute-start.6 = (bf16[256,128]{1,0:T(8,128)(2,1)S(1)}, bf16[256,128]{1,0:T(8,128)(2,1)S(1)}, u32[]{:S(2)}, u32[]{:S(2)}) collective-permute-start(bf16[256,128]{1,0:T(8,128)(2,1)S(1)} %get-tuple-element.18), channel_id=1, source_target_pairs={{0,1},{1,2},{2,4},{3,6},{4,0},{5,3},{6,5},{8,9},{9,10},{10,12},{11... | collective-permute-start | bytes 196616 | tf_op jit(solution)/shard_map/ppermute | solution.py:319
  63.8 53.2 %copy-start.3 = (bf16[256,512]{1,0:T(8,128)(2,1)S(1)}, bf16[256,512]{1,0:T(8,128)(2,1)}, u32[]{:S(2)}) copy-start(bf16[256,512]{1,0:T(8,128)(2,1)} %param.23) | copy-start | bytes 786436
  63.8 55.2 %copy-start.4 = (bf16[4096]{0:T(1024)(128)(2,1)S(1)}, bf16[4096]{0:T(1024)(128)(2,1)}, u32[]{:S(2)}) copy-start(bf16[4096]{0:T(1024)(128)(2,1)} %param.25) | copy-start | bytes 24580
  76.4 70.5 %all-gather.5.cloned.1.call-start = ((), (), s32[]{:S(2)}) async-start(), calls=%async_computation.4 | async-start | bytes 2359296 | tf_op jit(solution)/shard_map/all_gather | solution.py:362
  118.8 85.0 %reduce-scatter.5.cloned.1.call-start = ((), (), s32[]{:S(2)}) async-start(), calls=%async_computation.5 | async-start | bytes 2359296 | tf_op jit(solution)/shard_map/reduce_scatter | solution.py:363
  146.9 56.8 %copy-start.1 = (bf16[256,512]{1,0:T(8,128)(2,1)S(1)}, bf16[256,512]{1,0:T(8,128)(2,1)}, u32[]{:S(2)}) copy-start(bf16[256,512]{1,0:T(8,128)(2,1)} %add_convert_fusion.1) | copy-start | bytes 786436
Sparse Core Ops, SparseCore 0:
  9.6 31.7 all-gather.2
  76.5 40.4 reduce-scatter.2
  119.2 27.6 all-gather.4
  168.4 35.2 reduce-scatter.4

commit v13 on v12

--- a/solution.py
+++ b/solution.py
@@ -205,9 +205,10 @@
 def feed_forward(full_mid, gain, w_gate, w_up, w_down):
     rows, width = full_mid.shape
     units = w_gate.shape[1]
-    chunk = 1024 if width % 1024 == 0 else width
+    chunk = 512 if width % 512 == 0 else width
+    out_chunk = 1024 if w_down.shape[1] % 1024 == 0 else w_down.shape[1]
     first = width // chunk
-    outs = w_down.shape[1] // chunk
+    outs = w_down.shape[1] // out_chunk
     last = first - 1
     return pl.pallas_call(
         functools.partial(ffn_kernel, first, chunk),
@@ -218,9 +219,9 @@
             pl.BlockSpec((1, width), lambda i: (0, 0)),
             pl.BlockSpec((units, chunk), lambda i: (0, jnp.minimum(i, last))),
             pl.BlockSpec((units, chunk), lambda i: (0, jnp.minimum(i, last))),
-            pl.BlockSpec((units, chunk), lambda i: (0, jnp.maximum(i - first, 0))),
+            pl.BlockSpec((units, out_chunk), lambda i: (0, jnp.maximum(i - first, 0))),
         ],
-        out_specs=pl.BlockSpec((rows, chunk), lambda i: (0, jnp.maximum(i - first, 0))),
+        out_specs=pl.BlockSpec((rows, out_chunk), lambda i: (0, jnp.maximum(i - first, 0))),
         scratch_shapes=[
             pltpu.VMEM((rows, 1), jnp.float32),
             pltpu.VMEM((rows, units), jnp.float32),

time: 213 us -> 215 us (level)
  Pallas kernels: 33.9 us -> 42.1 us
  waiting for transfers between devices: 118 us -> 113 us
    pallas_call x1, Pallas kernels: 12.5 us -> 19.4 us  [local_attention(): pl.pallas_call(attn_kernel, out_shape=jax.ShapeDtypeStruct((span_size, wi...]
    reduce_scatter x1, waiting for transfers between devices: 40.6 us -> 34.9 us  [per_device(): lax.psum_scatter(head_term, 'tp', scatter_dimension=1, tiled=True)]
where the time goes in v13:
time: 215 us
  waiting for transfers between devices  113 us (53%)
  Pallas kernels  42.1 us (20%)
  other arithmetic  19.7 us (9%)
  between operations  14 us (7%)
  starting transfers between devices  11.9 us (6%)
  local copies, waits for them, and re-layouts  10.5 us (5%)
  matrix products  3.88 us (2%)
    reduce_scatter x1, waiting for transfers between devices, per_device(): lax.psum_scatter(feed_forward(full_mid, mlp_gain, w_gate, w_up, w_down),...  35.4 us
    reduce_scatter x1, waiting for transfers between devices, per_device(): lax.psum_scatter(head_term, 'tp', scatter_dimension=1, tiled=True)  34.9 us
    all_gather x1, waiting for transfers between devices, per_device(): full_mid = lax.all_gather(mid, 'tp', axis=1, tiled=True)  27.5 us
    pallas_call x1, Pallas kernels, feed_forward(): pl.pallas_call(functools.partial(ffn_kernel, first, chunk), out_shape=jax...  22.7 us
    pallas_call x1, Pallas kernels, local_attention(): pl.pallas_call(attn_kernel, out_shape=jax.ShapeDtypeStruct((span_size, wi...  19.4 us
    ppermute x6, waiting for transfers between devices, gather_ctx(): parts.append(lax.ppermute(value, 'ctx', pairs))  11 us
    ppermute x6, starting transfers between devices, gather_ctx(): parts.append(lax.ppermute(value, 'ctx', pairs))  8.9 us
  transfers between devices with their start and end apart: 12, of which 5 were waited for; matrix products, arithmetic and copies ran while one was open for 10% of the time, Pallas kernels for 0%

profile of v13, /device:TPU:0, one launch (start us, length us, event | category | flops | bytes accessed | tf_op | source)
XLA Modules:
  0.0 214.7 jit_solution(1071690016524702798)
XLA Ops:
  7.2 0.7 all-gather.3.cloned.1.call-update
  8.0 0.7 pad_add_fusion
  8.6 3.9 %collective-permute-start.2 = (s32[2,8]{1,0:T(2,128)S(1)}, s32[2,8]{1,0:T(2,128)S(1)}, u32[]{:S(2)}, u32[]{:S(2)}) collective-permute-start(s32[2,8]{1,0:T(2,128)S(1)} %pad_add_fusion), channel_id=1, source_target_pairs={{0,24},{8,0},{16,8},{24,16},{1,25},{9,1},{17,9},{25,17},{2,26},{10... | collective-permute-start | bytes 200 | tf_op jit(solution)/shard_map/ppermute | solution.py:270
  12.5 0.5 collective-permute-start.1
  13.0 0.6 collective-permute-start
  13.6 1.1 constant_dynamic-slice_fusion.1
  14.7 0.1 pad_maximum_fusion.1
  14.8 2.4 %collective-permute-start.5 = (bf16[8,128,256]{2,1,0:T(8,128)(2,1)S(1)}, bf16[8,128,256]{2,1,0:T(8,128)(2,1)S(1)}, u32[]{:S(2)}, u32[]{:S(2)}) collective-permute-start(bf16[8,128,256]{2,1,0:T(8,128)(2,1)S(1)} %pad_maximum_fusion.1), channel_id=1, source_target_pairs={{0,24},{8,0},{16,8},{24,16},{1,25},{9,1},{17,9},{25,17},{2,26},{10... | collective-permute-start | bytes 1572872 | tf_op jit(solution)/shard_map/ppermute | solution.py:270
  17.2 1.5 collective-permute-start.4
  18.7 1.2 dynamic_slice.40.span_ref
  19.9 1.3 dynamic_slice.41
  21.2 1.3 dynamic_slice.48
  22.5 1.2 dynamic_slice.47
  23.7 1.3 dynamic_slice.46
  25.0 1.2 dynamic_slice.45
  26.2 1.3 dynamic_slice.44
  27.6 0.6 iota_compare_fusion.1
  28.1 0.7 add_convert_fusion.3
  28.8 0.5 multiply_cosine_fusion.1
  29.3 0.7 convert_element_type.53
  30.1 0.8 pad_add_fusion.1
  30.8 0.7 fusion.29.limit_ref
  31.5 0.7 fusion.28.bias_ref
  32.2 11.0 %collective-permute-done.3 = bf16[8,128,256]{2,1,0:T(8,128)(2,1)S(1)} collective-permute-done((bf16[8,128,256]{2,1,0:T(8,128)(2,1)S(1)}, bf16[8,128,256]{2,1,0:T(8,128)(2,1)S(1)}, u32[]{:S(2)}, u32[]{:S(2)}) %collective-permute-start.3) | collective-permute-done | bytes 524320 | tf_op jit(solution)/shard_map/ppermute | solution.py:270
  43.2 1.4 pad_maximum_fusion.cache_ref
  44.6 2.2 %fusion = f32[256]{0:T(256)S(1)} fusion(bf16[256,4096]{1,0:T(8,128)(2,1)} %all-gather.3.cloned.1.call-done), kind=kLoop, calls=%fused_computation.2 | loop fusion | flops 3145472 | bytes 2098176 | tf_op jit(solution)/shard_map/reduce_sum | solution.py:23
  46.9 2.6 %bitcast_convert_fusion = (f32[256,1,128]{2,0,1:T(8,128)S(1)}, bf16[256,128]{1,0:T(8,128)(2,1)S(1)}) fusion(bf16[4096,128]{1,0:T(8,128)(2,1)S(1)} %copy-done, bf16[256,4096]{1,0:T(8,128)(2,1)} %all-gather.3.cloned.1.call-done, f32[4096]{0:T(1024)S(1)} %convert_element_type.53, f32[256]{0:T(256)S(1)} %add_rsqrt_fusion), kind=kOutput, calls=%fused_computation.38 | convolution fusion | flops 272695296 | bytes 3359744 | tf_op jit(solution)/shard_map/dot_general | solution.py:316
  49.5 0.7 collective-permute-start.7
  50.2 2.0 collective-permute-start.6
  52.1 1.3 fusion.4
  53.4 0.2 reshape.196
  53.6 0.6 fusion.25
  54.2 0.3 fusion.30
  54.5 0.1 subtract_convert_fusion
  54.7 0.9 pad_maximum_fusion.2
  55.5 3.2 %collective-permute-done.6 = bf16[256,128]{1,0:T(8,128)(2,1)S(1)} collective-permute-done((bf16[256,128]{1,0:T(8,128)(2,1)S(1)}, bf16[256,128]{1,0:T(8,128)(2,1)S(1)}, u32[]{:S(2)}, u32[]{:S(2)}) %collective-permute-start.6) | collective-permute-done | bytes 65568 | tf_op jit(solution)/shard_map/ppermute | solution.py:320
  58.7 3.8 %select_add_fusion = (bf16[256,128]{1,0:T(8,128)(2,1)}, f32[256,1,128]{2,0,1:T(8,128)S(1)}, bf16[256,128]{1,0:T(8,128)(2,1)}) fusion(bf16[256,128]{1,0:T(8,128)(2,1)S(1)} %collective-permute-done.7, bf16[256,128]{1,0:T(8,128)(2,1)S(1)} %collective-permute-done.6, bf16[256,128]{1,0:T(8,128)(2,1)S(1)} %get-tuple-element.18, pred[]{:T(512)} %bitcast.15, ...), kind=kLoop, calls=%fused_computation.40 | loop fusion | flops 819200 | bytes 524550 | tf_op jit(solution)/shard_map/add | solution.py:327
  62.5 0.6 fusion.27
  63.1 0.7 pad_maximum_fusion.3.nk_ref
  63.9 19.4 %shard_map.230 = bf16[256,4096]{1,0:T(8,128)(2,1)} custom-call(s32[32]{0:T(128)} %copy-done.5, s32[1]{0:T(128)} %dynamic_slice.40.span_ref, bf16[1024,128]{1,0:T(8,128)(2,1)} %bitcast.35, bf16[32,128,256]{2,1,0:T(8,128)(2,1)} %pad_maximum_fusion.cache_ref, f32[32,128]{1,0:T(8,128)} %fusion.28.bias_ref, bf16[256,128]{1,0:T(8,128)(2,1)} %pad_maximum_fusion.3.nk_ref, ...), custom_call_target="tpu_custom_call" | custom-call | tf_op jit(solution)/shard_map/pallas_call | solution.py:147
  83.3 34.9 %reduce-scatter.3.cloned.1.call-done = bf16[256,512]{1,0:T(8,128)(2,1)} async-done(((bf16[256,4096]{1,0:T(8,128)(2,1)}), bf16[256,512]{1,0:T(8,128)(2,1)}) %reduce-scatter.3.cloned.1.call-update) | async-done | bytes 262160 | tf_op jit(solution)/shard_map/reduce_scatter | solution.py:361
  118.2 1.7 add_convert_fusion.1
  119.9 0.2 reduce-scatter.5.cloned.1.call-start
  120.2 0.6 reshape.206
  120.8 27.5 %all-gather.5.cloned.1.call-done.x_ref = bf16[256,4096]{1,0:T(8,128)(2,1)} async-done(((bf16[256,512]{1,0:T(8,128)(2,1)}), bf16[256,4096]{1,0:T(8,128)(2,1)}) %all-gather.5.cloned.1.call-update) | async-done | bytes 2097168 | tf_op jit(solution)/shard_map/all_gather | solution.py:363
  148.3 22.7 %shard_map.231 = bf16[256,4096]{1,0:T(8,128)(2,1)} custom-call(bf16[256,4096]{1,0:T(8,128)(2,1)} %all-gather.5.cloned.1.call-done.x_ref, f32[1,4096]{1,0:T(1,128)} %bitcast.36, bf16[1376,4096]{1,0:T(8,128)(2,1)} %bitcast.33, bf16[1376,4096]{1,0:T(8,128)(2,1)} %bitcast.34, bf16[1376,4096]{1,0:T(8,128)(2,1)} %wd_ref.1), custom_call_target="tpu_custom_call" | custom-call | tf_op jit(solution)/shard_map/pallas_call | solution.py:213
  171.0 35.4 %reduce-scatter.5.cloned.1.call-done = bf16[256,512]{1,0:T(8,128)(2,1)} async-done(((bf16[256,4096]{1,0:T(8,128)(2,1)}), bf16[256,512]{1,0:T(8,128)(2,1)}) %reduce-scatter.5.cloned.1.call-update) | async-done | bytes 262160 | tf_op jit(solution)/shard_map/reduce_scatter | solution.py:364
  206.4 1.8 fusion.6
  (30 shorter events, 0.2 us)
Async XLA Ops:
  7.2 39.7 %copy-start = (bf16[4096,128]{1,0:T(8,128)(2,1)S(1)}, bf16[4096,128]{1,0:T(8,128)(2,1)}, u32[]{:S(2)}) copy-start(bf16[4096,128]{1,0:T(8,128)(2,1)} %param.27) | copy-start | bytes 3145732
  7.2 37.4 %all-gather.3.cloned.1.call-start = ((), (), s32[]{:S(2)}) async-start(), calls=%async_computation.2 | async-start | bytes 2359296 | tf_op jit(solution)/shard_map/all_gather | solution.py:314
  7.9 110.3 %reduce-scatter.3.cloned.1.call-start = ((), (), s32[]{:S(2)}) async-start(), calls=%async_computation.3 | async-start | bytes 2359296 | tf_op jit(solution)/shard_map/reduce_scatter | solution.py:361
  8.6 21.4 %collective-permute-start.2 = (s32[2,8]{1,0:T(2,128)S(1)}, s32[2,8]{1,0:T(2,128)S(1)}, u32[]{:S(2)}, u32[]{:S(2)}) collective-permute-start(s32[2,8]{1,0:T(2,128)S(1)} %pad_add_fusion), channel_id=1, source_target_pairs={{0,24},{8,0},{16,8},{24,16},{1,25},{9,1},{17,9},{25,17},{2,26},{10... | collective-permute-start | bytes 200 | tf_op jit(solution)/shard_map/ppermute | solution.py:270
  12.5 17.5 %collective-permute-start.1 = (s32[2,8]{1,0:T(2,128)S(1)}, s32[2,8]{1,0:T(2,128)S(1)}, u32[]{:S(2)}, u32[]{:S(2)}) collective-permute-start(s32[2,8]{1,0:T(2,128)S(1)} %pad_add_fusion), channel_id=1, source_target_pairs={{0,16},{8,24},{16,0},{24,8},{1,17},{9,25},{17,1},{25,9},{2,18},{10... | collective-permute-start | bytes 200 | tf_op jit(solution)/shard_map/ppermute | solution.py:270
  13.0 17.0 %collective-permute-start = (s32[2,8]{1,0:T(2,128)S(1)}, s32[2,8]{1,0:T(2,128)S(1)}, u32[]{:S(2)}, u32[]{:S(2)}) collective-permute-start(s32[2,8]{1,0:T(2,128)S(1)} %pad_add_fusion), channel_id=1, source_target_pairs={{0,8},{8,16},{16,24},{24,0},{1,9},{9,17},{17,25},{25,1},{2,10},{10... | collective-permute-start | bytes 200 | tf_op jit(solution)/shard_map/ppermute | solution.py:270
  14.8 17.4 %collective-permute-start.5 = (bf16[8,128,256]{2,1,0:T(8,128)(2,1)S(1)}, bf16[8,128,256]{2,1,0:T(8,128)(2,1)S(1)}, u32[]{:S(2)}, u32[]{:S(2)}) collective-permute-start(bf16[8,128,256]{2,1,0:T(8,128)(2,1)S(1)} %pad_maximum_fusion.1), channel_id=1, source_target_pairs={{0,24},{8,0},{16,8},{24,16},{1,25},{9,1},{17,9},{25,17},{2,26},{10... | collective-permute-start | bytes 1572872 | tf_op jit(solution)/shard_map/ppermute | solution.py:270
  17.2 15.0 %collective-permute-start.4 = (bf16[8,128,256]{2,1,0:T(8,128)(2,1)S(1)}, bf16[8,128,256]{2,1,0:T(8,128)(2,1)S(1)}, u32[]{:S(2)}, u32[]{:S(2)}) collective-permute-start(bf16[8,128,256]{2,1,0:T(8,128)(2,1)S(1)} %pad_maximum_fusion.1), channel_id=1, source_target_pairs={{0,16},{8,24},{16,0},{24,8},{1,17},{9,25},{17,1},{25,9},{2,18},{10... | collective-permute-start | bytes 1572872 | tf_op jit(solution)/shard_map/ppermute | solution.py:270
  30.0 13.2 %collective-permute-start.3 = (bf16[8,128,256]{2,1,0:T(8,128)(2,1)S(1)}, bf16[8,128,256]{2,1,0:T(8,128)(2,1)S(1)}, u32[]{:S(2)}, u32[]{:S(2)}) collective-permute-start(bf16[8,128,256]{2,1,0:T(8,128)(2,1)S(1)} %pad_maximum_fusion.1), channel_id=1, source_target_pairs={{0,8},{8,16},{16,24},{24,0},{1,9},{9,17},{17,25},{25,1},{2,10},{10... | collective-permute-start | bytes 1572872 | tf_op jit(solution)/shard_map/ppermute | solution.py:270
  31.5 18.0 %copy-start.5 = (s32[32]{0:T(128)}, s32[32]{0:T(128)S(1)}, u32[]{:S(2)}) copy-start(s32[32]{0:T(128)S(1)} %fusion.29.limit_ref) | copy-start | bytes 388
  44.6 7.5 %copy-start.2 = (bf16[256,4096]{1,0:T(8,128)(2,1)S(1)}, bf16[256,4096]{1,0:T(8,128)(2,1)}, u32[]{:S(2)}) copy-start(bf16[256,4096]{1,0:T(8,128)(2,1)} %all-gather.3.cloned.1.call-done) | copy-start | bytes 6291460
  44.6 7.5 %copy-start.6 = (bf16[4096,512]{1,0:T(8,128)(2,1)S(1)}, bf16[4096,512]{1,0:T(8,128)(2,1)}, u32[]{:S(2)}) copy-start(bf16[4096,512]{1,0:T(8,128)(2,1)} %param.26) | copy-start | bytes 12582916
  49.5 6.1 %collective-permute-start.7 = (bf16[256,128]{1,0:T(8,128)(2,1)S(1)}, bf16[256,128]{1,0:T(8,128)(2,1)S(1)}, u32[]{:S(2)}, u32[]{:S(2)}) collective-permute-start(bf16[256,128]{1,0:T(8,128)(2,1)S(1)} %get-tuple-element.18), channel_id=1, source_target_pairs={{1,3},{2,5},{3,7},{4,1},{5,2},{6,4},{7,6},{9,11},{10,13},{11,15},{... | collective-permute-start | bytes 196616 | tf_op jit(solution)/shard_map/ppermute | solution.py:320
  50.2 8.6 %collective-permute-start.6 = (bf16[256,128]{1,0:T(8,128)(2,1)S(1)}, bf16[256,128]{1,0:T(8,128)(2,1)S(1)}, u32[]{:S(2)}, u32[]{:S(2)}) collective-permute-start(bf16[256,128]{1,0:T(8,128)(2,1)S(1)} %get-tuple-element.18), channel_id=1, source_target_pairs={{0,1},{1,2},{2,4},{3,6},{4,0},{5,3},{6,5},{8,9},{9,10},{10,12},{11... | collective-permute-start | bytes 196616 | tf_op jit(solution)/shard_map/ppermute | solution.py:320
  63.8 54.3 %copy-start.3 = (bf16[256,512]{1,0:T(8,128)(2,1)S(1)}, bf16[256,512]{1,0:T(8,128)(2,1)}, u32[]{:S(2)}) copy-start(bf16[256,512]{1,0:T(8,128)(2,1)} %param.23) | copy-start | bytes 786436
  63.8 56.3 %copy-start.4 = (bf16[4096]{0:T(1024)(128)(2,1)S(1)}, bf16[4096]{0:T(1024)(128)(2,1)}, u32[]{:S(2)}) copy-start(bf16[4096]{0:T(1024)(128)(2,1)} %param.25) | copy-start | bytes 24580
  83.3 65.0 %all-gather.5.cloned.1.call-start = ((), (), s32[]{:S(2)}) async-start(), calls=%async_computation.4 | async-start | bytes 2359296 | tf_op jit(solution)/shard_map/all_gather | solution.py:363
  119.9 86.5 %reduce-scatter.5.cloned.1.call-start = ((), (), s32[]{:S(2)}) async-start(), calls=%async_computation.5 | async-start | bytes 2359296 | tf_op jit(solution)/shard_map/reduce_scatter | solution.py:364
  148.3 58.1 %copy-start.1 = (bf16[256,512]{1,0:T(8,128)(2,1)S(1)}, bf16[256,512]{1,0:T(8,128)(2,1)}, u32[]{:S(2)}) copy-start(bf16[256,512]{1,0:T(8,128)(2,1)} %add_convert_fusion.1) | copy-start | bytes 786436
Sparse Core Ops, SparseCore 0:
  9.6 31.7 all-gather.2
  83.4 34.7 reduce-scatter.2
  120.4 27.8 all-gather.4
  171.1 35.2 reduce-scatter.4

commit v14 on v11

--- a/solution.py
+++ b/solution.py
@@ -302,15 +302,11 @@
     kv_width = kv_piece.shape[1]
     tp_count = lax.axis_size("tp")
     per_head, colours, slot, selfs = kv_routes(tp_count, kv_width)
-    received = [lax.ppermute(kv_piece, "tp", pairs) for pairs in colours]
-    zeros = jnp.zeros_like(kv_piece)
+    stacked = jnp.stack([kv_piece] + [lax.ppermute(kv_piece, "tp", pairs) for pairs in colours])
     blocks = []
     for entry in range(len(slot)):
-        got = jnp.where(jnp.asarray(selfs[entry])[tp_rank], kv_piece, zeros)
-        for index, value in enumerate(received):
-            hit = jnp.asarray([slot[entry][dev] == index for dev in range(tp_count)])[tp_rank]
-            got = got + jnp.where(hit, value, zeros)
-        blocks.append(got)
+        pick = jnp.asarray([0 if selfs[entry][dev] else 1 + slot[entry][dev] for dev in range(tp_count)])
+        blocks.append(lax.dynamic_index_in_dim(stacked, pick[tp_rank], 0, keepdims=False))
 
     def head_of(parts):
         return jnp.concatenate(parts, axis=1) if len(parts) > 1 else parts[0]

time: 214 us -> 210 us (0.981)
  local copies, waits for them, and re-layouts: 10.5 us -> 6.6 us
  between operations: 14 us -> 17.9 us
  other arithmetic: 19.7 us -> 16.8 us
    dynamic_slice x5 -> x2, local copies, waits for them, and re-layouts: 6.35 us -> 2.51 us  [per_device(): pick[tp_rank]]
    add x1 -> x0, other arithmetic: 3.84 us -> none  [per_device(): got = got + jnp.where(hit, value, zeros)]
  transfers between devices with their start and end apart: 12 -> 12, of which waited for: 5 -> 5; matrix products, arithmetic and copies ran while one was open for 10% -> 8% of each run, Pallas kernels for 0% -> 0%
where the time goes in v14:
time: 210 us; the launch traced here: 209 us
  waiting for transfers between devices  120 us (57%)
  Pallas kernels  32.3 us (15%)
  between operations  17.9 us (9%)
  other arithmetic  16.8 us (8%)
  starting transfers between devices  11.9 us (6%)
  local copies, waits for them, and re-layouts  6.6 us (3%)
  matrix products  3.89 us (2%)
    reduce_scatter x1, waiting for transfers between devices, per_device(): lax.psum_scatter(head_term, 'tp', scatter_dimension=1, tiled=True)  43 us
    reduce_scatter x1, waiting for transfers between devices, per_device(): lax.psum_scatter(feed_forward(full_mid, mlp_gain, w_gate, w_up, w_down),...  34 us
    all_gather x1, waiting for transfers between devices, per_device(): full_mid = lax.all_gather(mid, 'tp', axis=1, tiled=True)  27.2 us
    pallas_call x1, Pallas kernels, feed_forward(): pl.pallas_call(functools.partial(ffn_kernel, first, chunk), out_shape=jax...  21.3 us
    ppermute x6, waiting for transfers between devices, gather_ctx(): parts.append(lax.ppermute(value, 'ctx', pairs))  11 us
    pallas_call x1, Pallas kernels, local_attention(): pl.pallas_call(attn_kernel, out_shape=jax.ShapeDtypeStruct((span_size, wi...  10.9 us
    ppermute x6, starting transfers between devices, gather_ctx(): parts.append(lax.ppermute(value, 'ctx', pairs))  8.95 us
  transfers between devices with their start and end apart: 12, of which 5 were waited for; matrix products, arithmetic and copies ran while one was open for 8% of the time, Pallas kernels for 0%

profile of v14, /device:TPU:0, one launch (start us, length us, event | category | flops | bytes accessed | tf_op | source)
XLA Modules:
  0.0 209.1 jit_solution(14659119969592777621)
XLA Ops:
  7.2 0.7 all-gather.3.cloned.1.call-update
  7.9 0.0 reduce-scatter.3.cloned.1.call-start
  8.0 0.7 pad_add_fusion
  8.6 3.9 %collective-permute-start.2 = (s32[2,8]{1,0:T(2,128)S(1)}, s32[2,8]{1,0:T(2,128)S(1)}, u32[]{:S(2)}, u32[]{:S(2)}) collective-permute-start(s32[2,8]{1,0:T(2,128)S(1)} %pad_add_fusion), channel_id=1, source_target_pairs={{0,24},{8,0},{16,8},{24,16},{1,25},{9,1},{17,9},{25,17},{2,26},{10... | collective-permute-start | bytes 200 | tf_op jit(solution)/shard_map/ppermute | solution.py:255
  12.5 0.5 collective-permute-start.1
  13.0 0.6 collective-permute-start
  13.6 1.1 constant_dynamic-slice_fusion.1
  14.7 0.1 pad_maximum_fusion.1
  14.8 2.4 %collective-permute-start.5 = (bf16[8,128,256]{2,1,0:T(8,128)(2,1)S(1)}, bf16[8,128,256]{2,1,0:T(8,128)(2,1)S(1)}, u32[]{:S(2)}, u32[]{:S(2)}) collective-permute-start(bf16[8,128,256]{2,1,0:T(8,128)(2,1)S(1)} %pad_maximum_fusion.1), channel_id=1, source_target_pairs={{0,24},{8,0},{16,8},{24,16},{1,25},{9,1},{17,9},{25,17},{2,26},{10... | collective-permute-start | bytes 1572872 | tf_op jit(solution)/shard_map/ppermute | solution.py:255
  17.2 1.5 collective-permute-start.4
  18.7 1.2 dynamic_slice.38
  21.2 1.3 dynamic_slice.36
  23.8 1.2 dynamic_slice.32.span_ref
  25.0 1.2 dynamic_slice.33
  26.3 0.7 convert_element_type.77
  27.6 0.7 add_convert_fusion.3
  28.3 0.5 multiply_cosine_fusion.1
  29.5 0.1 collective-permute-start.3
  29.6 0.8 pad_add_fusion.1
  30.3 0.7 fusion.29.limit_ref
  31.0 0.7 fusion.28.bias_ref
  31.7 11.0 %collective-permute-done.3 = bf16[8,128,256]{2,1,0:T(8,128)(2,1)S(1)} collective-permute-done((bf16[8,128,256]{2,1,0:T(8,128)(2,1)S(1)}, bf16[8,128,256]{2,1,0:T(8,128)(2,1)S(1)}, u32[]{:S(2)}, u32[]{:S(2)}) %collective-permute-start.3) | collective-permute-done | bytes 524320 | tf_op jit(solution)/shard_map/ppermute | solution.py:255
  42.7 1.4 pad_maximum_fusion.cache_ref
  44.1 2.2 %fusion = f32[256]{0:T(256)S(1)} fusion(bf16[256,4096]{1,0:T(8,128)(2,1)} %all-gather.3.cloned.1.call-done), kind=kLoop, calls=%fused_computation.2 | loop fusion | flops 3145472 | bytes 2098176 | tf_op jit(solution)/shard_map/reduce_sum | solution.py:23
  46.4 2.6 %bitcast_convert_fusion = (f32[256,1,128]{2,0,1:T(8,128)S(1)}, bf16[256,128]{1,0:T(8,128)(2,1)S(1)}) fusion(bf16[4096,128]{1,0:T(8,128)(2,1)S(1)} %copy-done, bf16[256,4096]{1,0:T(8,128)(2,1)} %all-gather.3.cloned.1.call-done, f32[4096]{0:T(1024)S(1)} %convert_element_type.77, f32[256]{0:T(256)S(1)} %add_rsqrt_fusion), kind=kOutput, calls=%fused_computation.39 | convolution fusion | flops 272695296 | bytes 3359744 | tf_op jit(solution)/shard_map/dot_general | solution.py:301
  49.0 0.7 collective-permute-start.7
  49.7 2.0 collective-permute-start.6
  51.7 1.3 fusion.4
  53.0 0.2 reshape.210
  53.1 0.3 fusion.30
  53.5 0.1 subtract_convert_fusion
  53.6 0.9 pad_maximum_fusion.2
  54.5 3.7 %collective-permute-done.6 = bf16[256,128]{1,0:T(8,128)(2,1)S(1)} collective-permute-done((bf16[256,128]{1,0:T(8,128)(2,1)S(1)}, bf16[256,128]{1,0:T(8,128)(2,1)S(1)}, u32[]{:S(2)}, u32[]{:S(2)}) %collective-permute-start.6) | collective-permute-done | bytes 65568 | tf_op jit(solution)/shard_map/ppermute | solution.py:305
  58.3 0.7 dynamic-slice_bitcast_fusion
  58.9 0.6 fusion.25
  59.5 0.7 pad_maximum_fusion.4.nk_ref
  60.2 10.9 %shard_map.176 = bf16[256,4096]{1,0:T(8,128)(2,1)} custom-call(s32[32]{0:T(128)} %copy-done.5, s32[1]{0:T(128)} %dynamic_slice.32.span_ref, bf16[1024,128]{1,0:T(8,128)(2,1)} %bitcast.37, bf16[32,128,256]{2,1,0:T(8,128)(2,1)} %pad_maximum_fusion.cache_ref, f32[32,128]{1,0:T(8,128)} %fusion.28.bias_ref, bf16[256,128]{1,0:T(8,128)(2,1)} %pad_maximum_fusion.4.nk_ref, ...), custom_call_target="tpu_custom_call" | custom-call | tf_op jit(solution)/shard_map/pallas_call | solution.py:133
  71.2 0.0 all-gather.5.cloned.1.call-start
  71.2 43.0 %reduce-scatter.3.cloned.1.call-done = bf16[256,512]{1,0:T(8,128)(2,1)} async-done(((bf16[256,4096]{1,0:T(8,128)(2,1)}), bf16[256,512]{1,0:T(8,128)(2,1)}) %reduce-scatter.3.cloned.1.call-update) | async-done | bytes 262160 | tf_op jit(solution)/shard_map/reduce_scatter | solution.py:342
  114.2 1.7 add_convert_fusion.1
  116.0 0.2 reduce-scatter.5.cloned.1.call-start
  116.2 0.6 reshape.216
  116.8 27.2 %all-gather.5.cloned.1.call-done.x_ref = bf16[256,4096]{1,0:T(8,128)(2,1)} async-done(((bf16[256,512]{1,0:T(8,128)(2,1)}), bf16[256,4096]{1,0:T(8,128)(2,1)}) %all-gather.5.cloned.1.call-update) | async-done | bytes 2097168 | tf_op jit(solution)/shard_map/all_gather | solution.py:344
  144.1 21.3 %shard_map.177 = bf16[256,4096]{1,0:T(8,128)(2,1)} custom-call(bf16[256,4096]{1,0:T(8,128)(2,1)} %all-gather.5.cloned.1.call-done.x_ref, f32[1,4096]{1,0:T(1,128)} %bitcast.39, bf16[1376,4096]{1,0:T(8,128)(2,1)} %bitcast.35, bf16[1376,4096]{1,0:T(8,128)(2,1)} %bitcast.36, bf16[1376,4096]{1,0:T(8,128)(2,1)} %wd_ref.1), custom_call_target="tpu_custom_call" | custom-call | tf_op jit(solution)/shard_map/pallas_call | solution.py:198
  165.5 0.6 iota_compare_fusion.1
  166.0 0.8 fusion.23
  166.8 34.0 %reduce-scatter.5.cloned.1.call-done = bf16[256,512]{1,0:T(8,128)(2,1)} async-done(((bf16[256,4096]{1,0:T(8,128)(2,1)}), bf16[256,512]{1,0:T(8,128)(2,1)}) %reduce-scatter.5.cloned.1.call-update) | async-done | bytes 262160 | tf_op jit(solution)/shard_map/reduce_scatter | solution.py:345
  200.8 1.8 fusion.6
  (28 shorter events, 0.2 us)
Async XLA Ops:
  7.2 39.2 %copy-start = (bf16[4096,128]{1,0:T(8,128)(2,1)S(1)}, bf16[4096,128]{1,0:T(8,128)(2,1)}, u32[]{:S(2)}) copy-start(bf16[4096,128]{1,0:T(8,128)(2,1)} %param.21) | copy-start | bytes 3145732
  7.2 36.9 %all-gather.3.cloned.1.call-start = ((), (), s32[]{:S(2)}) async-start(), calls=%async_computation.2 | async-start | bytes 2359296 | tf_op jit(solution)/shard_map/all_gather | solution.py:299
  7.9 106.3 %reduce-scatter.3.cloned.1.call-start = ((), (), s32[]{:S(2)}) async-start(), calls=%async_computation.3 | async-start | bytes 2359296 | tf_op jit(solution)/shard_map/reduce_scatter | solution.py:342
  8.6 20.8 %collective-permute-start.2 = (s32[2,8]{1,0:T(2,128)S(1)}, s32[2,8]{1,0:T(2,128)S(1)}, u32[]{:S(2)}, u32[]{:S(2)}) collective-permute-start(s32[2,8]{1,0:T(2,128)S(1)} %pad_add_fusion), channel_id=1, source_target_pairs={{0,24},{8,0},{16,8},{24,16},{1,25},{9,1},{17,9},{25,17},{2,26},{10... | collective-permute-start | bytes 200 | tf_op jit(solution)/shard_map/ppermute | solution.py:255
  12.5 17.0 %collective-permute-start.1 = (s32[2,8]{1,0:T(2,128)S(1)}, s32[2,8]{1,0:T(2,128)S(1)}, u32[]{:S(2)}, u32[]{:S(2)}) collective-permute-start(s32[2,8]{1,0:T(2,128)S(1)} %pad_add_fusion), channel_id=1, source_target_pairs={{0,16},{8,24},{16,0},{24,8},{1,17},{9,25},{17,1},{25,9},{2,18},{10... | collective-permute-start | bytes 200 | tf_op jit(solution)/shard_map/ppermute | solution.py:255
  13.0 16.5 %collective-permute-start = (s32[2,8]{1,0:T(2,128)S(1)}, s32[2,8]{1,0:T(2,128)S(1)}, u32[]{:S(2)}, u32[]{:S(2)}) collective-permute-start(s32[2,8]{1,0:T(2,128)S(1)} %pad_add_fusion), channel_id=1, source_target_pairs={{0,8},{8,16},{16,24},{24,0},{1,9},{9,17},{17,25},{25,1},{2,10},{10... | collective-permute-start | bytes 200 | tf_op jit(solution)/shard_map/ppermute | solution.py:255
  14.8 16.9 %collective-permute-start.5 = (bf16[8,128,256]{2,1,0:T(8,128)(2,1)S(1)}, bf16[8,128,256]{2,1,0:T(8,128)(2,1)S(1)}, u32[]{:S(2)}, u32[]{:S(2)}) collective-permute-start(bf16[8,128,256]{2,1,0:T(8,128)(2,1)S(1)} %pad_maximum_fusion.1), channel_id=1, source_target_pairs={{0,24},{8,0},{16,8},{24,16},{1,25},{9,1},{17,9},{25,17},{2,26},{10... | collective-permute-start | bytes 1572872 | tf_op jit(solution)/shard_map/ppermute | solution.py:255
  17.2 14.5 %collective-permute-start.4 = (bf16[8,128,256]{2,1,0:T(8,128)(2,1)S(1)}, bf16[8,128,256]{2,1,0:T(8,128)(2,1)S(1)}, u32[]{:S(2)}, u32[]{:S(2)}) collective-permute-start(bf16[8,128,256]{2,1,0:T(8,128)(2,1)S(1)} %pad_maximum_fusion.1), channel_id=1, source_target_pairs={{0,16},{8,24},{16,0},{24,8},{1,17},{9,25},{17,1},{25,9},{2,18},{10... | collective-permute-start | bytes 1572872 | tf_op jit(solution)/shard_map/ppermute | solution.py:255
  29.5 13.2 %collective-permute-start.3 = (bf16[8,128,256]{2,1,0:T(8,128)(2,1)S(1)}, bf16[8,128,256]{2,1,0:T(8,128)(2,1)S(1)}, u32[]{:S(2)}, u32[]{:S(2)}) collective-permute-start(bf16[8,128,256]{2,1,0:T(8,128)(2,1)S(1)} %pad_maximum_fusion.1), channel_id=1, source_target_pairs={{0,8},{8,16},{16,24},{24,0},{1,9},{9,17},{17,25},{25,1},{2,10},{10... | collective-permute-start | bytes 1572872 | tf_op jit(solution)/shard_map/ppermute | solution.py:255
  31.0 18.0 %copy-start.5 = (s32[32]{0:T(128)}, s32[32]{0:T(128)S(1)}, u32[]{:S(2)}) copy-start(s32[32]{0:T(128)S(1)} %fusion.29.limit_ref) | copy-start | bytes 388
  44.1 7.5 %copy-start.2 = (bf16[256,4096]{1,0:T(8,128)(2,1)S(1)}, bf16[256,4096]{1,0:T(8,128)(2,1)}, u32[]{:S(2)}) copy-start(bf16[256,4096]{1,0:T(8,128)(2,1)} %all-gather.3.cloned.1.call-done) | copy-start | bytes 6291460
  44.1 7.5 %copy-start.6 = (bf16[4096,512]{1,0:T(8,128)(2,1)S(1)}, bf16[4096,512]{1,0:T(8,128)(2,1)}, u32[]{:S(2)}) copy-start(bf16[4096,512]{1,0:T(8,128)(2,1)} %param.20) | copy-start | bytes 12582916
  49.0 5.5 %collective-permute-start.7 = (bf16[256,128]{1,0:T(8,128)(2,1)S(1)}, bf16[256,128]{1,0:T(8,128)(2,1)S(1)}, u32[]{:S(2)}, u32[]{:S(2)}) collective-permute-start(bf16[256,128]{1,0:T(8,128)(2,1)S(1)} %get-tuple-element.19), channel_id=1, source_target_pairs={{1,3},{2,5},{3,7},{4,1},{5,2},{6,4},{7,6},{9,11},{10,13},{11,15},{... | collective-permute-start | bytes 196616 | tf_op jit(solution)/shard_map/ppermute | solution.py:305
  49.7 8.6 %collective-permute-start.6 = (bf16[256,128]{1,0:T(8,128)(2,1)S(1)}, bf16[256,128]{1,0:T(8,128)(2,1)S(1)}, u32[]{:S(2)}, u32[]{:S(2)}) collective-permute-start(bf16[256,128]{1,0:T(8,128)(2,1)S(1)} %get-tuple-element.19), channel_id=1, source_target_pairs={{0,1},{1,2},{2,4},{3,6},{4,0},{5,3},{6,5},{8,9},{9,10},{10,12},{11... | collective-permute-start | bytes 196616 | tf_op jit(solution)/shard_map/ppermute | solution.py:305
  60.2 54.0 %copy-start.3 = (bf16[256,512]{1,0:T(8,128)(2,1)S(1)}, bf16[256,512]{1,0:T(8,128)(2,1)}, u32[]{:S(2)}) copy-start(bf16[256,512]{1,0:T(8,128)(2,1)} %param.17) | copy-start | bytes 786436
  60.2 56.0 %copy-start.4 = (bf16[4096]{0:T(1024)(128)(2,1)S(1)}, bf16[4096]{0:T(1024)(128)(2,1)}, u32[]{:S(2)}) copy-start(bf16[4096]{0:T(1024)(128)(2,1)} %param.19) | copy-start | bytes 24580
  71.2 72.9 %all-gather.5.cloned.1.call-start = ((), (), s32[]{:S(2)}) async-start(), calls=%async_computation.4 | async-start | bytes 2359296 | tf_op jit(solution)/shard_map/all_gather | solution.py:344
  116.0 84.8 %reduce-scatter.5.cloned.1.call-start = ((), (), s32[]{:S(2)}) async-start(), calls=%async_computation.5 | async-start | bytes 2359296 | tf_op jit(solution)/shard_map/reduce_scatter | solution.py:345
  144.1 56.7 %copy-start.1 = (bf16[256,512]{1,0:T(8,128)(2,1)S(1)}, bf16[256,512]{1,0:T(8,128)(2,1)}, u32[]{:S(2)}) copy-start(bf16[256,512]{1,0:T(8,128)(2,1)} %add_convert_fusion.1) | copy-start | bytes 786436
Sparse Core Ops, SparseCore 0:
  9.6 31.7 all-gather.2
  71.3 42.8 reduce-scatter.2
  116.4 27.6 all-gather.4
  165.6 35.2 reduce-scatter.4

commit v15 on v14

--- a/solution.py
+++ b/solution.py
@@ -110,13 +110,8 @@
         summed = acc_scr[part, :] + jnp.dot(
             w.astype(jnp.bfloat16), nv_ref[...], preferred_element_type=jnp.float32
         )
-        head_out = (summed / total).astype(jnp.bfloat16)
-        term = jnp.dot(head_out, wo_ref[h * HD : (h + 1) * HD, :], preferred_element_type=jnp.float32)
-        if h == 0:
-            out_scr[...] = term
-        else:
-            out_scr[...] += term
-    o_ref[...] = out_scr[...].astype(o_ref.dtype)
+        out_scr[:, h * HD : (h + 1) * HD] = (summed / total).astype(out_scr.dtype)
+    o_ref[...] = jnp.dot(out_scr[...], wo_ref[...], preferred_element_type=jnp.float32).astype(o_ref.dtype)
 
 
 def local_attention(limit, span, q_rows, cache_all, new_keys, new_vals, w_out):
@@ -149,7 +144,7 @@
                 pltpu.VMEM((rows, BLK), jnp.float32),
                 pltpu.VMEM((rows, BLK), jnp.float32),
                 pltpu.VMEM((rows, HD), jnp.float32),
-                pltpu.VMEM((span_size, width), jnp.float32),
+                pltpu.VMEM((span_size, w_out.shape[0]), jnp.bfloat16),
                 pltpu.VMEM(w_out.shape, w_out.dtype),
                 pltpu.SemaphoreType.DMA(()),
             ],

time: 210 us -> 208 us (level)
  Pallas kernels: 32.3 us -> 30 us
    pallas_call x1, Pallas kernels: 10.9 us -> 8.67 us  [local_attention(): pl.pallas_call(attn_kernel, out_shape=jax.ShapeDtypeStruct((span_size, wi...]
where the time goes in v15:
time: 208 us
  waiting for transfers between devices  121 us (58%)
  Pallas kernels  30 us (14%)
  between operations  17.9 us (9%)
  other arithmetic  16.8 us (8%)
  starting transfers between devices  11.9 us (6%)
  local copies, waits for them, and re-layouts  6.6 us (3%)
  matrix products  3.89 us (2%)
    reduce_scatter x1, waiting for transfers between devices, per_device(): lax.psum_scatter(head_term, 'tp', scatter_dimension=1, tiled=True)  43.6 us
    reduce_scatter x1, waiting for transfers between devices, per_device(): lax.psum_scatter(feed_forward(full_mid, mlp_gain, w_gate, w_up, w_down),...  34.1 us
    all_gather x1, waiting for transfers between devices, per_device(): full_mid = lax.all_gather(mid, 'tp', axis=1, tiled=True)  27.3 us
    pallas_call x1, Pallas kernels, feed_forward(): pl.pallas_call(functools.partial(ffn_kernel, first, chunk), out_shape=jax...  21.3 us
    ppermute x6, waiting for transfers between devices, gather_ctx(): parts.append(lax.ppermute(value, 'ctx', pairs))  11 us
    ppermute x6, starting transfers between devices, gather_ctx(): parts.append(lax.ppermute(value, 'ctx', pairs))  8.95 us
    pallas_call x1, Pallas kernels, local_attention(): pl.pallas_call(attn_kernel, out_shape=jax.ShapeDtypeStruct((span_size, wi...  8.67 us
  transfers between devices with their start and end apart: 12, of which 5 were waited for; matrix products, arithmetic and copies ran while one was open for 8% of the time, Pallas kernels for 0%

profile of v15, /device:TPU:0, one launch (start us, length us, event | category | flops | bytes accessed | tf_op | source)
XLA Modules:
  0.0 207.7 jit_solution(2592507071215971131)
XLA Ops:
  7.2 0.7 all-gather.3.cloned.1.call-update
  7.9 0.0 reduce-scatter.3.cloned.1.call-start
  8.0 0.7 pad_add_fusion
  8.6 3.9 %collective-permute-start.2 = (s32[2,8]{1,0:T(2,128)S(1)}, s32[2,8]{1,0:T(2,128)S(1)}, u32[]{:S(2)}, u32[]{:S(2)}) collective-permute-start(s32[2,8]{1,0:T(2,128)S(1)} %pad_add_fusion), channel_id=1, source_target_pairs={{0,24},{8,0},{16,8},{24,16},{1,25},{9,1},{17,9},{25,17},{2,26},{10... | collective-permute-start | bytes 200 | tf_op jit(solution)/shard_map/ppermute | solution.py:250
  12.5 0.5 collective-permute-start.1
  13.0 0.6 collective-permute-start
  13.6 1.1 constant_dynamic-slice_fusion.1
  14.7 0.1 pad_maximum_fusion.1
  14.8 2.4 %collective-permute-start.5 = (bf16[8,128,256]{2,1,0:T(8,128)(2,1)S(1)}, bf16[8,128,256]{2,1,0:T(8,128)(2,1)S(1)}, u32[]{:S(2)}, u32[]{:S(2)}) collective-permute-start(bf16[8,128,256]{2,1,0:T(8,128)(2,1)S(1)} %pad_maximum_fusion.1), channel_id=1, source_target_pairs={{0,24},{8,0},{16,8},{24,16},{1,25},{9,1},{17,9},{25,17},{2,26},{10... | collective-permute-start | bytes 1572872 | tf_op jit(solution)/shard_map/ppermute | solution.py:250
  17.2 1.5 collective-permute-start.4
  18.7 1.2 dynamic_slice.38
  21.2 1.3 dynamic_slice.36
  23.8 1.2 dynamic_slice.32.span_ref
  25.0 1.2 dynamic_slice.33
  26.3 0.7 convert_element_type.77
  27.6 0.7 add_convert_fusion.3
  28.3 0.5 multiply_cosine_fusion.1
  29.5 0.1 collective-permute-start.3
  29.6 0.8 pad_add_fusion.1
  30.3 0.7 fusion.29.limit_ref
  31.0 0.7 fusion.28.bias_ref
  31.7 11.0 %collective-permute-done.3 = bf16[8,128,256]{2,1,0:T(8,128)(2,1)S(1)} collective-permute-done((bf16[8,128,256]{2,1,0:T(8,128)(2,1)S(1)}, bf16[8,128,256]{2,1,0:T(8,128)(2,1)S(1)}, u32[]{:S(2)}, u32[]{:S(2)}) %collective-permute-start.3) | collective-permute-done | bytes 524320 | tf_op jit(solution)/shard_map/ppermute | solution.py:250
  42.7 1.4 pad_maximum_fusion.cache_ref
  44.1 2.2 %fusion = f32[256]{0:T(256)S(1)} fusion(bf16[256,4096]{1,0:T(8,128)(2,1)} %all-gather.3.cloned.1.call-done), kind=kLoop, calls=%fused_computation.2 | loop fusion | flops 3145472 | bytes 2098176 | tf_op jit(solution)/shard_map/reduce_sum | solution.py:23
  46.4 2.6 %bitcast_convert_fusion = (f32[256,1,128]{2,0,1:T(8,128)S(1)}, bf16[256,128]{1,0:T(8,128)(2,1)S(1)}) fusion(bf16[4096,128]{1,0:T(8,128)(2,1)S(1)} %copy-done, bf16[256,4096]{1,0:T(8,128)(2,1)} %all-gather.3.cloned.1.call-done, f32[4096]{0:T(1024)S(1)} %convert_element_type.77, f32[256]{0:T(256)S(1)} %add_rsqrt_fusion), kind=kOutput, calls=%fused_computation.39 | convolution fusion | flops 272695296 | bytes 3359744 | tf_op jit(solution)/shard_map/dot_general | solution.py:296
  49.0 0.7 collective-permute-start.7
  49.7 2.0 collective-permute-start.6
  51.7 1.3 fusion.4
  53.0 0.2 reshape.210
  53.1 0.3 fusion.30
  53.5 0.1 subtract_convert_fusion
  53.6 0.9 pad_maximum_fusion.2
  54.5 3.7 %collective-permute-done.6 = bf16[256,128]{1,0:T(8,128)(2,1)S(1)} collective-permute-done((bf16[256,128]{1,0:T(8,128)(2,1)S(1)}, bf16[256,128]{1,0:T(8,128)(2,1)S(1)}, u32[]{:S(2)}, u32[]{:S(2)}) %collective-permute-start.6) | collective-permute-done | bytes 65568 | tf_op jit(solution)/shard_map/ppermute | solution.py:300
  58.3 0.7 dynamic-slice_bitcast_fusion
  58.9 0.6 fusion.25
  59.5 0.7 pad_maximum_fusion.4.nk_ref
  60.2 8.7 %shard_map.176 = bf16[256,4096]{1,0:T(8,128)(2,1)} custom-call(s32[32]{0:T(128)} %copy-done.5, s32[1]{0:T(128)} %dynamic_slice.32.span_ref, bf16[1024,128]{1,0:T(8,128)(2,1)} %bitcast.37, bf16[32,128,256]{2,1,0:T(8,128)(2,1)} %pad_maximum_fusion.cache_ref, f32[32,128]{1,0:T(8,128)} %fusion.28.bias_ref, bf16[256,128]{1,0:T(8,128)(2,1)} %pad_maximum_fusion.4.nk_ref, ...), custom_call_target="tpu_custom_call" | custom-call | tf_op jit(solution)/shard_map/pallas_call | solution.py:128
  68.9 0.0 all-gather.5.cloned.1.call-start
  69.0 43.6 %reduce-scatter.3.cloned.1.call-done = bf16[256,512]{1,0:T(8,128)(2,1)} async-done(((bf16[256,4096]{1,0:T(8,128)(2,1)}), bf16[256,512]{1,0:T(8,128)(2,1)}) %reduce-scatter.3.cloned.1.call-update) | async-done | bytes 262160 | tf_op jit(solution)/shard_map/reduce_scatter | solution.py:337
  112.6 1.7 add_convert_fusion.1
  114.4 0.2 reduce-scatter.5.cloned.1.call-start
  114.6 0.6 reshape.216
  115.2 27.3 %all-gather.5.cloned.1.call-done.x_ref = bf16[256,4096]{1,0:T(8,128)(2,1)} async-done(((bf16[256,512]{1,0:T(8,128)(2,1)}), bf16[256,4096]{1,0:T(8,128)(2,1)}) %all-gather.5.cloned.1.call-update) | async-done | bytes 2097168 | tf_op jit(solution)/shard_map/all_gather | solution.py:339
  142.6 21.3 %shard_map.177 = bf16[256,4096]{1,0:T(8,128)(2,1)} custom-call(bf16[256,4096]{1,0:T(8,128)(2,1)} %all-gather.5.cloned.1.call-done.x_ref, f32[1,4096]{1,0:T(1,128)} %bitcast.39, bf16[1376,4096]{1,0:T(8,128)(2,1)} %bitcast.35, bf16[1376,4096]{1,0:T(8,128)(2,1)} %bitcast.36, bf16[1376,4096]{1,0:T(8,128)(2,1)} %wd_ref.1), custom_call_target="tpu_custom_call" | custom-call | tf_op jit(solution)/shard_map/pallas_call | solution.py:193
  163.9 0.6 iota_compare_fusion.1
  164.5 0.8 fusion.23
  165.3 34.1 %reduce-scatter.5.cloned.1.call-done = bf16[256,512]{1,0:T(8,128)(2,1)} async-done(((bf16[256,4096]{1,0:T(8,128)(2,1)}), bf16[256,512]{1,0:T(8,128)(2,1)}) %reduce-scatter.5.cloned.1.call-update) | async-done | bytes 262160 | tf_op jit(solution)/shard_map/reduce_scatter | solution.py:340
  199.4 1.8 fusion.6
  (28 shorter events, 0.2 us)
Async XLA Ops:
  7.2 39.2 %copy-start = (bf16[4096,128]{1,0:T(8,128)(2,1)S(1)}, bf16[4096,128]{1,0:T(8,128)(2,1)}, u32[]{:S(2)}) copy-start(bf16[4096,128]{1,0:T(8,128)(2,1)} %param.21) | copy-start | bytes 3145732
  7.2 36.9 %all-gather.3.cloned.1.call-start = ((), (), s32[]{:S(2)}) async-start(), calls=%async_computation.2 | async-start | bytes 2359296 | tf_op jit(solution)/shard_map/all_gather | solution.py:294
  7.9 104.7 %reduce-scatter.3.cloned.1.call-start = ((), (), s32[]{:S(2)}) async-start(), calls=%async_computation.3 | async-start | bytes 2359296 | tf_op jit(solution)/shard_map/reduce_scatter | solution.py:337
  8.6 20.8 %collective-permute-start.2 = (s32[2,8]{1,0:T(2,128)S(1)}, s32[2,8]{1,0:T(2,128)S(1)}, u32[]{:S(2)}, u32[]{:S(2)}) collective-permute-start(s32[2,8]{1,0:T(2,128)S(1)} %pad_add_fusion), channel_id=1, source_target_pairs={{0,24},{8,0},{16,8},{24,16},{1,25},{9,1},{17,9},{25,17},{2,26},{10... | collective-permute-start | bytes 200 | tf_op jit(solution)/shard_map/ppermute | solution.py:250
  12.5 17.0 %collective-permute-start.1 = (s32[2,8]{1,0:T(2,128)S(1)}, s32[2,8]{1,0:T(2,128)S(1)}, u32[]{:S(2)}, u32[]{:S(2)}) collective-permute-start(s32[2,8]{1,0:T(2,128)S(1)} %pad_add_fusion), channel_id=1, source_target_pairs={{0,16},{8,24},{16,0},{24,8},{1,17},{9,25},{17,1},{25,9},{2,18},{10... | collective-permute-start | bytes 200 | tf_op jit(solution)/shard_map/ppermute | solution.py:250
  13.0 16.5 %collective-permute-start = (s32[2,8]{1,0:T(2,128)S(1)}, s32[2,8]{1,0:T(2,128)S(1)}, u32[]{:S(2)}, u32[]{:S(2)}) collective-permute-start(s32[2,8]{1,0:T(2,128)S(1)} %pad_add_fusion), channel_id=1, source_target_pairs={{0,8},{8,16},{16,24},{24,0},{1,9},{9,17},{17,25},{25,1},{2,10},{10... | collective-permute-start | bytes 200 | tf_op jit(solution)/shard_map/ppermute | solution.py:250
  14.8 16.9 %collective-permute-start.5 = (bf16[8,128,256]{2,1,0:T(8,128)(2,1)S(1)}, bf16[8,128,256]{2,1,0:T(8,128)(2,1)S(1)}, u32[]{:S(2)}, u32[]{:S(2)}) collective-permute-start(bf16[8,128,256]{2,1,0:T(8,128)(2,1)S(1)} %pad_maximum_fusion.1), channel_id=1, source_target_pairs={{0,24},{8,0},{16,8},{24,16},{1,25},{9,1},{17,9},{25,17},{2,26},{10... | collective-permute-start | bytes 1572872 | tf_op jit(solution)/shard_map/ppermute | solution.py:250
  17.2 14.5 %collective-permute-start.4 = (bf16[8,128,256]{2,1,0:T(8,128)(2,1)S(1)}, bf16[8,128,256]{2,1,0:T(8,128)(2,1)S(1)}, u32[]{:S(2)}, u32[]{:S(2)}) collective-permute-start(bf16[8,128,256]{2,1,0:T(8,128)(2,1)S(1)} %pad_maximum_fusion.1), channel_id=1, source_target_pairs={{0,16},{8,24},{16,0},{24,8},{1,17},{9,25},{17,1},{25,9},{2,18},{10... | collective-permute-start | bytes 1572872 | tf_op jit(solution)/shard_map/ppermute | solution.py:250
  29.5 13.2 %collective-permute-start.3 = (bf16[8,128,256]{2,1,0:T(8,128)(2,1)S(1)}, bf16[8,128,256]{2,1,0:T(8,128)(2,1)S(1)}, u32[]{:S(2)}, u32[]{:S(2)}) collective-permute-start(bf16[8,128,256]{2,1,0:T(8,128)(2,1)S(1)} %pad_maximum_fusion.1), channel_id=1, source_target_pairs={{0,8},{8,16},{16,24},{24,0},{1,9},{9,17},{17,25},{25,1},{2,10},{10... | collective-permute-start | bytes 1572872 | tf_op jit(solution)/shard_map/ppermute | solution.py:250
  31.0 18.0 %copy-start.5 = (s32[32]{0:T(128)}, s32[32]{0:T(128)S(1)}, u32[]{:S(2)}) copy-start(s32[32]{0:T(128)S(1)} %fusion.29.limit_ref) | copy-start | bytes 388
  44.1 7.5 %copy-start.2 = (bf16[256,4096]{1,0:T(8,128)(2,1)S(1)}, bf16[256,4096]{1,0:T(8,128)(2,1)}, u32[]{:S(2)}) copy-start(bf16[256,4096]{1,0:T(8,128)(2,1)} %all-gather.3.cloned.1.call-done) | copy-start | bytes 6291460
  44.1 7.5 %copy-start.6 = (bf16[4096,512]{1,0:T(8,128)(2,1)S(1)}, bf16[4096,512]{1,0:T(8,128)(2,1)}, u32[]{:S(2)}) copy-start(bf16[4096,512]{1,0:T(8,128)(2,1)} %param.20) | copy-start | bytes 12582916
  49.0 5.5 %collective-permute-start.7 = (bf16[256,128]{1,0:T(8,128)(2,1)S(1)}, bf16[256,128]{1,0:T(8,128)(2,1)S(1)}, u32[]{:S(2)}, u32[]{:S(2)}) collective-permute-start(bf16[256,128]{1,0:T(8,128)(2,1)S(1)} %get-tuple-element.19), channel_id=1, source_target_pairs={{1,3},{2,5},{3,7},{4,1},{5,2},{6,4},{7,6},{9,11},{10,13},{11,15},{... | collective-permute-start | bytes 196616 | tf_op jit(solution)/shard_map/ppermute | solution.py:300
  49.7 8.6 %collective-permute-start.6 = (bf16[256,128]{1,0:T(8,128)(2,1)S(1)}, bf16[256,128]{1,0:T(8,128)(2,1)S(1)}, u32[]{:S(2)}, u32[]{:S(2)}) collective-permute-start(bf16[256,128]{1,0:T(8,128)(2,1)S(1)} %get-tuple-element.19), channel_id=1, source_target_pairs={{0,1},{1,2},{2,4},{3,6},{4,0},{5,3},{6,5},{8,9},{9,10},{10,12},{11... | collective-permute-start | bytes 196616 | tf_op jit(solution)/shard_map/ppermute | solution.py:300
  60.2 52.4 %copy-start.3 = (bf16[256,512]{1,0:T(8,128)(2,1)S(1)}, bf16[256,512]{1,0:T(8,128)(2,1)}, u32[]{:S(2)}) copy-start(bf16[256,512]{1,0:T(8,128)(2,1)} %param.17) | copy-start | bytes 786436
  60.2 54.4 %copy-start.4 = (bf16[4096]{0:T(1024)(128)(2,1)S(1)}, bf16[4096]{0:T(1024)(128)(2,1)}, u32[]{:S(2)}) copy-start(bf16[4096]{0:T(1024)(128)(2,1)} %param.19) | copy-start | bytes 24580
  68.9 73.6 %all-gather.5.cloned.1.call-start = ((), (), s32[]{:S(2)}) async-start(), calls=%async_computation.4 | async-start | bytes 2359296 | tf_op jit(solution)/shard_map/all_gather | solution.py:339
  114.4 85.0 %reduce-scatter.5.cloned.1.call-start = ((), (), s32[]{:S(2)}) async-start(), calls=%async_computation.5 | async-start | bytes 2359296 | tf_op jit(solution)/shard_map/reduce_scatter | solution.py:340
  142.6 56.8 %copy-start.1 = (bf16[256,512]{1,0:T(8,128)(2,1)S(1)}, bf16[256,512]{1,0:T(8,128)(2,1)}, u32[]{:S(2)}) copy-start(bf16[256,512]{1,0:T(8,128)(2,1)} %add_convert_fusion.1) | copy-start | bytes 786436
Sparse Core Ops, SparseCore 0:
  9.6 31.7 all-gather.2
  69.1 43.5 reduce-scatter.2
  114.8 27.7 all-gather.4
  164.1 35.2 reduce-scatter.4

commit v16 on v15

--- a/solution.py
+++ b/solution.py
@@ -187,8 +187,9 @@
     rows, width = full_mid.shape
     units = w_gate.shape[1]
     chunk = 1024 if width % 1024 == 0 else width
+    out_chunk = 2048 if w_down.shape[1] % 2048 == 0 else w_down.shape[1]
     first = width // chunk
-    outs = w_down.shape[1] // chunk
+    outs = w_down.shape[1] // out_chunk
     last = first - 1
     return pl.pallas_call(
         functools.partial(ffn_kernel, first, chunk),
@@ -199,9 +200,9 @@
             pl.BlockSpec((1, width), lambda i: (0, 0)),
             pl.BlockSpec((units, chunk), lambda i: (0, jnp.minimum(i, last))),
             pl.BlockSpec((units, chunk), lambda i: (0, jnp.minimum(i, last))),
-            pl.BlockSpec((units, chunk), lambda i: (0, jnp.maximum(i - first, 0))),
+            pl.BlockSpec((units, out_chunk), lambda i: (0, jnp.maximum(i - first, 0))),
         ],
-        out_specs=pl.BlockSpec((rows, chunk), lambda i: (0, jnp.maximum(i - first, 0))),
+        out_specs=pl.BlockSpec((rows, out_chunk), lambda i: (0, jnp.maximum(i - first, 0))),
         scratch_shapes=[
             pltpu.VMEM((rows, 1), jnp.float32),
             pltpu.VMEM((rows, units), jnp.float32),

time: 208 us -> 208 us (level)
  no operation moved by 1% of the time
where the time goes in v16:
time: 208 us; the launch traced here: 207 us
  waiting for transfers between devices  120 us (58%)
  Pallas kernels  30.2 us (15%)
  between operations  17.9 us (9%)
  other arithmetic  16.8 us (8%)
  starting transfers between devices  11.9 us (6%)
  local copies, waits for them, and re-layouts  6.6 us (3%)
  matrix products  3.89 us (2%)
    reduce_scatter x1, waiting for transfers between devices, per_device(): lax.psum_scatter(head_term, 'tp', scatter_dimension=1, tiled=True)  43 us
    reduce_scatter x1, waiting for transfers between devices, per_device(): lax.psum_scatter(feed_forward(full_mid, mlp_gain, w_gate, w_up, w_down),...  34.1 us
    all_gather x1, waiting for transfers between devices, per_device(): full_mid = lax.all_gather(mid, 'tp', axis=1, tiled=True)  27.3 us
    pallas_call x1, Pallas kernels, feed_forward(): pl.pallas_call(functools.partial(ffn_kernel, first, chunk), out_shape=jax...  20.8 us
    ppermute x6, waiting for transfers between devices, gather_ctx(): parts.append(lax.ppermute(value, 'ctx', pairs))  11 us
    pallas_call x1, Pallas kernels, local_attention(): pl.pallas_call(attn_kernel, out_shape=jax.ShapeDtypeStruct((span_size, wi...  9.31 us
    ppermute x6, starting transfers between devices, gather_ctx(): parts.append(lax.ppermute(value, 'ctx', pairs))  8.95 us
  transfers between devices with their start and end apart: 12, of which 5 were waited for; matrix products, arithmetic and copies ran while one was open for 8% of the time, Pallas kernels for 0%

profile of v16, /device:TPU:0, one launch (start us, length us, event | category | flops | bytes accessed | tf_op | source)
XLA Modules:
  0.0 207.2 jit_solution(2992163714107839611)
XLA Ops:
  7.2 0.7 all-gather.3.cloned.1.call-update
  7.9 0.0 reduce-scatter.3.cloned.1.call-start
  8.0 0.7 pad_add_fusion
  8.6 3.9 %collective-permute-start.2 = (s32[2,8]{1,0:T(2,128)S(1)}, s32[2,8]{1,0:T(2,128)S(1)}, u32[]{:S(2)}, u32[]{:S(2)}) collective-permute-start(s32[2,8]{1,0:T(2,128)S(1)} %pad_add_fusion), channel_id=1, source_target_pairs={{0,24},{8,0},{16,8},{24,16},{1,25},{9,1},{17,9},{25,17},{2,26},{10... | collective-permute-start | bytes 200 | tf_op jit(solution)/shard_map/ppermute | solution.py:251
  12.5 0.5 collective-permute-start.1
  13.0 0.6 collective-permute-start
  13.6 1.1 constant_dynamic-slice_fusion.1
  14.7 0.1 pad_maximum_fusion.1
  14.8 2.4 %collective-permute-start.5 = (bf16[8,128,256]{2,1,0:T(8,128)(2,1)S(1)}, bf16[8,128,256]{2,1,0:T(8,128)(2,1)S(1)}, u32[]{:S(2)}, u32[]{:S(2)}) collective-permute-start(bf16[8,128,256]{2,1,0:T(8,128)(2,1)S(1)} %pad_maximum_fusion.1), channel_id=1, source_target_pairs={{0,24},{8,0},{16,8},{24,16},{1,25},{9,1},{17,9},{25,17},{2,26},{10... | collective-permute-start | bytes 1572872 | tf_op jit(solution)/shard_map/ppermute | solution.py:251
  17.2 1.5 collective-permute-start.4
  18.7 1.2 dynamic_slice.38
  21.2 1.3 dynamic_slice.36
  23.8 1.2 dynamic_slice.32.span_ref
  25.0 1.2 dynamic_slice.33
  26.3 0.7 convert_element_type.77
  27.6 0.7 add_convert_fusion.3
  28.3 0.5 multiply_cosine_fusion.1
  29.5 0.1 collective-permute-start.3
  29.6 0.8 pad_add_fusion.1
  30.3 0.7 fusion.29.limit_ref
  31.0 0.7 fusion.28.bias_ref
  31.7 11.0 %collective-permute-done.3 = bf16[8,128,256]{2,1,0:T(8,128)(2,1)S(1)} collective-permute-done((bf16[8,128,256]{2,1,0:T(8,128)(2,1)S(1)}, bf16[8,128,256]{2,1,0:T(8,128)(2,1)S(1)}, u32[]{:S(2)}, u32[]{:S(2)}) %collective-permute-start.3) | collective-permute-done | bytes 524320 | tf_op jit(solution)/shard_map/ppermute | solution.py:251
  42.7 1.4 pad_maximum_fusion.cache_ref
  44.1 2.2 %fusion = f32[256]{0:T(256)S(1)} fusion(bf16[256,4096]{1,0:T(8,128)(2,1)} %all-gather.3.cloned.1.call-done), kind=kLoop, calls=%fused_computation.2 | loop fusion | flops 3145472 | bytes 2098176 | tf_op jit(solution)/shard_map/reduce_sum | solution.py:23
  46.4 2.6 %bitcast_convert_fusion = (f32[256,1,128]{2,0,1:T(8,128)S(1)}, bf16[256,128]{1,0:T(8,128)(2,1)S(1)}) fusion(bf16[4096,128]{1,0:T(8,128)(2,1)S(1)} %copy-done, bf16[256,4096]{1,0:T(8,128)(2,1)} %all-gather.3.cloned.1.call-done, f32[4096]{0:T(1024)S(1)} %convert_element_type.77, f32[256]{0:T(256)S(1)} %add_rsqrt_fusion), kind=kOutput, calls=%fused_computation.39 | convolution fusion | flops 272695296 | bytes 3359744 | tf_op jit(solution)/shard_map/dot_general | solution.py:297
  49.0 0.7 collective-permute-start.7
  49.7 2.0 collective-permute-start.6
  51.7 1.3 fusion.4
  53.0 0.2 reshape.210
  53.1 0.3 fusion.30
  53.5 0.1 subtract_convert_fusion
  53.6 0.9 pad_maximum_fusion.2
  54.5 3.7 %collective-permute-done.6 = bf16[256,128]{1,0:T(8,128)(2,1)S(1)} collective-permute-done((bf16[256,128]{1,0:T(8,128)(2,1)S(1)}, bf16[256,128]{1,0:T(8,128)(2,1)S(1)}, u32[]{:S(2)}, u32[]{:S(2)}) %collective-permute-start.6) | collective-permute-done | bytes 65568 | tf_op jit(solution)/shard_map/ppermute | solution.py:301
  58.3 0.7 dynamic-slice_bitcast_fusion
  58.9 0.6 fusion.25
  59.5 0.7 pad_maximum_fusion.4.nk_ref
  60.2 9.3 %shard_map.176 = bf16[256,4096]{1,0:T(8,128)(2,1)} custom-call(s32[32]{0:T(128)} %copy-done.5, s32[1]{0:T(128)} %dynamic_slice.32.span_ref, bf16[1024,128]{1,0:T(8,128)(2,1)} %bitcast.37, bf16[32,128,256]{2,1,0:T(8,128)(2,1)} %pad_maximum_fusion.cache_ref, f32[32,128]{1,0:T(8,128)} %fusion.28.bias_ref, bf16[256,128]{1,0:T(8,128)(2,1)} %pad_maximum_fusion.4.nk_ref, ...), custom_call_target="tpu_custom_call" | custom-call | tf_op jit(solution)/shard_map/pallas_call | solution.py:128
  69.6 0.0 all-gather.5.cloned.1.call-start
  69.6 43.0 %reduce-scatter.3.cloned.1.call-done = bf16[256,512]{1,0:T(8,128)(2,1)} async-done(((bf16[256,4096]{1,0:T(8,128)(2,1)}), bf16[256,512]{1,0:T(8,128)(2,1)}) %reduce-scatter.3.cloned.1.call-update) | async-done | bytes 262160 | tf_op jit(solution)/shard_map/reduce_scatter | solution.py:338
  112.6 1.7 add_convert_fusion.1
  114.4 0.2 reduce-scatter.5.cloned.1.call-start
  114.6 0.6 reshape.216
  115.2 27.3 %all-gather.5.cloned.1.call-done.x_ref = bf16[256,4096]{1,0:T(8,128)(2,1)} async-done(((bf16[256,512]{1,0:T(8,128)(2,1)}), bf16[256,4096]{1,0:T(8,128)(2,1)}) %all-gather.5.cloned.1.call-update) | async-done | bytes 2097168 | tf_op jit(solution)/shard_map/all_gather | solution.py:340
  142.6 20.8 %shard_map.177 = bf16[256,4096]{1,0:T(8,128)(2,1)} custom-call(bf16[256,4096]{1,0:T(8,128)(2,1)} %all-gather.5.cloned.1.call-done.x_ref, f32[1,4096]{1,0:T(1,128)} %bitcast.39, bf16[1376,4096]{1,0:T(8,128)(2,1)} %bitcast.35, bf16[1376,4096]{1,0:T(8,128)(2,1)} %bitcast.36, bf16[1376,4096]{1,0:T(8,128)(2,1)} %wd_ref.1), custom_call_target="tpu_custom_call" | custom-call | tf_op jit(solution)/shard_map/pallas_call | solution.py:194
  163.4 0.6 iota_compare_fusion.1
  164.0 0.8 fusion.23
  164.8 34.1 %reduce-scatter.5.cloned.1.call-done = bf16[256,512]{1,0:T(8,128)(2,1)} async-done(((bf16[256,4096]{1,0:T(8,128)(2,1)}), bf16[256,512]{1,0:T(8,128)(2,1)}) %reduce-scatter.5.cloned.1.call-update) | async-done | bytes 262160 | tf_op jit(solution)/shard_map/reduce_scatter | solution.py:341
  198.9 1.8 fusion.6
  (28 shorter events, 0.2 us)
Async XLA Ops:
  7.2 39.2 %copy-start = (bf16[4096,128]{1,0:T(8,128)(2,1)S(1)}, bf16[4096,128]{1,0:T(8,128)(2,1)}, u32[]{:S(2)}) copy-start(bf16[4096,128]{1,0:T(8,128)(2,1)} %param.21) | copy-start | bytes 3145732
  7.2 36.9 %all-gather.3.cloned.1.call-start = ((), (), s32[]{:S(2)}) async-start(), calls=%async_computation.2 | async-start | bytes 2359296 | tf_op jit(solution)/shard_map/all_gather | solution.py:295
  7.9 104.7 %reduce-scatter.3.cloned.1.call-start = ((), (), s32[]{:S(2)}) async-start(), calls=%async_computation.3 | async-start | bytes 2359296 | tf_op jit(solution)/shard_map/reduce_scatter | solution.py:338
  8.6 20.8 %collective-permute-start.2 = (s32[2,8]{1,0:T(2,128)S(1)}, s32[2,8]{1,0:T(2,128)S(1)}, u32[]{:S(2)}, u32[]{:S(2)}) collective-permute-start(s32[2,8]{1,0:T(2,128)S(1)} %pad_add_fusion), channel_id=1, source_target_pairs={{0,24},{8,0},{16,8},{24,16},{1,25},{9,1},{17,9},{25,17},{2,26},{10... | collective-permute-start | bytes 200 | tf_op jit(solution)/shard_map/ppermute | solution.py:251
  12.5 17.0 %collective-permute-start.1 = (s32[2,8]{1,0:T(2,128)S(1)}, s32[2,8]{1,0:T(2,128)S(1)}, u32[]{:S(2)}, u32[]{:S(2)}) collective-permute-start(s32[2,8]{1,0:T(2,128)S(1)} %pad_add_fusion), channel_id=1, source_target_pairs={{0,16},{8,24},{16,0},{24,8},{1,17},{9,25},{17,1},{25,9},{2,18},{10... | collective-permute-start | bytes 200 | tf_op jit(solution)/shard_map/ppermute | solution.py:251
  13.0 16.5 %collective-permute-start = (s32[2,8]{1,0:T(2,128)S(1)}, s32[2,8]{1,0:T(2,128)S(1)}, u32[]{:S(2)}, u32[]{:S(2)}) collective-permute-start(s32[2,8]{1,0:T(2,128)S(1)} %pad_add_fusion), channel_id=1, source_target_pairs={{0,8},{8,16},{16,24},{24,0},{1,9},{9,17},{17,25},{25,1},{2,10},{10... | collective-permute-start | bytes 200 | tf_op jit(solution)/shard_map/ppermute | solution.py:251
  14.8 16.9 %collective-permute-start.5 = (bf16[8,128,256]{2,1,0:T(8,128)(2,1)S(1)}, bf16[8,128,256]{2,1,0:T(8,128)(2,1)S(1)}, u32[]{:S(2)}, u32[]{:S(2)}) collective-permute-start(bf16[8,128,256]{2,1,0:T(8,128)(2,1)S(1)} %pad_maximum_fusion.1), channel_id=1, source_target_pairs={{0,24},{8,0},{16,8},{24,16},{1,25},{9,1},{17,9},{25,17},{2,26},{10... | collective-permute-start | bytes 1572872 | tf_op jit(solution)/shard_map/ppermute | solution.py:251
  17.2 14.5 %collective-permute-start.4 = (bf16[8,128,256]{2,1,0:T(8,128)(2,1)S(1)}, bf16[8,128,256]{2,1,0:T(8,128)(2,1)S(1)}, u32[]{:S(2)}, u32[]{:S(2)}) collective-permute-start(bf16[8,128,256]{2,1,0:T(8,128)(2,1)S(1)} %pad_maximum_fusion.1), channel_id=1, source_target_pairs={{0,16},{8,24},{16,0},{24,8},{1,17},{9,25},{17,1},{25,9},{2,18},{10... | collective-permute-start | bytes 1572872 | tf_op jit(solution)/shard_map/ppermute | solution.py:251
  29.5 13.2 %collective-permute-start.3 = (bf16[8,128,256]{2,1,0:T(8,128)(2,1)S(1)}, bf16[8,128,256]{2,1,0:T(8,128)(2,1)S(1)}, u32[]{:S(2)}, u32[]{:S(2)}) collective-permute-start(bf16[8,128,256]{2,1,0:T(8,128)(2,1)S(1)} %pad_maximum_fusion.1), channel_id=1, source_target_pairs={{0,8},{8,16},{16,24},{24,0},{1,9},{9,17},{17,25},{25,1},{2,10},{10... | collective-permute-start | bytes 1572872 | tf_op jit(solution)/shard_map/ppermute | solution.py:251
  31.0 18.0 %copy-start.5 = (s32[32]{0:T(128)}, s32[32]{0:T(128)S(1)}, u32[]{:S(2)}) copy-start(s32[32]{0:T(128)S(1)} %fusion.29.limit_ref) | copy-start | bytes 388
  44.1 7.5 %copy-start.2 = (bf16[256,4096]{1,0:T(8,128)(2,1)S(1)}, bf16[256,4096]{1,0:T(8,128)(2,1)}, u32[]{:S(2)}) copy-start(bf16[256,4096]{1,0:T(8,128)(2,1)} %all-gather.3.cloned.1.call-done) | copy-start | bytes 6291460
  44.1 7.5 %copy-start.6 = (bf16[4096,512]{1,0:T(8,128)(2,1)S(1)}, bf16[4096,512]{1,0:T(8,128)(2,1)}, u32[]{:S(2)}) copy-start(bf16[4096,512]{1,0:T(8,128)(2,1)} %param.20) | copy-start | bytes 12582916
  49.0 5.5 %collective-permute-start.7 = (bf16[256,128]{1,0:T(8,128)(2,1)S(1)}, bf16[256,128]{1,0:T(8,128)(2,1)S(1)}, u32[]{:S(2)}, u32[]{:S(2)}) collective-permute-start(bf16[256,128]{1,0:T(8,128)(2,1)S(1)} %get-tuple-element.19), channel_id=1, source_target_pairs={{1,3},{2,5},{3,7},{4,1},{5,2},{6,4},{7,6},{9,11},{10,13},{11,15},{... | collective-permute-start | bytes 196616 | tf_op jit(solution)/shard_map/ppermute | solution.py:301
  49.7 8.6 %collective-permute-start.6 = (bf16[256,128]{1,0:T(8,128)(2,1)S(1)}, bf16[256,128]{1,0:T(8,128)(2,1)S(1)}, u32[]{:S(2)}, u32[]{:S(2)}) collective-permute-start(bf16[256,128]{1,0:T(8,128)(2,1)S(1)} %get-tuple-element.19), channel_id=1, source_target_pairs={{0,1},{1,2},{2,4},{3,6},{4,0},{5,3},{6,5},{8,9},{9,10},{10,12},{11... | collective-permute-start | bytes 196616 | tf_op jit(solution)/shard_map/ppermute | solution.py:301
  60.2 52.4 %copy-start.3 = (bf16[256,512]{1,0:T(8,128)(2,1)S(1)}, bf16[256,512]{1,0:T(8,128)(2,1)}, u32[]{:S(2)}) copy-start(bf16[256,512]{1,0:T(8,128)(2,1)} %param.17) | copy-start | bytes 786436
  60.2 54.4 %copy-start.4 = (bf16[4096]{0:T(1024)(128)(2,1)S(1)}, bf16[4096]{0:T(1024)(128)(2,1)}, u32[]{:S(2)}) copy-start(bf16[4096]{0:T(1024)(128)(2,1)} %param.19) | copy-start | bytes 24580
  69.6 73.0 %all-gather.5.cloned.1.call-start = ((), (), s32[]{:S(2)}) async-start(), calls=%async_computation.4 | async-start | bytes 2359296 | tf_op jit(solution)/shard_map/all_gather | solution.py:340
  114.4 84.5 %reduce-scatter.5.cloned.1.call-start = ((), (), s32[]{:S(2)}) async-start(), calls=%async_computation.5 | async-start | bytes 2359296 | tf_op jit(solution)/shard_map/reduce_scatter | solution.py:341
  142.6 56.3 %copy-start.1 = (bf16[256,512]{1,0:T(8,128)(2,1)S(1)}, bf16[256,512]{1,0:T(8,128)(2,1)}, u32[]{:S(2)}) copy-start(bf16[256,512]{1,0:T(8,128)(2,1)} %add_convert_fusion.1) | copy-start | bytes 786436
Sparse Core Ops, SparseCore 0:
  9.6 31.7 all-gather.2
  69.7 42.8 reduce-scatter.2
  114.8 27.7 all-gather.4
  163.6 35.2 reduce-scatter.4

commit v17 on v16

--- a/solution.py
+++ b/solution.py
@@ -45,13 +45,15 @@
 
 
 def attn_kernel(
-    limit_ref, span_ref, q_ref, cache_ref, bias_ref, nk_ref, nv_ref, wo_hbm, o_ref,
-    top_scr, tot_scr, acc_scr, out_scr, wo_ref, wo_sem
+    limit_ref, span_ref, q_ref, cache_hbm, bias_ref, nk_ref, nv_ref, wo_hbm, o_ref,
+    top_scr, tot_scr, acc_scr, out_scr, wo_ref, wo_sem, cache_ref, cache_sem
 ):
     slots = cache_ref.shape[0]
     span_size = nk_ref.shape[0]
     heads = q_ref.shape[0] // span_size
     scale = HD ** (-0.5)
+    cache_copy = pltpu.make_async_copy(cache_hbm, cache_ref, cache_sem)
+    cache_copy.start()
     wo_copy = pltpu.make_async_copy(wo_hbm, wo_ref, wo_sem)
     wo_copy.start()
     q_all = q_ref[...]
@@ -67,7 +69,11 @@
         rows = q_ref[h * span_size : (h + 1) * span_size, :]
         return lax.dot_general(rows, nk_ref[...], dims, preferred_element_type=jnp.float32)
 
+    new_tops = [
+        jnp.max(jnp.where(new_ok, new_raw(h), NEG), axis=1, keepdims=True) for h in range(heads)
+    ]
     top_scr[...] = jnp.full(top_scr.shape, NEG, jnp.float32)
+    cache_copy.wait()
 
     def max_step(s, carry):
         @pl.when(limit_ref[s] > 0)
@@ -80,10 +86,7 @@
     peaks = []
     for h in range(heads):
         part = slice(h * span_size, (h + 1) * span_size)
-        raw_top = jnp.maximum(
-            jnp.max(top_scr[part, :], axis=1, keepdims=True),
-            jnp.max(jnp.where(new_ok, new_raw(h), NEG), axis=1, keepdims=True),
-        )
+        raw_top = jnp.maximum(jnp.max(top_scr[part, :], axis=1, keepdims=True), new_tops[h])
         peaks.append(raw_top * scale)
     peak = jnp.concatenate(peaks, axis=0)
 
@@ -133,7 +136,7 @@
             grid=(1,),
             in_specs=[
                 whole(q_rows.shape),
-                whole(cache_all.shape),
+                pl.BlockSpec(memory_space=pl.ANY),
                 whole(bias.shape),
                 whole(new_keys.shape),
                 whole(new_vals.shape),
@@ -146,6 +149,8 @@
                 pltpu.VMEM((rows, HD), jnp.float32),
                 pltpu.VMEM((span_size, w_out.shape[0]), jnp.bfloat16),
                 pltpu.VMEM(w_out.shape, w_out.dtype),
+                pltpu.SemaphoreType.DMA(()),
+                pltpu.VMEM(cache_all.shape, cache_all.dtype),
                 pltpu.SemaphoreType.DMA(()),
             ],
         ),

time: 208 us -> 209 us (level)
  no operation moved by 1% of the time
where the time goes in v17:
time: 209 us; the launch traced here: 208 us
  waiting for transfers between devices  120 us (57%)
  Pallas kernels  31.4 us (15%)
  between operations  17.9 us (9%)
  other arithmetic  16.8 us (8%)
  starting transfers between devices  11.9 us (6%)
  local copies, waits for them, and re-layouts  6.6 us (3%)
  matrix products  3.89 us (2%)
    reduce_scatter x1, waiting for transfers between devices, per_device(): lax.psum_scatter(head_term, 'tp', scatter_dimension=1, tiled=True)  43 us
    reduce_scatter x1, waiting for transfers between devices, per_device(): lax.psum_scatter(feed_forward(full_mid, mlp_gain, w_gate, w_up, w_down),...  34 us
    all_gather x1, waiting for transfers between devices, per_device(): full_mid = lax.all_gather(mid, 'tp', axis=1, tiled=True)  27.4 us
    pallas_call x1, Pallas kernels, feed_forward(): pl.pallas_call(functools.partial(ffn_kernel, first, chunk), out_shape=jax...  20.8 us
    ppermute x6, waiting for transfers between devices, gather_ctx(): parts.append(lax.ppermute(value, 'ctx', pairs))  11 us
    pallas_call x1, Pallas kernels, local_attention(): pl.pallas_call(attn_kernel, out_shape=jax.ShapeDtypeStruct((span_size, wi...  10.5 us
    ppermute x6, starting transfers between devices, gather_ctx(): parts.append(lax.ppermute(value, 'ctx', pairs))  8.95 us
  transfers between devices with their start and end apart: 12, of which 5 were waited for; matrix products, arithmetic and copies ran while one was open for 8% of the time, Pallas kernels for 0%

profile of v17, /device:TPU:0, one launch (start us, length us, event | category | flops | bytes accessed | tf_op | source)
XLA Modules:
  0.0 208.4 jit_solution(15925070573894204568)
XLA Ops:
  7.2 0.7 all-gather.3.cloned.1.call-update
  7.9 0.0 reduce-scatter.3.cloned.1.call-start
  8.0 0.7 pad_add_fusion
  8.6 3.9 %collective-permute-start.2 = (s32[2,8]{1,0:T(2,128)S(1)}, s32[2,8]{1,0:T(2,128)S(1)}, u32[]{:S(2)}, u32[]{:S(2)}) collective-permute-start(s32[2,8]{1,0:T(2,128)S(1)} %pad_add_fusion), channel_id=1, source_target_pairs={{0,24},{8,0},{16,8},{24,16},{1,25},{9,1},{17,9},{25,17},{2,26},{10... | collective-permute-start | bytes 200 | tf_op jit(solution)/shard_map/ppermute | solution.py:256
  12.5 0.5 collective-permute-start.1
  13.0 0.6 collective-permute-start
  13.6 1.1 constant_dynamic-slice_fusion.1
  14.7 0.1 pad_maximum_fusion.1
  14.8 2.4 %collective-permute-start.5 = (bf16[8,128,256]{2,1,0:T(8,128)(2,1)S(1)}, bf16[8,128,256]{2,1,0:T(8,128)(2,1)S(1)}, u32[]{:S(2)}, u32[]{:S(2)}) collective-permute-start(bf16[8,128,256]{2,1,0:T(8,128)(2,1)S(1)} %pad_maximum_fusion.1), channel_id=1, source_target_pairs={{0,24},{8,0},{16,8},{24,16},{1,25},{9,1},{17,9},{25,17},{2,26},{10... | collective-permute-start | bytes 1572872 | tf_op jit(solution)/shard_map/ppermute | solution.py:256
  17.2 1.5 collective-permute-start.4
  18.7 1.2 dynamic_slice.38
  21.2 1.3 dynamic_slice.36
  23.8 1.2 dynamic_slice.32.span_ref
  25.0 1.2 dynamic_slice.33
  26.3 0.7 convert_element_type.77
  27.6 0.7 add_convert_fusion.3
  28.3 0.5 multiply_cosine_fusion.1
  29.5 0.1 collective-permute-start.3
  29.6 0.8 pad_add_fusion.1
  30.3 0.7 fusion.29.limit_ref
  31.0 0.7 fusion.28.bias_ref
  31.7 11.0 %collective-permute-done.3 = bf16[8,128,256]{2,1,0:T(8,128)(2,1)S(1)} collective-permute-done((bf16[8,128,256]{2,1,0:T(8,128)(2,1)S(1)}, bf16[8,128,256]{2,1,0:T(8,128)(2,1)S(1)}, u32[]{:S(2)}, u32[]{:S(2)}) %collective-permute-start.3) | collective-permute-done | bytes 524320 | tf_op jit(solution)/shard_map/ppermute | solution.py:256
  42.7 1.4 pad_maximum_fusion.cache_hbm
  44.1 2.2 %fusion = f32[256]{0:T(256)S(1)} fusion(bf16[256,4096]{1,0:T(8,128)(2,1)} %all-gather.3.cloned.1.call-done), kind=kLoop, calls=%fused_computation.2 | loop fusion | flops 3145472 | bytes 2098176 | tf_op jit(solution)/shard_map/reduce_sum | solution.py:23
  46.4 2.6 %bitcast_convert_fusion = (f32[256,1,128]{2,0,1:T(8,128)S(1)}, bf16[256,128]{1,0:T(8,128)(2,1)S(1)}) fusion(bf16[4096,128]{1,0:T(8,128)(2,1)S(1)} %copy-done, bf16[256,4096]{1,0:T(8,128)(2,1)} %all-gather.3.cloned.1.call-done, f32[4096]{0:T(1024)S(1)} %convert_element_type.77, f32[256]{0:T(256)S(1)} %add_rsqrt_fusion), kind=kOutput, calls=%fused_computation.39 | convolution fusion | flops 272695296 | bytes 3359744 | tf_op jit(solution)/shard_map/dot_general | solution.py:302
  49.0 0.7 collective-permute-start.7
  49.7 2.0 collective-permute-start.6
  51.7 1.3 fusion.4
  53.0 0.2 reshape.210
  53.1 0.3 fusion.30
  53.5 0.1 subtract_convert_fusion
  53.6 0.9 pad_maximum_fusion.2
  54.5 3.7 %collective-permute-done.6 = bf16[256,128]{1,0:T(8,128)(2,1)S(1)} collective-permute-done((bf16[256,128]{1,0:T(8,128)(2,1)S(1)}, bf16[256,128]{1,0:T(8,128)(2,1)S(1)}, u32[]{:S(2)}, u32[]{:S(2)}) %collective-permute-start.6) | collective-permute-done | bytes 65568 | tf_op jit(solution)/shard_map/ppermute | solution.py:306
  58.3 0.7 dynamic-slice_bitcast_fusion
  58.9 0.6 fusion.25
  59.5 0.7 pad_maximum_fusion.4.nk_ref
  60.2 10.5 %shard_map.176 = bf16[256,4096]{1,0:T(8,128)(2,1)} custom-call(s32[32]{0:T(128)} %copy-done.5, s32[1]{0:T(128)} %dynamic_slice.32.span_ref, bf16[1024,128]{1,0:T(8,128)(2,1)} %bitcast.37, bf16[32,128,256]{2,1,0:T(8,128)(2,1)} %pad_maximum_fusion.cache_hbm, f32[32,128]{1,0:T(8,128)} %fusion.28.bias_ref, bf16[256,128]{1,0:T(8,128)(2,1)} %pad_maximum_fusion.4.nk_ref, ...), custom_call_target="tpu_custom_call" | custom-call | tf_op jit(solution)/shard_map/pallas_call | solution.py:131
  70.8 0.0 all-gather.5.cloned.1.call-start
  70.8 43.0 %reduce-scatter.3.cloned.1.call-done = bf16[256,512]{1,0:T(8,128)(2,1)} async-done(((bf16[256,4096]{1,0:T(8,128)(2,1)}), bf16[256,512]{1,0:T(8,128)(2,1)}) %reduce-scatter.3.cloned.1.call-update) | async-done | bytes 262160 | tf_op jit(solution)/shard_map/reduce_scatter | solution.py:343
  113.8 1.7 add_convert_fusion.1
  115.6 0.2 reduce-scatter.5.cloned.1.call-start
  115.8 0.6 reshape.216
  116.4 27.4 %all-gather.5.cloned.1.call-done.x_ref = bf16[256,4096]{1,0:T(8,128)(2,1)} async-done(((bf16[256,512]{1,0:T(8,128)(2,1)}), bf16[256,4096]{1,0:T(8,128)(2,1)}) %all-gather.5.cloned.1.call-update) | async-done | bytes 2097168 | tf_op jit(solution)/shard_map/all_gather | solution.py:345
  143.8 20.8 %shard_map.177 = bf16[256,4096]{1,0:T(8,128)(2,1)} custom-call(bf16[256,4096]{1,0:T(8,128)(2,1)} %all-gather.5.cloned.1.call-done.x_ref, f32[1,4096]{1,0:T(1,128)} %bitcast.39, bf16[1376,4096]{1,0:T(8,128)(2,1)} %bitcast.35, bf16[1376,4096]{1,0:T(8,128)(2,1)} %bitcast.36, bf16[1376,4096]{1,0:T(8,128)(2,1)} %wd_ref.1), custom_call_target="tpu_custom_call" | custom-call | tf_op jit(solution)/shard_map/pallas_call | solution.py:199
  164.7 0.6 iota_compare_fusion.1
  165.3 0.8 fusion.23
  166.0 34.0 %reduce-scatter.5.cloned.1.call-done = bf16[256,512]{1,0:T(8,128)(2,1)} async-done(((bf16[256,4096]{1,0:T(8,128)(2,1)}), bf16[256,512]{1,0:T(8,128)(2,1)}) %reduce-scatter.5.cloned.1.call-update) | async-done | bytes 262160 | tf_op jit(solution)/shard_map/reduce_scatter | solution.py:346
  200.1 1.8 fusion.6
  (28 shorter events, 0.2 us)
Async XLA Ops:
  7.2 39.2 %copy-start = (bf16[4096,128]{1,0:T(8,128)(2,1)S(1)}, bf16[4096,128]{1,0:T(8,128)(2,1)}, u32[]{:S(2)}) copy-start(bf16[4096,128]{1,0:T(8,128)(2,1)} %param.21) | copy-start | bytes 3145732
  7.2 36.9 %all-gather.3.cloned.1.call-start = ((), (), s32[]{:S(2)}) async-start(), calls=%async_computation.2 | async-start | bytes 2359296 | tf_op jit(solution)/shard_map/all_gather | solution.py:300
  7.9 105.9 %reduce-scatter.3.cloned.1.call-start = ((), (), s32[]{:S(2)}) async-start(), calls=%async_computation.3 | async-start | bytes 2359296 | tf_op jit(solution)/shard_map/reduce_scatter | solution.py:343
  8.6 20.8 %collective-permute-start.2 = (s32[2,8]{1,0:T(2,128)S(1)}, s32[2,8]{1,0:T(2,128)S(1)}, u32[]{:S(2)}, u32[]{:S(2)}) collective-permute-start(s32[2,8]{1,0:T(2,128)S(1)} %pad_add_fusion), channel_id=1, source_target_pairs={{0,24},{8,0},{16,8},{24,16},{1,25},{9,1},{17,9},{25,17},{2,26},{10... | collective-permute-start | bytes 200 | tf_op jit(solution)/shard_map/ppermute | solution.py:256
  12.5 17.0 %collective-permute-start.1 = (s32[2,8]{1,0:T(2,128)S(1)}, s32[2,8]{1,0:T(2,128)S(1)}, u32[]{:S(2)}, u32[]{:S(2)}) collective-permute-start(s32[2,8]{1,0:T(2,128)S(1)} %pad_add_fusion), channel_id=1, source_target_pairs={{0,16},{8,24},{16,0},{24,8},{1,17},{9,25},{17,1},{25,9},{2,18},{10... | collective-permute-start | bytes 200 | tf_op jit(solution)/shard_map/ppermute | solution.py:256
  13.0 16.5 %collective-permute-start = (s32[2,8]{1,0:T(2,128)S(1)}, s32[2,8]{1,0:T(2,128)S(1)}, u32[]{:S(2)}, u32[]{:S(2)}) collective-permute-start(s32[2,8]{1,0:T(2,128)S(1)} %pad_add_fusion), channel_id=1, source_target_pairs={{0,8},{8,16},{16,24},{24,0},{1,9},{9,17},{17,25},{25,1},{2,10},{10... | collective-permute-start | bytes 200 | tf_op jit(solution)/shard_map/ppermute | solution.py:256
  14.8 16.9 %collective-permute-start.5 = (bf16[8,128,256]{2,1,0:T(8,128)(2,1)S(1)}, bf16[8,128,256]{2,1,0:T(8,128)(2,1)S(1)}, u32[]{:S(2)}, u32[]{:S(2)}) collective-permute-start(bf16[8,128,256]{2,1,0:T(8,128)(2,1)S(1)} %pad_maximum_fusion.1), channel_id=1, source_target_pairs={{0,24},{8,0},{16,8},{24,16},{1,25},{9,1},{17,9},{25,17},{2,26},{10... | collective-permute-start | bytes 1572872 | tf_op jit(solution)/shard_map/ppermute | solution.py:256
  17.2 14.5 %collective-permute-start.4 = (bf16[8,128,256]{2,1,0:T(8,128)(2,1)S(1)}, bf16[8,128,256]{2,1,0:T(8,128)(2,1)S(1)}, u32[]{:S(2)}, u32[]{:S(2)}) collective-permute-start(bf16[8,128,256]{2,1,0:T(8,128)(2,1)S(1)} %pad_maximum_fusion.1), channel_id=1, source_target_pairs={{0,16},{8,24},{16,0},{24,8},{1,17},{9,25},{17,1},{25,9},{2,18},{10... | collective-permute-start | bytes 1572872 | tf_op jit(solution)/shard_map/ppermute | solution.py:256
  29.5 13.2 %collective-permute-start.3 = (bf16[8,128,256]{2,1,0:T(8,128)(2,1)S(1)}, bf16[8,128,256]{2,1,0:T(8,128)(2,1)S(1)}, u32[]{:S(2)}, u32[]{:S(2)}) collective-permute-start(bf16[8,128,256]{2,1,0:T(8,128)(2,1)S(1)} %pad_maximum_fusion.1), channel_id=1, source_target_pairs={{0,8},{8,16},{16,24},{24,0},{1,9},{9,17},{17,25},{25,1},{2,10},{10... | collective-permute-start | bytes 1572872 | tf_op jit(solution)/shard_map/ppermute | solution.py:256
  31.0 18.0 %copy-start.5 = (s32[32]{0:T(128)}, s32[32]{0:T(128)S(1)}, u32[]{:S(2)}) copy-start(s32[32]{0:T(128)S(1)} %fusion.29.limit_ref) | copy-start | bytes 388
  44.1 7.5 %copy-start.2 = (bf16[256,4096]{1,0:T(8,128)(2,1)S(1)}, bf16[256,4096]{1,0:T(8,128)(2,1)}, u32[]{:S(2)}) copy-start(bf16[256,4096]{1,0:T(8,128)(2,1)} %all-gather.3.cloned.1.call-done) | copy-start | bytes 6291460
  44.1 7.5 %copy-start.6 = (bf16[4096,512]{1,0:T(8,128)(2,1)S(1)}, bf16[4096,512]{1,0:T(8,128)(2,1)}, u32[]{:S(2)}) copy-start(bf16[4096,512]{1,0:T(8,128)(2,1)} %param.20) | copy-start | bytes 12582916
  49.0 5.5 %collective-permute-start.7 = (bf16[256,128]{1,0:T(8,128)(2,1)S(1)}, bf16[256,128]{1,0:T(8,128)(2,1)S(1)}, u32[]{:S(2)}, u32[]{:S(2)}) collective-permute-start(bf16[256,128]{1,0:T(8,128)(2,1)S(1)} %get-tuple-element.19), channel_id=1, source_target_pairs={{1,3},{2,5},{3,7},{4,1},{5,2},{6,4},{7,6},{9,11},{10,13},{11,15},{... | collective-permute-start | bytes 196616 | tf_op jit(solution)/shard_map/ppermute | solution.py:306
  49.7 8.6 %collective-permute-start.6 = (bf16[256,128]{1,0:T(8,128)(2,1)S(1)}, bf16[256,128]{1,0:T(8,128)(2,1)S(1)}, u32[]{:S(2)}, u32[]{:S(2)}) collective-permute-start(bf16[256,128]{1,0:T(8,128)(2,1)S(1)} %get-tuple-element.19), channel_id=1, source_target_pairs={{0,1},{1,2},{2,4},{3,6},{4,0},{5,3},{6,5},{8,9},{9,10},{10,12},{11... | collective-permute-start | bytes 196616 | tf_op jit(solution)/shard_map/ppermute | solution.py:306
  60.2 53.6 %copy-start.3 = (bf16[256,512]{1,0:T(8,128)(2,1)S(1)}, bf16[256,512]{1,0:T(8,128)(2,1)}, u32[]{:S(2)}) copy-start(bf16[256,512]{1,0:T(8,128)(2,1)} %param.17) | copy-start | bytes 786436
  60.2 55.6 %copy-start.4 = (bf16[4096]{0:T(1024)(128)(2,1)S(1)}, bf16[4096]{0:T(1024)(128)(2,1)}, u32[]{:S(2)}) copy-start(bf16[4096]{0:T(1024)(128)(2,1)} %param.19) | copy-start | bytes 24580
  70.8 73.0 %all-gather.5.cloned.1.call-start = ((), (), s32[]{:S(2)}) async-start(), calls=%async_computation.4 | async-start | bytes 2359296 | tf_op jit(solution)/shard_map/all_gather | solution.py:345
  115.6 84.5 %reduce-scatter.5.cloned.1.call-start = ((), (), s32[]{:S(2)}) async-start(), calls=%async_computation.5 | async-start | bytes 2359296 | tf_op jit(solution)/shard_map/reduce_scatter | solution.py:346
  143.8 56.2 %copy-start.1 = (bf16[256,512]{1,0:T(8,128)(2,1)S(1)}, bf16[256,512]{1,0:T(8,128)(2,1)}, u32[]{:S(2)}) copy-start(bf16[256,512]{1,0:T(8,128)(2,1)} %add_convert_fusion.1) | copy-start | bytes 786436
Sparse Core Ops, SparseCore 0:
  9.6 31.7 all-gather.2
  70.9 42.8 reduce-scatter.2
  116.0 27.7 all-gather.4
  164.8 35.2 reduce-scatter.4

commit v18 on v16

--- a/solution.py
+++ b/solution.py
@@ -70,7 +70,13 @@
     top_scr[...] = jnp.full(top_scr.shape, NEG, jnp.float32)
 
     def max_step(s, carry):
-        @pl.when(limit_ref[s] > 0)
+        lim = limit_ref[s]
+
+        @pl.when(lim == BLK)
+        def _():
+            top_scr[...] = jnp.maximum(top_scr[...], cache_raw(s))
+
+        @pl.when((lim > 0) & (lim < BLK))
         def _():
             top_scr[...] = jnp.maximum(top_scr[...], cache_raw(s) + bias_ref[pl.ds(s, 1), :])
 
@@ -90,14 +96,22 @@
     tot_scr[...] = jnp.zeros(tot_scr.shape, jnp.float32)
     acc_scr[...] = jnp.zeros(acc_scr.shape, jnp.float32)
 
+    def add_weights(s, w):
+        tot_scr[...] += w
+        acc_scr[...] += jnp.dot(
+            w.astype(jnp.bfloat16), cache_ref[s, :, HD:], preferred_element_type=jnp.float32
+        )
+
     def sum_step(s, carry):
-        @pl.when(limit_ref[s] > 0)
+        lim = limit_ref[s]
+
+        @pl.when(lim == BLK)
         def _():
-            w = jnp.exp(cache_raw(s) * scale + bias_ref[pl.ds(s, 1), :] - peak)
-            tot_scr[...] += w
-            acc_scr[...] += jnp.dot(
-                w.astype(jnp.bfloat16), cache_ref[s, :, HD:], preferred_element_type=jnp.float32
-            )
+            add_weights(s, jnp.exp(cache_raw(s) * scale - peak))
+
+        @pl.when((lim > 0) & (lim < BLK))
+        def _():
+            add_weights(s, jnp.exp(cache_raw(s) * scale + bias_ref[pl.ds(s, 1), :] - peak))
 
         return carry
 

time: 208 us -> 208 us (level)
  no operation moved by 1% of the time
where the time goes in v18:
time: 208 us; the launch traced here: 207 us
  waiting for transfers between devices  120 us (58%)
  Pallas kernels  29.9 us (14%)
  between operations  17.9 us (9%)
  other arithmetic  16.8 us (8%)
  starting transfers between devices  11.9 us (6%)
  local copies, waits for them, and re-layouts  6.6 us (3%)
  matrix products  3.89 us (2%)
    reduce_scatter x1, waiting for transfers between devices, per_device(): lax.psum_scatter(head_term, 'tp', scatter_dimension=1, tiled=True)  43.5 us
    reduce_scatter x1, waiting for transfers between devices, per_device(): lax.psum_scatter(feed_forward(full_mid, mlp_gain, w_gate, w_up, w_down),...  34.1 us
    all_gather x1, waiting for transfers between devices, per_device(): full_mid = lax.all_gather(mid, 'tp', axis=1, tiled=True)  27.2 us
    pallas_call x1, Pallas kernels, feed_forward(): pl.pallas_call(functools.partial(ffn_kernel, first, chunk), out_shape=jax...  20.8 us
    ppermute x6, waiting for transfers between devices, gather_ctx(): parts.append(lax.ppermute(value, 'ctx', pairs))  11 us
    pallas_call x1, Pallas kernels, local_attention(): pl.pallas_call(attn_kernel, out_shape=jax.ShapeDtypeStruct((span_size, wi...  9.03 us
    ppermute x6, starting transfers between devices, gather_ctx(): parts.append(lax.ppermute(value, 'ctx', pairs))  8.95 us
  transfers between devices with their start and end apart: 12, of which 5 were waited for; matrix products, arithmetic and copies ran while one was open for 8% of the time, Pallas kernels for 0%

profile of v18, /device:TPU:0, one launch (start us, length us, event | category | flops | bytes accessed | tf_op | source)
XLA Modules:
  0.0 207.3 jit_solution(7712434776319971104)
XLA Ops:
  7.2 0.7 all-gather.3.cloned.1.call-update
  7.9 0.0 reduce-scatter.3.cloned.1.call-start
  8.0 0.7 pad_add_fusion
  8.6 3.9 %collective-permute-start.2 = (s32[2,8]{1,0:T(2,128)S(1)}, s32[2,8]{1,0:T(2,128)S(1)}, u32[]{:S(2)}, u32[]{:S(2)}) collective-permute-start(s32[2,8]{1,0:T(2,128)S(1)} %pad_add_fusion), channel_id=1, source_target_pairs={{0,24},{8,0},{16,8},{24,16},{1,25},{9,1},{17,9},{25,17},{2,26},{10... | collective-permute-start | bytes 200 | tf_op jit(solution)/shard_map/ppermute | solution.py:265
  12.5 0.5 collective-permute-start.1
  13.0 0.6 collective-permute-start
  13.6 1.1 constant_dynamic-slice_fusion.1
  14.7 0.1 pad_maximum_fusion.1
  14.8 2.4 %collective-permute-start.5 = (bf16[8,128,256]{2,1,0:T(8,128)(2,1)S(1)}, bf16[8,128,256]{2,1,0:T(8,128)(2,1)S(1)}, u32[]{:S(2)}, u32[]{:S(2)}) collective-permute-start(bf16[8,128,256]{2,1,0:T(8,128)(2,1)S(1)} %pad_maximum_fusion.1), channel_id=1, source_target_pairs={{0,24},{8,0},{16,8},{24,16},{1,25},{9,1},{17,9},{25,17},{2,26},{10... | collective-permute-start | bytes 1572872 | tf_op jit(solution)/shard_map/ppermute | solution.py:265
  17.2 1.5 collective-permute-start.4
  18.7 1.2 dynamic_slice.38
  21.2 1.3 dynamic_slice.36
  23.8 1.2 dynamic_slice.32.span_ref
  25.0 1.2 dynamic_slice.33
  26.3 0.7 convert_element_type.77
  27.6 0.7 add_convert_fusion.3
  28.3 0.5 multiply_cosine_fusion.1
  29.5 0.1 collective-permute-start.3
  29.6 0.8 pad_add_fusion.1
  30.3 0.7 fusion.29.limit_ref
  31.0 0.7 fusion.28.bias_ref
  31.7 11.0 %collective-permute-done.3 = bf16[8,128,256]{2,1,0:T(8,128)(2,1)S(1)} collective-permute-done((bf16[8,128,256]{2,1,0:T(8,128)(2,1)S(1)}, bf16[8,128,256]{2,1,0:T(8,128)(2,1)S(1)}, u32[]{:S(2)}, u32[]{:S(2)}) %collective-permute-start.3) | collective-permute-done | bytes 524320 | tf_op jit(solution)/shard_map/ppermute | solution.py:265
  42.7 1.4 pad_maximum_fusion.cache_ref
  44.1 2.2 %fusion = f32[256]{0:T(256)S(1)} fusion(bf16[256,4096]{1,0:T(8,128)(2,1)} %all-gather.3.cloned.1.call-done), kind=kLoop, calls=%fused_computation.2 | loop fusion | flops 3145472 | bytes 2098176 | tf_op jit(solution)/shard_map/reduce_sum | solution.py:23
  46.4 2.6 %bitcast_convert_fusion = (f32[256,1,128]{2,0,1:T(8,128)S(1)}, bf16[256,128]{1,0:T(8,128)(2,1)S(1)}) fusion(bf16[4096,128]{1,0:T(8,128)(2,1)S(1)} %copy-done, bf16[256,4096]{1,0:T(8,128)(2,1)} %all-gather.3.cloned.1.call-done, f32[4096]{0:T(1024)S(1)} %convert_element_type.77, f32[256]{0:T(256)S(1)} %add_rsqrt_fusion), kind=kOutput, calls=%fused_computation.39 | convolution fusion | flops 272695296 | bytes 3359744 | tf_op jit(solution)/shard_map/dot_general | solution.py:311
  49.0 0.7 collective-permute-start.7
  49.7 2.0 collective-permute-start.6
  51.7 1.3 fusion.4
  53.0 0.2 reshape.210
  53.1 0.3 fusion.30
  53.5 0.1 subtract_convert_fusion
  53.6 0.9 pad_maximum_fusion.2
  54.5 3.7 %collective-permute-done.6 = bf16[256,128]{1,0:T(8,128)(2,1)S(1)} collective-permute-done((bf16[256,128]{1,0:T(8,128)(2,1)S(1)}, bf16[256,128]{1,0:T(8,128)(2,1)S(1)}, u32[]{:S(2)}, u32[]{:S(2)}) %collective-permute-start.6) | collective-permute-done | bytes 65568 | tf_op jit(solution)/shard_map/ppermute | solution.py:315
  58.3 0.7 dynamic-slice_bitcast_fusion
  58.9 0.6 fusion.25
  59.5 0.7 pad_maximum_fusion.4.nk_ref
  60.2 9.0 %shard_map.176 = bf16[256,4096]{1,0:T(8,128)(2,1)} custom-call(s32[32]{0:T(128)} %copy-done.5, s32[1]{0:T(128)} %dynamic_slice.32.span_ref, bf16[1024,128]{1,0:T(8,128)(2,1)} %bitcast.37, bf16[32,128,256]{2,1,0:T(8,128)(2,1)} %pad_maximum_fusion.cache_ref, f32[32,128]{1,0:T(8,128)} %fusion.28.bias_ref, bf16[256,128]{1,0:T(8,128)(2,1)} %pad_maximum_fusion.4.nk_ref, ...), custom_call_target="tpu_custom_call" | custom-call | tf_op jit(solution)/shard_map/pallas_call | solution.py:142
  69.3 0.0 all-gather.5.cloned.1.call-start
  69.4 43.5 %reduce-scatter.3.cloned.1.call-done = bf16[256,512]{1,0:T(8,128)(2,1)} async-done(((bf16[256,4096]{1,0:T(8,128)(2,1)}), bf16[256,512]{1,0:T(8,128)(2,1)}) %reduce-scatter.3.cloned.1.call-update) | async-done | bytes 262160 | tf_op jit(solution)/shard_map/reduce_scatter | solution.py:352
  112.9 1.7 add_convert_fusion.1
  114.6 0.2 reduce-scatter.5.cloned.1.call-start
  114.9 0.6 reshape.216
  115.5 27.2 %all-gather.5.cloned.1.call-done.x_ref = bf16[256,4096]{1,0:T(8,128)(2,1)} async-done(((bf16[256,512]{1,0:T(8,128)(2,1)}), bf16[256,4096]{1,0:T(8,128)(2,1)}) %all-gather.5.cloned.1.call-update) | async-done | bytes 2097168 | tf_op jit(solution)/shard_map/all_gather | solution.py:354
  142.7 20.8 %shard_map.177 = bf16[256,4096]{1,0:T(8,128)(2,1)} custom-call(bf16[256,4096]{1,0:T(8,128)(2,1)} %all-gather.5.cloned.1.call-done.x_ref, f32[1,4096]{1,0:T(1,128)} %bitcast.39, bf16[1376,4096]{1,0:T(8,128)(2,1)} %bitcast.35, bf16[1376,4096]{1,0:T(8,128)(2,1)} %bitcast.36, bf16[1376,4096]{1,0:T(8,128)(2,1)} %wd_ref.1), custom_call_target="tpu_custom_call" | custom-call | tf_op jit(solution)/shard_map/pallas_call | solution.py:208
  163.6 0.6 iota_compare_fusion.1
  164.2 0.8 fusion.23
  164.9 34.1 %reduce-scatter.5.cloned.1.call-done = bf16[256,512]{1,0:T(8,128)(2,1)} async-done(((bf16[256,4096]{1,0:T(8,128)(2,1)}), bf16[256,512]{1,0:T(8,128)(2,1)}) %reduce-scatter.5.cloned.1.call-update) | async-done | bytes 262160 | tf_op jit(solution)/shard_map/reduce_scatter | solution.py:355
  199.0 1.8 fusion.6
  (28 shorter events, 0.2 us)
Async XLA Ops:
  7.2 39.2 %copy-start = (bf16[4096,128]{1,0:T(8,128)(2,1)S(1)}, bf16[4096,128]{1,0:T(8,128)(2,1)}, u32[]{:S(2)}) copy-start(bf16[4096,128]{1,0:T(8,128)(2,1)} %param.21) | copy-start | bytes 3145732
  7.2 36.9 %all-gather.3.cloned.1.call-start = ((), (), s32[]{:S(2)}) async-start(), calls=%async_computation.2 | async-start | bytes 2359296 | tf_op jit(solution)/shard_map/all_gather | solution.py:309
  7.9 105.0 %reduce-scatter.3.cloned.1.call-start = ((), (), s32[]{:S(2)}) async-start(), calls=%async_computation.3 | async-start | bytes 2359296 | tf_op jit(solution)/shard_map/reduce_scatter | solution.py:352
  8.6 20.8 %collective-permute-start.2 = (s32[2,8]{1,0:T(2,128)S(1)}, s32[2,8]{1,0:T(2,128)S(1)}, u32[]{:S(2)}, u32[]{:S(2)}) collective-permute-start(s32[2,8]{1,0:T(2,128)S(1)} %pad_add_fusion), channel_id=1, source_target_pairs={{0,24},{8,0},{16,8},{24,16},{1,25},{9,1},{17,9},{25,17},{2,26},{10... | collective-permute-start | bytes 200 | tf_op jit(solution)/shard_map/ppermute | solution.py:265
  12.5 17.0 %collective-permute-start.1 = (s32[2,8]{1,0:T(2,128)S(1)}, s32[2,8]{1,0:T(2,128)S(1)}, u32[]{:S(2)}, u32[]{:S(2)}) collective-permute-start(s32[2,8]{1,0:T(2,128)S(1)} %pad_add_fusion), channel_id=1, source_target_pairs={{0,16},{8,24},{16,0},{24,8},{1,17},{9,25},{17,1},{25,9},{2,18},{10... | collective-permute-start | bytes 200 | tf_op jit(solution)/shard_map/ppermute | solution.py:265
  13.0 16.5 %collective-permute-start = (s32[2,8]{1,0:T(2,128)S(1)}, s32[2,8]{1,0:T(2,128)S(1)}, u32[]{:S(2)}, u32[]{:S(2)}) collective-permute-start(s32[2,8]{1,0:T(2,128)S(1)} %pad_add_fusion), channel_id=1, source_target_pairs={{0,8},{8,16},{16,24},{24,0},{1,9},{9,17},{17,25},{25,1},{2,10},{10... | collective-permute-start | bytes 200 | tf_op jit(solution)/shard_map/ppermute | solution.py:265
  14.8 16.9 %collective-permute-start.5 = (bf16[8,128,256]{2,1,0:T(8,128)(2,1)S(1)}, bf16[8,128,256]{2,1,0:T(8,128)(2,1)S(1)}, u32[]{:S(2)}, u32[]{:S(2)}) collective-permute-start(bf16[8,128,256]{2,1,0:T(8,128)(2,1)S(1)} %pad_maximum_fusion.1), channel_id=1, source_target_pairs={{0,24},{8,0},{16,8},{24,16},{1,25},{9,1},{17,9},{25,17},{2,26},{10... | collective-permute-start | bytes 1572872 | tf_op jit(solution)/shard_map/ppermute | solution.py:265
  17.2 14.5 %collective-permute-start.4 = (bf16[8,128,256]{2,1,0:T(8,128)(2,1)S(1)}, bf16[8,128,256]{2,1,0:T(8,128)(2,1)S(1)}, u32[]{:S(2)}, u32[]{:S(2)}) collective-permute-start(bf16[8,128,256]{2,1,0:T(8,128)(2,1)S(1)} %pad_maximum_fusion.1), channel_id=1, source_target_pairs={{0,16},{8,24},{16,0},{24,8},{1,17},{9,25},{17,1},{25,9},{2,18},{10... | collective-permute-start | bytes 1572872 | tf_op jit(solution)/shard_map/ppermute | solution.py:265
  29.5 13.2 %collective-permute-start.3 = (bf16[8,128,256]{2,1,0:T(8,128)(2,1)S(1)}, bf16[8,128,256]{2,1,0:T(8,128)(2,1)S(1)}, u32[]{:S(2)}, u32[]{:S(2)}) collective-permute-start(bf16[8,128,256]{2,1,0:T(8,128)(2,1)S(1)} %pad_maximum_fusion.1), channel_id=1, source_target_pairs={{0,8},{8,16},{16,24},{24,0},{1,9},{9,17},{17,25},{25,1},{2,10},{10... | collective-permute-start | bytes 1572872 | tf_op jit(solution)/shard_map/ppermute | solution.py:265
  31.0 18.0 %copy-start.5 = (s32[32]{0:T(128)}, s32[32]{0:T(128)S(1)}, u32[]{:S(2)}) copy-start(s32[32]{0:T(128)S(1)} %fusion.29.limit_ref) | copy-start | bytes 388
  44.1 7.5 %copy-start.2 = (bf16[256,4096]{1,0:T(8,128)(2,1)S(1)}, bf16[256,4096]{1,0:T(8,128)(2,1)}, u32[]{:S(2)}) copy-start(bf16[256,4096]{1,0:T(8,128)(2,1)} %all-gather.3.cloned.1.call-done) | copy-start | bytes 6291460
  44.1 7.5 %copy-start.6 = (bf16[4096,512]{1,0:T(8,128)(2,1)S(1)}, bf16[4096,512]{1,0:T(8,128)(2,1)}, u32[]{:S(2)}) copy-start(bf16[4096,512]{1,0:T(8,128)(2,1)} %param.20) | copy-start | bytes 12582916
  49.0 5.5 %collective-permute-start.7 = (bf16[256,128]{1,0:T(8,128)(2,1)S(1)}, bf16[256,128]{1,0:T(8,128)(2,1)S(1)}, u32[]{:S(2)}, u32[]{:S(2)}) collective-permute-start(bf16[256,128]{1,0:T(8,128)(2,1)S(1)} %get-tuple-element.19), channel_id=1, source_target_pairs={{1,3},{2,5},{3,7},{4,1},{5,2},{6,4},{7,6},{9,11},{10,13},{11,15},{... | collective-permute-start | bytes 196616 | tf_op jit(solution)/shard_map/ppermute | solution.py:315
  49.7 8.6 %collective-permute-start.6 = (bf16[256,128]{1,0:T(8,128)(2,1)S(1)}, bf16[256,128]{1,0:T(8,128)(2,1)S(1)}, u32[]{:S(2)}, u32[]{:S(2)}) collective-permute-start(bf16[256,128]{1,0:T(8,128)(2,1)S(1)} %get-tuple-element.19), channel_id=1, source_target_pairs={{0,1},{1,2},{2,4},{3,6},{4,0},{5,3},{6,5},{8,9},{9,10},{10,12},{11... | collective-permute-start | bytes 196616 | tf_op jit(solution)/shard_map/ppermute | solution.py:315
  60.2 52.7 %copy-start.3 = (bf16[256,512]{1,0:T(8,128)(2,1)S(1)}, bf16[256,512]{1,0:T(8,128)(2,1)}, u32[]{:S(2)}) copy-start(bf16[256,512]{1,0:T(8,128)(2,1)} %param.17) | copy-start | bytes 786436
  60.2 54.6 %copy-start.4 = (bf16[4096]{0:T(1024)(128)(2,1)S(1)}, bf16[4096]{0:T(1024)(128)(2,1)}, u32[]{:S(2)}) copy-start(bf16[4096]{0:T(1024)(128)(2,1)} %param.19) | copy-start | bytes 24580
  69.3 73.4 %all-gather.5.cloned.1.call-start = ((), (), s32[]{:S(2)}) async-start(), calls=%async_computation.4 | async-start | bytes 2359296 | tf_op jit(solution)/shard_map/all_gather | solution.py:354
  114.6 84.4 %reduce-scatter.5.cloned.1.call-start = ((), (), s32[]{:S(2)}) async-start(), calls=%async_computation.5 | async-start | bytes 2359296 | tf_op jit(solution)/shard_map/reduce_scatter | solution.py:355
  142.7 56.3 %copy-start.1 = (bf16[256,512]{1,0:T(8,128)(2,1)S(1)}, bf16[256,512]{1,0:T(8,128)(2,1)}, u32[]{:S(2)}) copy-start(bf16[256,512]{1,0:T(8,128)(2,1)} %add_convert_fusion.1) | copy-start | bytes 786436
Sparse Core Ops, SparseCore 0:
  9.6 31.7 all-gather.2
  69.4 43.4 reduce-scatter.2
  115.1 27.5 all-gather.4
  163.7 35.2 reduce-scatter.4

commit v19 on v18

--- a/solution.py
+++ b/solution.py
@@ -84,11 +84,12 @@
 
     lax.fori_loop(0, slots, max_step, 0)
     peaks = []
+    new_sc = [new_raw(h) for h in range(heads)]
     for h in range(heads):
         part = slice(h * span_size, (h + 1) * span_size)
         raw_top = jnp.maximum(
             jnp.max(top_scr[part, :], axis=1, keepdims=True),
-            jnp.max(jnp.where(new_ok, new_raw(h), NEG), axis=1, keepdims=True),
+            jnp.max(jnp.where(new_ok, new_sc[h], NEG), axis=1, keepdims=True),
         )
         peaks.append(raw_top * scale)
     peak = jnp.concatenate(peaks, axis=0)
@@ -119,7 +120,7 @@
     wo_copy.wait()
     for h in range(heads):
         part = slice(h * span_size, (h + 1) * span_size)
-        w = jnp.where(new_ok, jnp.exp(new_raw(h) * scale - peak[part, :]), 0.0)
+        w = jnp.where(new_ok, jnp.exp(new_sc[h] * scale - peak[part, :]), 0.0)
         total = jnp.sum(tot_scr[part, :], axis=1, keepdims=True) + jnp.sum(w, axis=1, keepdims=True)
         summed = acc_scr[part, :] + jnp.dot(
             w.astype(jnp.bfloat16), nv_ref[...], preferred_element_type=jnp.float32

time: 208 us -> 208 us (level)
  no operation moved by 1% of the time
where the time goes in v19:
time: 208 us; the launch traced here: 207 us
  waiting for transfers between devices  120 us (58%)
  Pallas kernels  29.8 us (14%)
  between operations  17.9 us (9%)
  other arithmetic  16.8 us (8%)
  starting transfers between devices  11.9 us (6%)
  local copies, waits for them, and re-layouts  6.6 us (3%)
  matrix products  3.89 us (2%)
    reduce_scatter x1, waiting for transfers between devices, per_device(): lax.psum_scatter(head_term, 'tp', scatter_dimension=1, tiled=True)  43.6 us
    reduce_scatter x1, waiting for transfers between devices, per_device(): lax.psum_scatter(feed_forward(full_mid, mlp_gain, w_gate, w_up, w_down),...  34.1 us
    all_gather x1, waiting for transfers between devices, per_device(): full_mid = lax.all_gather(mid, 'tp', axis=1, tiled=True)  27.3 us
    pallas_call x1, Pallas kernels, feed_forward(): pl.pallas_call(functools.partial(ffn_kernel, first, chunk), out_shape=jax...  20.8 us
    ppermute x6, waiting for transfers between devices, gather_ctx(): parts.append(lax.ppermute(value, 'ctx', pairs))  11 us
    ppermute x6, starting transfers between devices, gather_ctx(): parts.append(lax.ppermute(value, 'ctx', pairs))  8.95 us
    pallas_call x1, Pallas kernels, local_attention(): pl.pallas_call(attn_kernel, out_shape=jax.ShapeDtypeStruct((span_size, wi...  8.94 us
  transfers between devices with their start and end apart: 12, of which 5 were waited for; matrix products, arithmetic and copies ran while one was open for 8% of the time, Pallas kernels for 0%

profile of v19, /device:TPU:0, one launch (start us, length us, event | category | flops | bytes accessed | tf_op | source)
XLA Modules:
  0.0 207.3 jit_solution(6316875049539796968)
XLA Ops:
  7.2 0.7 all-gather.3.cloned.1.call-update
  7.9 0.0 reduce-scatter.3.cloned.1.call-start
  8.0 0.7 pad_add_fusion
  8.6 3.9 %collective-permute-start.2 = (s32[2,8]{1,0:T(2,128)S(1)}, s32[2,8]{1,0:T(2,128)S(1)}, u32[]{:S(2)}, u32[]{:S(2)}) collective-permute-start(s32[2,8]{1,0:T(2,128)S(1)} %pad_add_fusion), channel_id=1, source_target_pairs={{0,24},{8,0},{16,8},{24,16},{1,25},{9,1},{17,9},{25,17},{2,26},{10... | collective-permute-start | bytes 200 | tf_op jit(solution)/shard_map/ppermute | solution.py:266
  12.5 0.5 collective-permute-start.1
  13.0 0.6 collective-permute-start
  13.6 1.1 constant_dynamic-slice_fusion.1
  14.7 0.1 pad_maximum_fusion.1
  14.8 2.4 %collective-permute-start.5 = (bf16[8,128,256]{2,1,0:T(8,128)(2,1)S(1)}, bf16[8,128,256]{2,1,0:T(8,128)(2,1)S(1)}, u32[]{:S(2)}, u32[]{:S(2)}) collective-permute-start(bf16[8,128,256]{2,1,0:T(8,128)(2,1)S(1)} %pad_maximum_fusion.1), channel_id=1, source_target_pairs={{0,24},{8,0},{16,8},{24,16},{1,25},{9,1},{17,9},{25,17},{2,26},{10... | collective-permute-start | bytes 1572872 | tf_op jit(solution)/shard_map/ppermute | solution.py:266
  17.2 1.5 collective-permute-start.4
  18.7 1.2 dynamic_slice.38
  21.2 1.3 dynamic_slice.36
  23.8 1.2 dynamic_slice.32.span_ref
  25.0 1.2 dynamic_slice.33
  26.3 0.7 convert_element_type.77
  27.6 0.7 add_convert_fusion.3
  28.3 0.5 multiply_cosine_fusion.1
  29.5 0.1 collective-permute-start.3
  29.6 0.8 pad_add_fusion.1
  30.3 0.7 fusion.29.limit_ref
  31.0 0.7 fusion.28.bias_ref
  31.7 11.0 %collective-permute-done.3 = bf16[8,128,256]{2,1,0:T(8,128)(2,1)S(1)} collective-permute-done((bf16[8,128,256]{2,1,0:T(8,128)(2,1)S(1)}, bf16[8,128,256]{2,1,0:T(8,128)(2,1)S(1)}, u32[]{:S(2)}, u32[]{:S(2)}) %collective-permute-start.3) | collective-permute-done | bytes 524320 | tf_op jit(solution)/shard_map/ppermute | solution.py:266
  42.7 1.4 pad_maximum_fusion.cache_ref
  44.1 2.2 %fusion = f32[256]{0:T(256)S(1)} fusion(bf16[256,4096]{1,0:T(8,128)(2,1)} %all-gather.3.cloned.1.call-done), kind=kLoop, calls=%fused_computation.2 | loop fusion | flops 3145472 | bytes 2098176 | tf_op jit(solution)/shard_map/reduce_sum | solution.py:23
  46.4 2.6 %bitcast_convert_fusion = (f32[256,1,128]{2,0,1:T(8,128)S(1)}, bf16[256,128]{1,0:T(8,128)(2,1)S(1)}) fusion(bf16[4096,128]{1,0:T(8,128)(2,1)S(1)} %copy-done, bf16[256,4096]{1,0:T(8,128)(2,1)} %all-gather.3.cloned.1.call-done, f32[4096]{0:T(1024)S(1)} %convert_element_type.77, f32[256]{0:T(256)S(1)} %add_rsqrt_fusion), kind=kOutput, calls=%fused_computation.39 | convolution fusion | flops 272695296 | bytes 3359744 | tf_op jit(solution)/shard_map/dot_general | solution.py:312
  49.0 0.7 collective-permute-start.7
  49.7 2.0 collective-permute-start.6
  51.7 1.3 fusion.4
  53.0 0.2 reshape.210
  53.1 0.3 fusion.30
  53.5 0.1 subtract_convert_fusion
  53.6 0.9 pad_maximum_fusion.2
  54.5 3.7 %collective-permute-done.6 = bf16[256,128]{1,0:T(8,128)(2,1)S(1)} collective-permute-done((bf16[256,128]{1,0:T(8,128)(2,1)S(1)}, bf16[256,128]{1,0:T(8,128)(2,1)S(1)}, u32[]{:S(2)}, u32[]{:S(2)}) %collective-permute-start.6) | collective-permute-done | bytes 65568 | tf_op jit(solution)/shard_map/ppermute | solution.py:316
  58.3 0.7 dynamic-slice_bitcast_fusion
  58.9 0.6 fusion.25
  59.5 0.7 pad_maximum_fusion.4.nk_ref
  60.2 8.9 %shard_map.176 = bf16[256,4096]{1,0:T(8,128)(2,1)} custom-call(s32[32]{0:T(128)} %copy-done.5, s32[1]{0:T(128)} %dynamic_slice.32.span_ref, bf16[1024,128]{1,0:T(8,128)(2,1)} %bitcast.37, bf16[32,128,256]{2,1,0:T(8,128)(2,1)} %pad_maximum_fusion.cache_ref, f32[32,128]{1,0:T(8,128)} %fusion.28.bias_ref, bf16[256,128]{1,0:T(8,128)(2,1)} %pad_maximum_fusion.4.nk_ref, ...), custom_call_target="tpu_custom_call" | custom-call | tf_op jit(solution)/shard_map/pallas_call | solution.py:143
  69.2 0.0 all-gather.5.cloned.1.call-start
  69.3 43.6 %reduce-scatter.3.cloned.1.call-done = bf16[256,512]{1,0:T(8,128)(2,1)} async-done(((bf16[256,4096]{1,0:T(8,128)(2,1)}), bf16[256,512]{1,0:T(8,128)(2,1)}) %reduce-scatter.3.cloned.1.call-update) | async-done | bytes 262160 | tf_op jit(solution)/shard_map/reduce_scatter | solution.py:353
  112.8 1.7 add_convert_fusion.1
  114.6 0.2 reduce-scatter.5.cloned.1.call-start
  114.8 0.6 reshape.216
  115.4 27.3 %all-gather.5.cloned.1.call-done.x_ref = bf16[256,4096]{1,0:T(8,128)(2,1)} async-done(((bf16[256,512]{1,0:T(8,128)(2,1)}), bf16[256,4096]{1,0:T(8,128)(2,1)}) %all-gather.5.cloned.1.call-update) | async-done | bytes 2097168 | tf_op jit(solution)/shard_map/all_gather | solution.py:355
  142.8 20.8 %shard_map.177 = bf16[256,4096]{1,0:T(8,128)(2,1)} custom-call(bf16[256,4096]{1,0:T(8,128)(2,1)} %all-gather.5.cloned.1.call-done.x_ref, f32[1,4096]{1,0:T(1,128)} %bitcast.39, bf16[1376,4096]{1,0:T(8,128)(2,1)} %bitcast.35, bf16[1376,4096]{1,0:T(8,128)(2,1)} %bitcast.36, bf16[1376,4096]{1,0:T(8,128)(2,1)} %wd_ref.1), custom_call_target="tpu_custom_call" | custom-call | tf_op jit(solution)/shard_map/pallas_call | solution.py:209
  163.6 0.6 iota_compare_fusion.1
  164.2 0.8 fusion.23
  165.0 34.1 %reduce-scatter.5.cloned.1.call-done = bf16[256,512]{1,0:T(8,128)(2,1)} async-done(((bf16[256,4096]{1,0:T(8,128)(2,1)}), bf16[256,512]{1,0:T(8,128)(2,1)}) %reduce-scatter.5.cloned.1.call-update) | async-done | bytes 262160 | tf_op jit(solution)/shard_map/reduce_scatter | solution.py:356
  199.0 1.8 fusion.6
  (28 shorter events, 0.2 us)
Async XLA Ops:
  7.2 39.2 %copy-start = (bf16[4096,128]{1,0:T(8,128)(2,1)S(1)}, bf16[4096,128]{1,0:T(8,128)(2,1)}, u32[]{:S(2)}) copy-start(bf16[4096,128]{1,0:T(8,128)(2,1)} %param.21) | copy-start | bytes 3145732
  7.2 36.9 %all-gather.3.cloned.1.call-start = ((), (), s32[]{:S(2)}) async-start(), calls=%async_computation.2 | async-start | bytes 2359296 | tf_op jit(solution)/shard_map/all_gather | solution.py:310
  7.9 104.9 %reduce-scatter.3.cloned.1.call-start = ((), (), s32[]{:S(2)}) async-start(), calls=%async_computation.3 | async-start | bytes 2359296 | tf_op jit(solution)/shard_map/reduce_scatter | solution.py:353
  8.6 20.8 %collective-permute-start.2 = (s32[2,8]{1,0:T(2,128)S(1)}, s32[2,8]{1,0:T(2,128)S(1)}, u32[]{:S(2)}, u32[]{:S(2)}) collective-permute-start(s32[2,8]{1,0:T(2,128)S(1)} %pad_add_fusion), channel_id=1, source_target_pairs={{0,24},{8,0},{16,8},{24,16},{1,25},{9,1},{17,9},{25,17},{2,26},{10... | collective-permute-start | bytes 200 | tf_op jit(solution)/shard_map/ppermute | solution.py:266
  12.5 17.0 %collective-permute-start.1 = (s32[2,8]{1,0:T(2,128)S(1)}, s32[2,8]{1,0:T(2,128)S(1)}, u32[]{:S(2)}, u32[]{:S(2)}) collective-permute-start(s32[2,8]{1,0:T(2,128)S(1)} %pad_add_fusion), channel_id=1, source_target_pairs={{0,16},{8,24},{16,0},{24,8},{1,17},{9,25},{17,1},{25,9},{2,18},{10... | collective-permute-start | bytes 200 | tf_op jit(solution)/shard_map/ppermute | solution.py:266
  13.0 16.5 %collective-permute-start = (s32[2,8]{1,0:T(2,128)S(1)}, s32[2,8]{1,0:T(2,128)S(1)}, u32[]{:S(2)}, u32[]{:S(2)}) collective-permute-start(s32[2,8]{1,0:T(2,128)S(1)} %pad_add_fusion), channel_id=1, source_target_pairs={{0,8},{8,16},{16,24},{24,0},{1,9},{9,17},{17,25},{25,1},{2,10},{10... | collective-permute-start | bytes 200 | tf_op jit(solution)/shard_map/ppermute | solution.py:266
  14.8 16.9 %collective-permute-start.5 = (bf16[8,128,256]{2,1,0:T(8,128)(2,1)S(1)}, bf16[8,128,256]{2,1,0:T(8,128)(2,1)S(1)}, u32[]{:S(2)}, u32[]{:S(2)}) collective-permute-start(bf16[8,128,256]{2,1,0:T(8,128)(2,1)S(1)} %pad_maximum_fusion.1), channel_id=1, source_target_pairs={{0,24},{8,0},{16,8},{24,16},{1,25},{9,1},{17,9},{25,17},{2,26},{10... | collective-permute-start | bytes 1572872 | tf_op jit(solution)/shard_map/ppermute | solution.py:266
  17.2 14.5 %collective-permute-start.4 = (bf16[8,128,256]{2,1,0:T(8,128)(2,1)S(1)}, bf16[8,128,256]{2,1,0:T(8,128)(2,1)S(1)}, u32[]{:S(2)}, u32[]{:S(2)}) collective-permute-start(bf16[8,128,256]{2,1,0:T(8,128)(2,1)S(1)} %pad_maximum_fusion.1), channel_id=1, source_target_pairs={{0,16},{8,24},{16,0},{24,8},{1,17},{9,25},{17,1},{25,9},{2,18},{10... | collective-permute-start | bytes 1572872 | tf_op jit(solution)/shard_map/ppermute | solution.py:266
  29.5 13.2 %collective-permute-start.3 = (bf16[8,128,256]{2,1,0:T(8,128)(2,1)S(1)}, bf16[8,128,256]{2,1,0:T(8,128)(2,1)S(1)}, u32[]{:S(2)}, u32[]{:S(2)}) collective-permute-start(bf16[8,128,256]{2,1,0:T(8,128)(2,1)S(1)} %pad_maximum_fusion.1), channel_id=1, source_target_pairs={{0,8},{8,16},{16,24},{24,0},{1,9},{9,17},{17,25},{25,1},{2,10},{10... | collective-permute-start | bytes 1572872 | tf_op jit(solution)/shard_map/ppermute | solution.py:266
  31.0 18.0 %copy-start.5 = (s32[32]{0:T(128)}, s32[32]{0:T(128)S(1)}, u32[]{:S(2)}) copy-start(s32[32]{0:T(128)S(1)} %fusion.29.limit_ref) | copy-start | bytes 388
  44.1 7.5 %copy-start.2 = (bf16[256,4096]{1,0:T(8,128)(2,1)S(1)}, bf16[256,4096]{1,0:T(8,128)(2,1)}, u32[]{:S(2)}) copy-start(bf16[256,4096]{1,0:T(8,128)(2,1)} %all-gather.3.cloned.1.call-done) | copy-start | bytes 6291460
  44.1 7.5 %copy-start.6 = (bf16[4096,512]{1,0:T(8,128)(2,1)S(1)}, bf16[4096,512]{1,0:T(8,128)(2,1)}, u32[]{:S(2)}) copy-start(bf16[4096,512]{1,0:T(8,128)(2,1)} %param.20) | copy-start | bytes 12582916
  49.0 5.5 %collective-permute-start.7 = (bf16[256,128]{1,0:T(8,128)(2,1)S(1)}, bf16[256,128]{1,0:T(8,128)(2,1)S(1)}, u32[]{:S(2)}, u32[]{:S(2)}) collective-permute-start(bf16[256,128]{1,0:T(8,128)(2,1)S(1)} %get-tuple-element.19), channel_id=1, source_target_pairs={{1,3},{2,5},{3,7},{4,1},{5,2},{6,4},{7,6},{9,11},{10,13},{11,15},{... | collective-permute-start | bytes 196616 | tf_op jit(solution)/shard_map/ppermute | solution.py:316
  49.7 8.6 %collective-permute-start.6 = (bf16[256,128]{1,0:T(8,128)(2,1)S(1)}, bf16[256,128]{1,0:T(8,128)(2,1)S(1)}, u32[]{:S(2)}, u32[]{:S(2)}) collective-permute-start(bf16[256,128]{1,0:T(8,128)(2,1)S(1)} %get-tuple-element.19), channel_id=1, source_target_pairs={{0,1},{1,2},{2,4},{3,6},{4,0},{5,3},{6,5},{8,9},{9,10},{10,12},{11... | collective-permute-start | bytes 196616 | tf_op jit(solution)/shard_map/ppermute | solution.py:316
  60.2 52.6 %copy-start.3 = (bf16[256,512]{1,0:T(8,128)(2,1)S(1)}, bf16[256,512]{1,0:T(8,128)(2,1)}, u32[]{:S(2)}) copy-start(bf16[256,512]{1,0:T(8,128)(2,1)} %param.17) | copy-start | bytes 786436
  60.2 54.6 %copy-start.4 = (bf16[4096]{0:T(1024)(128)(2,1)S(1)}, bf16[4096]{0:T(1024)(128)(2,1)}, u32[]{:S(2)}) copy-start(bf16[4096]{0:T(1024)(128)(2,1)} %param.19) | copy-start | bytes 24580
  69.2 73.5 %all-gather.5.cloned.1.call-start = ((), (), s32[]{:S(2)}) async-start(), calls=%async_computation.4 | async-start | bytes 2359296 | tf_op jit(solution)/shard_map/all_gather | solution.py:355
  114.6 84.4 %reduce-scatter.5.cloned.1.call-start = ((), (), s32[]{:S(2)}) async-start(), calls=%async_computation.5 | async-start | bytes 2359296 | tf_op jit(solution)/shard_map/reduce_scatter | solution.py:356
  142.8 56.3 %copy-start.1 = (bf16[256,512]{1,0:T(8,128)(2,1)S(1)}, bf16[256,512]{1,0:T(8,128)(2,1)}, u32[]{:S(2)}) copy-start(bf16[256,512]{1,0:T(8,128)(2,1)} %add_convert_fusion.1) | copy-start | bytes 786436
Sparse Core Ops, SparseCore 0:
  9.6 31.7 all-gather.2
  69.3 43.4 reduce-scatter.2
  115.0 27.6 all-gather.4
  163.8 35.2 reduce-scatter.4

commit v20 on v19

--- a/solution.py
+++ b/solution.py
@@ -201,7 +201,7 @@
 def feed_forward(full_mid, gain, w_gate, w_up, w_down):
     rows, width = full_mid.shape
     units = w_gate.shape[1]
-    chunk = 1024 if width % 1024 == 0 else width
+    chunk = 2048 if width % 2048 == 0 else width
     out_chunk = 2048 if w_down.shape[1] % 2048 == 0 else w_down.shape[1]
     first = width // chunk
     outs = w_down.shape[1] // out_chunk

time: 208 us -> 208 us (level)
  Pallas kernels: 29.8 us -> 39.5 us
  waiting for transfers between devices: 120 us -> 112 us
    pallas_call x1, Pallas kernels: 8.94 us -> 17.7 us  [local_attention(): pl.pallas_call(attn_kernel, out_shape=jax.ShapeDtypeStruct((span_size, wi...]
    reduce_scatter x1, waiting for transfers between devices: 43.6 us -> 34.9 us  [per_device(): lax.psum_scatter(head_term, 'tp', scatter_dimension=1, tiled=True)]
where the time goes in v20:
time: 208 us
  waiting for transfers between devices  112 us (54%)
  Pallas kernels  39.5 us (19%)
  between operations  17.9 us (9%)
  other arithmetic  16.8 us (8%)
  starting transfers between devices  11.9 us (6%)
  local copies, waits for them, and re-layouts  6.6 us (3%)
  matrix products  3.89 us (2%)
    reduce_scatter x1, waiting for transfers between devices, per_device(): lax.psum_scatter(head_term, 'tp', scatter_dimension=1, tiled=True)  34.9 us
    reduce_scatter x1, waiting for transfers between devices, per_device(): lax.psum_scatter(feed_forward(full_mid, mlp_gain, w_gate, w_up, w_down),...  34 us
    all_gather x1, waiting for transfers between devices, per_device(): full_mid = lax.all_gather(mid, 'tp', axis=1, tiled=True)  27.4 us
    pallas_call x1, Pallas kernels, feed_forward(): pl.pallas_call(functools.partial(ffn_kernel, first, chunk), out_shape=jax...  21.8 us
    pallas_call x1, Pallas kernels, local_attention(): pl.pallas_call(attn_kernel, out_shape=jax.ShapeDtypeStruct((span_size, wi...  17.7 us
    ppermute x6, waiting for transfers between devices, gather_ctx(): parts.append(lax.ppermute(value, 'ctx', pairs))  11 us
    ppermute x6, starting transfers between devices, gather_ctx(): parts.append(lax.ppermute(value, 'ctx', pairs))  8.95 us
  transfers between devices with their start and end apart: 12, of which 5 were waited for; matrix products, arithmetic and copies ran while one was open for 8% of the time, Pallas kernels for 0%

profile of v20, /device:TPU:0, one launch (start us, length us, event | category | flops | bytes accessed | tf_op | source)
XLA Modules:
  0.0 208.4 jit_solution(5021517696168909492)
XLA Ops:
  7.2 0.7 all-gather.3.cloned.1.call-update
  7.9 0.0 reduce-scatter.3.cloned.1.call-start
  8.0 0.7 pad_add_fusion
  8.6 3.9 %collective-permute-start.2 = (s32[2,8]{1,0:T(2,128)S(1)}, s32[2,8]{1,0:T(2,128)S(1)}, u32[]{:S(2)}, u32[]{:S(2)}) collective-permute-start(s32[2,8]{1,0:T(2,128)S(1)} %pad_add_fusion), channel_id=1, source_target_pairs={{0,24},{8,0},{16,8},{24,16},{1,25},{9,1},{17,9},{25,17},{2,26},{10... | collective-permute-start | bytes 200 | tf_op jit(solution)/shard_map/ppermute | solution.py:266
  12.5 0.5 collective-permute-start.1
  13.0 0.6 collective-permute-start
  13.6 1.1 constant_dynamic-slice_fusion.1
  14.7 0.1 pad_maximum_fusion.1
  14.8 2.4 %collective-permute-start.5 = (bf16[8,128,256]{2,1,0:T(8,128)(2,1)S(1)}, bf16[8,128,256]{2,1,0:T(8,128)(2,1)S(1)}, u32[]{:S(2)}, u32[]{:S(2)}) collective-permute-start(bf16[8,128,256]{2,1,0:T(8,128)(2,1)S(1)} %pad_maximum_fusion.1), channel_id=1, source_target_pairs={{0,24},{8,0},{16,8},{24,16},{1,25},{9,1},{17,9},{25,17},{2,26},{10... | collective-permute-start | bytes 1572872 | tf_op jit(solution)/shard_map/ppermute | solution.py:266
  17.2 1.5 collective-permute-start.4
  18.7 1.2 dynamic_slice.38
  21.2 1.3 dynamic_slice.36
  23.8 1.2 dynamic_slice.32.span_ref
  25.0 1.2 dynamic_slice.33
  26.3 0.7 convert_element_type.77
  27.6 0.7 add_convert_fusion.3
  28.3 0.5 multiply_cosine_fusion.1
  29.5 0.1 collective-permute-start.3
  29.6 0.8 pad_add_fusion.1
  30.3 0.7 fusion.29.limit_ref
  31.0 0.7 fusion.28.bias_ref
  31.7 11.0 %collective-permute-done.3 = bf16[8,128,256]{2,1,0:T(8,128)(2,1)S(1)} collective-permute-done((bf16[8,128,256]{2,1,0:T(8,128)(2,1)S(1)}, bf16[8,128,256]{2,1,0:T(8,128)(2,1)S(1)}, u32[]{:S(2)}, u32[]{:S(2)}) %collective-permute-start.3) | collective-permute-done | bytes 524320 | tf_op jit(solution)/shard_map/ppermute | solution.py:266
  42.7 1.4 pad_maximum_fusion.cache_ref
  44.1 2.2 %fusion = f32[256]{0:T(256)S(1)} fusion(bf16[256,4096]{1,0:T(8,128)(2,1)} %all-gather.3.cloned.1.call-done), kind=kLoop, calls=%fused_computation.2 | loop fusion | flops 3145472 | bytes 2098176 | tf_op jit(solution)/shard_map/reduce_sum | solution.py:23
  46.4 2.6 %bitcast_convert_fusion = (f32[256,1,128]{2,0,1:T(8,128)S(1)}, bf16[256,128]{1,0:T(8,128)(2,1)S(1)}) fusion(bf16[4096,128]{1,0:T(8,128)(2,1)S(1)} %copy-done, bf16[256,4096]{1,0:T(8,128)(2,1)} %all-gather.3.cloned.1.call-done, f32[4096]{0:T(1024)S(1)} %convert_element_type.77, f32[256]{0:T(256)S(1)} %add_rsqrt_fusion), kind=kOutput, calls=%fused_computation.39 | convolution fusion | flops 272695296 | bytes 3359744 | tf_op jit(solution)/shard_map/dot_general | solution.py:312
  49.0 0.7 collective-permute-start.7
  49.7 2.0 collective-permute-start.6
  51.7 1.3 fusion.4
  53.0 0.2 reshape.210
  53.1 0.3 fusion.30
  53.5 0.1 subtract_convert_fusion
  53.6 0.9 pad_maximum_fusion.2
  54.5 3.7 %collective-permute-done.6 = bf16[256,128]{1,0:T(8,128)(2,1)S(1)} collective-permute-done((bf16[256,128]{1,0:T(8,128)(2,1)S(1)}, bf16[256,128]{1,0:T(8,128)(2,1)S(1)}, u32[]{:S(2)}, u32[]{:S(2)}) %collective-permute-start.6) | collective-permute-done | bytes 65568 | tf_op jit(solution)/shard_map/ppermute | solution.py:316
  58.3 0.7 dynamic-slice_bitcast_fusion
  58.9 0.6 fusion.25
  59.5 0.7 pad_maximum_fusion.4.nk_ref
  60.2 17.7 %shard_map.176 = bf16[256,4096]{1,0:T(8,128)(2,1)} custom-call(s32[32]{0:T(128)} %copy-done.5, s32[1]{0:T(128)} %dynamic_slice.32.span_ref, bf16[1024,128]{1,0:T(8,128)(2,1)} %bitcast.37, bf16[32,128,256]{2,1,0:T(8,128)(2,1)} %pad_maximum_fusion.cache_ref, f32[32,128]{1,0:T(8,128)} %fusion.28.bias_ref, bf16[256,128]{1,0:T(8,128)(2,1)} %pad_maximum_fusion.4.nk_ref, ...), custom_call_target="tpu_custom_call" | custom-call | tf_op jit(solution)/shard_map/pallas_call | solution.py:143
  77.9 0.0 all-gather.5.cloned.1.call-start
  78.0 34.9 %reduce-scatter.3.cloned.1.call-done = bf16[256,512]{1,0:T(8,128)(2,1)} async-done(((bf16[256,4096]{1,0:T(8,128)(2,1)}), bf16[256,512]{1,0:T(8,128)(2,1)}) %reduce-scatter.3.cloned.1.call-update) | async-done | bytes 262160 | tf_op jit(solution)/shard_map/reduce_scatter | solution.py:353
  112.9 1.7 add_convert_fusion.1
  114.6 0.2 reduce-scatter.5.cloned.1.call-start
  114.8 0.6 reshape.216
  115.5 27.4 %all-gather.5.cloned.1.call-done.x_ref = bf16[256,4096]{1,0:T(8,128)(2,1)} async-done(((bf16[256,512]{1,0:T(8,128)(2,1)}), bf16[256,4096]{1,0:T(8,128)(2,1)}) %all-gather.5.cloned.1.call-update) | async-done | bytes 2097168 | tf_op jit(solution)/shard_map/all_gather | solution.py:355
  142.9 21.8 %shard_map.177 = bf16[256,4096]{1,0:T(8,128)(2,1)} custom-call(bf16[256,4096]{1,0:T(8,128)(2,1)} %all-gather.5.cloned.1.call-done.x_ref, f32[1,4096]{1,0:T(1,128)} %bitcast.39, bf16[1376,4096]{1,0:T(8,128)(2,1)} %bitcast.35, bf16[1376,4096]{1,0:T(8,128)(2,1)} %bitcast.36, bf16[1376,4096]{1,0:T(8,128)(2,1)} %wd_ref.1), custom_call_target="tpu_custom_call" | custom-call | tf_op jit(solution)/shard_map/pallas_call | solution.py:209
  164.7 0.6 iota_compare_fusion.1
  165.3 0.8 fusion.23
  166.0 34.0 %reduce-scatter.5.cloned.1.call-done = bf16[256,512]{1,0:T(8,128)(2,1)} async-done(((bf16[256,4096]{1,0:T(8,128)(2,1)}), bf16[256,512]{1,0:T(8,128)(2,1)}) %reduce-scatter.5.cloned.1.call-update) | async-done | bytes 262160 | tf_op jit(solution)/shard_map/reduce_scatter | solution.py:356
  200.1 1.8 fusion.6
  (28 shorter events, 0.2 us)
Async XLA Ops:
  7.2 39.2 %copy-start = (bf16[4096,128]{1,0:T(8,128)(2,1)S(1)}, bf16[4096,128]{1,0:T(8,128)(2,1)}, u32[]{:S(2)}) copy-start(bf16[4096,128]{1,0:T(8,128)(2,1)} %param.21) | copy-start | bytes 3145732
  7.2 36.9 %all-gather.3.cloned.1.call-start = ((), (), s32[]{:S(2)}) async-start(), calls=%async_computation.2 | async-start | bytes 2359296 | tf_op jit(solution)/shard_map/all_gather | solution.py:310
  7.9 105.0 %reduce-scatter.3.cloned.1.call-start = ((), (), s32[]{:S(2)}) async-start(), calls=%async_computation.3 | async-start | bytes 2359296 | tf_op jit(solution)/shard_map/reduce_scatter | solution.py:353
  8.6 20.8 %collective-permute-start.2 = (s32[2,8]{1,0:T(2,128)S(1)}, s32[2,8]{1,0:T(2,128)S(1)}, u32[]{:S(2)}, u32[]{:S(2)}) collective-permute-start(s32[2,8]{1,0:T(2,128)S(1)} %pad_add_fusion), channel_id=1, source_target_pairs={{0,24},{8,0},{16,8},{24,16},{1,25},{9,1},{17,9},{25,17},{2,26},{10... | collective-permute-start | bytes 200 | tf_op jit(solution)/shard_map/ppermute | solution.py:266
  12.5 17.0 %collective-permute-start.1 = (s32[2,8]{1,0:T(2,128)S(1)}, s32[2,8]{1,0:T(2,128)S(1)}, u32[]{:S(2)}, u32[]{:S(2)}) collective-permute-start(s32[2,8]{1,0:T(2,128)S(1)} %pad_add_fusion), channel_id=1, source_target_pairs={{0,16},{8,24},{16,0},{24,8},{1,17},{9,25},{17,1},{25,9},{2,18},{10... | collective-permute-start | bytes 200 | tf_op jit(solution)/shard_map/ppermute | solution.py:266
  13.0 16.5 %collective-permute-start = (s32[2,8]{1,0:T(2,128)S(1)}, s32[2,8]{1,0:T(2,128)S(1)}, u32[]{:S(2)}, u32[]{:S(2)}) collective-permute-start(s32[2,8]{1,0:T(2,128)S(1)} %pad_add_fusion), channel_id=1, source_target_pairs={{0,8},{8,16},{16,24},{24,0},{1,9},{9,17},{17,25},{25,1},{2,10},{10... | collective-permute-start | bytes 200 | tf_op jit(solution)/shard_map/ppermute | solution.py:266
  14.8 16.9 %collective-permute-start.5 = (bf16[8,128,256]{2,1,0:T(8,128)(2,1)S(1)}, bf16[8,128,256]{2,1,0:T(8,128)(2,1)S(1)}, u32[]{:S(2)}, u32[]{:S(2)}) collective-permute-start(bf16[8,128,256]{2,1,0:T(8,128)(2,1)S(1)} %pad_maximum_fusion.1), channel_id=1, source_target_pairs={{0,24},{8,0},{16,8},{24,16},{1,25},{9,1},{17,9},{25,17},{2,26},{10... | collective-permute-start | bytes 1572872 | tf_op jit(solution)/shard_map/ppermute | solution.py:266
  17.2 14.5 %collective-permute-start.4 = (bf16[8,128,256]{2,1,0:T(8,128)(2,1)S(1)}, bf16[8,128,256]{2,1,0:T(8,128)(2,1)S(1)}, u32[]{:S(2)}, u32[]{:S(2)}) collective-permute-start(bf16[8,128,256]{2,1,0:T(8,128)(2,1)S(1)} %pad_maximum_fusion.1), channel_id=1, source_target_pairs={{0,16},{8,24},{16,0},{24,8},{1,17},{9,25},{17,1},{25,9},{2,18},{10... | collective-permute-start | bytes 1572872 | tf_op jit(solution)/shard_map/ppermute | solution.py:266
  29.5 13.2 %collective-permute-start.3 = (bf16[8,128,256]{2,1,0:T(8,128)(2,1)S(1)}, bf16[8,128,256]{2,1,0:T(8,128)(2,1)S(1)}, u32[]{:S(2)}, u32[]{:S(2)}) collective-permute-start(bf16[8,128,256]{2,1,0:T(8,128)(2,1)S(1)} %pad_maximum_fusion.1), channel_id=1, source_target_pairs={{0,8},{8,16},{16,24},{24,0},{1,9},{9,17},{17,25},{25,1},{2,10},{10... | collective-permute-start | bytes 1572872 | tf_op jit(solution)/shard_map/ppermute | solution.py:266
  31.0 18.0 %copy-start.5 = (s32[32]{0:T(128)}, s32[32]{0:T(128)S(1)}, u32[]{:S(2)}) copy-start(s32[32]{0:T(128)S(1)} %fusion.29.limit_ref) | copy-start | bytes 388
  44.1 7.5 %copy-start.2 = (bf16[256,4096]{1,0:T(8,128)(2,1)S(1)}, bf16[256,4096]{1,0:T(8,128)(2,1)}, u32[]{:S(2)}) copy-start(bf16[256,4096]{1,0:T(8,128)(2,1)} %all-gather.3.cloned.1.call-done) | copy-start | bytes 6291460
  44.1 7.5 %copy-start.6 = (bf16[4096,512]{1,0:T(8,128)(2,1)S(1)}, bf16[4096,512]{1,0:T(8,128)(2,1)}, u32[]{:S(2)}) copy-start(bf16[4096,512]{1,0:T(8,128)(2,1)} %param.20) | copy-start | bytes 12582916
  49.0 5.5 %collective-permute-start.7 = (bf16[256,128]{1,0:T(8,128)(2,1)S(1)}, bf16[256,128]{1,0:T(8,128)(2,1)S(1)}, u32[]{:S(2)}, u32[]{:S(2)}) collective-permute-start(bf16[256,128]{1,0:T(8,128)(2,1)S(1)} %get-tuple-element.19), channel_id=1, source_target_pairs={{1,3},{2,5},{3,7},{4,1},{5,2},{6,4},{7,6},{9,11},{10,13},{11,15},{... | collective-permute-start | bytes 196616 | tf_op jit(solution)/shard_map/ppermute | solution.py:316
  49.7 8.6 %collective-permute-start.6 = (bf16[256,128]{1,0:T(8,128)(2,1)S(1)}, bf16[256,128]{1,0:T(8,128)(2,1)S(1)}, u32[]{:S(2)}, u32[]{:S(2)}) collective-permute-start(bf16[256,128]{1,0:T(8,128)(2,1)S(1)} %get-tuple-element.19), channel_id=1, source_target_pairs={{0,1},{1,2},{2,4},{3,6},{4,0},{5,3},{6,5},{8,9},{9,10},{10,12},{11... | collective-permute-start | bytes 196616 | tf_op jit(solution)/shard_map/ppermute | solution.py:316
  60.2 52.6 %copy-start.3 = (bf16[256,512]{1,0:T(8,128)(2,1)S(1)}, bf16[256,512]{1,0:T(8,128)(2,1)}, u32[]{:S(2)}) copy-start(bf16[256,512]{1,0:T(8,128)(2,1)} %param.17) | copy-start | bytes 786436
  60.2 54.6 %copy-start.4 = (bf16[4096]{0:T(1024)(128)(2,1)S(1)}, bf16[4096]{0:T(1024)(128)(2,1)}, u32[]{:S(2)}) copy-start(bf16[4096]{0:T(1024)(128)(2,1)} %param.19) | copy-start | bytes 24580
  77.9 64.9 %all-gather.5.cloned.1.call-start = ((), (), s32[]{:S(2)}) async-start(), calls=%async_computation.4 | async-start | bytes 2359296 | tf_op jit(solution)/shard_map/all_gather | solution.py:355
  114.6 85.5 %reduce-scatter.5.cloned.1.call-start = ((), (), s32[]{:S(2)}) async-start(), calls=%async_computation.5 | async-start | bytes 2359296 | tf_op jit(solution)/shard_map/reduce_scatter | solution.py:356
  142.9 57.2 %copy-start.1 = (bf16[256,512]{1,0:T(8,128)(2,1)S(1)}, bf16[256,512]{1,0:T(8,128)(2,1)}, u32[]{:S(2)}) copy-start(bf16[256,512]{1,0:T(8,128)(2,1)} %add_convert_fusion.1) | copy-start | bytes 786436
Sparse Core Ops, SparseCore 0:
  9.6 31.7 all-gather.2
  78.1 34.7 reduce-scatter.2
  115.0 27.7 all-gather.4
  164.8 35.2 reduce-scatter.4
